TPU v7x, 256 devices: a whole 4x4x8 slice. The times are simulated.
256 devices in a mesh: tp: 8 (over x, core), ha: 8 (over y, z_lo), wa: 4 (over z_hi).
Axes of the slice: x: 4, y: 4, z: 8 (z_hi: 4, z_lo: 2; z = z_hi * 2 + z_lo), core: 2. Of those that a mesh axis runs over, the one named last changes fastest.
Arguments:
- queries: bfloat16 [1, 16, 8, 128, 3072], P(None, 'ha', 'wa', None, 'tp'), may hold values from -128 to 128
- keys: bfloat16 [1, 16, 8, 128, 3072], P(None, 'ha', 'wa', None, 'tp'), may hold values from -4.5 to 4.5
- values: bfloat16 [1, 16, 8, 128, 3072], P(None, 'ha', 'wa', None, 'tp'), may hold values from -6 to 6
- grad_out: bfloat16 [1, 16, 8, 128, 3072], P(None, 'ha', 'wa', None, 'tp'), may hold values from -6 to 6
- out_proj: bfloat16 [3072, 3072], P(('ha', 'wa'), 'tp'), may hold values from -0.109375 to 0.109375
Outputs:
- grad_queries: bfloat16 [1, 16, 8, 128, 3072], P(None, 'ha', 'wa', None, 'tp')
- grad_keys: bfloat16 [1, 16, 8, 128, 3072], P(None, 'ha', 'wa', None, 'tp')
- grad_values: bfloat16 [1, 16, 8, 128, 3072], P(None, 'ha', 'wa', None, 'tp')
All inputs are finite; a program needn't handle non-finite values.
Results may differ from a plain program's by a relative error of at most 0.014.
Values may be sent and summed in bfloat16 or wider, within the bound.
No kernel may reach another device: no remote copies, remote signals or barrier semaphores. Data moves between devices by JAX's collectives and lax.ppermute only.
A program may use at most 128 MiB of HBM per device.

v0:
```python
import jax
import jax.numpy as jnp
from jax import lax
from jax.sharding import PartitionSpec as P

HEAD = 128


def passed_along(value, axis, steps):
    count = lax.axis_size(axis)
    first, last = (max(0, -steps), min(count, count - steps))
    return lax.ppermute(value, axis, [(source, source + steps) for source in range(first, last)])


def extended_2(array, sides, width):
    for axis, dim in sides:
        peers, length = (lax.axis_size(axis), array.shape[dim])
        up = [(i, (i + 1) % peers) for i in range(peers - 1)]
        down = [(j, i) for i, j in up]
        last = lax.slice_in_dim(array, length - width, length, axis=dim)
        first = lax.slice_in_dim(array, 0, width, axis=dim)
        before = lax.ppermute(last, axis, up)
        after = lax.ppermute(first, axis, down)
        array = jnp.concatenate([before, array, after], axis=dim)
    return array


def tile_backward(query_blk, key_blk, value_blk, grad_blk, softmax_scale):
    f32 = jnp.float32
    scores = (
        jnp.einsum("qtd,qld->qtl", query_blk, key_blk, preferred_element_type=f32) * softmax_scale
    )
    scores = scores - jnp.max(scores, axis=-1, keepdims=True)
    expo = jnp.exp(scores)
    probs = expo / jnp.sum(expo, axis=-1, keepdims=True)
    probs_lo = probs.astype(jnp.bfloat16)
    attn = jnp.einsum("qtl,qld->qtd", probs_lo, value_blk, preferred_element_type=f32)
    delta = jnp.sum(grad_blk.astype(f32) * attn, axis=-1, keepdims=True)
    grad_probs = jnp.einsum("qtd,qld->qtl", grad_blk, value_blk, preferred_element_type=f32)
    grad_scores = (probs * (grad_probs - delta) * softmax_scale).astype(jnp.bfloat16)
    grad_query = jnp.einsum("qtl,qld->qtd", grad_scores, key_blk, preferred_element_type=f32)
    grad_key = jnp.einsum("qtl,qtd->qld", grad_scores, query_blk, preferred_element_type=f32)
    grad_value = jnp.einsum("qtl,qtd->qld", probs_lo, grad_blk, preferred_element_type=f32)
    return (grad_query, grad_key, grad_value)


def fold_cols(totals):
    from_left = passed_along(totals[:, :, :, -1].astype(jnp.bfloat16), "wa", 1).astype(jnp.float32)
    from_right = passed_along(totals[:, :, :, 0].astype(jnp.bfloat16), "wa", -1).astype(jnp.float32)
    inner = totals[:, :, :, 1:-1]
    inner = inner.at[:, :, :, 0].add(from_left)
    return inner.at[:, :, :, -1].add(from_right)


def fold_rows(totals):
    from_above = passed_along(totals[:, :, -1].astype(jnp.bfloat16), "ha", 1).astype(jnp.float32)
    from_below = passed_along(totals[:, :, 0].astype(jnp.bfloat16), "ha", -1).astype(jnp.float32)
    inner = totals[:, :, 1:-1]
    inner = inner.at[:, :, 0].add(from_above)
    return inner.at[:, :, -1].add(from_below)


def local(queries, keys, values, grad_out, out_proj):
    frames, tile_rows, tile_cols, tile_len, columns = queries.shape
    head_count = columns // HEAD
    whole = lax.all_gather(grad_out, "tp", axis=4, tiled=True)
    flat_rows = whole.reshape(-1, whole.shape[-1])
    grad_attn = jnp.dot(
        flat_rows,
        lax.all_gather(out_proj, ("ha", "wa"), axis=0, tiled=True),
        preferred_element_type=jnp.float32,
    )
    grad_attn = grad_attn.astype(jnp.bfloat16).reshape(queries.shape)
    stacked = jnp.stack([keys, values])
    extended = extended_2(stacked, (("ha", 2), ("wa", 3)), 1)
    row_base = lax.axis_index("ha") * tile_rows
    col_base = lax.axis_index("wa") * tile_cols
    rows_all = tile_rows * lax.axis_size("ha")
    cols_all = tile_cols * lax.axis_size("wa")
    span = min(3, frames)
    grid_f, grid_r, grid_c = jnp.meshgrid(
        jnp.arange(frames, dtype=jnp.int32),
        jnp.arange(tile_rows, dtype=jnp.int32),
        jnp.arange(tile_cols, dtype=jnp.int32),
        indexing="ij",
    )
    start_f = jnp.clip(grid_f.reshape(-1) - 1, 0, frames - span).astype(jnp.int32)
    start_r = (jnp.clip(row_base + grid_r.reshape(-1) - 1, 0, rows_all - 3) - row_base + 1).astype(
        jnp.int32
    )
    start_c = (jnp.clip(col_base + grid_c.reshape(-1) - 1, 0, cols_all - 3) - col_base + 1).astype(
        jnp.int32
    )
    tile_count = start_f.shape[0]
    zero_idx = jnp.zeros((), jnp.int32)
    softmax_scale = HEAD ** (-0.5)
    grad_q_parts = []
    total_parts = []
    for head_idx in range(head_count):
        lower = head_idx * HEAD
        both = extended[..., lower : lower + HEAD]

        def take(first, second, third):
            return lax.dynamic_slice(
                both,
                (zero_idx, first, second, third, zero_idx, zero_idx),
                (2, span, 3, 3, tile_len, HEAD),
            )

        window = jax.vmap(take)(start_f, start_r, start_c)
        key_blk = window[:, 0].reshape(tile_count, -1, HEAD)
        value_blk = window[:, 1].reshape(tile_count, -1, HEAD)
        query_blk = queries[..., lower : lower + HEAD].reshape(tile_count, tile_len, HEAD)
        grad_blk = grad_attn[..., lower : lower + HEAD].reshape(tile_count, tile_len, HEAD)
        grad_query, grad_key, grad_value = tile_backward(
            query_blk, key_blk, value_blk, grad_blk, softmax_scale
        )
        pieces = jnp.stack([grad_key, grad_value], 1).reshape(
            tile_count, 2, span, 3, 3, tile_len, HEAD
        )
        totals = jnp.zeros((2, frames, tile_rows + 2, tile_cols + 2, tile_len, HEAD), jnp.float32)

        def add_one(index, totals):
            start = (zero_idx, start_f[index], start_r[index], start_c[index], zero_idx, zero_idx)
            current = lax.dynamic_slice(totals, start, (2, span, 3, 3, tile_len, HEAD))
            return lax.dynamic_update_slice(totals, current + pieces[index], start)

        total_parts.append(lax.fori_loop(0, tile_count, add_one, totals))
        grad_q_parts.append(grad_query.reshape(frames, tile_rows, tile_cols, tile_len, HEAD))
    grad_queries = jnp.concatenate(grad_q_parts, axis=-1).astype(jnp.bfloat16)
    totals = jnp.concatenate(total_parts, axis=-1)
    folded = fold_rows(fold_cols(totals))
    return (grad_queries, folded[0].astype(jnp.bfloat16), folded[1].astype(jnp.bfloat16))


def solution(mesh):
    in_specs = (
        P(None, "ha", "wa", None, "tp"),
        P(None, "ha", "wa", None, "tp"),
        P(None, "ha", "wa", None, "tp"),
        P(None, "ha", "wa", None, "tp"),
        P(("ha", "wa"), "tp"),
    )
    out_specs = (
        P(None, "ha", "wa", None, "tp"),
        P(None, "ha", "wa", None, "tp"),
        P(None, "ha", "wa", None, "tp"),
    )
    return jax.shard_map(local, mesh=mesh, in_specs=in_specs, out_specs=out_specs, check_vma=False)
```

profile of v0, /device:TPU:64, one launch (start us, length us, event | category | flops | bytes accessed | tf_op | source)
XLA Modules:
  0.0 426.3 jit_solution(2551073699201183226)
XLA Ops:
  11.3 4.6 %collective-permute-start = (bf16[2,1,1,2,128,384]{5,4,0,1,3,2:T(8,128)(2,1)S(1)}, bf16[2,1,1,2,128,384]{5,4,0,1,3,2:T(8,128)(2,1)S(1)}, u32[]{:S(2)}, u32[]{:S(2)}) collective-permute-start(bf16[2,1,1,2,128,384]{5,4,0,1,3,2:T(8,128)(2,1)S(1)} %get-tuple-element.416), channel_id=1, source_target_pairs={{0,4},{4,8},{8,12},{12,16},{16,20},{20,24},{24,28},{1,5},{5,9},{9,... | collective-permute-start | bytes 1179656 | tf_op jit(solution)/shard_map/ppermute | solution.py:22
  15.8 8.0 %collective-permute-done.1 = bf16[2,1,1,2,128,384]{5,4,0,1,3,2:T(8,128)(2,1)S(1)} collective-permute-done((bf16[2,1,1,2,128,384]{5,4,0,1,3,2:T(8,128)(2,1)S(1)}, bf16[2,1,1,2,128,384]{5,4,0,1,3,2:T(8,128)(2,1)S(1)}, u32[]{:S(2)}, u32[]{:S(2)}) %collective-permute-start.1) | collective-permute-done | bytes 393248 | tf_op jit(solution)/shard_map/ppermute | solution.py:23
  30.4 7.0 %collective-permute-start.2 = (bf16[2,1,4,1,128,384]{5,4,0,1,3,2:T(8,128)(2,1)}, bf16[2,1,4,1,128,384]{5,4,0,1,3,2:T(8,128)(2,1)S(1)}, u32[]{:S(2)}, u32[]{:S(2)}) collective-permute-start(bf16[2,1,4,1,128,384]{5,4,0,1,3,2:T(8,128)(2,1)} %get-tuple-element.412), channel_id=1, source_target_pairs={{0,1},{1,2},{2,3},{4,5},{5,6},{6,7},{8,9},{9,10},{10,11},{12,13},{... | collective-permute-start | bytes 2359304 | tf_op jit(solution)/shard_map/ppermute | solution.py:22
  39.7 12.6 %collective-permute-done.3 = bf16[2,1,4,1,128,384]{5,4,0,1,3,2:T(8,128)(2,1)S(1)} collective-permute-done((bf16[2,1,4,1,128,384]{5,4,0,1,3,2:T(8,128)(2,1)}, bf16[2,1,4,1,128,384]{5,4,0,1,3,2:T(8,128)(2,1)S(1)}, u32[]{:S(2)}, u32[]{:S(2)}) %collective-permute-start.3) | collective-permute-done | bytes 786464 | tf_op jit(solution)/shard_map/ppermute | solution.py:23
  61.7 3.6 fusion.61
  68.4 4.3 fusion.65
  77.3 106.3 %all-gather.5.cloned.1.call-done = bf16[3072,384]{1,0:T(8,128)(2,1)} async-done(((bf16[96,384]{1,0:T(8,128)(2,1)}), bf16[3072,384]{1,0:T(8,128)(2,1)}) %all-gather.5.cloned.1.call-update) | async-done | bytes 2359312 | tf_op jit(solution)/shard_map/all_gather | solution.py:70
  183.7 32.8 %all-gather.3.cloned.1.call-done = bf16[1,2,2,128,3072]{4,3,2,1,0:T(8,128)(2,1)} async-done(((bf16[1,2,2,128,384]{4,3,2,1,0:T(8,128)(2,1)}), bf16[1,2,2,128,3072]{4,3,2,1,0:T(8,128)(2,1)}) %all-gather.3.cloned.1.call-update) | async-done | bytes 3145744 | tf_op jit(solution)/shard_map/all_gather | solution.py:66
  216.4 4.4 %convolution_convert_fusion = bf16[512,384]{1,0:T(8,128)(2,1)S(1)} fusion(bf16[512,3072]{1,0:T(8,128)(2,1)} %bitcast.264, bf16[3072,384]{1,0:T(8,128)(2,1)} %all-gather.5.cloned.1.call-done), kind=kOutput, calls=%fused_computation.47 | convolution fusion | flops 1208156160 | bytes 5898240 | tf_op jit(solution)/shard_map/dot_general | solution.py:68
  221.6 4.0 fusion.49
  225.6 3.4 fusion.29
  229.0 3.6 fusion.52
  232.6 3.0 fusion.28
  235.7 3.6 fusion.55
  248.8 26.2 %while.45 = (s32[]{:T(128)}, f32[2,1,4,4,128,128]{5,4,3,2,1,0:T(8,128)S(1)}, s32[4]{0:T(128)S(1)}, s32[4]{0:T(128)S(1)}, f32[4,2,1,3,3,128,128]{6,5,4,3,1,2,0:T(8,128)}, /*index=5*/s32[]{:T(128)}, s32[]{:T(128)}, s32[]{:T(128)}) while((s32[]{:T(128)}, f32[2,1,4,4,128,128]{5,4,3,2,1,0:T(8,128)S(1)}, s32[4]{0:T(128)S(1)}, s32[4]{0:T(128)S(1)}, ...), condition=%wide.region_14.15_spmd, body=%wide.region_13.14_spmd.sunk | while | flops 294920 | bytes 3539141 | solution.py:128
  275.0 3.4 fusion.22
  283.5 26.2 %while.44 = (s32[]{:T(128)}, f32[2,1,4,4,128,128]{5,4,3,2,1,0:T(8,128)S(1)}, s32[4]{0:T(128)S(1)}, s32[4]{0:T(128)S(1)}, f32[4,2,1,3,3,128,128]{6,5,4,3,1,2,0:T(8,128)}, /*index=5*/s32[]{:T(128)}, s32[]{:T(128)}, s32[]{:T(128)}) while((s32[]{:T(128)}, f32[2,1,4,4,128,128]{5,4,3,2,1,0:T(8,128)S(1)}, s32[4]{0:T(128)S(1)}, s32[4]{0:T(128)S(1)}, ...), condition=%wide.region_12.13_spmd, body=%wide.region_11.12_spmd.sunk | while | flops 294920 | bytes 3539141 | solution.py:128
  309.7 3.3 fusion.23
  318.1 26.2 %while.43 = (s32[]{:T(128)}, f32[2,1,4,4,128,128]{5,4,3,2,1,0:T(8,128)S(1)}, s32[4]{0:T(128)S(1)}, s32[4]{0:T(128)S(1)}, f32[4,2,1,3,3,128,128]{6,5,4,3,1,2,0:T(8,128)}, /*index=5*/s32[]{:T(128)}, s32[]{:T(128)}, s32[]{:T(128)}) while((s32[]{:T(128)}, f32[2,1,4,4,128,128]{5,4,3,2,1,0:T(8,128)S(1)}, s32[4]{0:T(128)S(1)}, s32[4]{0:T(128)S(1)}, ...), condition=%wide.region_10.11_spmd, body=%wide.region_9.10_spmd.sunk | while | flops 294920 | bytes 3539141 | solution.py:128
  347.3 5.6 %collective-permute-start.4 = (bf16[2,1,4,128,384]{4,3,0,2,1:T(8,128)(2,1)}, bf16[2,1,4,128,384]{4,3,0,2,1:T(8,128)(2,1)}, u32[]{:S(2)}, u32[]{:S(2)}) collective-permute-start(bf16[2,1,4,128,384]{4,3,0,2,1:T(8,128)(2,1)} %get-tuple-element.400), channel_id=1, source_target_pairs={{0,1},{1,2},{2,3},{4,5},{5,6},{6,7},{8,9},{9,10},{10,11},{12,13},{... | collective-permute-start | bytes 2359304 | tf_op jit(solution)/shard_map/ppermute | solution.py:12
  361.2 26.1 %collective-permute-done.4 = bf16[2,1,4,128,384]{4,3,0,2,1:T(8,128)(2,1)} collective-permute-done((bf16[2,1,4,128,384]{4,3,0,2,1:T(8,128)(2,1)}, bf16[2,1,4,128,384]{4,3,0,2,1:T(8,128)(2,1)}, u32[]{:S(2)}, u32[]{:S(2)}) %collective-permute-start.4) | collective-permute-done | bytes 786464 | tf_op jit(solution)/shard_map/ppermute | solution.py:12
  388.8 4.6 %collective-permute-done.5 = bf16[2,1,4,128,384]{4,3,0,2,1:T(8,128)(2,1)} collective-permute-done((bf16[2,1,4,128,384]{4,3,0,2,1:T(8,128)(2,1)}, bf16[2,1,4,128,384]{4,3,0,2,1:T(8,128)(2,1)}, u32[]{:S(2)}, u32[]{:S(2)}) %collective-permute-start.5) | collective-permute-done | bytes 786464 | tf_op jit(solution)/shard_map/ppermute | solution.py:12
  395.9 4.1 collective-permute-start.6
  407.4 10.9 %collective-permute-done.7 = bf16[2,1,2,128,384]{4,3,2,0,1:T(8,128)(2,1)S(1)} collective-permute-done((bf16[2,1,2,128,384]{4,3,2,0,1:T(8,128)(2,1)}, bf16[2,1,2,128,384]{4,3,2,0,1:T(8,128)(2,1)S(1)}, u32[]{:S(2)}, u32[]{:S(2)}) %collective-permute-start.7) | collective-permute-done | bytes 393248 | tf_op jit(solution)/shard_map/ppermute | solution.py:12
  (158 shorter events, 105.7 us)
Async XLA Ops:
  7.2 176.5 %all-gather.5.cloned.1.call-start = ((), (), s32[]{:S(2)}) async-start(), calls=%async_computation.1 | async-start | bytes 2433024 | tf_op jit(solution)/shard_map/all_gather | solution.py:70
  7.9 208.5 %all-gather.3.cloned.1.call-start = ((), (), s32[]{:S(2)}) async-start(), calls=%async_computation | async-start | bytes 3538944 | tf_op jit(solution)/shard_map/all_gather | solution.py:66
  10.0 13.9 %collective-permute-start.1 = (bf16[2,1,1,2,128,384]{5,4,0,1,3,2:T(8,128)(2,1)S(1)}, bf16[2,1,1,2,128,384]{5,4,0,1,3,2:T(8,128)(2,1)S(1)}, u32[]{:S(2)}, u32[]{:S(2)}) collective-permute-start(bf16[2,1,1,2,128,384]{5,4,0,1,3,2:T(8,128)(2,1)S(1)} %get-tuple-element.417), channel_id=1, source_target_pairs={{4,0},{8,4},{12,8},{16,12},{20,16},{24,20},{28,24},{5,1},{9,5},{13... | collective-permute-start | bytes 1179656 | tf_op jit(solution)/shard_map/ppermute | solution.py:23
  11.3 14.5 %collective-permute-start = (bf16[2,1,1,2,128,384]{5,4,0,1,3,2:T(8,128)(2,1)S(1)}, bf16[2,1,1,2,128,384]{5,4,0,1,3,2:T(8,128)(2,1)S(1)}, u32[]{:S(2)}, u32[]{:S(2)}) collective-permute-start(bf16[2,1,1,2,128,384]{5,4,0,1,3,2:T(8,128)(2,1)S(1)} %get-tuple-element.416), channel_id=1, source_target_pairs={{0,4},{4,8},{8,12},{12,16},{16,20},{20,24},{24,28},{1,5},{5,9},{9,... | collective-permute-start | bytes 1179656 | tf_op jit(solution)/shard_map/ppermute | solution.py:22
  27.1 27.5 %copy-start.12 = (bf16[1,2,2,128,384]{4,3,2,1,0:T(8,128)(2,1)S(1)}, bf16[1,2,2,128,384]{4,3,2,1,0:T(8,128)(2,1)}, u32[]{:S(2)}) copy-start(bf16[1,2,2,128,384]{4,3,2,1,0:T(8,128)(2,1)} %param.20) | copy-start | bytes 1179652
  27.1 27.5 %copy-start.13 = (bf16[1,2,2,128,384]{4,3,2,1,0:T(8,128)(2,1)S(1)}, bf16[1,2,2,128,384]{4,3,2,1,0:T(8,128)(2,1)}, u32[]{:S(2)}) copy-start(bf16[1,2,2,128,384]{4,3,2,1,0:T(8,128)(2,1)} %param.21) | copy-start | bytes 1179652
  28.5 23.8 %collective-permute-start.3 = (bf16[2,1,4,1,128,384]{5,4,0,1,3,2:T(8,128)(2,1)}, bf16[2,1,4,1,128,384]{5,4,0,1,3,2:T(8,128)(2,1)S(1)}, u32[]{:S(2)}, u32[]{:S(2)}) collective-permute-start(bf16[2,1,4,1,128,384]{5,4,0,1,3,2:T(8,128)(2,1)} %get-tuple-element.413), channel_id=1, source_target_pairs={{1,0},{2,1},{3,2},{5,4},{6,5},{7,6},{9,8},{10,9},{11,10},{13,12},{... | collective-permute-start | bytes 2359304 | tf_op jit(solution)/shard_map/ppermute | solution.py:23
  30.4 24.2 %collective-permute-start.2 = (bf16[2,1,4,1,128,384]{5,4,0,1,3,2:T(8,128)(2,1)}, bf16[2,1,4,1,128,384]{5,4,0,1,3,2:T(8,128)(2,1)S(1)}, u32[]{:S(2)}, u32[]{:S(2)}) collective-permute-start(bf16[2,1,4,1,128,384]{5,4,0,1,3,2:T(8,128)(2,1)} %get-tuple-element.412), channel_id=1, source_target_pairs={{0,1},{1,2},{2,3},{4,5},{5,6},{6,7},{8,9},{9,10},{10,11},{12,13},{... | collective-permute-start | bytes 2359304 | tf_op jit(solution)/shard_map/ppermute | solution.py:22
  39.7 35.3 %copy-start.20 = (bf16[1,2,2,128,128]{4,3,2,1,0:T(8,128)(2,1)}, bf16[1,2,2,128,128]{4,3,2,1,0:T(8,128)(2,1)S(1)}, u32[]{:S(2)}) copy-start(bf16[1,2,2,128,128]{4,3,2,1,0:T(8,128)(2,1)S(1)} %get-tuple-element.418) | copy-start | bytes 393220
  68.4 4.3 %copy-start.10 = (bf16[4,1,1,3,3,128,128]{6,5,1,4,3,0,2:T(8,128)(2,1)S(1)}, bf16[4,1,1,3,3,128,128]{6,5,1,4,3,0,2:T(8,128)(2,1)}, u32[]{:S(2)}) copy-start(bf16[4,1,1,3,3,128,128]{6,5,1,4,3,0,2:T(8,128)(2,1)} %get-tuple-element.406) | copy-start | bytes 3538948
  68.4 4.3 %copy-start.22 = (bf16[1,2,2,128,128]{4,3,2,1,0:T(8,128)(2,1)S(1)}, bf16[1,2,2,128,128]{4,3,2,1,0:T(8,128)(2,1)}, u32[]{:S(2)}) copy-start(bf16[1,2,2,128,128]{4,3,2,1,0:T(8,128)(2,1)} %get-tuple-element.420) | copy-start | bytes 393220
  221.6 4.0 copy-start.19
  235.7 3.6 copy-start.21
  235.7 3.6 copy-start.26
  283.4 26.3 %copy-start.27 = (f32[4,128]{1,0:T(4,128)S(1)}, f32[4,128]{1,0:T(4,128)}, u32[]{:S(2)}) copy-start(f32[4,128]{1,0:T(4,128)} %fusion.27) | copy-start | bytes 6148
  344.3 8.7 %copy-start.11 = (bf16[4,1,1,3,3,128,128]{6,5,1,4,3,0,2:T(8,128)(2,1)S(1)}, bf16[4,1,1,3,3,128,128]{6,5,1,4,3,0,2:T(8,128)(2,1)}, u32[]{:S(2)}) copy-start(bf16[4,1,1,3,3,128,128]{6,5,1,4,3,0,2:T(8,128)(2,1)} %get-tuple-element.408) | copy-start | bytes 3538948
  347.3 39.9 %collective-permute-start.4 = (bf16[2,1,4,128,384]{4,3,0,2,1:T(8,128)(2,1)}, bf16[2,1,4,128,384]{4,3,0,2,1:T(8,128)(2,1)}, u32[]{:S(2)}, u32[]{:S(2)}) collective-permute-start(bf16[2,1,4,128,384]{4,3,0,2,1:T(8,128)(2,1)} %get-tuple-element.400), channel_id=1, source_target_pairs={{0,1},{1,2},{2,3},{4,5},{5,6},{6,7},{8,9},{9,10},{10,11},{12,13},{... | collective-permute-start | bytes 2359304 | tf_op jit(solution)/shard_map/ppermute | solution.py:12
  353.7 39.7 %collective-permute-start.5 = (bf16[2,1,4,128,384]{4,3,0,2,1:T(8,128)(2,1)}, bf16[2,1,4,128,384]{4,3,0,2,1:T(8,128)(2,1)}, u32[]{:S(2)}, u32[]{:S(2)}) collective-permute-start(bf16[2,1,4,128,384]{4,3,0,2,1:T(8,128)(2,1)} %get-tuple-element.399), channel_id=1, source_target_pairs={{1,0},{2,1},{3,2},{5,4},{6,5},{7,6},{9,8},{10,9},{11,10},{13,12},{... | collective-permute-start | bytes 2359304 | tf_op jit(solution)/shard_map/ppermute | solution.py:12
  360.9 26.4 %copy-start.1 = (f32[2,1,4,4,128,128]{5,4,3,2,1,0:T(8,128)S(1)}, f32[2,1,4,4,128,128]{5,4,3,2,1,0:T(8,128)}, u32[]{:S(2)}) copy-start(f32[2,1,4,4,128,128]{5,4,3,2,1,0:T(8,128)} %copy-done) | copy-start | bytes 6291460
  360.9 26.4 %copy-start.3 = (f32[2,1,4,4,128,128]{5,4,3,2,1,0:T(8,128)S(1)}, f32[2,1,4,4,128,128]{5,4,3,2,1,0:T(8,128)}, u32[]{:S(2)}) copy-start(f32[2,1,4,4,128,128]{5,4,3,2,1,0:T(8,128)} %copy-done.2) | copy-start | bytes 6291460
  394.7 5.3 %copy-start.7 = (bf16[4,128,1152]{1,2,0:T(8,128)(2,1)S(1)}, bf16[4,128,1152]{1,2,0:T(8,128)(2,1)}, u32[]{:S(2)}) copy-start(bf16[4,128,1152]{1,2,0:T(8,128)(2,1)} %copy-done.6) | copy-start | bytes 3538948
  394.7 5.3 %copy-start.9 = (bf16[4,1,1,3,3,128,128]{6,5,1,4,3,0,2:T(8,128)(2,1)S(1)}, bf16[4,1,1,3,3,128,128]{6,5,1,4,3,0,2:T(8,128)(2,1)}, u32[]{:S(2)}) copy-start(bf16[4,1,1,3,3,128,128]{6,5,1,4,3,0,2:T(8,128)(2,1)} %get-tuple-element.404) | copy-start | bytes 3538948
  395.9 10.3 %collective-permute-start.6 = (bf16[2,1,2,128,384]{4,3,2,0,1:T(8,128)(2,1)}, bf16[2,1,2,128,384]{4,3,2,0,1:T(8,128)(2,1)}, u32[]{:S(2)}, u32[]{:S(2)}) collective-permute-start(bf16[2,1,2,128,384]{4,3,2,0,1:T(8,128)(2,1)} %get-tuple-element.411), channel_id=1, source_target_pairs={{0,4},{4,8},{8,12},{12,16},{16,20},{20,24},{24,28},{1,5},{5,9},{9,... | collective-permute-start | bytes 1179656 | tf_op jit(solution)/shard_map/ppermute | solution.py:12
  401.4 17.0 %collective-permute-start.7 = (bf16[2,1,2,128,384]{4,3,2,0,1:T(8,128)(2,1)}, bf16[2,1,2,128,384]{4,3,2,0,1:T(8,128)(2,1)S(1)}, u32[]{:S(2)}, u32[]{:S(2)}) collective-permute-start(bf16[2,1,2,128,384]{4,3,2,0,1:T(8,128)(2,1)} %get-tuple-element.410), channel_id=1, source_target_pairs={{4,0},{8,4},{12,8},{16,12},{20,16},{24,20},{28,24},{5,1},{9,5},{13... | collective-permute-start | bytes 1179656 | tf_op jit(solution)/shard_map/ppermute | solution.py:12
  (14 other events, 35.4 us)
Sparse Core Ops, SparseCore 0:
  9.8 173.8 all-gather.4
  185.5 30.8 all-gather.2
where the time goes:
time: 428 us; the launch traced here: 426 us
  waiting for transfers between devices  209 us (49%)
  matrix products  47.1 us (11%)
  loops' own time  46.9 us (11%)
  local copies, waits for them, and re-layouts  40.8 us (10%)
  other arithmetic  40.5 us (9%)
  starting transfers between devices  27.8 us (6%)
  between operations  14.5 us (3%)
    all_gather x1, waiting for transfers between devices, local(): lax.all_gather(out_proj, ('ha', 'wa'), axis=0, tiled=True)  106 us
    another operation x3, loops' own time, local(): total_parts.append(lax.fori_loop(0, tile_count, add_one, totals))  46.9 us
    ppermute x4, waiting for transfers between devices, passed_along(): lax.ppermute(value, axis, [(source, source + steps) for source in range(f...  43.4 us
    all_gather x1, waiting for transfers between devices, local(): whole = lax.all_gather(grad_out, 'tp', axis=4, tiled=True)  32.8 us
    ppermute x2, waiting for transfers between devices, extended_2(): after = lax.ppermute(first, axis, down)  20.6 us
    dynamic_update_slice x12, other arithmetic, add_one(): return lax.dynamic_update_slice(totals, current + pieces[index], start)  17.7 us
    ppermute x4, starting transfers between devices, passed_along(): lax.ppermute(value, axis, [(source, source + steps) for source in range(f...  13 us
    ppermute x2, starting transfers between devices, extended_2(): before = lax.ppermute(last, axis, up)  11.5 us
  transfers between devices with their start and end apart: 10, of which 10 were waited for; matrix products, arithmetic and copies ran while one was open for 10% of the time, Pallas kernels for 0%

commit v1 on v0

v1 whole, which is shorter than its diff:
```python
import jax
import jax.numpy as jnp
from jax import lax
from jax.sharding import PartitionSpec as P

HEAD = 128


def doubling_gather(block, steps):
    sizes = {"ha": lax.axis_size("ha"), "wa": lax.axis_size("wa")}
    index = {"ha": lax.axis_index("ha"), "wa": lax.axis_index("wa")}
    buf = block
    for axis, bit in steps:
        count = sizes[axis]
        other = lax.ppermute(buf, axis, [(i, i ^ bit) for i in range(count)])
        low = (index[axis] // bit) % 2 == 0
        buf = jnp.where(low, jnp.concatenate([buf, other], 0), jnp.concatenate([other, buf], 0))
    return buf


def gather_rows(out_proj):
    ha, wa = lax.axis_size("ha"), lax.axis_size("wa")
    ha_bits = [1 << b for b in range(ha.bit_length() - 1)]
    wa_bits = [1 << b for b in range(wa.bit_length() - 1)]
    steps = [("wa", b) for b in reversed(wa_bits)] + [("ha", b) for b in reversed(ha_bits)]
    buf = doubling_gather(out_proj, steps)
    rows, cols = out_proj.shape
    order = list(reversed(steps))
    buf = buf.reshape([2] * len(steps) + [rows, cols])
    natural = [("ha", b) for b in reversed(ha_bits)] + [("wa", b) for b in reversed(wa_bits)]
    perm = [order.index(s) for s in natural] + [len(steps), len(steps) + 1]
    return buf.transpose(perm).reshape(-1, cols)


def pick(length, d):
    if d < 0:
        return slice(length - 1, length)
    if d > 0:
        return slice(0, 1)
    return slice(0, length)


def neighbour_pairs(d_r, d_c):
    ha, wa = lax.axis_size("ha"), lax.axis_size("wa")
    pairs = []
    for i in range(ha):
        for j in range(wa):
            ti, tj = i - d_r, j - d_c
            if 0 <= ti < ha and 0 <= tj < wa:
                pairs.append((i * wa + j, ti * wa + tj))
    return pairs


DIRS = [(-1, -1), (-1, 0), (-1, 1), (0, -1), (0, 1), (1, -1), (1, 0), (1, 1)]


def extended(stacked):
    _, _, rows, cols = stacked.shape[:4]
    out = jnp.pad(stacked, ((0, 0), (0, 0), (1, 1), (1, 1), (0, 0), (0, 0)))
    for d_r, d_c in DIRS:
        piece = stacked[:, :, pick(rows, d_r), pick(cols, d_c)]
        got = lax.ppermute(piece, ("ha", "wa"), neighbour_pairs(d_r, d_c))
        r0 = 0 if d_r < 0 else (rows + 1 if d_r > 0 else 1)
        c0 = 0 if d_c < 0 else (cols + 1 if d_c > 0 else 1)
        out = lax.dynamic_update_slice(out, got, (0, 0, r0, c0, 0, 0))
    return out


def folded(totals):
    rows, cols = totals.shape[2] - 2, totals.shape[3] - 2
    own = totals[:, :, 1:-1, 1:-1]
    for d_r, d_c in DIRS:
        r0 = 0 if d_r < 0 else (rows + 1 if d_r > 0 else 1)
        c0 = 0 if d_c < 0 else (cols + 1 if d_c > 0 else 1)
        nr = rows if d_r == 0 else 1
        nc = cols if d_c == 0 else 1
        piece = totals[:, :, r0 : r0 + nr, c0 : c0 + nc].astype(jnp.bfloat16)
        got = lax.ppermute(piece, ("ha", "wa"), neighbour_pairs(-d_r, -d_c)).astype(jnp.float32)
        rs, cs = pick(rows, d_r), pick(cols, d_c)
        own = own.at[:, :, rs, cs].add(got)
    return own


def local(queries, keys, values, grad_out, out_proj):
    frames, tile_rows, tile_cols, tile_len, columns = queries.shape
    heads = columns // HEAD
    f32, bf16 = jnp.float32, jnp.bfloat16
    whole = lax.all_gather(grad_out, "tp", axis=4, tiled=True)
    weight = gather_rows(out_proj)
    ext = extended(jnp.stack([keys, values]))
    ext_r, ext_c = tile_rows + 2, tile_cols + 2
    row_base = lax.axis_index("ha") * tile_rows
    col_base = lax.axis_index("wa") * tile_cols
    rows_all = tile_rows * lax.axis_size("ha")
    cols_all = tile_cols * lax.axis_size("wa")
    qr = jnp.arange(tile_rows, dtype=jnp.int32)
    qc = jnp.arange(tile_cols, dtype=jnp.int32)
    sr = jnp.clip(row_base + qr - 1, 0, rows_all - 3) - row_base + 1
    sc = jnp.clip(col_base + qc - 1, 0, cols_all - 3) - col_base + 1
    kr = jnp.arange(ext_r, dtype=jnp.int32)
    kc = jnp.arange(ext_c, dtype=jnp.int32)
    in_r = (kr[None, :] >= sr[:, None]) & (kr[None, :] < sr[:, None] + 3)
    in_c = (kc[None, :] >= sc[:, None]) & (kc[None, :] < sc[:, None] + 3)
    inside = in_r[:, None, :, None] & in_c[None, :, None, :]
    inside = inside.reshape(tile_rows * tile_cols, 1, ext_r * ext_c, 1)
    inside = jnp.broadcast_to(inside, (tile_rows * tile_cols, 1, ext_r * ext_c, tile_len))
    inside = inside.reshape(tile_rows * tile_cols, 1, 1, ext_r * ext_c * tile_len)
    q_tiles = tile_rows * tile_cols
    keys_n = ext_r * ext_c * tile_len
    scale = HEAD ** (-0.5)

    key_e = ext[0].reshape(keys_n, heads, HEAD)
    val_e = ext[1].reshape(keys_n, heads, HEAD)
    query = queries.reshape(q_tiles, tile_len, heads, HEAD)

    scores = jnp.einsum("qthd,lhd->qhtl", query, key_e, preferred_element_type=f32) * scale
    scores = jnp.where(inside, scores, -jnp.inf)
    scores = scores - jnp.max(scores, axis=-1, keepdims=True)
    expo = jnp.exp(scores)
    probs = expo / jnp.sum(expo, axis=-1, keepdims=True)
    probs_lo = probs.astype(bf16)

    grad_attn = jnp.dot(
        whole.reshape(-1, whole.shape[-1]), weight, preferred_element_type=f32
    ).astype(bf16)
    grad = grad_attn.reshape(q_tiles, tile_len, heads, HEAD)

    attn = jnp.einsum("qhtl,lhd->qthd", probs_lo, val_e, preferred_element_type=f32)
    delta = jnp.sum(grad.astype(f32) * attn, axis=-1)
    delta = jnp.transpose(delta, (0, 2, 1))[..., None]
    grad_probs = jnp.einsum("qthd,lhd->qhtl", grad, val_e, preferred_element_type=f32)
    grad_scores = (probs * (grad_probs - delta) * scale).astype(bf16)
    grad_q = jnp.einsum("qhtl,lhd->qthd", grad_scores, key_e, preferred_element_type=f32)
    grad_k = jnp.einsum("qhtl,qthd->lhd", grad_scores, query, preferred_element_type=f32)
    grad_v = jnp.einsum("qhtl,qthd->lhd", probs_lo, grad, preferred_element_type=f32)

    grad_queries = grad_q.reshape(queries.shape).astype(bf16)
    totals = jnp.stack([grad_k, grad_v]).reshape(2, frames, ext_r, ext_c, tile_len, columns)
    own = folded(totals)
    return (grad_queries, own[0].astype(bf16), own[1].astype(bf16))


def solution(mesh):
    in_specs = (
        P(None, "ha", "wa", None, "tp"),
        P(None, "ha", "wa", None, "tp"),
        P(None, "ha", "wa", None, "tp"),
        P(None, "ha", "wa", None, "tp"),
        P(("ha", "wa"), "tp"),
    )
    out_specs = (
        P(None, "ha", "wa", None, "tp"),
        P(None, "ha", "wa", None, "tp"),
        P(None, "ha", "wa", None, "tp"),
    )
    return jax.shard_map(local, mesh=mesh, in_specs=in_specs, out_specs=out_specs, check_vma=False)
```

time: 428 us -> 257 us (0.60)
  the two profiles are of different devices: /device:TPU:64 before, /device:TPU:184 now
where the time goes in v1:
time: 257 us; the launch traced here: 255 us
  starting transfers between devices  65.5 us (25%)
  waiting for transfers between devices  65.3 us (25%)
  local copies, waits for them, and re-layouts  46.6 us (18%)
  other arithmetic  38.2 us (15%)
  matrix products  25.2 us (10%)
  between operations  14.7 us (6%)
    ppermute x8, starting transfers between devices, extended(): got = lax.ppermute(piece, ('ha', 'wa'), neighbour_pairs(d_r, d_c))  37.1 us
    ppermute x8, waiting for transfers between devices, folded(): lax.ppermute(piece, ('ha', 'wa'), neighbour_pairs(-d_r, -d_c))  29.5 us
    ppermute x8, starting transfers between devices, folded(): lax.ppermute(piece, ('ha', 'wa'), neighbour_pairs(-d_r, -d_c))  24.6 us
    another operation x4, local copies, waits for them, and re-layouts, local(): jnp.stack([grad_k, grad_v])  21.4 us
    ppermute x5, waiting for transfers between devices, doubling_gather(): other = lax.ppermute(buf, axis, [(i, i ^ bit) for i in range(count)])  18.6 us
    ppermute x8, waiting for transfers between devices, extended(): got = lax.ppermute(piece, ('ha', 'wa'), neighbour_pairs(d_r, d_c))  16.5 us
    convert_element_type x1, other arithmetic, local(): probs_lo = probs.astype(bf16)  8.48 us
    scatter-add x8, other arithmetic, folded(): own = own.at[:, :, rs, cs].add(got)  7.03 us
  transfers between devices with their start and end apart: 22, of which 8 were waited for; matrix products, arithmetic and copies ran while one was open for 23% of the time, Pallas kernels for 0%

profile of v1, /device:TPU:184, one launch (start us, length us, event | category | flops | bytes accessed | tf_op | source)
XLA Modules:
  0.0 255.5 jit_solution(13408679428299427408)
XLA Ops:
  17.1 4.3 %collective-permute-start.3 = (bf16[2,1,2,1,128,384]{5,4,3,2,1,0:T(8,128)(2,1)}, bf16[2,1,2,1,128,384]{5,4,3,2,1,0:T(8,128)(2,1)S(1)}, u32[]{:S(2)}, u32[]{:S(2)}) collective-permute-start(bf16[2,1,2,1,128,384]{5,4,3,2,1,0:T(8,128)(2,1)} %get-tuple-element.137), channel_id=1, source_target_pairs={{0,1},{1,2},{2,3},{4,5},{5,6},{6,7},{8,9},{9,10},{10,11},{12,13},{... | collective-permute-start | bytes 1179656 | tf_op jit(solution)/shard_map/ppermute | solution.py:62
  23.4 9.3 %collective-permute-done = bf16[2,1,1,1,128,384]{5,4,3,2,1,0:T(8,128)(2,1)S(1)} collective-permute-done((bf16[2,1,1,1,128,384]{5,4,3,2,1,0:T(8,128)(2,1)S(1)}, bf16[2,1,1,1,128,384]{5,4,3,2,1,0:T(8,128)(2,1)S(1)}, u32[]{:S(2)}, u32[]{:S(2)}) %collective-permute-start) | collective-permute-done | bytes 196640 | tf_op jit(solution)/shard_map/ppermute | solution.py:62
  36.2 20.4 %collective-permute-start.5 = (bf16[2,1,1,1,128,384]{5,4,3,2,1,0:T(8,128)(2,1)}, bf16[2,1,1,1,128,384]{5,4,3,2,1,0:T(8,128)(2,1)S(1)}, u32[]{:S(2)}, u32[]{:S(2)}) collective-permute-start(bf16[2,1,1,1,128,384]{5,4,3,2,1,0:T(8,128)(2,1)} %get-tuple-element.133), channel_id=1, source_target_pairs={{4,1},{5,2},{6,3},{8,5},{9,6},{10,7},{12,9},{13,10},{14,11},{16,13... | collective-permute-start | bytes 589832 | tf_op jit(solution)/shard_map/ppermute | solution.py:62
  59.8 5.4 %collective-permute-start.7 = (bf16[2,1,1,1,128,384]{5,4,3,2,1,0:T(8,128)(2,1)S(1)}, bf16[2,1,1,1,128,384]{5,4,3,2,1,0:T(8,128)(2,1)S(1)}, u32[]{:S(2)}, u32[]{:S(2)}) collective-permute-start(bf16[2,1,1,1,128,384]{5,4,3,2,1,0:T(8,128)(2,1)S(1)} %copy-done.12), channel_id=1, source_target_pairs={{5,0},{6,1},{7,2},{9,4},{10,5},{11,6},{13,8},{14,9},{15,10},{17,12... | collective-permute-start | bytes 589832 | tf_op jit(solution)/shard_map/ppermute | solution.py:62
  68.4 5.0 %collective-permute-done.6 = bf16[2,1,1,2,128,384]{5,4,3,2,1,0:T(8,128)(2,1)S(1)} collective-permute-done((bf16[2,1,1,2,128,384]{5,4,3,2,1,0:T(8,128)(2,1)S(1)}, bf16[2,1,1,2,128,384]{5,4,3,2,1,0:T(8,128)(2,1)S(1)}, u32[]{:S(2)}, u32[]{:S(2)}) %collective-permute-start.6) | collective-permute-done | bytes 393248 | tf_op jit(solution)/shard_map/ppermute | solution.py:62
  85.7 6.7 %fusion.60 = (f32[4,3,128]{2,0,1:T(4,128)S(1)}, f32[4,3,128,2048]{2,3,0,1:T(8,128)}) fusion(f32[3,2048,4,128]{3,1,2,0:T(8,128)S(1)} %fusion.12, pred[4,2048]{1,0:T(4,128)(4,1)S(1)} %bitcast.117), kind=kOutput, calls=%fused_computation.114 | output fusion | flops 18876416 | bytes 25180160 | tf_op jit(solution)/shard_map/sub | solution.py:118
  92.4 3.0 %copy.102 = bf16[1,1,4,4,128,384]{4,3,2,5,1,0:T(4,128)(2,1)S(1)} copy(bf16[1,1,4,4,128,384]{5,4,3,2,1,0:T(8,128)(2,1)} %get-tuple-element.126) | data formatting | bytes 3145728 | tf_op jit(solution)/shard_map/slice | solution.py:113
  105.1 8.5 %fusion.9 = bf16[4,3,128,2048]{2,3,0,1:T(8,128)(2,1)} fusion(f32[4,3,128,2048]{2,3,0,1:T(8,128)} %get-tuple-element.141, f32[4,3,128]{2,0,1:T(4,128)S(1)} %get-tuple-element.140), kind=kLoop, calls=%fused_computation.18 | loop fusion | flops 6291456 | bytes 18880512 | tf_op jit(solution)/shard_map/convert_element_type | solution.py:121
  113.5 18.1 %collective-permute-done.12 = bf16[1536,384]{1,0:T(8,128)(2,1)S(1)} collective-permute-done((bf16[1536,384]{1,0:T(8,128)(2,1)S(1)}, bf16[1536,384]{1,0:T(8,128)(2,1)S(1)}, u32[]{:S(2)}, u32[]{:S(2)}) %collective-permute-start.12) | collective-permute-done | bytes 1179680 | tf_op jit(solution)/shard_map/ppermute | solution.py:15
  132.6 3.3 %fusion.30 = bf16[512,384]{0,1:T(8,128)(2,1)S(1)} fusion(bf16[3072,384]{1,0:T(8,128)(2,1)S(1)} %bitcast.115, bf16[512,3072]{1,0:T(8,128)(2,1)} %bitcast.119), kind=kOutput, calls=%fused_computation.52 | convolution fusion | flops 1208156160 | bytes 5898240 | tf_op jit(solution)/shard_map/dot_general | solution.py:123
  136.1 6.6 %convolution_bitcast_fusion = f32[2048,3,128]{0,2,1:T(8,128)} fusion(bf16[4,3,128,2048]{2,3,0,1:T(8,128)(2,1)} %fusion.9, bf16[4,128,3,128]{1,0,3,2:T(4,128)(2,1)S(1)} %reshape.571), kind=kOutput, calls=%fused_computation.19 | convolution fusion | flops 805306368 | bytes 9830400 | tf_op jit(solution)/shard_map/qhtl,qthd->lhd/dot_general | solution.py:135
  142.7 3.9 %stack.22 = f32[1,1,4,4,128,384]{4,3,2,5,1,0:T(4,128)S(1)} reshape(f32[2048,3,128]{0,2,1:T(8,128)} %convolution_bitcast_fusion) | data formatting | bytes 6291456 | tf_op jit(solution)/shard_map/stack | solution.py:138
  146.6 3.1 %copy.115 = f32[1,1,4,4,128,384]{5,4,3,2,1,0:T(8,128)} copy(f32[1,1,4,4,128,384]{4,3,2,5,1,0:T(4,128)S(1)} %stack.22) | data formatting | bytes 6291456 | tf_op jit(solution)/shard_map/stack | solution.py:138
  149.6 4.4 %fusion.27 = f32[4,128,3]{1,0,2:T(4,128)S(1)} fusion(bf16[4,3,128,2048]{2,3,0,1:T(8,128)(2,1)} %fusion.9, bf16[2048,3,128,1]{0,2,1,3:T(8,128)(2,1)} %reshape.576, bf16[4,128,3,128]{1,0,3,2:T(4,128)(2,1)S(1)} %reshape.571), kind=kOutput, calls=%fused_computation.51 | convolution fusion | flops 805894656 | bytes 8263680 | tf_op jit(solution)/shard_map/qhtl,lhd->qthd/dot_general | solution.py:128
  154.1 6.2 %fusion.3 = bf16[4,3,128,2048]{2,3,0,1:T(8,128)(2,1)S(1)} fusion(f32[4,3,128]{2,0,1:T(4,128)S(1)} %bitcast.118, f32[4,3,128,2048]{2,3,0,1:T(8,128)} %get-tuple-element.141, f32[4,3,128]{2,0,1:T(4,128)S(1)} %get-tuple-element.140, bf16[2048,3,128]{0,2,1:T(8,128)(2,1)S(1)} %copy-done.8, bf16[4,128,3,128]{1,0,3,2:T(4,128)(2,1)S(1)} %reshape.571), kind=kOutput, calls=%fused_computation.4 | convolution fusion | flops 821035008 | bytes 20852736 | tf_op jit(solution)/shard_map/qthd,lhd->qhtl/dot_general | solution.py:131
  163.0 10.0 %copy.134 = f32[2048,3,128]{2,1,0:T(4,128)} copy(f32[2048,3,128]{2,0,1:T(8,128)S(1)} %convolution_bitcast_fusion.1) | data formatting | bytes 6291456 | tf_op jit(solution)/shard_map/stack | solution.py:138
  172.9 4.5 %reshape.582 = f32[1,1,4,4,128,384]{5,4,3,2,1,0:T(8,128)S(1)} reshape(f32[2048,3,128]{2,1,0:T(4,128)} %copy.134) | data formatting | bytes 6291456 | tf_op jit(solution)/shard_map/stack | solution.py:138
  177.5 2.5 fusion.5
  182.9 6.9 %collective-permute-start.13 = (bf16[2,1,1,1,128,384]{5,4,3,2,1,0:T(8,128)(2,1)}, bf16[2,1,1,1,128,384]{5,4,3,2,1,0:T(8,128)(2,1)}, u32[]{:S(2)}, u32[]{:S(2)}) collective-permute-start(bf16[2,1,1,1,128,384]{5,4,3,2,1,0:T(8,128)(2,1)} %get-tuple-element.121), channel_id=1, source_target_pairs={{5,0},{6,1},{7,2},{9,4},{10,5},{11,6},{13,8},{14,9},{15,10},{17,12... | collective-permute-start | bytes 589832 | tf_op jit(solution)/shard_map/ppermute | solution.py:78
  189.8 3.9 %collective-permute-start.14 = (bf16[2,1,1,2,128,384]{5,4,3,2,1,0:T(8,128)(2,1)}, bf16[2,1,1,2,128,384]{5,4,3,2,1,0:T(8,128)(2,1)}, u32[]{:S(2)}, u32[]{:S(2)}) collective-permute-start(bf16[2,1,1,2,128,384]{5,4,3,2,1,0:T(8,128)(2,1)} %get-tuple-element.123), channel_id=1, source_target_pairs={{4,0},{5,1},{6,2},{7,3},{8,4},{9,5},{10,6},{11,7},{12,8},{13,9},{1... | collective-permute-start | bytes 1179656 | tf_op jit(solution)/shard_map/ppermute | solution.py:78
  195.7 5.6 %collective-permute-start.16 = (bf16[2,1,2,1,128,384]{5,4,3,2,1,0:T(8,128)(2,1)}, bf16[2,1,2,1,128,384]{5,4,3,2,1,0:T(8,128)(2,1)}, u32[]{:S(2)}, u32[]{:S(2)}) collective-permute-start(bf16[2,1,2,1,128,384]{5,4,3,2,1,0:T(8,128)(2,1)} %get-tuple-element.125), channel_id=1, source_target_pairs={{1,0},{2,1},{3,2},{5,4},{6,5},{7,6},{9,8},{10,9},{11,10},{13,12},{... | collective-permute-start | bytes 1179656 | tf_op jit(solution)/shard_map/ppermute | solution.py:78
  214.1 5.2 %collective-permute-done.16 = bf16[2,1,2,1,128,384]{5,4,3,2,1,0:T(8,128)(2,1)} collective-permute-done((bf16[2,1,2,1,128,384]{5,4,3,2,1,0:T(8,128)(2,1)}, bf16[2,1,2,1,128,384]{5,4,3,2,1,0:T(8,128)(2,1)}, u32[]{:S(2)}, u32[]{:S(2)}) %collective-permute-start.16) | collective-permute-done | bytes 393248 | tf_op jit(solution)/shard_map/ppermute | solution.py:78
  223.0 15.9 %collective-permute-done.19 = bf16[2,1,1,2,128,384]{5,4,3,2,1,0:T(8,128)(2,1)S(1)} collective-permute-done((bf16[2,1,1,2,128,384]{5,4,3,2,1,0:T(8,128)(2,1)S(1)}, bf16[2,1,1,2,128,384]{5,4,3,2,1,0:T(8,128)(2,1)S(1)}, u32[]{:S(2)}, u32[]{:S(2)}) %collective-permute-start.19) | collective-permute-done | bytes 393248 | tf_op jit(solution)/shard_map/ppermute | solution.py:78
  239.1 8.4 %collective-permute-done.20 = bf16[2,1,1,1,128,384]{5,4,3,2,1,0:T(8,128)(2,1)S(1)} collective-permute-done((bf16[2,1,1,1,128,384]{5,4,3,2,1,0:T(8,128)(2,1)S(1)}, bf16[2,1,1,1,128,384]{5,4,3,2,1,0:T(8,128)(2,1)S(1)}, u32[]{:S(2)}, u32[]{:S(2)}) %collective-permute-start.20) | collective-permute-done | bytes 196640 | tf_op jit(solution)/shard_map/ppermute | solution.py:78
  (123 shorter events, 69.8 us)
Async XLA Ops:
  7.2 125.4 %all-gather.2.cloned.1.call-start = ((), (), s32[]{:S(2)}) async-start(), calls=%async_computation | async-start | bytes 3538944 | tf_op jit(solution)/shard_map/all_gather | solution.py:88
  7.2 14.7 %collective-permute-start.8 = (bf16[96,384]{1,0:T(8,128)(2,1)}, bf16[96,384]{1,0:T(8,128)(2,1)S(1)}, u32[]{:S(2)}, u32[]{:S(2)}) collective-permute-start(bf16[96,384]{1,0:T(8,128)(2,1)} %param.25), channel_id=1, source_target_pairs={{0,2},{1,3},{2,0},{3,1},{4,6},{5,7},{6,4},{7,5},{8,10},{9,11},{10,... | collective-permute-start | bytes 221192 | tf_op jit(solution)/shard_map/ppermute | solution.py:15
  10.1 22.6 %collective-permute-start = (bf16[2,1,1,1,128,384]{5,4,3,2,1,0:T(8,128)(2,1)S(1)}, bf16[2,1,1,1,128,384]{5,4,3,2,1,0:T(8,128)(2,1)S(1)}, u32[]{:S(2)}, u32[]{:S(2)}) collective-permute-start(bf16[2,1,1,1,128,384]{5,4,3,2,1,0:T(8,128)(2,1)S(1)} %get-tuple-element.131), channel_id=1, source_target_pairs={{0,5},{1,6},{2,7},{4,9},{5,10},{6,11},{8,13},{9,14},{10,15},{12,17... | collective-permute-start | bytes 589832 | tf_op jit(solution)/shard_map/ppermute | solution.py:62
  13.5 44.9 %collective-permute-start.1 = (bf16[2,1,1,2,128,384]{5,4,3,2,1,0:T(8,128)(2,1)}, bf16[2,1,1,2,128,384]{5,4,3,2,1,0:T(8,128)(2,1)S(1)}, u32[]{:S(2)}, u32[]{:S(2)}) collective-permute-start(bf16[2,1,1,2,128,384]{5,4,3,2,1,0:T(8,128)(2,1)} %get-tuple-element.135), channel_id=1, source_target_pairs={{0,4},{1,5},{2,6},{3,7},{4,8},{5,9},{6,10},{7,11},{8,12},{9,13},{1... | collective-permute-start | bytes 1179656 | tf_op jit(solution)/shard_map/ppermute | solution.py:62
  14.8 45.0 %collective-permute-start.2 = (bf16[2,1,1,1,128,384]{5,4,3,2,1,0:T(8,128)(2,1)}, bf16[2,1,1,1,128,384]{5,4,3,2,1,0:T(8,128)(2,1)}, u32[]{:S(2)}, u32[]{:S(2)}) collective-permute-start(bf16[2,1,1,1,128,384]{5,4,3,2,1,0:T(8,128)(2,1)} %get-tuple-element.132), channel_id=1, source_target_pairs={{1,4},{2,5},{3,6},{5,8},{6,9},{7,10},{9,12},{10,13},{11,14},{13,16... | collective-permute-start | bytes 589832 | tf_op jit(solution)/shard_map/ppermute | solution.py:62
  17.1 49.1 %collective-permute-start.3 = (bf16[2,1,2,1,128,384]{5,4,3,2,1,0:T(8,128)(2,1)}, bf16[2,1,2,1,128,384]{5,4,3,2,1,0:T(8,128)(2,1)S(1)}, u32[]{:S(2)}, u32[]{:S(2)}) collective-permute-start(bf16[2,1,2,1,128,384]{5,4,3,2,1,0:T(8,128)(2,1)} %get-tuple-element.137), channel_id=1, source_target_pairs={{0,1},{1,2},{2,3},{4,5},{5,6},{6,7},{8,9},{9,10},{10,11},{12,13},{... | collective-permute-start | bytes 1179656 | tf_op jit(solution)/shard_map/ppermute | solution.py:62
  22.0 14.2 %collective-permute-start.9 = (bf16[192,384]{1,0:T(8,128)(2,1)S(1)}, bf16[192,384]{1,0:T(8,128)(2,1)}, u32[]{:S(2)}, u32[]{:S(2)}) collective-permute-start(bf16[192,384]{1,0:T(8,128)(2,1)S(1)} %maximum_select_fusion.4), channel_id=1, source_target_pairs={{0,1},{1,0},{2,3},{3,2},{4,5},{5,4},{6,7},{7,6},{8,9},{9,8},{10,11... | collective-permute-start | bytes 442376 | tf_op jit(solution)/shard_map/ppermute | solution.py:15
  22.7 37.1 %copy-start.12 = (bf16[2,1,1,1,128,384]{5,4,3,2,1,0:T(8,128)(2,1)S(1)}, bf16[2,1,1,1,128,384]{5,4,3,2,1,0:T(8,128)(2,1)}, u32[]{:S(2)}) copy-start(bf16[2,1,1,1,128,384]{5,4,3,2,1,0:T(8,128)(2,1)} %get-tuple-element.130) | copy-start | bytes 589828
  22.9 57.3 %copy-start.6 = (bf16[1,2,2,128,384]{3,4,2,1,0:T(8,128)(2,1)}, bf16[1,2,2,128,384]{3,4,2,1,0:T(8,128)(2,1)S(1)}, u32[]{:S(2)}) copy-start(bf16[1,2,2,128,384]{3,4,2,1,0:T(8,128)(2,1)S(1)} %copy.99) | copy-start | bytes 1179652
  33.4 34.9 %collective-permute-start.4 = (bf16[2,1,2,1,128,384]{5,4,3,2,1,0:T(8,128)(2,1)}, bf16[2,1,2,1,128,384]{5,4,3,2,1,0:T(8,128)(2,1)S(1)}, u32[]{:S(2)}, u32[]{:S(2)}) collective-permute-start(bf16[2,1,2,1,128,384]{5,4,3,2,1,0:T(8,128)(2,1)} %get-tuple-element.136), channel_id=1, source_target_pairs={{1,0},{2,1},{3,2},{5,4},{6,5},{7,6},{9,8},{10,9},{11,10},{13,12},{... | collective-permute-start | bytes 1179656 | tf_op jit(solution)/shard_map/ppermute | solution.py:62
  36.2 32.1 %collective-permute-start.5 = (bf16[2,1,1,1,128,384]{5,4,3,2,1,0:T(8,128)(2,1)}, bf16[2,1,1,1,128,384]{5,4,3,2,1,0:T(8,128)(2,1)S(1)}, u32[]{:S(2)}, u32[]{:S(2)}) collective-permute-start(bf16[2,1,1,1,128,384]{5,4,3,2,1,0:T(8,128)(2,1)} %get-tuple-element.133), channel_id=1, source_target_pairs={{4,1},{5,2},{6,3},{8,5},{9,6},{10,7},{12,9},{13,10},{14,11},{16,13... | collective-permute-start | bytes 589832 | tf_op jit(solution)/shard_map/ppermute | solution.py:62
  58.4 15.0 %collective-permute-start.6 = (bf16[2,1,1,2,128,384]{5,4,3,2,1,0:T(8,128)(2,1)S(1)}, bf16[2,1,1,2,128,384]{5,4,3,2,1,0:T(8,128)(2,1)S(1)}, u32[]{:S(2)}, u32[]{:S(2)}) collective-permute-start(bf16[2,1,1,2,128,384]{5,4,3,2,1,0:T(8,128)(2,1)S(1)} %copy-done.10), channel_id=1, source_target_pairs={{4,0},{5,1},{6,2},{7,3},{8,4},{9,5},{10,6},{11,7},{12,8},{13,9},{1... | collective-permute-start | bytes 1179656 | tf_op jit(solution)/shard_map/ppermute | solution.py:62
  59.8 15.9 %collective-permute-start.7 = (bf16[2,1,1,1,128,384]{5,4,3,2,1,0:T(8,128)(2,1)S(1)}, bf16[2,1,1,1,128,384]{5,4,3,2,1,0:T(8,128)(2,1)S(1)}, u32[]{:S(2)}, u32[]{:S(2)}) collective-permute-start(bf16[2,1,1,1,128,384]{5,4,3,2,1,0:T(8,128)(2,1)S(1)} %copy-done.12), channel_id=1, source_target_pairs={{5,0},{6,1},{7,2},{9,4},{10,5},{11,6},{13,8},{14,9},{15,10},{17,12... | collective-permute-start | bytes 589832 | tf_op jit(solution)/shard_map/ppermute | solution.py:62
  66.2 16.4 %collective-permute-start.10 = (bf16[384,384]{1,0:T(8,128)(2,1)}, bf16[384,384]{1,0:T(8,128)(2,1)}, u32[]{:S(2)}, u32[]{:S(2)}) collective-permute-start(bf16[384,384]{1,0:T(8,128)(2,1)} %maximum_select_fusion.3), channel_id=1, source_target_pairs={{0,16},{4,20},{8,24},{12,28},{16,0},{20,4},{24,8},{28,12},{1,17},{... | collective-permute-start | bytes 884744 | tf_op jit(solution)/shard_map/ppermute | solution.py:15
  84.7 17.9 %collective-permute-start.11 = (bf16[768,384]{1,0:T(8,128)(2,1)}, bf16[768,384]{1,0:T(8,128)(2,1)}, u32[]{:S(2)}, u32[]{:S(2)}) collective-permute-start(bf16[768,384]{1,0:T(8,128)(2,1)} %maximum_select_fusion.2), channel_id=1, source_target_pairs={{0,8},{4,12},{8,0},{12,4},{16,24},{20,28},{24,16},{28,20},{1,9},{5... | collective-permute-start | bytes 1769480 | tf_op jit(solution)/shard_map/ppermute | solution.py:15
  104.5 27.2 %collective-permute-start.12 = (bf16[1536,384]{1,0:T(8,128)(2,1)S(1)}, bf16[1536,384]{1,0:T(8,128)(2,1)S(1)}, u32[]{:S(2)}, u32[]{:S(2)}) collective-permute-start(bf16[1536,384]{1,0:T(8,128)(2,1)S(1)} %maximum_select_fusion.1), channel_id=1, source_target_pairs={{0,4},{4,0},{8,12},{12,8},{16,20},{20,16},{24,28},{28,24},{1,5},{5... | collective-permute-start | bytes 3538952 | tf_op jit(solution)/shard_map/ppermute | solution.py:15
  182.9 24.0 %collective-permute-start.13 = (bf16[2,1,1,1,128,384]{5,4,3,2,1,0:T(8,128)(2,1)}, bf16[2,1,1,1,128,384]{5,4,3,2,1,0:T(8,128)(2,1)}, u32[]{:S(2)}, u32[]{:S(2)}) collective-permute-start(bf16[2,1,1,1,128,384]{5,4,3,2,1,0:T(8,128)(2,1)} %get-tuple-element.121), channel_id=1, source_target_pairs={{5,0},{6,1},{7,2},{9,4},{10,5},{11,6},{13,8},{14,9},{15,10},{17,12... | collective-permute-start | bytes 589832 | tf_op jit(solution)/shard_map/ppermute | solution.py:78
  189.8 19.5 %collective-permute-start.14 = (bf16[2,1,1,2,128,384]{5,4,3,2,1,0:T(8,128)(2,1)}, bf16[2,1,1,2,128,384]{5,4,3,2,1,0:T(8,128)(2,1)}, u32[]{:S(2)}, u32[]{:S(2)}) collective-permute-start(bf16[2,1,1,2,128,384]{5,4,3,2,1,0:T(8,128)(2,1)} %get-tuple-element.123), channel_id=1, source_target_pairs={{4,0},{5,1},{6,2},{7,3},{8,4},{9,5},{10,6},{11,7},{12,8},{13,9},{1... | collective-permute-start | bytes 1179656 | tf_op jit(solution)/shard_map/ppermute | solution.py:78
  193.7 18.1 %collective-permute-start.15 = (bf16[2,1,1,1,128,384]{5,4,3,2,1,0:T(8,128)(2,1)}, bf16[2,1,1,1,128,384]{5,4,3,2,1,0:T(8,128)(2,1)}, u32[]{:S(2)}, u32[]{:S(2)}) collective-permute-start(bf16[2,1,1,1,128,384]{5,4,3,2,1,0:T(8,128)(2,1)} %get-tuple-element.120), channel_id=1, source_target_pairs={{4,1},{5,2},{6,3},{8,5},{9,6},{10,7},{12,9},{13,10},{14,11},{16,13... | collective-permute-start | bytes 589832 | tf_op jit(solution)/shard_map/ppermute | solution.py:78
  195.7 23.7 %collective-permute-start.16 = (bf16[2,1,2,1,128,384]{5,4,3,2,1,0:T(8,128)(2,1)}, bf16[2,1,2,1,128,384]{5,4,3,2,1,0:T(8,128)(2,1)}, u32[]{:S(2)}, u32[]{:S(2)}) collective-permute-start(bf16[2,1,2,1,128,384]{5,4,3,2,1,0:T(8,128)(2,1)} %get-tuple-element.125), channel_id=1, source_target_pairs={{1,0},{2,1},{3,2},{5,4},{6,5},{7,6},{9,8},{10,9},{11,10},{13,12},{... | collective-permute-start | bytes 1179656 | tf_op jit(solution)/shard_map/ppermute | solution.py:78
  201.3 19.2 %collective-permute-start.17 = (bf16[2,1,2,1,128,384]{5,4,3,2,1,0:T(8,128)(2,1)}, bf16[2,1,2,1,128,384]{5,4,3,2,1,0:T(8,128)(2,1)}, u32[]{:S(2)}, u32[]{:S(2)}) collective-permute-start(bf16[2,1,2,1,128,384]{5,4,3,2,1,0:T(8,128)(2,1)} %get-tuple-element.124), channel_id=1, source_target_pairs={{0,1},{1,2},{2,3},{4,5},{5,6},{6,7},{8,9},{9,10},{10,11},{12,13},{... | collective-permute-start | bytes 1179656 | tf_op jit(solution)/shard_map/ppermute | solution.py:78
  206.9 14.8 %collective-permute-start.18 = (bf16[2,1,1,1,128,384]{5,4,3,2,1,0:T(8,128)(2,1)S(1)}, bf16[2,1,1,1,128,384]{5,4,3,2,1,0:T(8,128)(2,1)S(1)}, u32[]{:S(2)}, u32[]{:S(2)}) collective-permute-start(bf16[2,1,1,1,128,384]{5,4,3,2,1,0:T(8,128)(2,1)S(1)} %copy-done.14), channel_id=1, source_target_pairs={{1,4},{2,5},{3,6},{5,8},{6,9},{7,10},{9,12},{10,13},{11,14},{13,16... | collective-permute-start | bytes 589832 | tf_op jit(solution)/shard_map/ppermute | solution.py:78
  209.3 29.6 %collective-permute-start.19 = (bf16[2,1,1,2,128,384]{5,4,3,2,1,0:T(8,128)(2,1)S(1)}, bf16[2,1,1,2,128,384]{5,4,3,2,1,0:T(8,128)(2,1)S(1)}, u32[]{:S(2)}, u32[]{:S(2)}) collective-permute-start(bf16[2,1,1,2,128,384]{5,4,3,2,1,0:T(8,128)(2,1)S(1)} %copy-done.11), channel_id=1, source_target_pairs={{0,4},{1,5},{2,6},{3,7},{4,8},{5,9},{6,10},{7,11},{8,12},{9,13},{1... | collective-permute-start | bytes 1179656 | tf_op jit(solution)/shard_map/ppermute | solution.py:78
  211.8 35.7 %collective-permute-start.20 = (bf16[2,1,1,1,128,384]{5,4,3,2,1,0:T(8,128)(2,1)S(1)}, bf16[2,1,1,1,128,384]{5,4,3,2,1,0:T(8,128)(2,1)S(1)}, u32[]{:S(2)}, u32[]{:S(2)}) collective-permute-start(bf16[2,1,1,1,128,384]{5,4,3,2,1,0:T(8,128)(2,1)S(1)} %copy-done.13), channel_id=1, source_target_pairs={{0,5},{1,6},{2,7},{4,9},{5,10},{6,11},{8,13},{9,14},{10,15},{12,17... | collective-permute-start | bytes 589832 | tf_op jit(solution)/shard_map/ppermute | solution.py:78
  (15 other events, 158.3 us)
Sparse Core Ops, SparseCore 0:
  9.8 31.0 all-gather.1

commit v2 on v1

--- a/solution.py
+++ b/solution.py
@@ -86,7 +86,7 @@
     heads = columns // HEAD
     f32, bf16 = jnp.float32, jnp.bfloat16
     whole = lax.all_gather(grad_out, "tp", axis=4, tiled=True)
-    weight = gather_rows(out_proj)
+    weight = lax.all_gather(lax.all_gather(out_proj, "wa", axis=0, tiled=True), "ha", axis=0, tiled=True)
     ext = extended(jnp.stack([keys, values]))
     ext_r, ext_c = tile_rows + 2, tile_cols + 2
     row_base = lax.axis_index("ha") * tile_rows

time: 257 us -> 287 us (1.12)
  waiting for transfers between devices: 65.3 us -> 97.4 us
  blocking collectives: 0 us -> 15.2 us
  starting transfers between devices: 65.5 us -> 50.5 us
  other arithmetic: 38.2 us -> 31.8 us
  local copies, waits for them, and re-layouts: 46.6 us -> 49.6 us
    all_gather x1, waiting for transfers between devices: 0.02 us -> 34.7 us  [local(): whole = lax.all_gather(grad_out, 'tp', axis=4, tiled=True)]
    ppermute x8, waiting for transfers between devices: 16.5 us -> 37.2 us  [extended(): got = lax.ppermute(piece, ('ha', 'wa'), neighbour_pairs(d_r, d_c))]
    ppermute x5 -> x0, waiting for transfers between devices: 18.6 us -> none  [doubling_gather(): other = lax.ppermute(buf, axis, [(i, i ^ bit) for i in range(count)])]
    all_gather x0 -> x1, blocking collectives: none -> 15.2 us  [local(): lax.all_gather(out_proj, 'wa', axis=0, tiled=True)]
    ppermute x8, starting transfers between devices: 37.1 us -> 27.3 us  [extended(): got = lax.ppermute(piece, ('ha', 'wa'), neighbour_pairs(d_r, d_c))]
    select_n x5 -> x0, other arithmetic: 6.46 us -> none  [doubling_gather(): jnp.where(low, jnp.concatenate([buf, other], 0), jnp.concatenate([other,...]
    ppermute x8, waiting for transfers between devices: 29.5 us -> 25.4 us  [folded(): lax.ppermute(piece, ('ha', 'wa'), neighbour_pairs(-d_r, -d_c))]
    ppermute x5 -> x0, starting transfers between devices: 3.79 us -> none  [doubling_gather(): other = lax.ppermute(buf, axis, [(i, i ^ bit) for i in range(count)])]
  transfers between devices with their start and end apart: 22 -> 18, of which waited for: 8 -> 8; matrix products, arithmetic and copies ran while one was open for 23% -> 19% of each run, Pallas kernels for 0% -> 0%
where the time goes in v2:
time: 287 us; the launch traced here: 285 us
  waiting for transfers between devices  97.4 us (34%)
  starting transfers between devices  50.5 us (18%)
  local copies, waits for them, and re-layouts  49.6 us (17%)
  other arithmetic  31.8 us (11%)
  matrix products  26.1 us (9%)
  blocking collectives  15.2 us (5%)
  between operations  14.7 us (5%)
    ppermute x8, waiting for transfers between devices, extended(): got = lax.ppermute(piece, ('ha', 'wa'), neighbour_pairs(d_r, d_c))  37.2 us
    all_gather x1, waiting for transfers between devices, local(): whole = lax.all_gather(grad_out, 'tp', axis=4, tiled=True)  34.7 us
    ppermute x8, starting transfers between devices, extended(): got = lax.ppermute(piece, ('ha', 'wa'), neighbour_pairs(d_r, d_c))  27.3 us
    ppermute x8, waiting for transfers between devices, folded(): lax.ppermute(piece, ('ha', 'wa'), neighbour_pairs(-d_r, -d_c))  25.4 us
    another operation x4, local copies, waits for them, and re-layouts, local(): jnp.stack([grad_k, grad_v])  24.8 us
    ppermute x8, starting transfers between devices, folded(): lax.ppermute(piece, ('ha', 'wa'), neighbour_pairs(-d_r, -d_c))  23.1 us
    all_gather x1, blocking collectives, local(): lax.all_gather(out_proj, 'wa', axis=0, tiled=True)  15.2 us
    convert_element_type x1, other arithmetic, local(): probs_lo = probs.astype(bf16)  8.48 us
  transfers between devices with their start and end apart: 18, of which 8 were waited for; matrix products, arithmetic and copies ran while one was open for 19% of the time, Pallas kernels for 0%

profile of v2, /device:TPU:184, one launch (start us, length us, event | category | flops | bytes accessed | tf_op | source)
XLA Modules:
  0.0 285.2 jit_solution(1090000292719335338)
XLA Ops:
  7.2 15.2 %all_gather.10 = bf16[384,384]{1,0:T(8,128)(2,1)} all-gather(bf16[96,384]{1,0:T(8,128)(2,1)} %param.25), channel_id=1, replica_groups=mesh['tp'=8,'ha'=8,'wa'=4] {'wa'}, dimensions={0}, use_global_device_ids=true | all-gather | bytes 368640 | tf_op jit(solution)/shard_map/all_gather | solution.py:89
  35.2 4.5 %collective-permute-start.4 = (bf16[2,1,2,1,128,384]{5,4,3,2,1,0:T(8,128)(2,1)}, bf16[2,1,2,1,128,384]{5,4,3,2,1,0:T(8,128)(2,1)S(1)}, u32[]{:S(2)}, u32[]{:S(2)}) collective-permute-start(bf16[2,1,2,1,128,384]{5,4,3,2,1,0:T(8,128)(2,1)} %get-tuple-element.133), channel_id=1, source_target_pairs={{1,0},{2,1},{3,2},{5,4},{6,5},{7,6},{9,8},{10,9},{11,10},{13,12},{... | collective-permute-start | bytes 1179656 | tf_op jit(solution)/shard_map/ppermute | solution.py:62
  41.6 10.1 %collective-permute-done = bf16[2,1,1,1,128,384]{5,4,3,2,1,0:T(8,128)(2,1)} collective-permute-done((bf16[2,1,1,1,128,384]{5,4,3,2,1,0:T(8,128)(2,1)}, bf16[2,1,1,1,128,384]{5,4,3,2,1,0:T(8,128)(2,1)}, u32[]{:S(2)}, u32[]{:S(2)}) %collective-permute-start) | collective-permute-done | bytes 196640 | tf_op jit(solution)/shard_map/ppermute | solution.py:62
  54.0 13.0 %collective-permute-done.1 = bf16[2,1,1,2,128,384]{5,4,3,2,1,0:T(8,128)(2,1)S(1)} collective-permute-done((bf16[2,1,1,2,128,384]{5,4,3,2,1,0:T(8,128)(2,1)}, bf16[2,1,1,2,128,384]{5,4,3,2,1,0:T(8,128)(2,1)S(1)}, u32[]{:S(2)}, u32[]{:S(2)}) %collective-permute-start.1) | collective-permute-done | bytes 393248 | tf_op jit(solution)/shard_map/ppermute | solution.py:62
  69.8 11.4 %collective-permute-start.7 = (bf16[2,1,1,1,128,384]{5,4,3,2,1,0:T(8,128)(2,1)S(1)}, bf16[2,1,1,1,128,384]{5,4,3,2,1,0:T(8,128)(2,1)S(1)}, u32[]{:S(2)}, u32[]{:S(2)}) collective-permute-start(bf16[2,1,1,1,128,384]{5,4,3,2,1,0:T(8,128)(2,1)S(1)} %copy-done.10), channel_id=1, source_target_pairs={{5,0},{6,1},{7,2},{9,4},{10,5},{11,6},{13,8},{14,9},{15,10},{17,12... | collective-permute-start | bytes 589832 | tf_op jit(solution)/shard_map/ppermute | solution.py:62
  82.5 7.9 %collective-permute-done.6 = bf16[2,1,1,2,128,384]{5,4,3,2,1,0:T(8,128)(2,1)S(1)} collective-permute-done((bf16[2,1,1,2,128,384]{5,4,3,2,1,0:T(8,128)(2,1)S(1)}, bf16[2,1,1,2,128,384]{5,4,3,2,1,0:T(8,128)(2,1)S(1)}, u32[]{:S(2)}, u32[]{:S(2)}) %collective-permute-start.6) | collective-permute-done | bytes 393248 | tf_op jit(solution)/shard_map/ppermute | solution.py:62
  90.4 6.3 %collective-permute-done.7 = bf16[2,1,1,1,128,384]{5,4,3,2,1,0:T(8,128)(2,1)S(1)} collective-permute-done((bf16[2,1,1,1,128,384]{5,4,3,2,1,0:T(8,128)(2,1)S(1)}, bf16[2,1,1,1,128,384]{5,4,3,2,1,0:T(8,128)(2,1)S(1)}, u32[]{:S(2)}, u32[]{:S(2)}) %collective-permute-start.7) | collective-permute-done | bytes 196640 | tf_op jit(solution)/shard_map/ppermute | solution.py:62
  113.2 6.8 %fusion.57 = (f32[4,3,128]{2,0,1:T(4,128)S(1)}, f32[4,3,128,2048]{2,3,0,1:T(8,128)}) fusion(f32[3,2048,4,128]{3,1,2,0:T(8,128)S(1)} %fusion.12, pred[4,2048]{1,0:T(4,128)(4,1)S(1)} %bitcast.111), kind=kOutput, calls=%fused_computation.106 | output fusion | flops 18876416 | bytes 25180160 | tf_op jit(solution)/shard_map/sub | solution.py:118
  119.9 8.5 %fusion.9 = bf16[4,3,128,2048]{2,3,0,1:T(8,128)(2,1)} fusion(f32[4,3,128,2048]{2,3,0,1:T(8,128)} %get-tuple-element.138, f32[4,3,128]{2,0,1:T(4,128)S(1)} %get-tuple-element.137), kind=kLoop, calls=%fused_computation.18 | loop fusion | flops 6291456 | bytes 18880512 | tf_op jit(solution)/shard_map/convert_element_type | solution.py:121
  128.4 34.7 %all-gather.3.cloned.1.call-done = bf16[1,2,2,128,3072]{4,3,2,1,0:T(8,128)(2,1)} async-done(((bf16[1,2,2,128,384]{4,3,2,1,0:T(8,128)(2,1)}), bf16[1,2,2,128,3072]{4,3,2,1,0:T(8,128)(2,1)}) %all-gather.3.cloned.1.call-update) | async-done | bytes 3145744 | tf_op jit(solution)/shard_map/all_gather | solution.py:88
  163.1 4.4 %convolution_convert_fusion = bf16[512,384]{1,0:T(8,128)(2,1)S(1)} fusion(bf16[512,3072]{1,0:T(8,128)(2,1)} %bitcast.113, bf16[3072,384]{1,0:T(8,128)(2,1)} %all-gather.5.cloned.1.call-done), kind=kOutput, calls=%fused_computation.49 | convolution fusion | flops 1208156160 | bytes 5898240 | tf_op jit(solution)/shard_map/dot_general | solution.py:123
  168.0 6.8 %convolution_bitcast_fusion = f32[2048,3,128]{0,2,1:T(8,128)} fusion(bf16[4,128,3,128]{1,3,0,2:T(8,128)(2,1)S(1)} %copy.88, bf16[4,3,128,2048]{2,3,0,1:T(8,128)(2,1)} %fusion.9), kind=kOutput, calls=%fused_computation.19 | convolution fusion | flops 805306368 | bytes 9830400 | tf_op jit(solution)/shard_map/qhtl,qthd->lhd/dot_general | solution.py:135
  176.2 6.4 %fusion.3 = bf16[4,3,128,2048]{2,3,0,1:T(8,128)(2,1)S(1)} fusion(f32[4,3,128]{2,0,1:T(4,128)S(1)} %bitcast.112, bf16[4,128,3,128]{1,3,0,2:T(8,128)(2,1)S(1)} %copy.88, f32[4,3,128,2048]{2,3,0,1:T(8,128)} %get-tuple-element.138, f32[4,3,128]{2,0,1:T(4,128)S(1)} %get-tuple-element.137, bf16[2048,3,128]{0,2,1:T(8,128)(2,1)S(1)} %copy-done.6), kind=kOutput, calls=%fused_computation.4 | convolution fusion | flops 821035008 | bytes 20852736 | tf_op jit(solution)/shard_map/qthd,lhd->qhtl/dot_general | solution.py:131
  185.3 10.0 %copy.116 = f32[2048,3,128]{2,1,0:T(4,128)} copy(f32[2048,3,128]{2,0,1:T(8,128)S(1)} %convolution_bitcast_fusion.1) | data formatting | bytes 6291456 | tf_op jit(solution)/shard_map/stack | solution.py:138
  195.3 4.5 %reshape.573 = f32[1,1,4,4,128,384]{5,4,3,2,1,0:T(8,128)S(1)} reshape(f32[2048,3,128]{2,1,0:T(4,128)} %copy.116) | data formatting | bytes 6291456 | tf_op jit(solution)/shard_map/stack | solution.py:138
  199.8 5.3 %stack.22 = f32[1,1,4,4,128,384]{4,3,2,5,1,0:T(4,128)} reshape(f32[2048,3,128]{0,2,1:T(8,128)} %convolution_bitcast_fusion) | data formatting | bytes 6291456 | tf_op jit(solution)/shard_map/stack | solution.py:138
  205.1 5.0 %copy.97 = f32[1,1,4,4,128,384]{5,4,3,2,1,0:T(8,128)} copy(f32[1,1,4,4,128,384]{4,3,2,5,1,0:T(4,128)} %stack.22) | data formatting | bytes 6291456 | tf_op jit(solution)/shard_map/stack | solution.py:138
  215.3 3.8 %collective-permute-start.8 = (bf16[2,1,1,1,128,384]{5,4,3,2,1,0:T(8,128)(2,1)}, bf16[2,1,1,1,128,384]{5,4,3,2,1,0:T(8,128)(2,1)}, u32[]{:S(2)}, u32[]{:S(2)}) collective-permute-start(bf16[2,1,1,1,128,384]{5,4,3,2,1,0:T(8,128)(2,1)} %get-tuple-element.118), channel_id=1, source_target_pairs={{5,0},{6,1},{7,2},{9,4},{10,5},{11,6},{13,8},{14,9},{15,10},{17,12... | collective-permute-start | bytes 589832 | tf_op jit(solution)/shard_map/ppermute | solution.py:78
  222.0 5.0 %collective-permute-start.10 = (bf16[2,1,1,1,128,384]{5,4,3,2,1,0:T(8,128)(2,1)}, bf16[2,1,1,1,128,384]{5,4,3,2,1,0:T(8,128)(2,1)}, u32[]{:S(2)}, u32[]{:S(2)}) collective-permute-start(bf16[2,1,1,1,128,384]{5,4,3,2,1,0:T(8,128)(2,1)} %get-tuple-element.117), channel_id=1, source_target_pairs={{4,1},{5,2},{6,3},{8,5},{9,6},{10,7},{12,9},{13,10},{14,11},{16,13... | collective-permute-start | bytes 589832 | tf_op jit(solution)/shard_map/ppermute | solution.py:78
  229.8 4.6 %collective-permute-start.12 = (bf16[2,1,2,1,128,384]{5,4,3,2,1,0:T(8,128)(2,1)}, bf16[2,1,2,1,128,384]{5,4,3,2,1,0:T(8,128)(2,1)}, u32[]{:S(2)}, u32[]{:S(2)}) collective-permute-start(bf16[2,1,2,1,128,384]{5,4,3,2,1,0:T(8,128)(2,1)} %get-tuple-element.121), channel_id=1, source_target_pairs={{0,1},{1,2},{2,3},{4,5},{5,6},{6,7},{8,9},{9,10},{10,11},{12,13},{... | collective-permute-start | bytes 1179656 | tf_op jit(solution)/shard_map/ppermute | solution.py:78
  234.5 3.9 %fusion.30 = bf16[4,128,3,128]{1,3,0,2:T(8,128)(2,1)S(1)} fusion(bf16[4,3,128,2048]{2,3,0,1:T(8,128)(2,1)} %copy-done.1, bf16[2048,3,128,1]{0,2,1,3:T(8,128)(2,1)S(1)} %copy-done.5), kind=kOutput, calls=%fused_computation.51 | convolution fusion | flops 805502976 | bytes 8257536 | tf_op jit(solution)/shard_map/qhtl,lhd->qthd/dot_general | solution.py:133
  248.0 4.8 %collective-permute-done.11 = bf16[2,1,2,1,128,384]{5,4,3,2,1,0:T(8,128)(2,1)} collective-permute-done((bf16[2,1,2,1,128,384]{5,4,3,2,1,0:T(8,128)(2,1)}, bf16[2,1,2,1,128,384]{5,4,3,2,1,0:T(8,128)(2,1)}, u32[]{:S(2)}, u32[]{:S(2)}) %collective-permute-start.11) | collective-permute-done | bytes 393248 | tf_op jit(solution)/shard_map/ppermute | solution.py:78
  256.5 12.6 %collective-permute-done.14 = bf16[2,1,1,2,128,384]{5,4,3,2,1,0:T(8,128)(2,1)S(1)} collective-permute-done((bf16[2,1,1,2,128,384]{5,4,3,2,1,0:T(8,128)(2,1)S(1)}, bf16[2,1,1,2,128,384]{5,4,3,2,1,0:T(8,128)(2,1)S(1)}, u32[]{:S(2)}, u32[]{:S(2)}) %collective-permute-start.14) | collective-permute-done | bytes 393248 | tf_op jit(solution)/shard_map/ppermute | solution.py:78
  269.3 8.0 %collective-permute-done.15 = bf16[2,1,1,1,128,384]{5,4,3,2,1,0:T(8,128)(2,1)S(1)} collective-permute-done((bf16[2,1,1,1,128,384]{5,4,3,2,1,0:T(8,128)(2,1)S(1)}, bf16[2,1,1,1,128,384]{5,4,3,2,1,0:T(8,128)(2,1)S(1)}, u32[]{:S(2)}, u32[]{:S(2)}) %collective-permute-start.15) | collective-permute-done | bytes 196640 | tf_op jit(solution)/shard_map/ppermute | solution.py:78
  (111 shorter events, 67.2 us)
Async XLA Ops:
  7.2 23.6 %copy-start.4 = (bf16[1,2,2,128,384]{4,3,2,1,0:T(8,128)(2,1)S(1)}, bf16[1,2,2,128,384]{4,3,2,1,0:T(8,128)(2,1)}, u32[]{:S(2)}) copy-start(bf16[1,2,2,128,384]{4,3,2,1,0:T(8,128)(2,1)} %param.22) | copy-start | bytes 1179652
  7.2 23.6 %copy-start.3 = (bf16[1,2,2,128,384]{4,3,2,1,0:T(8,128)(2,1)S(1)}, bf16[1,2,2,128,384]{4,3,2,1,0:T(8,128)(2,1)}, u32[]{:S(2)}) copy-start(bf16[1,2,2,128,384]{4,3,2,1,0:T(8,128)(2,1)} %param.23) | copy-start | bytes 1179652
  7.2 121.2 %all-gather.5.cloned.1.call-start = ((), (), s32[]{:S(2)}) async-start(), calls=%async_computation.1 | async-start | bytes 2654208 | tf_op jit(solution)/shard_map/all_gather | solution.py:89
  22.5 140.7 %all-gather.3.cloned.1.call-start = ((), (), s32[]{:S(2)}) async-start(), calls=%async_computation | async-start | bytes 3538944 | tf_op jit(solution)/shard_map/all_gather | solution.py:88
  22.5 18.4 %copy-start.7 = (bf16[1,2,2,128,384]{4,3,2,1,0:T(8,128)(2,1)S(1)}, bf16[1,2,2,128,384]{4,3,2,1,0:T(8,128)(2,1)}, u32[]{:S(2)}) copy-start(bf16[1,2,2,128,384]{4,3,2,1,0:T(8,128)(2,1)} %param.21) | copy-start | bytes 1179652
  24.7 27.0 %collective-permute-start = (bf16[2,1,1,1,128,384]{5,4,3,2,1,0:T(8,128)(2,1)}, bf16[2,1,1,1,128,384]{5,4,3,2,1,0:T(8,128)(2,1)}, u32[]{:S(2)}, u32[]{:S(2)}) collective-permute-start(bf16[2,1,1,1,128,384]{5,4,3,2,1,0:T(8,128)(2,1)} %get-tuple-element.128), channel_id=1, source_target_pairs={{0,5},{1,6},{2,7},{4,9},{5,10},{6,11},{8,13},{9,14},{10,15},{12,17... | collective-permute-start | bytes 589832 | tf_op jit(solution)/shard_map/ppermute | solution.py:62
  28.2 38.7 %collective-permute-start.1 = (bf16[2,1,1,2,128,384]{5,4,3,2,1,0:T(8,128)(2,1)}, bf16[2,1,1,2,128,384]{5,4,3,2,1,0:T(8,128)(2,1)S(1)}, u32[]{:S(2)}, u32[]{:S(2)}) collective-permute-start(bf16[2,1,1,2,128,384]{5,4,3,2,1,0:T(8,128)(2,1)} %get-tuple-element.132), channel_id=1, source_target_pairs={{0,4},{1,5},{2,6},{3,7},{4,8},{5,9},{6,10},{7,11},{8,12},{9,13},{1... | collective-permute-start | bytes 1179656 | tf_op jit(solution)/shard_map/ppermute | solution.py:62
  29.5 40.3 %collective-permute-start.2 = (bf16[2,1,1,1,128,384]{5,4,3,2,1,0:T(8,128)(2,1)}, bf16[2,1,1,1,128,384]{5,4,3,2,1,0:T(8,128)(2,1)}, u32[]{:S(2)}, u32[]{:S(2)}) collective-permute-start(bf16[2,1,1,1,128,384]{5,4,3,2,1,0:T(8,128)(2,1)} %get-tuple-element.129), channel_id=1, source_target_pairs={{1,4},{2,5},{3,6},{5,8},{6,9},{7,10},{9,12},{10,13},{11,14},{13,16... | collective-permute-start | bytes 589832 | tf_op jit(solution)/shard_map/ppermute | solution.py:62
  31.8 50.5 %collective-permute-start.3 = (bf16[2,1,2,1,128,384]{5,4,3,2,1,0:T(8,128)(2,1)}, bf16[2,1,2,1,128,384]{5,4,3,2,1,0:T(8,128)(2,1)S(1)}, u32[]{:S(2)}, u32[]{:S(2)}) collective-permute-start(bf16[2,1,2,1,128,384]{5,4,3,2,1,0:T(8,128)(2,1)} %get-tuple-element.134), channel_id=1, source_target_pairs={{0,1},{1,2},{2,3},{4,5},{5,6},{6,7},{8,9},{9,10},{10,11},{12,13},{... | collective-permute-start | bytes 1179656 | tf_op jit(solution)/shard_map/ppermute | solution.py:62
  35.2 47.1 %collective-permute-start.4 = (bf16[2,1,2,1,128,384]{5,4,3,2,1,0:T(8,128)(2,1)}, bf16[2,1,2,1,128,384]{5,4,3,2,1,0:T(8,128)(2,1)S(1)}, u32[]{:S(2)}, u32[]{:S(2)}) collective-permute-start(bf16[2,1,2,1,128,384]{5,4,3,2,1,0:T(8,128)(2,1)} %get-tuple-element.133), channel_id=1, source_target_pairs={{1,0},{2,1},{3,2},{5,4},{6,5},{7,6},{9,8},{10,9},{11,10},{13,12},{... | collective-permute-start | bytes 1179656 | tf_op jit(solution)/shard_map/ppermute | solution.py:62
  40.3 26.6 %copy-start.8 = (bf16[2,1,1,2,128,384]{5,4,3,2,1,0:T(8,128)(2,1)S(1)}, bf16[2,1,1,2,128,384]{5,4,3,2,1,0:T(8,128)(2,1)}, u32[]{:S(2)}) copy-start(bf16[2,1,1,2,128,384]{5,4,3,2,1,0:T(8,128)(2,1)} %get-tuple-element.131) | copy-start | bytes 1179652
  40.3 29.5 %copy-start.10 = (bf16[2,1,1,1,128,384]{5,4,3,2,1,0:T(8,128)(2,1)S(1)}, bf16[2,1,1,1,128,384]{5,4,3,2,1,0:T(8,128)(2,1)}, u32[]{:S(2)}) copy-start(bf16[2,1,1,1,128,384]{5,4,3,2,1,0:T(8,128)(2,1)} %get-tuple-element.127) | copy-start | bytes 589828
  51.7 30.7 %collective-permute-start.5 = (bf16[2,1,1,1,128,384]{5,4,3,2,1,0:T(8,128)(2,1)S(1)}, bf16[2,1,1,1,128,384]{5,4,3,2,1,0:T(8,128)(2,1)S(1)}, u32[]{:S(2)}, u32[]{:S(2)}) collective-permute-start(bf16[2,1,1,1,128,384]{5,4,3,2,1,0:T(8,128)(2,1)S(1)} %copy-done.11), channel_id=1, source_target_pairs={{4,1},{5,2},{6,3},{8,5},{9,6},{10,7},{12,9},{13,10},{14,11},{16,13... | collective-permute-start | bytes 589832 | tf_op jit(solution)/shard_map/ppermute | solution.py:62
  67.0 23.4 %collective-permute-start.6 = (bf16[2,1,1,2,128,384]{5,4,3,2,1,0:T(8,128)(2,1)S(1)}, bf16[2,1,1,2,128,384]{5,4,3,2,1,0:T(8,128)(2,1)S(1)}, u32[]{:S(2)}, u32[]{:S(2)}) collective-permute-start(bf16[2,1,1,2,128,384]{5,4,3,2,1,0:T(8,128)(2,1)S(1)} %copy-done.8), channel_id=1, source_target_pairs={{4,0},{5,1},{6,2},{7,3},{8,4},{9,5},{10,6},{11,7},{12,8},{13,9},{1... | collective-permute-start | bytes 1179656 | tf_op jit(solution)/shard_map/ppermute | solution.py:62
  69.8 26.8 %collective-permute-start.7 = (bf16[2,1,1,1,128,384]{5,4,3,2,1,0:T(8,128)(2,1)S(1)}, bf16[2,1,1,1,128,384]{5,4,3,2,1,0:T(8,128)(2,1)S(1)}, u32[]{:S(2)}, u32[]{:S(2)}) collective-permute-start(bf16[2,1,1,1,128,384]{5,4,3,2,1,0:T(8,128)(2,1)S(1)} %copy-done.10), channel_id=1, source_target_pairs={{5,0},{6,1},{7,2},{9,4},{10,5},{11,6},{13,8},{14,9},{15,10},{17,12... | collective-permute-start | bytes 589832 | tf_op jit(solution)/shard_map/ppermute | solution.py:62
  212.5 22.0 %copy-start.5 = (bf16[2048,3,128,1]{0,2,1,3:T(8,128)(2,1)S(1)}, bf16[2048,3,128,1]{0,2,1,3:T(8,128)(2,1)}, u32[]{:S(2)}) copy-start(bf16[2048,3,128,1]{0,2,1,3:T(8,128)(2,1)} %reshape.568) | copy-start | bytes 4718596
  215.3 25.4 %collective-permute-start.8 = (bf16[2,1,1,1,128,384]{5,4,3,2,1,0:T(8,128)(2,1)}, bf16[2,1,1,1,128,384]{5,4,3,2,1,0:T(8,128)(2,1)}, u32[]{:S(2)}, u32[]{:S(2)}) collective-permute-start(bf16[2,1,1,1,128,384]{5,4,3,2,1,0:T(8,128)(2,1)} %get-tuple-element.118), channel_id=1, source_target_pairs={{5,0},{6,1},{7,2},{9,4},{10,5},{11,6},{13,8},{14,9},{15,10},{17,12... | collective-permute-start | bytes 589832 | tf_op jit(solution)/shard_map/ppermute | solution.py:78
  219.1 24.1 %collective-permute-start.9 = (bf16[2,1,1,2,128,384]{5,4,3,2,1,0:T(8,128)(2,1)}, bf16[2,1,1,2,128,384]{5,4,3,2,1,0:T(8,128)(2,1)}, u32[]{:S(2)}, u32[]{:S(2)}) collective-permute-start(bf16[2,1,1,2,128,384]{5,4,3,2,1,0:T(8,128)(2,1)} %get-tuple-element.120), channel_id=1, source_target_pairs={{4,0},{5,1},{6,2},{7,3},{8,4},{9,5},{10,6},{11,7},{12,8},{13,9},{1... | collective-permute-start | bytes 1179656 | tf_op jit(solution)/shard_map/ppermute | solution.py:78
  222.0 23.7 %collective-permute-start.10 = (bf16[2,1,1,1,128,384]{5,4,3,2,1,0:T(8,128)(2,1)}, bf16[2,1,1,1,128,384]{5,4,3,2,1,0:T(8,128)(2,1)}, u32[]{:S(2)}, u32[]{:S(2)}) collective-permute-start(bf16[2,1,1,1,128,384]{5,4,3,2,1,0:T(8,128)(2,1)} %get-tuple-element.117), channel_id=1, source_target_pairs={{4,1},{5,2},{6,3},{8,5},{9,6},{10,7},{12,9},{13,10},{14,11},{16,13... | collective-permute-start | bytes 589832 | tf_op jit(solution)/shard_map/ppermute | solution.py:78
  227.0 25.8 %collective-permute-start.11 = (bf16[2,1,2,1,128,384]{5,4,3,2,1,0:T(8,128)(2,1)}, bf16[2,1,2,1,128,384]{5,4,3,2,1,0:T(8,128)(2,1)}, u32[]{:S(2)}, u32[]{:S(2)}) collective-permute-start(bf16[2,1,2,1,128,384]{5,4,3,2,1,0:T(8,128)(2,1)} %get-tuple-element.122), channel_id=1, source_target_pairs={{1,0},{2,1},{3,2},{5,4},{6,5},{7,6},{9,8},{10,9},{11,10},{13,12},{... | collective-permute-start | bytes 1179656 | tf_op jit(solution)/shard_map/ppermute | solution.py:78
  229.8 24.2 %collective-permute-start.12 = (bf16[2,1,2,1,128,384]{5,4,3,2,1,0:T(8,128)(2,1)}, bf16[2,1,2,1,128,384]{5,4,3,2,1,0:T(8,128)(2,1)}, u32[]{:S(2)}, u32[]{:S(2)}) collective-permute-start(bf16[2,1,2,1,128,384]{5,4,3,2,1,0:T(8,128)(2,1)} %get-tuple-element.121), channel_id=1, source_target_pairs={{0,1},{1,2},{2,3},{4,5},{5,6},{6,7},{8,9},{9,10},{10,11},{12,13},{... | collective-permute-start | bytes 1179656 | tf_op jit(solution)/shard_map/ppermute | solution.py:78
  240.8 14.4 %collective-permute-start.13 = (bf16[2,1,1,1,128,384]{5,4,3,2,1,0:T(8,128)(2,1)S(1)}, bf16[2,1,1,1,128,384]{5,4,3,2,1,0:T(8,128)(2,1)S(1)}, u32[]{:S(2)}, u32[]{:S(2)}) collective-permute-start(bf16[2,1,1,1,128,384]{5,4,3,2,1,0:T(8,128)(2,1)S(1)} %copy-done.13), channel_id=1, source_target_pairs={{1,4},{2,5},{3,6},{5,8},{6,9},{7,10},{9,12},{10,13},{11,14},{13,16... | collective-permute-start | bytes 589832 | tf_op jit(solution)/shard_map/ppermute | solution.py:78
  243.2 25.9 %collective-permute-start.14 = (bf16[2,1,1,2,128,384]{5,4,3,2,1,0:T(8,128)(2,1)S(1)}, bf16[2,1,1,2,128,384]{5,4,3,2,1,0:T(8,128)(2,1)S(1)}, u32[]{:S(2)}, u32[]{:S(2)}) collective-permute-start(bf16[2,1,1,2,128,384]{5,4,3,2,1,0:T(8,128)(2,1)S(1)} %copy-done.9), channel_id=1, source_target_pairs={{0,4},{1,5},{2,6},{3,7},{4,8},{5,9},{6,10},{7,11},{8,12},{9,13},{1... | collective-permute-start | bytes 1179656 | tf_op jit(solution)/shard_map/ppermute | solution.py:78
  245.7 31.6 %collective-permute-start.15 = (bf16[2,1,1,1,128,384]{5,4,3,2,1,0:T(8,128)(2,1)S(1)}, bf16[2,1,1,1,128,384]{5,4,3,2,1,0:T(8,128)(2,1)S(1)}, u32[]{:S(2)}, u32[]{:S(2)}) collective-permute-start(bf16[2,1,1,1,128,384]{5,4,3,2,1,0:T(8,128)(2,1)S(1)} %copy-done.12), channel_id=1, source_target_pairs={{0,5},{1,6},{2,7},{4,9},{5,10},{6,11},{8,13},{9,14},{10,15},{12,17... | collective-permute-start | bytes 589832 | tf_op jit(solution)/shard_map/ppermute | solution.py:78
  (10 other events, 48.1 us)
Sparse Core Ops, SparseCore 0:
  22.6 104.1 all-gather.4
  128.6 34.4 all-gather.2

commit v3 on v2

--- a/solution.py
+++ b/solution.py
@@ -30,6 +30,17 @@
     natural = [("ha", b) for b in reversed(ha_bits)] + [("wa", b) for b in reversed(wa_bits)]
     perm = [order.index(s) for s in natural] + [len(steps), len(steps) + 1]
     return buf.transpose(perm).reshape(-1, cols)
+
+
+def shift_gather(block, axis):
+    count, index = lax.axis_size(axis), lax.axis_index(axis)
+    rows = block.shape[0]
+    buf = jnp.zeros((count * rows,) + block.shape[1:], block.dtype)
+    buf = lax.dynamic_update_slice(buf, block, (index * rows, 0))
+    for shift in range(1, count):
+        got = lax.ppermute(block, axis, [(k, (k + shift) % count) for k in range(count)])
+        buf = lax.dynamic_update_slice(buf, got, (((index - shift) % count) * rows, 0))
+    return buf
 
 
 def pick(length, d):
@@ -86,7 +97,7 @@
     heads = columns // HEAD
     f32, bf16 = jnp.float32, jnp.bfloat16
     whole = lax.all_gather(grad_out, "tp", axis=4, tiled=True)
-    weight = lax.all_gather(lax.all_gather(out_proj, "wa", axis=0, tiled=True), "ha", axis=0, tiled=True)
+    weight = shift_gather(shift_gather(out_proj, "wa"), "ha")
     ext = extended(jnp.stack([keys, values]))
     ext_r, ext_c = tile_rows + 2, tile_cols + 2
     row_base = lax.axis_index("ha") * tile_rows

time: 287 us -> 271 us (0.944)
  the two profiles are of different devices: /device:TPU:184 before, /device:TPU:180 now
where the time goes in v3:
time: 271 us; the launch traced here: 270 us
  starting transfers between devices  94.6 us (35%)
  waiting for transfers between devices  58.5 us (22%)
  local copies, waits for them, and re-layouts  44.4 us (16%)
  other arithmetic  32.1 us (12%)
  matrix products  25.4 us (9%)
  between operations  15.2 us (6%)
    ppermute x8, starting transfers between devices, extended(): got = lax.ppermute(piece, ('ha', 'wa'), neighbour_pairs(d_r, d_c))  38.6 us
    ppermute x8, starting transfers between devices, folded(): lax.ppermute(piece, ('ha', 'wa'), neighbour_pairs(-d_r, -d_c))  29.9 us
    ppermute x10, starting transfers between devices, shift_gather(): lax.ppermute(block, axis, [(k, (k + shift) % count) for k in range(count)])  26.1 us
    ppermute x8, waiting for transfers between devices, folded(): lax.ppermute(piece, ('ha', 'wa'), neighbour_pairs(-d_r, -d_c))  25 us
    ppermute x10, waiting for transfers between devices, shift_gather(): lax.ppermute(block, axis, [(k, (k + shift) % count) for k in range(count)])  21.6 us
    another operation x4, local copies, waits for them, and re-layouts, local(): jnp.stack([grad_k, grad_v])  21.4 us
    ppermute x8, waiting for transfers between devices, extended(): got = lax.ppermute(piece, ('ha', 'wa'), neighbour_pairs(d_r, d_c))  11.9 us
    convert_element_type x1, other arithmetic, local(): probs_lo = probs.astype(bf16)  8.63 us
  transfers between devices with their start and end apart: 27, of which 7 were waited for; matrix products, arithmetic and copies ran while one was open for 19% of the time, Pallas kernels for 0%

profile of v3, /device:TPU:180, one launch (start us, length us, event | category | flops | bytes accessed | tf_op | source)
XLA Modules:
  0.0 270.0 jit_solution(11942699863365833245)
XLA Ops:
  20.4 3.8 %collective-permute-start.1 = (bf16[2,1,1,2,128,384]{5,4,3,2,1,0:T(8,128)(2,1)}, bf16[2,1,1,2,128,384]{5,4,3,2,1,0:T(8,128)(2,1)S(1)}, u32[]{:S(2)}, u32[]{:S(2)}) collective-permute-start(bf16[2,1,1,2,128,384]{5,4,3,2,1,0:T(8,128)(2,1)} %get-tuple-element.132), channel_id=1, source_target_pairs={{0,4},{1,5},{2,6},{3,7},{4,8},{5,9},{6,10},{7,11},{8,12},{9,13},{1... | collective-permute-start | bytes 1179656 | tf_op jit(solution)/shard_map/ppermute | solution.py:73
  26.8 4.1 %collective-permute-start.2 = (bf16[2,1,1,1,128,384]{5,4,3,2,1,0:T(8,128)(2,1)}, bf16[2,1,1,1,128,384]{5,4,3,2,1,0:T(8,128)(2,1)S(1)}, u32[]{:S(2)}, u32[]{:S(2)}) collective-permute-start(bf16[2,1,1,1,128,384]{5,4,3,2,1,0:T(8,128)(2,1)} %get-tuple-element.129), channel_id=1, source_target_pairs={{1,4},{2,5},{3,6},{5,8},{6,9},{7,10},{9,12},{10,13},{11,14},{13,16... | collective-permute-start | bytes 589832 | tf_op jit(solution)/shard_map/ppermute | solution.py:73
  36.6 12.0 %collective-permute-done.11 = bf16[384,384]{1,0:T(8,128)(2,1)S(1)} collective-permute-done((bf16[384,384]{1,0:T(8,128)(2,1)S(1)}, bf16[384,384]{1,0:T(8,128)(2,1)S(1)}, u32[]{:S(2)}, u32[]{:S(2)}) %collective-permute-start.11) | collective-permute-done | bytes 294944 | tf_op jit(solution)/shard_map/ppermute | solution.py:41
  49.0 10.2 %collective-permute-start.15 = (bf16[384,384]{1,0:T(8,128)(2,1)S(1)}, bf16[384,384]{1,0:T(8,128)(2,1)S(1)}, u32[]{:S(2)}, u32[]{:S(2)}) collective-permute-start(bf16[384,384]{1,0:T(8,128)(2,1)S(1)} %constant_dynamic-update-slice_fusion.10), channel_id=1, source_target_pairs={{0,20},{4,24},{8,28},{12,0},{16,4},{20,8},{24,12},{28,16},{1,21},{... | collective-permute-start | bytes 884744 | tf_op jit(solution)/shard_map/ppermute | solution.py:41
  59.4 5.6 %collective-permute-start.17 = (bf16[384,384]{1,0:T(8,128)(2,1)S(1)}, bf16[384,384]{1,0:T(8,128)(2,1)S(1)}, u32[]{:S(2)}, u32[]{:S(2)}) collective-permute-start(bf16[384,384]{1,0:T(8,128)(2,1)S(1)} %constant_dynamic-update-slice_fusion.10), channel_id=1, source_target_pairs={{0,28},{4,0},{8,4},{12,8},{16,12},{20,16},{24,20},{28,24},{1,29},{... | collective-permute-start | bytes 884744 | tf_op jit(solution)/shard_map/ppermute | solution.py:41
  67.1 9.6 %collective-permute-done.16 = bf16[384,384]{1,0:T(8,128)(2,1)S(1)} collective-permute-done((bf16[384,384]{1,0:T(8,128)(2,1)S(1)}, bf16[384,384]{1,0:T(8,128)(2,1)S(1)}, u32[]{:S(2)}, u32[]{:S(2)}) %collective-permute-start.16) | collective-permute-done | bytes 294944 | tf_op jit(solution)/shard_map/ppermute | solution.py:41
  76.7 3.7 %collective-permute-start.4 = (bf16[2,1,2,1,128,384]{5,4,3,2,1,0:T(8,128)(2,1)S(1)}, bf16[2,1,2,1,128,384]{5,4,3,2,1,0:T(8,128)(2,1)S(1)}, u32[]{:S(2)}, u32[]{:S(2)}) collective-permute-start(bf16[2,1,2,1,128,384]{5,4,3,2,1,0:T(8,128)(2,1)S(1)} %copy-done.13), channel_id=1, source_target_pairs={{1,0},{2,1},{3,2},{5,4},{6,5},{7,6},{9,8},{10,9},{11,10},{13,12},{... | collective-permute-start | bytes 1179656 | tf_op jit(solution)/shard_map/ppermute | solution.py:73
  82.4 6.4 %collective-permute-start.6 = (bf16[2,1,1,2,128,384]{5,4,3,2,1,0:T(8,128)(2,1)S(1)}, bf16[2,1,1,2,128,384]{5,4,3,2,1,0:T(8,128)(2,1)S(1)}, u32[]{:S(2)}, u32[]{:S(2)}) collective-permute-start(bf16[2,1,1,2,128,384]{5,4,3,2,1,0:T(8,128)(2,1)S(1)} %copy-done.12), channel_id=1, source_target_pairs={{4,0},{5,1},{6,2},{7,3},{8,4},{9,5},{10,6},{11,7},{12,8},{13,9},{1... | collective-permute-start | bytes 1179656 | tf_op jit(solution)/shard_map/ppermute | solution.py:73
  89.0 13.2 %collective-permute-start.7 = (bf16[2,1,1,1,128,384]{5,4,3,2,1,0:T(8,128)(2,1)S(1)}, bf16[2,1,1,1,128,384]{5,4,3,2,1,0:T(8,128)(2,1)S(1)}, u32[]{:S(2)}, u32[]{:S(2)}) collective-permute-start(bf16[2,1,1,1,128,384]{5,4,3,2,1,0:T(8,128)(2,1)S(1)} %copy-done.15), channel_id=1, source_target_pairs={{5,0},{6,1},{7,2},{9,4},{10,5},{11,6},{13,8},{14,9},{15,10},{17,12... | collective-permute-start | bytes 589832 | tf_op jit(solution)/shard_map/ppermute | solution.py:73
  102.4 8.3 %collective-permute-done.5 = bf16[2,1,1,1,128,384]{5,4,3,2,1,0:T(8,128)(2,1)S(1)} collective-permute-done((bf16[2,1,1,1,128,384]{5,4,3,2,1,0:T(8,128)(2,1)S(1)}, bf16[2,1,1,1,128,384]{5,4,3,2,1,0:T(8,128)(2,1)S(1)}, u32[]{:S(2)}, u32[]{:S(2)}) %collective-permute-start.5) | collective-permute-done | bytes 196640 | tf_op jit(solution)/shard_map/ppermute | solution.py:73
  130.9 6.7 %fusion.60 = (f32[4,3,128]{2,0,1:T(4,128)S(1)}, f32[4,3,128,2048]{2,3,0,1:T(8,128)}) fusion(f32[3,2048,4,128]{3,1,2,0:T(8,128)S(1)} %fusion.12, pred[4,2048]{1,0:T(4,128)(4,1)S(1)} %bitcast.111), kind=kOutput, calls=%fused_computation.121 | output fusion | flops 18876416 | bytes 25180160 | tf_op jit(solution)/shard_map/sub | solution.py:129
  137.6 8.6 %fusion.9 = bf16[4,3,128,2048]{2,3,0,1:T(8,128)(2,1)} fusion(f32[4,3,128,2048]{2,3,0,1:T(8,128)} %get-tuple-element.138, f32[4,3,128]{2,0,1:T(4,128)S(1)} %get-tuple-element.137), kind=kLoop, calls=%fused_computation.18 | loop fusion | flops 6291456 | bytes 18880512 | tf_op jit(solution)/shard_map/convert_element_type | solution.py:132
  149.7 6.6 %convolution_bitcast_fusion = f32[2048,3,128]{0,2,1:T(8,128)} fusion(bf16[4,3,128,2048]{2,3,0,1:T(8,128)(2,1)} %fusion.9, bf16[4,128,3,128]{1,0,3,2:T(4,128)(2,1)S(1)} %reshape.562), kind=kOutput, calls=%fused_computation.19 | convolution fusion | flops 805306368 | bytes 9830400 | tf_op jit(solution)/shard_map/qhtl,qthd->lhd/dot_general | solution.py:146
  156.3 3.9 %stack.22 = f32[1,1,4,4,128,384]{4,3,2,5,1,0:T(4,128)S(1)} reshape(f32[2048,3,128]{0,2,1:T(8,128)} %convolution_bitcast_fusion) | data formatting | bytes 6291456 | tf_op jit(solution)/shard_map/stack | solution.py:149
  163.2 4.4 %fusion.27 = f32[4,128,3]{1,0,2:T(4,128)S(1)} fusion(bf16[4,3,128,2048]{2,3,0,1:T(8,128)(2,1)} %fusion.9, bf16[2048,3,128,1]{0,2,1,3:T(8,128)(2,1)} %reshape.567, bf16[4,128,3,128]{1,0,3,2:T(4,128)(2,1)S(1)} %reshape.562), kind=kOutput, calls=%fused_computation.50 | convolution fusion | flops 805894656 | bytes 8263680 | tf_op jit(solution)/shard_map/qhtl,lhd->qthd/dot_general | solution.py:139
  167.6 6.4 %fusion.3 = bf16[4,3,128,2048]{2,3,0,1:T(8,128)(2,1)S(1)} fusion(f32[4,3,128]{2,0,1:T(4,128)S(1)} %bitcast.112, f32[4,3,128,2048]{2,3,0,1:T(8,128)} %get-tuple-element.138, f32[4,3,128]{2,0,1:T(4,128)S(1)} %get-tuple-element.137, bf16[2048,3,128]{0,2,1:T(8,128)(2,1)S(1)} %copy-done.10, bf16[4,128,3,128]{1,0,3,2:T(4,128)(2,1)S(1)} %reshape.562), kind=kOutput, calls=%fused_computation.4 | convolution fusion | flops 821035008 | bytes 20852736 | tf_op jit(solution)/shard_map/qthd,lhd->qhtl/dot_general | solution.py:142
  176.7 9.9 %copy.112 = f32[2048,3,128]{2,1,0:T(4,128)} copy(f32[2048,3,128]{2,0,1:T(8,128)S(1)} %convolution_bitcast_fusion.1) | data formatting | bytes 6291456 | tf_op jit(solution)/shard_map/stack | solution.py:149
  186.7 4.5 %reshape.573 = f32[1,1,4,4,128,384]{5,4,3,2,1,0:T(8,128)S(1)} reshape(f32[2048,3,128]{2,1,0:T(4,128)} %copy.112) | data formatting | bytes 6291456 | tf_op jit(solution)/shard_map/stack | solution.py:149
  199.2 5.7 %collective-permute-start.19 = (bf16[2,1,1,2,128,384]{5,4,3,2,1,0:T(8,128)(2,1)}, bf16[2,1,1,2,128,384]{5,4,3,2,1,0:T(8,128)(2,1)}, u32[]{:S(2)}, u32[]{:S(2)}) collective-permute-start(bf16[2,1,1,2,128,384]{5,4,3,2,1,0:T(8,128)(2,1)} %get-tuple-element.120), channel_id=1, source_target_pairs={{4,0},{5,1},{6,2},{7,3},{8,4},{9,5},{10,6},{11,7},{12,8},{13,9},{1... | collective-permute-start | bytes 1179656 | tf_op jit(solution)/shard_map/ppermute | solution.py:89
  206.8 5.5 %collective-permute-start.21 = (bf16[2,1,2,1,128,384]{5,4,3,2,1,0:T(8,128)(2,1)}, bf16[2,1,2,1,128,384]{5,4,3,2,1,0:T(8,128)(2,1)}, u32[]{:S(2)}, u32[]{:S(2)}) collective-permute-start(bf16[2,1,2,1,128,384]{5,4,3,2,1,0:T(8,128)(2,1)} %get-tuple-element.122), channel_id=1, source_target_pairs={{1,0},{2,1},{3,2},{5,4},{6,5},{7,6},{9,8},{10,9},{11,10},{13,12},{... | collective-permute-start | bytes 1179656 | tf_op jit(solution)/shard_map/ppermute | solution.py:89
  217.7 8.4 %collective-permute-start.23 = (bf16[2,1,1,1,128,384]{5,4,3,2,1,0:T(8,128)(2,1)S(1)}, bf16[2,1,1,1,128,384]{5,4,3,2,1,0:T(8,128)(2,1)S(1)}, u32[]{:S(2)}, u32[]{:S(2)}) collective-permute-start(bf16[2,1,1,1,128,384]{5,4,3,2,1,0:T(8,128)(2,1)S(1)} %copy-done.18), channel_id=1, source_target_pairs={{1,4},{2,5},{3,6},{5,8},{6,9},{7,10},{9,12},{10,13},{11,14},{13,16... | collective-permute-start | bytes 589832 | tf_op jit(solution)/shard_map/ppermute | solution.py:89
  230.3 8.8 %collective-permute-done.20 = bf16[2,1,1,1,128,384]{5,4,3,2,1,0:T(8,128)(2,1)} collective-permute-done((bf16[2,1,1,1,128,384]{5,4,3,2,1,0:T(8,128)(2,1)}, bf16[2,1,1,1,128,384]{5,4,3,2,1,0:T(8,128)(2,1)}, u32[]{:S(2)}, u32[]{:S(2)}) %collective-permute-start.20) | collective-permute-done | bytes 196640 | tf_op jit(solution)/shard_map/ppermute | solution.py:89
  245.7 3.8 %collective-permute-done.24 = bf16[2,1,1,2,128,384]{5,4,3,2,1,0:T(8,128)(2,1)S(1)} collective-permute-done((bf16[2,1,1,2,128,384]{5,4,3,2,1,0:T(8,128)(2,1)S(1)}, bf16[2,1,1,2,128,384]{5,4,3,2,1,0:T(8,128)(2,1)S(1)}, u32[]{:S(2)}, u32[]{:S(2)}) %collective-permute-start.24) | collective-permute-done | bytes 393248 | tf_op jit(solution)/shard_map/ppermute | solution.py:89
  249.8 12.3 %collective-permute-done.25 = bf16[2,1,1,1,128,384]{5,4,3,2,1,0:T(8,128)(2,1)S(1)} collective-permute-done((bf16[2,1,1,1,128,384]{5,4,3,2,1,0:T(8,128)(2,1)S(1)}, bf16[2,1,1,1,128,384]{5,4,3,2,1,0:T(8,128)(2,1)S(1)}, u32[]{:S(2)}, u32[]{:S(2)}) %collective-permute-start.25) | collective-permute-done | bytes 196640 | tf_op jit(solution)/shard_map/ppermute | solution.py:89
  (147 shorter events, 82.3 us)
Async XLA Ops:
  7.2 139.1 %all-gather.2.cloned.1.call-start = ((), (), s32[]{:S(2)}) async-start(), calls=%async_computation | async-start | bytes 3538944 | tf_op jit(solution)/shard_map/all_gather | solution.py:99
  7.2 19.6 %collective-permute-start.8 = (bf16[96,384]{1,0:T(8,128)(2,1)}, bf16[96,384]{1,0:T(8,128)(2,1)S(1)}, u32[]{:S(2)}, u32[]{:S(2)}) collective-permute-start(bf16[96,384]{1,0:T(8,128)(2,1)} %param.25), channel_id=1, source_target_pairs={{0,1},{1,2},{2,3},{3,0},{4,5},{5,6},{6,7},{7,4},{8,9},{9,10},{10,1... | collective-permute-start | bytes 221192 | tf_op jit(solution)/shard_map/ppermute | solution.py:41
  8.8 22.2 %collective-permute-start.9 = (bf16[96,384]{1,0:T(8,128)(2,1)}, bf16[96,384]{1,0:T(8,128)(2,1)S(1)}, u32[]{:S(2)}, u32[]{:S(2)}) collective-permute-start(bf16[96,384]{1,0:T(8,128)(2,1)} %param.25), channel_id=1, source_target_pairs={{0,2},{1,3},{2,0},{3,1},{4,6},{5,7},{6,4},{7,5},{8,10},{9,11},{10,... | collective-permute-start | bytes 221192 | tf_op jit(solution)/shard_map/ppermute | solution.py:41
  10.2 20.8 %collective-permute-start.10 = (bf16[96,384]{1,0:T(8,128)(2,1)}, bf16[96,384]{1,0:T(8,128)(2,1)S(1)}, u32[]{:S(2)}, u32[]{:S(2)}) collective-permute-start(bf16[96,384]{1,0:T(8,128)(2,1)} %param.25), channel_id=1, source_target_pairs={{0,3},{1,0},{2,1},{3,2},{4,7},{5,4},{6,5},{7,6},{8,11},{9,8},{10,9... | collective-permute-start | bytes 221192 | tf_op jit(solution)/shard_map/ppermute | solution.py:41
  14.6 19.8 %collective-permute-start = (bf16[2,1,1,1,128,384]{5,4,3,2,1,0:T(8,128)(2,1)S(1)}, bf16[2,1,1,1,128,384]{5,4,3,2,1,0:T(8,128)(2,1)S(1)}, u32[]{:S(2)}, u32[]{:S(2)}) collective-permute-start(bf16[2,1,1,1,128,384]{5,4,3,2,1,0:T(8,128)(2,1)S(1)} %get-tuple-element.128), channel_id=1, source_target_pairs={{0,5},{1,6},{2,7},{4,9},{5,10},{6,11},{8,13},{9,14},{10,15},{12,17... | collective-permute-start | bytes 589832 | tf_op jit(solution)/shard_map/ppermute | solution.py:73
  20.4 62.1 %collective-permute-start.1 = (bf16[2,1,1,2,128,384]{5,4,3,2,1,0:T(8,128)(2,1)}, bf16[2,1,1,2,128,384]{5,4,3,2,1,0:T(8,128)(2,1)S(1)}, u32[]{:S(2)}, u32[]{:S(2)}) collective-permute-start(bf16[2,1,1,2,128,384]{5,4,3,2,1,0:T(8,128)(2,1)} %get-tuple-element.132), channel_id=1, source_target_pairs={{0,4},{1,5},{2,6},{3,7},{4,8},{5,9},{6,10},{7,11},{8,12},{9,13},{1... | collective-permute-start | bytes 1179656 | tf_op jit(solution)/shard_map/ppermute | solution.py:73
  26.8 62.2 %collective-permute-start.2 = (bf16[2,1,1,1,128,384]{5,4,3,2,1,0:T(8,128)(2,1)}, bf16[2,1,1,1,128,384]{5,4,3,2,1,0:T(8,128)(2,1)S(1)}, u32[]{:S(2)}, u32[]{:S(2)}) collective-permute-start(bf16[2,1,1,1,128,384]{5,4,3,2,1,0:T(8,128)(2,1)} %get-tuple-element.129), channel_id=1, source_target_pairs={{1,4},{2,5},{3,6},{5,8},{6,9},{7,10},{9,12},{10,13},{11,14},{13,16... | collective-permute-start | bytes 589832 | tf_op jit(solution)/shard_map/ppermute | solution.py:73
  31.0 17.6 %collective-permute-start.11 = (bf16[384,384]{1,0:T(8,128)(2,1)S(1)}, bf16[384,384]{1,0:T(8,128)(2,1)S(1)}, u32[]{:S(2)}, u32[]{:S(2)}) collective-permute-start(bf16[384,384]{1,0:T(8,128)(2,1)S(1)} %constant_dynamic-update-slice_fusion.10), channel_id=1, source_target_pairs={{0,4},{4,8},{8,12},{12,16},{16,20},{20,24},{24,28},{28,0},{1,5},{5... | collective-permute-start | bytes 884744 | tf_op jit(solution)/shard_map/ppermute | solution.py:41
  34.4 24.9 %collective-permute-start.13 = (bf16[384,384]{1,0:T(8,128)(2,1)S(1)}, bf16[384,384]{1,0:T(8,128)(2,1)S(1)}, u32[]{:S(2)}, u32[]{:S(2)}) collective-permute-start(bf16[384,384]{1,0:T(8,128)(2,1)S(1)} %constant_dynamic-update-slice_fusion.10), channel_id=1, source_target_pairs={{0,12},{4,16},{8,20},{12,24},{16,28},{20,0},{24,4},{28,8},{1,13},{... | collective-permute-start | bytes 884744 | tf_op jit(solution)/shard_map/ppermute | solution.py:41
  59.3 17.4 %collective-permute-start.16 = (bf16[384,384]{1,0:T(8,128)(2,1)S(1)}, bf16[384,384]{1,0:T(8,128)(2,1)S(1)}, u32[]{:S(2)}, u32[]{:S(2)}) collective-permute-start(bf16[384,384]{1,0:T(8,128)(2,1)S(1)} %constant_dynamic-update-slice_fusion.10), channel_id=1, source_target_pairs={{0,24},{4,28},{8,0},{12,4},{16,8},{20,12},{24,16},{28,20},{1,25},{... | collective-permute-start | bytes 884744 | tf_op jit(solution)/shard_map/ppermute | solution.py:41
  59.4 21.0 %collective-permute-start.17 = (bf16[384,384]{1,0:T(8,128)(2,1)S(1)}, bf16[384,384]{1,0:T(8,128)(2,1)S(1)}, u32[]{:S(2)}, u32[]{:S(2)}) collective-permute-start(bf16[384,384]{1,0:T(8,128)(2,1)S(1)} %constant_dynamic-update-slice_fusion.10), channel_id=1, source_target_pairs={{0,28},{4,0},{8,4},{12,8},{16,12},{20,16},{24,20},{28,24},{1,29},{... | collective-permute-start | bytes 884744 | tf_op jit(solution)/shard_map/ppermute | solution.py:41
  65.1 37.2 %collective-permute-start.3 = (bf16[2,1,2,1,128,384]{5,4,3,2,1,0:T(8,128)(2,1)}, bf16[2,1,2,1,128,384]{5,4,3,2,1,0:T(8,128)(2,1)S(1)}, u32[]{:S(2)}, u32[]{:S(2)}) collective-permute-start(bf16[2,1,2,1,128,384]{5,4,3,2,1,0:T(8,128)(2,1)} %get-tuple-element.134), channel_id=1, source_target_pairs={{0,1},{1,2},{2,3},{4,5},{5,6},{6,7},{8,9},{9,10},{10,11},{12,13},{... | collective-permute-start | bytes 1179656 | tf_op jit(solution)/shard_map/ppermute | solution.py:73
  76.7 25.7 %collective-permute-start.4 = (bf16[2,1,2,1,128,384]{5,4,3,2,1,0:T(8,128)(2,1)S(1)}, bf16[2,1,2,1,128,384]{5,4,3,2,1,0:T(8,128)(2,1)S(1)}, u32[]{:S(2)}, u32[]{:S(2)}) collective-permute-start(bf16[2,1,2,1,128,384]{5,4,3,2,1,0:T(8,128)(2,1)S(1)} %copy-done.13), channel_id=1, source_target_pairs={{1,0},{2,1},{3,2},{5,4},{6,5},{7,6},{9,8},{10,9},{11,10},{13,12},{... | collective-permute-start | bytes 1179656 | tf_op jit(solution)/shard_map/ppermute | solution.py:73
  80.4 30.3 %collective-permute-start.5 = (bf16[2,1,1,1,128,384]{5,4,3,2,1,0:T(8,128)(2,1)S(1)}, bf16[2,1,1,1,128,384]{5,4,3,2,1,0:T(8,128)(2,1)S(1)}, u32[]{:S(2)}, u32[]{:S(2)}) collective-permute-start(bf16[2,1,1,1,128,384]{5,4,3,2,1,0:T(8,128)(2,1)S(1)} %copy-done.16), channel_id=1, source_target_pairs={{4,1},{5,2},{6,3},{8,5},{9,6},{10,7},{12,9},{13,10},{14,11},{16,13... | collective-permute-start | bytes 589832 | tf_op jit(solution)/shard_map/ppermute | solution.py:73
  82.4 31.9 %collective-permute-start.6 = (bf16[2,1,1,2,128,384]{5,4,3,2,1,0:T(8,128)(2,1)S(1)}, bf16[2,1,1,2,128,384]{5,4,3,2,1,0:T(8,128)(2,1)S(1)}, u32[]{:S(2)}, u32[]{:S(2)}) collective-permute-start(bf16[2,1,1,2,128,384]{5,4,3,2,1,0:T(8,128)(2,1)S(1)} %copy-done.12), channel_id=1, source_target_pairs={{4,0},{5,1},{6,2},{7,3},{8,4},{9,5},{10,6},{11,7},{12,8},{13,9},{1... | collective-permute-start | bytes 1179656 | tf_op jit(solution)/shard_map/ppermute | solution.py:73
  89.0 25.4 %collective-permute-start.7 = (bf16[2,1,1,1,128,384]{5,4,3,2,1,0:T(8,128)(2,1)S(1)}, bf16[2,1,1,1,128,384]{5,4,3,2,1,0:T(8,128)(2,1)S(1)}, u32[]{:S(2)}, u32[]{:S(2)}) collective-permute-start(bf16[2,1,1,1,128,384]{5,4,3,2,1,0:T(8,128)(2,1)S(1)} %copy-done.15), channel_id=1, source_target_pairs={{5,0},{6,1},{7,2},{9,4},{10,5},{11,6},{13,8},{14,9},{15,10},{17,12... | collective-permute-start | bytes 589832 | tf_op jit(solution)/shard_map/ppermute | solution.py:73
  196.6 21.1 %collective-permute-start.18 = (bf16[2,1,1,1,128,384]{5,4,3,2,1,0:T(8,128)(2,1)}, bf16[2,1,1,1,128,384]{5,4,3,2,1,0:T(8,128)(2,1)}, u32[]{:S(2)}, u32[]{:S(2)}) collective-permute-start(bf16[2,1,1,1,128,384]{5,4,3,2,1,0:T(8,128)(2,1)} %get-tuple-element.118), channel_id=1, source_target_pairs={{5,0},{6,1},{7,2},{9,4},{10,5},{11,6},{13,8},{14,9},{15,10},{17,12... | collective-permute-start | bytes 589832 | tf_op jit(solution)/shard_map/ppermute | solution.py:89
  199.2 28.0 %collective-permute-start.19 = (bf16[2,1,1,2,128,384]{5,4,3,2,1,0:T(8,128)(2,1)}, bf16[2,1,1,2,128,384]{5,4,3,2,1,0:T(8,128)(2,1)}, u32[]{:S(2)}, u32[]{:S(2)}) collective-permute-start(bf16[2,1,1,2,128,384]{5,4,3,2,1,0:T(8,128)(2,1)} %get-tuple-element.120), channel_id=1, source_target_pairs={{4,0},{5,1},{6,2},{7,3},{8,4},{9,5},{10,6},{11,7},{12,8},{13,9},{1... | collective-permute-start | bytes 1179656 | tf_op jit(solution)/shard_map/ppermute | solution.py:89
  204.8 34.3 %collective-permute-start.20 = (bf16[2,1,1,1,128,384]{5,4,3,2,1,0:T(8,128)(2,1)}, bf16[2,1,1,1,128,384]{5,4,3,2,1,0:T(8,128)(2,1)}, u32[]{:S(2)}, u32[]{:S(2)}) collective-permute-start(bf16[2,1,1,1,128,384]{5,4,3,2,1,0:T(8,128)(2,1)} %get-tuple-element.117), channel_id=1, source_target_pairs={{4,1},{5,2},{6,3},{8,5},{9,6},{10,7},{12,9},{13,10},{14,11},{16,13... | collective-permute-start | bytes 589832 | tf_op jit(solution)/shard_map/ppermute | solution.py:89
  206.8 35.2 %collective-permute-start.21 = (bf16[2,1,2,1,128,384]{5,4,3,2,1,0:T(8,128)(2,1)}, bf16[2,1,2,1,128,384]{5,4,3,2,1,0:T(8,128)(2,1)}, u32[]{:S(2)}, u32[]{:S(2)}) collective-permute-start(bf16[2,1,2,1,128,384]{5,4,3,2,1,0:T(8,128)(2,1)} %get-tuple-element.122), channel_id=1, source_target_pairs={{1,0},{2,1},{3,2},{5,4},{6,5},{7,6},{9,8},{10,9},{11,10},{13,12},{... | collective-permute-start | bytes 1179656 | tf_op jit(solution)/shard_map/ppermute | solution.py:89
  212.2 31.0 %collective-permute-start.22 = (bf16[2,1,2,1,128,384]{5,4,3,2,1,0:T(8,128)(2,1)}, bf16[2,1,2,1,128,384]{5,4,3,2,1,0:T(8,128)(2,1)}, u32[]{:S(2)}, u32[]{:S(2)}) collective-permute-start(bf16[2,1,2,1,128,384]{5,4,3,2,1,0:T(8,128)(2,1)} %get-tuple-element.121), channel_id=1, source_target_pairs={{0,1},{1,2},{2,3},{4,5},{5,6},{6,7},{8,9},{9,10},{10,11},{12,13},{... | collective-permute-start | bytes 1179656 | tf_op jit(solution)/shard_map/ppermute | solution.py:89
  217.7 26.7 %collective-permute-start.23 = (bf16[2,1,1,1,128,384]{5,4,3,2,1,0:T(8,128)(2,1)S(1)}, bf16[2,1,1,1,128,384]{5,4,3,2,1,0:T(8,128)(2,1)S(1)}, u32[]{:S(2)}, u32[]{:S(2)}) collective-permute-start(bf16[2,1,1,1,128,384]{5,4,3,2,1,0:T(8,128)(2,1)S(1)} %copy-done.18), channel_id=1, source_target_pairs={{1,4},{2,5},{3,6},{5,8},{6,9},{7,10},{9,12},{10,13},{11,14},{13,16... | collective-permute-start | bytes 589832 | tf_op jit(solution)/shard_map/ppermute | solution.py:89
  227.1 22.4 %collective-permute-start.24 = (bf16[2,1,1,2,128,384]{5,4,3,2,1,0:T(8,128)(2,1)S(1)}, bf16[2,1,1,2,128,384]{5,4,3,2,1,0:T(8,128)(2,1)S(1)}, u32[]{:S(2)}, u32[]{:S(2)}) collective-permute-start(bf16[2,1,1,2,128,384]{5,4,3,2,1,0:T(8,128)(2,1)S(1)} %copy-done.14), channel_id=1, source_target_pairs={{0,4},{1,5},{2,6},{3,7},{4,8},{5,9},{6,10},{7,11},{8,12},{9,13},{1... | collective-permute-start | bytes 1179656 | tf_op jit(solution)/shard_map/ppermute | solution.py:89
  239.1 22.9 %collective-permute-start.25 = (bf16[2,1,1,1,128,384]{5,4,3,2,1,0:T(8,128)(2,1)S(1)}, bf16[2,1,1,1,128,384]{5,4,3,2,1,0:T(8,128)(2,1)S(1)}, u32[]{:S(2)}, u32[]{:S(2)}) collective-permute-start(bf16[2,1,1,1,128,384]{5,4,3,2,1,0:T(8,128)(2,1)S(1)} %copy-done.17), channel_id=1, source_target_pairs={{0,5},{1,6},{2,7},{4,9},{5,10},{6,11},{8,13},{9,14},{10,15},{12,17... | collective-permute-start | bytes 589832 | tf_op jit(solution)/shard_map/ppermute | solution.py:89
  (23 other events, 533.4 us)
Sparse Core Ops, SparseCore 0:
  12.6 30.0 all-gather.1

commit v4 on v1

--- a/solution.py
+++ b/solution.py
@@ -66,19 +66,23 @@
     return out
 
 
-def folded(totals):
-    rows, cols = totals.shape[2] - 2, totals.shape[3] - 2
-    own = totals[:, :, 1:-1, 1:-1]
+def folded(grad_k, grad_v):
+    rows, cols = grad_k.shape[1] - 2, grad_k.shape[2] - 2
+    own_k = grad_k[:, 1:-1, 1:-1]
+    own_v = grad_v[:, 1:-1, 1:-1]
     for d_r, d_c in DIRS:
         r0 = 0 if d_r < 0 else (rows + 1 if d_r > 0 else 1)
         c0 = 0 if d_c < 0 else (cols + 1 if d_c > 0 else 1)
         nr = rows if d_r == 0 else 1
         nc = cols if d_c == 0 else 1
-        piece = totals[:, :, r0 : r0 + nr, c0 : c0 + nc].astype(jnp.bfloat16)
+        piece = jnp.stack(
+            [grad_k[:, r0 : r0 + nr, c0 : c0 + nc], grad_v[:, r0 : r0 + nr, c0 : c0 + nc]]
+        ).astype(jnp.bfloat16)
         got = lax.ppermute(piece, ("ha", "wa"), neighbour_pairs(-d_r, -d_c)).astype(jnp.float32)
         rs, cs = pick(rows, d_r), pick(cols, d_c)
-        own = own.at[:, :, rs, cs].add(got)
-    return own
+        own_k = own_k.at[:, rs, cs].add(got[0])
+        own_v = own_v.at[:, rs, cs].add(got[1])
+    return own_k, own_v
 
 
 def local(queries, keys, values, grad_out, out_proj):
@@ -87,7 +91,15 @@
     f32, bf16 = jnp.float32, jnp.bfloat16
     whole = lax.all_gather(grad_out, "tp", axis=4, tiled=True)
     weight = gather_rows(out_proj)
-    ext = extended(jnp.stack([keys, values]))
+
+    def head_major(array):
+        split = array.reshape(frames * tile_rows, tile_cols, tile_len, heads, HEAD)
+        return jnp.transpose(split, (3, 0, 1, 2, 4))
+
+    def head_minor(array):
+        return jnp.transpose(array, (1, 2, 3, 0, 4)).reshape(queries.shape)
+
+    ext = extended(jnp.stack([head_major(keys), head_major(values)]))
     ext_r, ext_c = tile_rows + 2, tile_cols + 2
     row_base = lax.axis_index("ha") * tile_rows
     col_base = lax.axis_index("wa") * tile_cols
@@ -104,16 +116,16 @@
     inside = in_r[:, None, :, None] & in_c[None, :, None, :]
     inside = inside.reshape(tile_rows * tile_cols, 1, ext_r * ext_c, 1)
     inside = jnp.broadcast_to(inside, (tile_rows * tile_cols, 1, ext_r * ext_c, tile_len))
-    inside = inside.reshape(tile_rows * tile_cols, 1, 1, ext_r * ext_c * tile_len)
+    inside = inside.reshape(1, tile_rows * tile_cols, 1, ext_r * ext_c * tile_len)
     q_tiles = tile_rows * tile_cols
     keys_n = ext_r * ext_c * tile_len
     scale = HEAD ** (-0.5)
 
-    key_e = ext[0].reshape(keys_n, heads, HEAD)
-    val_e = ext[1].reshape(keys_n, heads, HEAD)
-    query = queries.reshape(q_tiles, tile_len, heads, HEAD)
+    key_e = ext[0].reshape(heads, keys_n, HEAD)
+    val_e = ext[1].reshape(heads, keys_n, HEAD)
+    query = head_major(queries).reshape(heads, q_tiles, tile_len, HEAD)
 
-    scores = jnp.einsum("qthd,lhd->qhtl", query, key_e, preferred_element_type=f32) * scale
+    scores = jnp.einsum("hqtd,hld->hqtl", query, key_e, preferred_element_type=f32) * scale
     scores = jnp.where(inside, scores, -jnp.inf)
     scores = scores - jnp.max(scores, axis=-1, keepdims=True)
     expo = jnp.exp(scores)
@@ -123,21 +135,20 @@
     grad_attn = jnp.dot(
         whole.reshape(-1, whole.shape[-1]), weight, preferred_element_type=f32
     ).astype(bf16)
-    grad = grad_attn.reshape(q_tiles, tile_len, heads, HEAD)
+    grad = head_major(grad_attn.reshape(queries.shape)).reshape(heads, q_tiles, tile_len, HEAD)
 
-    attn = jnp.einsum("qhtl,lhd->qthd", probs_lo, val_e, preferred_element_type=f32)
-    delta = jnp.sum(grad.astype(f32) * attn, axis=-1)
-    delta = jnp.transpose(delta, (0, 2, 1))[..., None]
-    grad_probs = jnp.einsum("qthd,lhd->qhtl", grad, val_e, preferred_element_type=f32)
+    attn = jnp.einsum("hqtl,hld->hqtd", probs_lo, val_e, preferred_element_type=f32)
+    delta = jnp.sum(grad.astype(f32) * attn, axis=-1, keepdims=True)
+    grad_probs = jnp.einsum("hqtd,hld->hqtl", grad, val_e, preferred_element_type=f32)
     grad_scores = (probs * (grad_probs - delta) * scale).astype(bf16)
-    grad_q = jnp.einsum("qhtl,lhd->qthd", grad_scores, key_e, preferred_element_type=f32)
-    grad_k = jnp.einsum("qhtl,qthd->lhd", grad_scores, query, preferred_element_type=f32)
-    grad_v = jnp.einsum("qhtl,qthd->lhd", probs_lo, grad, preferred_element_type=f32)
+    grad_q = jnp.einsum("hqtl,hld->hqtd", grad_scores, key_e, preferred_element_type=f32)
+    grad_k = jnp.einsum("hqtl,hqtd->hld", grad_scores, query, preferred_element_type=f32)
+    grad_v = jnp.einsum("hqtl,hqtd->hld", probs_lo, grad, preferred_element_type=f32)
 
-    grad_queries = grad_q.reshape(queries.shape).astype(bf16)
-    totals = jnp.stack([grad_k, grad_v]).reshape(2, frames, ext_r, ext_c, tile_len, columns)
-    own = folded(totals)
-    return (grad_queries, own[0].astype(bf16), own[1].astype(bf16))
+    grad_q = grad_q.astype(bf16).reshape(heads, frames * tile_rows, tile_cols, tile_len, HEAD)
+    shape_e = (heads, frames * ext_r, ext_c, tile_len, HEAD)
+    own_k, own_v = folded(grad_k.reshape(shape_e), grad_v.reshape(shape_e))
+    return (head_minor(grad_q), head_minor(own_k.astype(bf16)), head_minor(own_v.astype(bf16)))
 
 
 def solution(mesh):

time: 257 us -> 253 us (0.984)
  the two profiles are of different devices: /device:TPU:184 before, /device:TPU:64 now
where the time goes in v4:
time: 253 us; the launch traced here: 251 us
  waiting for transfers between devices  74.7 us (30%)
  starting transfers between devices  70.3 us (28%)
  other arithmetic  32.5 us (13%)
  matrix products  30.1 us (12%)
  local copies, waits for them, and re-layouts  28.1 us (11%)
  between operations  14.9 us (6%)
    ppermute x5, waiting for transfers between devices, doubling_gather(): other = lax.ppermute(buf, axis, [(i, i ^ bit) for i in range(count)])  49.3 us
    ppermute x8, starting transfers between devices, folded(): lax.ppermute(piece, ('ha', 'wa'), neighbour_pairs(-d_r, -d_c))  30.8 us
    ppermute x8, starting transfers between devices, extended(): got = lax.ppermute(piece, ('ha', 'wa'), neighbour_pairs(d_r, d_c))  27.1 us
    ppermute x8, waiting for transfers between devices, extended(): got = lax.ppermute(piece, ('ha', 'wa'), neighbour_pairs(d_r, d_c))  14.6 us
    ppermute x5, starting transfers between devices, doubling_gather(): other = lax.ppermute(buf, axis, [(i, i ^ bit) for i in range(count)])  12.4 us
    ppermute x8, waiting for transfers between devices, folded(): lax.ppermute(piece, ('ha', 'wa'), neighbour_pairs(-d_r, -d_c))  10.8 us
    convert_element_type x1, other arithmetic, local(): probs_lo = probs.astype(bf16)  8.48 us
    sub x1, matrix products, local(): scores = scores - jnp.max(scores, axis=-1, keepdims=True)  7.12 us
  transfers between devices with their start and end apart: 22, of which 8 were waited for; matrix products, arithmetic and copies ran while one was open for 19% of the time, Pallas kernels for 0%

profile of v4, /device:TPU:64, one launch (start us, length us, event | category | flops | bytes accessed | tf_op | source)
XLA Modules:
  0.0 250.7 jit_solution(12804589717683658641)
XLA Ops:
  10.5 7.0 %collective-permute-start = (bf16[2,3,1,1,128,128]{4,5,1,3,2,0:T(8,128)(2,1)S(1)}, bf16[2,3,1,1,128,128]{4,5,1,3,2,0:T(8,128)(2,1)S(1)}, u32[]{:S(2)}, u32[]{:S(2)}) collective-permute-start(bf16[2,3,1,1,128,128]{4,5,1,3,2,0:T(8,128)(2,1)S(1)} %get-tuple-element.226), channel_id=1, source_target_pairs={{0,5},{1,6},{2,7},{4,9},{5,10},{6,11},{8,13},{9,14},{10,15},{12,17... | collective-permute-start | bytes 589832 | tf_op jit(solution)/shard_map/ppermute | solution.py:62
  18.4 3.0 %collective-permute-start.1 = (bf16[2,3,1,2,128,128]{4,5,1,3,2,0:T(8,128)(2,1)}, bf16[2,3,1,2,128,128]{4,5,1,3,2,0:T(8,128)(2,1)S(1)}, u32[]{:S(2)}, u32[]{:S(2)}) collective-permute-start(bf16[2,3,1,2,128,128]{4,5,1,3,2,0:T(8,128)(2,1)} %get-tuple-element.230), channel_id=1, source_target_pairs={{0,4},{1,5},{2,6},{3,7},{4,8},{5,9},{6,10},{7,11},{8,12},{9,13},{1... | collective-permute-start | bytes 1179656 | tf_op jit(solution)/shard_map/ppermute | solution.py:62
  24.8 6.7 %collective-permute-start.3 = (bf16[2,3,2,1,128,128]{4,5,1,3,2,0:T(8,128)(2,1)}, bf16[2,3,2,1,128,128]{4,5,1,3,2,0:T(8,128)(2,1)S(1)}, u32[]{:S(2)}, u32[]{:S(2)}) collective-permute-start(bf16[2,3,2,1,128,128]{4,5,1,3,2,0:T(8,128)(2,1)} %get-tuple-element.232), channel_id=1, source_target_pairs={{0,1},{1,2},{2,3},{4,5},{5,6},{6,7},{8,9},{9,10},{10,11},{12,13},{... | collective-permute-start | bytes 1179656 | tf_op jit(solution)/shard_map/ppermute | solution.py:62
  32.2 24.2 %collective-permute-done.8 = bf16[96,384]{1,0:T(8,128)(2,1)S(1)} collective-permute-done((bf16[96,384]{1,0:T(8,128)(2,1)S(1)}, bf16[96,384]{1,0:T(8,128)(2,1)S(1)}, u32[]{:S(2)}, u32[]{:S(2)}) %collective-permute-start.8) | collective-permute-done | bytes 73760 | tf_op jit(solution)/shard_map/ppermute | solution.py:15
  59.5 4.2 %collective-permute-start.4 = (bf16[2,3,2,1,128,128]{4,5,1,3,2,0:T(8,128)(2,1)}, bf16[2,3,2,1,128,128]{4,5,1,3,2,0:T(8,128)(2,1)S(1)}, u32[]{:S(2)}, u32[]{:S(2)}) collective-permute-start(bf16[2,3,2,1,128,128]{4,5,1,3,2,0:T(8,128)(2,1)} %get-tuple-element.231), channel_id=1, source_target_pairs={{1,0},{2,1},{3,2},{5,4},{6,5},{7,6},{9,8},{10,9},{11,10},{13,12},{... | collective-permute-start | bytes 1179656 | tf_op jit(solution)/shard_map/ppermute | solution.py:62
  71.4 9.6 %collective-permute-start.10 = (bf16[384,384]{1,0:T(8,128)(2,1)}, bf16[384,384]{1,0:T(8,128)(2,1)}, u32[]{:S(2)}, u32[]{:S(2)}) collective-permute-start(bf16[384,384]{1,0:T(8,128)(2,1)} %maximum_select_fusion.3), channel_id=1, source_target_pairs={{0,16},{4,20},{8,24},{12,28},{16,0},{20,4},{24,8},{28,12},{1,17},{... | collective-permute-start | bytes 884744 | tf_op jit(solution)/shard_map/ppermute | solution.py:15
  81.2 4.2 %collective-permute-done.6 = bf16[2,3,1,2,128,128]{4,5,1,3,2,0:T(8,128)(2,1)S(1)} collective-permute-done((bf16[2,3,1,2,128,128]{4,5,1,3,2,0:T(8,128)(2,1)S(1)}, bf16[2,3,1,2,128,128]{4,5,1,3,2,0:T(8,128)(2,1)S(1)}, u32[]{:S(2)}, u32[]{:S(2)}) %collective-permute-start.6) | collective-permute-done | bytes 393248 | tf_op jit(solution)/shard_map/ppermute | solution.py:62
  85.5 10.3 %collective-permute-done.7 = bf16[2,3,1,1,128,128]{4,5,1,3,2,0:T(8,128)(2,1)S(1)} collective-permute-done((bf16[2,3,1,1,128,128]{4,5,1,3,2,0:T(8,128)(2,1)S(1)}, bf16[2,3,1,1,128,128]{4,5,1,3,2,0:T(8,128)(2,1)S(1)}, u32[]{:S(2)}, u32[]{:S(2)}) %collective-permute-start.7) | collective-permute-done | bytes 196640 | tf_op jit(solution)/shard_map/ppermute | solution.py:62
  102.5 7.1 %fusion.59 = (f32[3,4,128]{2,1,0:T(4,128)S(1)}, f32[3,4,128,2048]{2,3,1,0:T(8,128)}) fusion(pred[4,2048]{1,0:T(4,128)(4,1)S(1)} %bitcast.261, bf16[3,2048,128,1]{2,1,3,0:T(8,128)(2,1)S(1)} %bitcast.252, bf16[3,4,128,128]{2,3,0,1:T(8,128)(2,1)S(1)} %bitcast.247), kind=kOutput, calls=%fused_computation.149 | convolution fusion | flops 817891328 | bytes 14563328 | tf_op jit(solution)/shard_map/sub | solution.py:130
  109.6 6.5 %collective-permute-done.11 = bf16[768,384]{1,0:T(8,128)(2,1)S(1)} collective-permute-done((bf16[768,384]{1,0:T(8,128)(2,1)S(1)}, bf16[768,384]{1,0:T(8,128)(2,1)S(1)}, u32[]{:S(2)}, u32[]{:S(2)}) %collective-permute-start.11) | collective-permute-done | bytes 589856 | tf_op jit(solution)/shard_map/ppermute | solution.py:15
  116.9 8.5 %fusion.5 = bf16[3,4,128,2048]{2,3,1,0:T(8,128)(2,1)} fusion(f32[3,4,128,2048]{2,3,1,0:T(8,128)} %get-tuple-element.242, f32[3,4,128]{2,1,0:T(4,128)S(1)} %get-tuple-element.241), kind=kLoop, calls=%fused_computation.9 | loop fusion | flops 6291456 | bytes 18880512 | tf_op jit(solution)/shard_map/convert_element_type | solution.py:133
  125.4 18.5 %collective-permute-done.12 = bf16[1536,384]{1,0:T(8,128)(2,1)S(1)} collective-permute-done((bf16[1536,384]{1,0:T(8,128)(2,1)S(1)}, bf16[1536,384]{1,0:T(8,128)(2,1)S(1)}, u32[]{:S(2)}, u32[]{:S(2)}) %collective-permute-start.12) | collective-permute-done | bytes 1179680 | tf_op jit(solution)/shard_map/ppermute | solution.py:15
  144.9 4.1 %fusion.9 = bf16[512,384]{0,1:T(8,128)(2,1)} fusion(bf16[3072,384]{1,0:T(8,128)(2,1)S(1)} %bitcast.246, bf16[512,3072]{1,0:T(8,128)(2,1)} %bitcast.262), kind=kOutput, calls=%fused_computation.33 | convolution fusion | flops 1208156160 | bytes 5898240 | tf_op jit(solution)/shard_map/dot_general | solution.py:135
  150.3 6.4 %fusion.64 = f32[3,2048,128,1]{2,1,3,0:T(8,128)} fusion(bf16[3,4,128,2048]{2,3,1,0:T(8,128)(2,1)} %fusion.5, bf16[3,4,128,128]{2,3,1,0:T(8,128)(2,1)S(1)} %bitcast.249), kind=kOutput, calls=%fused_computation.150 | convolution fusion | flops 805306368 | bytes 9830400 | tf_op jit(solution)/shard_map/hqtl,hqtd->hld/dot_general | solution.py:146
  157.9 6.0 %multiply_convert_fusion = bf16[3,4,128,2048]{2,3,1,0:T(8,128)(2,1)S(1)} fusion(f32[3,4,128]{2,1,0:T(4,128)S(1)} %fusion.8, bf16[3,2048,128,1]{2,1,3,0:T(8,128)(2,1)S(1)} %bitcast.255, bf16[3,4,128,128]{2,3,1,0:T(8,128)(2,1)S(1)} %bitcast.251, f32[3,4,128,2048]{2,3,1,0:T(8,128)} %get-tuple-element.242, f32[3,4,128]{2,1,0:T(4,128)S(1)} %get-tuple-element.241), kind=kOutput, calls=%fused_computation.2 | convolution fusion | flops 821035008 | bytes 20852736 | tf_op jit(solution)/shard_map/hqtd,hld->hqtl/dot_general | solution.py:142
  165.7 3.5 %fusion.29 = f32[3,2048,128,1]{2,1,3,0:T(8,128)} fusion(bf16[3,4,128,2048]{2,3,1,0:T(8,128)(2,1)S(1)} %multiply_convert_fusion, bf16[3,4,128,128]{2,3,0,1:T(8,128)(2,1)S(1)} %bitcast.248), kind=kOutput, calls=%fused_computation.67 | convolution fusion | flops 805306368 | bytes 9830400 | tf_op jit(solution)/shard_map/hqtl,hqtd->hld/dot_general | solution.py:145
  169.2 2.4 copy.97
  173.8 3.5 %copy.93 = f32[3,4,4,128,128]{3,4,0,2,1:T(8,128)} copy(f32[3,4,4,128,128]{4,3,2,1,0:T(8,128)} %bitcast.236) | data formatting | bytes 6291456 | tf_op jit(solution)/shard_map/reshape | solution.py:150
  188.2 5.9 %collective-permute-start.18 = (bf16[2,3,1,1,128,128]{4,5,1,3,2,0:T(8,128)(2,1)}, bf16[2,3,1,1,128,128]{4,5,1,3,2,0:T(8,128)(2,1)}, u32[]{:S(2)}, u32[]{:S(2)}) collective-permute-start(bf16[2,3,1,1,128,128]{4,5,1,3,2,0:T(8,128)(2,1)} %pad_maximum_fusion.7), channel_id=1, source_target_pairs={{1,4},{2,5},{3,6},{5,8},{6,9},{7,10},{9,12},{10,13},{11,14},{13,16... | collective-permute-start | bytes 589832 | tf_op jit(solution)/shard_map/ppermute | solution.py:81
  194.8 11.7 %collective-permute-start.20 = (bf16[2,3,1,1,128,128]{4,5,1,3,2,0:T(8,128)(2,1)}, bf16[2,3,1,1,128,128]{4,5,1,3,2,0:T(8,128)(2,1)}, u32[]{:S(2)}, u32[]{:S(2)}) collective-permute-start(bf16[2,3,1,1,128,128]{4,5,1,3,2,0:T(8,128)(2,1)} %pad_maximum_fusion.8), channel_id=1, source_target_pairs={{0,5},{1,6},{2,7},{4,9},{5,10},{6,11},{8,13},{9,14},{10,15},{12,17... | collective-permute-start | bytes 589832 | tf_op jit(solution)/shard_map/ppermute | solution.py:81
  216.1 6.0 %collective-permute-start.17 = (bf16[2,3,2,1,128,128]{4,5,1,2,3,0:T(8,128)(2,1)}, bf16[2,3,2,1,128,128]{4,5,1,2,3,0:T(8,128)(2,1)S(1)}, u32[]{:S(2)}, u32[]{:S(2)}) collective-permute-start(bf16[2,3,2,1,128,128]{4,5,1,2,3,0:T(8,128)(2,1)} %pad_maximum_fusion.3), channel_id=1, source_target_pairs={{0,1},{1,2},{2,3},{4,5},{5,6},{6,7},{8,9},{9,10},{10,11},{12,13},{... | collective-permute-start | bytes 1179656 | tf_op jit(solution)/shard_map/ppermute | solution.py:81
  228.8 3.1 %collective-permute-done.16 = bf16[2,3,2,1,128,128]{4,5,1,2,3,0:T(8,128)(2,1)S(1)} collective-permute-done((bf16[2,3,2,1,128,128]{4,5,1,2,3,0:T(8,128)(2,1)}, bf16[2,3,2,1,128,128]{4,5,1,2,3,0:T(8,128)(2,1)S(1)}, u32[]{:S(2)}, u32[]{:S(2)}) %collective-permute-start.16) | collective-permute-done | bytes 393248 | tf_op jit(solution)/shard_map/ppermute | solution.py:81
  232.2 4.7 %collective-permute-done.17 = bf16[2,3,2,1,128,128]{4,5,1,2,3,0:T(8,128)(2,1)S(1)} collective-permute-done((bf16[2,3,2,1,128,128]{4,5,1,2,3,0:T(8,128)(2,1)}, bf16[2,3,2,1,128,128]{4,5,1,2,3,0:T(8,128)(2,1)S(1)}, u32[]{:S(2)}, u32[]{:S(2)}) %collective-permute-start.17) | collective-permute-done | bytes 393248 | tf_op jit(solution)/shard_map/ppermute | solution.py:81
  238.6 3.0 %collective-permute-done.19 = bf16[2,3,1,2,128,128]{4,5,1,3,2,0:T(8,128)(2,1)S(1)} collective-permute-done((bf16[2,3,1,2,128,128]{4,5,1,3,2,0:T(8,128)(2,1)S(1)}, bf16[2,3,1,2,128,128]{4,5,1,3,2,0:T(8,128)(2,1)S(1)}, u32[]{:S(2)}, u32[]{:S(2)}) %collective-permute-start.19) | collective-permute-done | bytes 393248 | tf_op jit(solution)/shard_map/ppermute | solution.py:81
  (151 shorter events, 65.7 us)
Async XLA Ops:
  7.2 137.7 %all-gather.2.cloned.1.call-start = ((), (), s32[]{:S(2)}) async-start(), calls=%async_computation | async-start | bytes 3538944 | tf_op jit(solution)/shard_map/all_gather | solution.py:92
  10.5 47.3 %copy-start.6 = (bf16[1,2,2,128,384]{4,3,2,1,0:T(8,128)(2,1)S(1)}, bf16[1,2,2,128,384]{4,3,2,1,0:T(8,128)(2,1)}, u32[]{:S(2)}) copy-start(bf16[1,2,2,128,384]{4,3,2,1,0:T(8,128)(2,1)} %param.37) | copy-start | bytes 1179652
  10.5 48.3 %collective-permute-start = (bf16[2,3,1,1,128,128]{4,5,1,3,2,0:T(8,128)(2,1)S(1)}, bf16[2,3,1,1,128,128]{4,5,1,3,2,0:T(8,128)(2,1)S(1)}, u32[]{:S(2)}, u32[]{:S(2)}) collective-permute-start(bf16[2,3,1,1,128,128]{4,5,1,3,2,0:T(8,128)(2,1)S(1)} %get-tuple-element.226), channel_id=1, source_target_pairs={{0,5},{1,6},{2,7},{4,9},{5,10},{6,11},{8,13},{9,14},{10,15},{12,17... | collective-permute-start | bytes 589832 | tf_op jit(solution)/shard_map/ppermute | solution.py:62
  18.4 49.3 %collective-permute-start.1 = (bf16[2,3,1,2,128,128]{4,5,1,3,2,0:T(8,128)(2,1)}, bf16[2,3,1,2,128,128]{4,5,1,3,2,0:T(8,128)(2,1)S(1)}, u32[]{:S(2)}, u32[]{:S(2)}) collective-permute-start(bf16[2,3,1,2,128,128]{4,5,1,3,2,0:T(8,128)(2,1)} %get-tuple-element.230), channel_id=1, source_target_pairs={{0,4},{1,5},{2,6},{3,7},{4,8},{5,9},{6,10},{7,11},{8,12},{9,13},{1... | collective-permute-start | bytes 1179656 | tf_op jit(solution)/shard_map/ppermute | solution.py:62
  21.5 47.6 %collective-permute-start.2 = (bf16[2,3,1,1,128,128]{4,5,1,3,2,0:T(8,128)(2,1)}, bf16[2,3,1,1,128,128]{4,5,1,3,2,0:T(8,128)(2,1)}, u32[]{:S(2)}, u32[]{:S(2)}) collective-permute-start(bf16[2,3,1,1,128,128]{4,5,1,3,2,0:T(8,128)(2,1)} %get-tuple-element.227), channel_id=1, source_target_pairs={{1,4},{2,5},{3,6},{5,8},{6,9},{7,10},{9,12},{10,13},{11,14},{13,16... | collective-permute-start | bytes 589832 | tf_op jit(solution)/shard_map/ppermute | solution.py:62
  24.8 46.6 %collective-permute-start.3 = (bf16[2,3,2,1,128,128]{4,5,1,3,2,0:T(8,128)(2,1)}, bf16[2,3,2,1,128,128]{4,5,1,3,2,0:T(8,128)(2,1)S(1)}, u32[]{:S(2)}, u32[]{:S(2)}) collective-permute-start(bf16[2,3,2,1,128,128]{4,5,1,3,2,0:T(8,128)(2,1)} %get-tuple-element.232), channel_id=1, source_target_pairs={{0,1},{1,2},{2,3},{4,5},{5,6},{6,7},{8,9},{9,10},{10,11},{12,13},{... | collective-permute-start | bytes 1179656 | tf_op jit(solution)/shard_map/ppermute | solution.py:62
  31.5 24.9 %collective-permute-start.8 = (bf16[96,384]{1,0:T(8,128)(2,1)S(1)}, bf16[96,384]{1,0:T(8,128)(2,1)S(1)}, u32[]{:S(2)}, u32[]{:S(2)}) collective-permute-start(bf16[96,384]{1,0:T(8,128)(2,1)S(1)} %copy-done.13), channel_id=1, source_target_pairs={{0,2},{1,3},{2,0},{3,1},{4,6},{5,7},{6,4},{7,5},{8,10},{9,11},{10,... | collective-permute-start | bytes 221192 | tf_op jit(solution)/shard_map/ppermute | solution.py:15
  32.2 35.5 %copy-start.10 = (bf16[2,3,1,2,128,128]{4,5,1,3,2,0:T(8,128)(2,1)S(1)}, bf16[2,3,1,2,128,128]{4,5,1,3,2,0:T(8,128)(2,1)}, u32[]{:S(2)}) copy-start(bf16[2,3,1,2,128,128]{4,5,1,3,2,0:T(8,128)(2,1)} %get-tuple-element.229) | copy-start | bytes 1179652
  56.4 8.2 %collective-permute-start.9 = (bf16[192,384]{1,0:T(8,128)(2,1)S(1)}, bf16[192,384]{1,0:T(8,128)(2,1)}, u32[]{:S(2)}, u32[]{:S(2)}) collective-permute-start(bf16[192,384]{1,0:T(8,128)(2,1)S(1)} %maximum_select_fusion.4), channel_id=1, source_target_pairs={{0,1},{1,0},{2,3},{3,2},{4,5},{5,4},{6,7},{7,6},{8,9},{9,8},{10,11... | collective-permute-start | bytes 442376 | tf_op jit(solution)/shard_map/ppermute | solution.py:15
  59.5 21.6 %collective-permute-start.4 = (bf16[2,3,2,1,128,128]{4,5,1,3,2,0:T(8,128)(2,1)}, bf16[2,3,2,1,128,128]{4,5,1,3,2,0:T(8,128)(2,1)S(1)}, u32[]{:S(2)}, u32[]{:S(2)}) collective-permute-start(bf16[2,3,2,1,128,128]{4,5,1,3,2,0:T(8,128)(2,1)} %get-tuple-element.231), channel_id=1, source_target_pairs={{1,0},{2,1},{3,2},{5,4},{6,5},{7,6},{9,8},{10,9},{11,10},{13,12},{... | collective-permute-start | bytes 1179656 | tf_op jit(solution)/shard_map/ppermute | solution.py:62
  64.6 16.5 %collective-permute-start.5 = (bf16[2,3,1,1,128,128]{4,5,1,3,2,0:T(8,128)(2,1)}, bf16[2,3,1,1,128,128]{4,5,1,3,2,0:T(8,128)(2,1)S(1)}, u32[]{:S(2)}, u32[]{:S(2)}) collective-permute-start(bf16[2,3,1,1,128,128]{4,5,1,3,2,0:T(8,128)(2,1)} %get-tuple-element.228), channel_id=1, source_target_pairs={{4,1},{5,2},{6,3},{8,5},{9,6},{10,7},{12,9},{13,10},{14,11},{16,13... | collective-permute-start | bytes 589832 | tf_op jit(solution)/shard_map/ppermute | solution.py:62
  67.7 17.7 %collective-permute-start.6 = (bf16[2,3,1,2,128,128]{4,5,1,3,2,0:T(8,128)(2,1)S(1)}, bf16[2,3,1,2,128,128]{4,5,1,3,2,0:T(8,128)(2,1)S(1)}, u32[]{:S(2)}, u32[]{:S(2)}) collective-permute-start(bf16[2,3,1,2,128,128]{4,5,1,3,2,0:T(8,128)(2,1)S(1)} %copy-done.10), channel_id=1, source_target_pairs={{4,0},{5,1},{6,2},{7,3},{8,4},{9,5},{10,6},{11,7},{12,8},{13,9},{1... | collective-permute-start | bytes 1179656 | tf_op jit(solution)/shard_map/ppermute | solution.py:62
  69.1 26.7 %collective-permute-start.7 = (bf16[2,3,1,1,128,128]{4,5,1,3,2,0:T(8,128)(2,1)S(1)}, bf16[2,3,1,1,128,128]{4,5,1,3,2,0:T(8,128)(2,1)S(1)}, u32[]{:S(2)}, u32[]{:S(2)}) collective-permute-start(bf16[2,3,1,1,128,128]{4,5,1,3,2,0:T(8,128)(2,1)S(1)} %copy-done.11), channel_id=1, source_target_pairs={{5,0},{6,1},{7,2},{9,4},{10,5},{11,6},{13,8},{14,9},{15,10},{17,12... | collective-permute-start | bytes 589832 | tf_op jit(solution)/shard_map/ppermute | solution.py:62
  71.4 28.1 %collective-permute-start.10 = (bf16[384,384]{1,0:T(8,128)(2,1)}, bf16[384,384]{1,0:T(8,128)(2,1)}, u32[]{:S(2)}, u32[]{:S(2)}) collective-permute-start(bf16[384,384]{1,0:T(8,128)(2,1)} %maximum_select_fusion.3), channel_id=1, source_target_pairs={{0,16},{4,20},{8,24},{12,28},{16,0},{20,4},{24,8},{28,12},{1,17},{... | collective-permute-start | bytes 884744 | tf_op jit(solution)/shard_map/ppermute | solution.py:15
  100.8 15.3 %collective-permute-start.11 = (bf16[768,384]{1,0:T(8,128)(2,1)S(1)}, bf16[768,384]{1,0:T(8,128)(2,1)S(1)}, u32[]{:S(2)}, u32[]{:S(2)}) collective-permute-start(bf16[768,384]{1,0:T(8,128)(2,1)S(1)} %maximum_select_fusion.2), channel_id=1, source_target_pairs={{0,8},{4,12},{8,0},{12,4},{16,24},{20,28},{24,16},{28,20},{1,9},{5... | collective-permute-start | bytes 1769480 | tf_op jit(solution)/shard_map/ppermute | solution.py:15
  116.6 27.3 %collective-permute-start.12 = (bf16[1536,384]{1,0:T(8,128)(2,1)S(1)}, bf16[1536,384]{1,0:T(8,128)(2,1)S(1)}, u32[]{:S(2)}, u32[]{:S(2)}) collective-permute-start(bf16[1536,384]{1,0:T(8,128)(2,1)S(1)} %maximum_select_fusion.1), channel_id=1, source_target_pairs={{0,4},{4,0},{8,12},{12,8},{16,20},{20,16},{24,28},{28,24},{1,5},{5... | collective-permute-start | bytes 3538952 | tf_op jit(solution)/shard_map/ppermute | solution.py:15
  182.1 31.2 %collective-permute-start.13 = (bf16[2,3,1,1,128,128]{4,5,1,3,2,0:T(8,128)(2,1)}, bf16[2,3,1,1,128,128]{4,5,1,3,2,0:T(8,128)(2,1)}, u32[]{:S(2)}, u32[]{:S(2)}) collective-permute-start(bf16[2,3,1,1,128,128]{4,5,1,3,2,0:T(8,128)(2,1)} %pad_maximum_fusion.5), channel_id=1, source_target_pairs={{5,0},{6,1},{7,2},{9,4},{10,5},{11,6},{13,8},{14,9},{15,10},{17,12... | collective-permute-start | bytes 589832 | tf_op jit(solution)/shard_map/ppermute | solution.py:81
  184.1 43.2 %collective-permute-start.14 = (bf16[2,3,1,2,128,128]{4,5,1,3,2,0:T(8,128)(2,1)}, bf16[2,3,1,2,128,128]{4,5,1,3,2,0:T(8,128)(2,1)}, u32[]{:S(2)}, u32[]{:S(2)}) collective-permute-start(bf16[2,3,1,2,128,128]{4,5,1,3,2,0:T(8,128)(2,1)} %pad_maximum_fusion.1), channel_id=1, source_target_pairs={{4,0},{5,1},{6,2},{7,3},{8,4},{9,5},{10,6},{11,7},{12,8},{13,9},{1... | collective-permute-start | bytes 1179656 | tf_op jit(solution)/shard_map/ppermute | solution.py:81
  186.3 29.9 %collective-permute-start.15 = (bf16[2,3,1,1,128,128]{4,5,1,3,2,0:T(8,128)(2,1)}, bf16[2,3,1,1,128,128]{4,5,1,3,2,0:T(8,128)(2,1)}, u32[]{:S(2)}, u32[]{:S(2)}) collective-permute-start(bf16[2,3,1,1,128,128]{4,5,1,3,2,0:T(8,128)(2,1)} %pad_maximum_fusion.6), channel_id=1, source_target_pairs={{4,1},{5,2},{6,3},{8,5},{9,6},{10,7},{12,9},{13,10},{14,11},{16,13... | collective-permute-start | bytes 589832 | tf_op jit(solution)/shard_map/ppermute | solution.py:81
  188.2 34.9 %collective-permute-start.18 = (bf16[2,3,1,1,128,128]{4,5,1,3,2,0:T(8,128)(2,1)}, bf16[2,3,1,1,128,128]{4,5,1,3,2,0:T(8,128)(2,1)}, u32[]{:S(2)}, u32[]{:S(2)}) collective-permute-start(bf16[2,3,1,1,128,128]{4,5,1,3,2,0:T(8,128)(2,1)} %pad_maximum_fusion.7), channel_id=1, source_target_pairs={{1,4},{2,5},{3,6},{5,8},{6,9},{7,10},{9,12},{10,13},{11,14},{13,16... | collective-permute-start | bytes 589832 | tf_op jit(solution)/shard_map/ppermute | solution.py:81
  194.8 30.6 %collective-permute-start.20 = (bf16[2,3,1,1,128,128]{4,5,1,3,2,0:T(8,128)(2,1)}, bf16[2,3,1,1,128,128]{4,5,1,3,2,0:T(8,128)(2,1)}, u32[]{:S(2)}, u32[]{:S(2)}) collective-permute-start(bf16[2,3,1,1,128,128]{4,5,1,3,2,0:T(8,128)(2,1)} %pad_maximum_fusion.8), channel_id=1, source_target_pairs={{0,5},{1,6},{2,7},{4,9},{5,10},{6,11},{8,13},{9,14},{10,15},{12,17... | collective-permute-start | bytes 589832 | tf_op jit(solution)/shard_map/ppermute | solution.py:81
  213.2 18.7 %collective-permute-start.16 = (bf16[2,3,2,1,128,128]{4,5,1,2,3,0:T(8,128)(2,1)}, bf16[2,3,2,1,128,128]{4,5,1,2,3,0:T(8,128)(2,1)S(1)}, u32[]{:S(2)}, u32[]{:S(2)}) collective-permute-start(bf16[2,3,2,1,128,128]{4,5,1,2,3,0:T(8,128)(2,1)} %pad_maximum_fusion.2), channel_id=1, source_target_pairs={{1,0},{2,1},{3,2},{5,4},{6,5},{7,6},{9,8},{10,9},{11,10},{13,12},{... | collective-permute-start | bytes 1179656 | tf_op jit(solution)/shard_map/ppermute | solution.py:81
  216.1 20.8 %collective-permute-start.17 = (bf16[2,3,2,1,128,128]{4,5,1,2,3,0:T(8,128)(2,1)}, bf16[2,3,2,1,128,128]{4,5,1,2,3,0:T(8,128)(2,1)S(1)}, u32[]{:S(2)}, u32[]{:S(2)}) collective-permute-start(bf16[2,3,2,1,128,128]{4,5,1,2,3,0:T(8,128)(2,1)} %pad_maximum_fusion.3), channel_id=1, source_target_pairs={{0,1},{1,2},{2,3},{4,5},{5,6},{6,7},{8,9},{9,10},{10,11},{12,13},{... | collective-permute-start | bytes 1179656 | tf_op jit(solution)/shard_map/ppermute | solution.py:81
  223.1 18.5 %collective-permute-start.19 = (bf16[2,3,1,2,128,128]{4,5,1,3,2,0:T(8,128)(2,1)S(1)}, bf16[2,3,1,2,128,128]{4,5,1,3,2,0:T(8,128)(2,1)S(1)}, u32[]{:S(2)}, u32[]{:S(2)}) collective-permute-start(bf16[2,3,1,2,128,128]{4,5,1,3,2,0:T(8,128)(2,1)S(1)} %pad_maximum_fusion.4), channel_id=1, source_target_pairs={{0,4},{1,5},{2,6},{3,7},{4,8},{5,9},{6,10},{7,11},{8,12},{9,13},{1... | collective-permute-start | bytes 1179656 | tf_op jit(solution)/shard_map/ppermute | solution.py:81
  (14 other events, 134.6 us)
Sparse Core Ops, SparseCore 0:
  31.7 31.0 all-gather.1

commit v5 on v4

--- a/solution.py
+++ b/solution.py
@@ -90,7 +90,9 @@
     heads = columns // HEAD
     f32, bf16 = jnp.float32, jnp.bfloat16
     whole = lax.all_gather(grad_out, "tp", axis=4, tiled=True)
-    weight = gather_rows(out_proj)
+    group = lax.axis_size("ha") * lax.axis_size("wa")
+    copies = jnp.broadcast_to(out_proj[None], (group,) + out_proj.shape).reshape(-1, out_proj.shape[1])
+    weight = lax.all_to_all(copies, ("ha", "wa"), 0, 0, tiled=True)
 
     def head_major(array):
         split = array.reshape(frames * tile_rows, tile_cols, tile_len, heads, HEAD)

time: 253 us -> 258 us (1.020)
  the two profiles are of different devices: /device:TPU:64 before, /device:TPU:34 now
where the time goes in v5:
time: 258 us; the launch traced here: 257 us
  starting transfers between devices  83.1 us (32%)
  waiting for transfers between devices  70.1 us (27%)
  matrix products  30.8 us (12%)
  local copies, waits for them, and re-layouts  30 us (12%)
  other arithmetic  28.6 us (11%)
  between operations  14.8 us (6%)
    ppermute x8, waiting for transfers between devices, extended(): got = lax.ppermute(piece, ('ha', 'wa'), neighbour_pairs(d_r, d_c))  55.2 us
    ppermute x8, starting transfers between devices, folded(): lax.ppermute(piece, ('ha', 'wa'), neighbour_pairs(-d_r, -d_c))  45.2 us
    ppermute x8, starting transfers between devices, extended(): got = lax.ppermute(piece, ('ha', 'wa'), neighbour_pairs(d_r, d_c))  25 us
    ppermute x8, waiting for transfers between devices, folded(): lax.ppermute(piece, ('ha', 'wa'), neighbour_pairs(-d_r, -d_c))  14.3 us
    all_to_all x1, starting transfers between devices, local(): weight = lax.all_to_all(copies, ('ha', 'wa'), 0, 0, tiled=True)  12.8 us
    convert_element_type x1, other arithmetic, local(): probs_lo = probs.astype(bf16)  8.48 us
    unnamed x40, local copies, waits for them, and re-layouts  8.2 us
    sub x1, matrix products, local(): scores = scores - jnp.max(scores, axis=-1, keepdims=True)  7.12 us
  transfers between devices with their start and end apart: 18, of which 5 were waited for; matrix products, arithmetic and copies ran while one was open for 19% of the time, Pallas kernels for 0%

profile of v5, /device:TPU:34, one launch (start us, length us, event | category | flops | bytes accessed | tf_op | source)
XLA Modules:
  0.0 257.4 jit_solution(11254697390766503943)
XLA Ops:
  11.3 5.5 %collective-permute-start = (bf16[2,3,1,1,128,128]{4,5,1,3,2,0:T(8,128)(2,1)}, bf16[2,3,1,1,128,128]{4,5,1,3,2,0:T(8,128)(2,1)}, u32[]{:S(2)}, u32[]{:S(2)}) collective-permute-start(bf16[2,3,1,1,128,128]{4,5,1,3,2,0:T(8,128)(2,1)} %get-tuple-element.223), channel_id=1, source_target_pairs={{0,5},{1,6},{2,7},{4,9},{5,10},{6,11},{8,13},{9,14},{10,15},{12,17... | collective-permute-start | bytes 589832 | tf_op jit(solution)/shard_map/ppermute | solution.py:62
  17.8 4.7 %collective-permute-start.1 = (bf16[2,3,1,2,128,128]{4,5,1,3,2,0:T(8,128)(2,1)}, bf16[2,3,1,2,128,128]{4,5,1,3,2,0:T(8,128)(2,1)S(1)}, u32[]{:S(2)}, u32[]{:S(2)}) collective-permute-start(bf16[2,3,1,2,128,128]{4,5,1,3,2,0:T(8,128)(2,1)} %get-tuple-element.227), channel_id=1, source_target_pairs={{0,4},{1,5},{2,6},{3,7},{4,8},{5,9},{6,10},{7,11},{8,12},{9,13},{1... | collective-permute-start | bytes 1179656 | tf_op jit(solution)/shard_map/ppermute | solution.py:62
  24.7 5.5 %collective-permute-start.3 = (bf16[2,3,2,1,128,128]{4,5,1,3,2,0:T(8,128)(2,1)}, bf16[2,3,2,1,128,128]{4,5,1,3,2,0:T(8,128)(2,1)S(1)}, u32[]{:S(2)}, u32[]{:S(2)}) collective-permute-start(bf16[2,3,2,1,128,128]{4,5,1,3,2,0:T(8,128)(2,1)} %get-tuple-element.229), channel_id=1, source_target_pairs={{0,1},{1,2},{2,3},{4,5},{5,6},{6,7},{8,9},{9,10},{10,11},{12,13},{... | collective-permute-start | bytes 1179656 | tf_op jit(solution)/shard_map/ppermute | solution.py:62
  33.2 12.8 %all-to-all-start = ((bf16[32,96,384]{2,1,0:T(8,128)(2,1)}), bf16[32,96,384]{2,1,0:T(8,128)(2,1)}, u32[]{:S(2)}, u32[]{:S(2)}) async-start(bf16[32,96,384]{2,1,0:T(8,128)(2,1)} %broadcast_in_dim.18), calls=%async_computation | async-start | bytes 4718592 | tf_op jit(solution)/shard_map/all_to_all | solution.py:95
  48.2 3.4 %collective-permute-start.5 = (bf16[2,3,1,1,128,128]{4,5,1,3,2,0:T(8,128)(2,1)S(1)}, bf16[2,3,1,1,128,128]{4,5,1,3,2,0:T(8,128)(2,1)S(1)}, u32[]{:S(2)}, u32[]{:S(2)}) collective-permute-start(bf16[2,3,1,1,128,128]{4,5,1,3,2,0:T(8,128)(2,1)S(1)} %copy-done.12), channel_id=1, source_target_pairs={{4,1},{5,2},{6,3},{8,5},{9,6},{10,7},{12,9},{13,10},{14,11},{16,13... | collective-permute-start | bytes 589832 | tf_op jit(solution)/shard_map/ppermute | solution.py:62
  57.1 4.2 %collective-permute-done.4 = bf16[2,3,2,1,128,128]{4,5,1,3,2,0:T(8,128)(2,1)S(1)} collective-permute-done((bf16[2,3,2,1,128,128]{4,5,1,3,2,0:T(8,128)(2,1)}, bf16[2,3,2,1,128,128]{4,5,1,3,2,0:T(8,128)(2,1)S(1)}, u32[]{:S(2)}, u32[]{:S(2)}) %collective-permute-start.4) | collective-permute-done | bytes 393248 | tf_op jit(solution)/shard_map/ppermute | solution.py:62
  61.3 40.1 %collective-permute-done.5 = bf16[2,3,1,1,128,128]{4,5,1,3,2,0:T(8,128)(2,1)S(1)} collective-permute-done((bf16[2,3,1,1,128,128]{4,5,1,3,2,0:T(8,128)(2,1)S(1)}, bf16[2,3,1,1,128,128]{4,5,1,3,2,0:T(8,128)(2,1)S(1)}, u32[]{:S(2)}, u32[]{:S(2)}) %collective-permute-start.5) | collective-permute-done | bytes 196640 | tf_op jit(solution)/shard_map/ppermute | solution.py:62
  101.5 10.8 %collective-permute-done.6 = bf16[2,3,1,2,128,128]{4,5,1,3,2,0:T(8,128)(2,1)S(1)} collective-permute-done((bf16[2,3,1,2,128,128]{4,5,1,3,2,0:T(8,128)(2,1)S(1)}, bf16[2,3,1,2,128,128]{4,5,1,3,2,0:T(8,128)(2,1)S(1)}, u32[]{:S(2)}, u32[]{:S(2)}) %collective-permute-start.6) | collective-permute-done | bytes 393248 | tf_op jit(solution)/shard_map/ppermute | solution.py:62
  116.0 7.1 %fusion.58 = (f32[3,4,128]{2,1,0:T(4,128)S(1)}, f32[3,4,128,2048]{2,3,1,0:T(8,128)}) fusion(pred[4,2048]{1,0:T(4,128)(4,1)S(1)} %bitcast.254, bf16[3,2048,128,1]{2,1,3,0:T(8,128)(2,1)S(1)} %bitcast.245, bf16[3,4,128,128]{2,3,0,1:T(8,128)(2,1)S(1)} %bitcast.240), kind=kOutput, calls=%fused_computation.143 | convolution fusion | flops 817891328 | bytes 14563328 | tf_op jit(solution)/shard_map/sub | solution.py:132
  123.2 8.5 %fusion.5 = bf16[3,4,128,2048]{2,3,1,0:T(8,128)(2,1)} fusion(f32[3,4,128,2048]{2,3,1,0:T(8,128)} %get-tuple-element.239, f32[3,4,128]{2,1,0:T(4,128)S(1)} %get-tuple-element.238), kind=kLoop, calls=%fused_computation.9 | loop fusion | flops 6291456 | bytes 18880512 | tf_op jit(solution)/shard_map/convert_element_type | solution.py:135
  131.6 4.4 %convolution_convert_fusion.1 = bf16[512,384]{1,0:T(8,128)(2,1)S(1)} fusion(bf16[512,3072]{1,0:T(8,128)(2,1)} %bitcast.255, bf16[3072,384]{1,0:T(8,128)(2,1)} %bitcast.14), kind=kOutput, calls=%fused_computation.30 | convolution fusion | flops 1208156160 | bytes 5898240 | tf_op jit(solution)/shard_map/dot_general | solution.py:137
  136.4 6.5 %fusion.63 = f32[3,2048,128,1]{2,1,3,0:T(8,128)} fusion(bf16[3,4,128,2048]{2,3,1,0:T(8,128)(2,1)} %fusion.5, bf16[3,4,128,128]{2,3,1,0:T(8,128)(2,1)S(1)} %bitcast.242), kind=kOutput, calls=%fused_computation.144 | convolution fusion | flops 805306368 | bytes 9830400 | tf_op jit(solution)/shard_map/hqtl,hqtd->hld/dot_general | solution.py:148
  146.1 4.1 %multiply_convert_fusion = bf16[3,4,128,2048]{2,3,1,0:T(8,128)(2,1)S(1)} fusion(f32[3,4,128]{2,1,0:T(4,128)S(1)} %fusion.8, bf16[3,2048,128,1]{2,1,3,0:T(8,128)(2,1)} %bitcast.247, bf16[3,4,128,128]{2,3,1,0:T(8,128)(2,1)S(1)} %bitcast.244, f32[3,4,128,2048]{2,3,1,0:T(8,128)S(1)} %copy-done, f32[3,4,128]{2,1,0:T(4,128)S(1)} %get-tuple-element.238), kind=kOutput, calls=%fused_computation.2 | convolution fusion | flops 821035008 | bytes 20852736 | tf_op jit(solution)/shard_map/hqtd,hld->hqtl/dot_general | solution.py:144
  150.2 3.7 %fusion.28 = f32[3,2048,128,1]{2,1,3,0:T(8,128)} fusion(bf16[3,4,128,2048]{2,3,1,0:T(8,128)(2,1)S(1)} %multiply_convert_fusion, bf16[3,4,128,128]{2,3,0,1:T(8,128)(2,1)S(1)} %bitcast.241), kind=kOutput, calls=%fused_computation.63 | convolution fusion | flops 805306368 | bytes 9830400 | tf_op jit(solution)/shard_map/hqtl,hqtd->hld/dot_general | solution.py:147
  153.9 2.4 copy.58
  158.5 3.6 %copy.62 = f32[3,4,4,128,128]{3,4,0,2,1:T(8,128)} copy(f32[3,4,4,128,128]{4,3,2,1,0:T(8,128)} %bitcast.230) | data formatting | bytes 6291456 | tf_op jit(solution)/shard_map/reshape | solution.py:152
  162.1 2.3 convert.53
  166.2 3.9 %convolution_convert_fusion = bf16[3,4,128,128]{2,3,1,0:T(8,128)(2,1)S(1)} fusion(bf16[3,4,128,2048]{2,3,1,0:T(8,128)(2,1)} %copy-done.2, bf16[3,2048,128,1]{2,1,3,0:T(8,128)(2,1)S(1)} %bitcast.246), kind=kOutput, calls=%fused_computation.29 | convolution fusion | flops 805502976 | bytes 8257536 | tf_op jit(solution)/shard_map/hqtl,hld->hqtd/dot_general | solution.py:146
  171.0 14.6 %collective-permute-start.9 = (bf16[2,3,1,2,128,128]{4,5,1,3,2,0:T(8,128)(2,1)}, bf16[2,3,1,2,128,128]{4,5,1,3,2,0:T(8,128)(2,1)}, u32[]{:S(2)}, u32[]{:S(2)}) collective-permute-start(bf16[2,3,1,2,128,128]{4,5,1,3,2,0:T(8,128)(2,1)} %pad_maximum_fusion.1), channel_id=1, source_target_pairs={{4,0},{5,1},{6,2},{7,3},{8,4},{9,5},{10,6},{11,7},{12,8},{13,9},{1... | collective-permute-start | bytes 1179656 | tf_op jit(solution)/shard_map/ppermute | solution.py:81
  188.3 6.4 %collective-permute-start.10 = (bf16[2,3,1,1,128,128]{4,5,1,3,2,0:T(8,128)(2,1)}, bf16[2,3,1,1,128,128]{4,5,1,3,2,0:T(8,128)(2,1)}, u32[]{:S(2)}, u32[]{:S(2)}) collective-permute-start(bf16[2,3,1,1,128,128]{4,5,1,3,2,0:T(8,128)(2,1)} %pad_maximum_fusion.6), channel_id=1, source_target_pairs={{4,1},{5,2},{6,3},{8,5},{9,6},{10,7},{12,9},{13,10},{14,11},{16,13... | collective-permute-start | bytes 589832 | tf_op jit(solution)/shard_map/ppermute | solution.py:81
  197.4 9.1 %collective-permute-start.15 = (bf16[2,3,1,1,128,128]{4,5,1,3,2,0:T(8,128)(2,1)}, bf16[2,3,1,1,128,128]{4,5,1,3,2,0:T(8,128)(2,1)}, u32[]{:S(2)}, u32[]{:S(2)}) collective-permute-start(bf16[2,3,1,1,128,128]{4,5,1,3,2,0:T(8,128)(2,1)} %pad_maximum_fusion.8), channel_id=1, source_target_pairs={{0,5},{1,6},{2,7},{4,9},{5,10},{6,11},{8,13},{9,14},{10,15},{12,17... | collective-permute-start | bytes 589832 | tf_op jit(solution)/shard_map/ppermute | solution.py:81
  213.2 5.9 %collective-permute-start.14 = (bf16[2,3,1,2,128,128]{4,5,1,3,2,0:T(8,128)(2,1)}, bf16[2,3,1,2,128,128]{4,5,1,3,2,0:T(8,128)(2,1)S(1)}, u32[]{:S(2)}, u32[]{:S(2)}) collective-permute-start(bf16[2,3,1,2,128,128]{4,5,1,3,2,0:T(8,128)(2,1)} %pad_maximum_fusion.4), channel_id=1, source_target_pairs={{0,4},{1,5},{2,6},{3,7},{4,8},{5,9},{6,10},{7,11},{8,12},{9,13},{1... | collective-permute-start | bytes 1179656 | tf_op jit(solution)/shard_map/ppermute | solution.py:81
  220.1 5.4 %collective-permute-start.12 = (bf16[2,3,2,1,128,128]{4,5,1,2,3,0:T(8,128)(2,1)}, bf16[2,3,2,1,128,128]{4,5,1,2,3,0:T(8,128)(2,1)S(1)}, u32[]{:S(2)}, u32[]{:S(2)}) collective-permute-start(bf16[2,3,2,1,128,128]{4,5,1,2,3,0:T(8,128)(2,1)} %pad_maximum_fusion.3), channel_id=1, source_target_pairs={{0,1},{1,2},{2,3},{4,5},{5,6},{6,7},{8,9},{9,10},{10,11},{12,13},{... | collective-permute-start | bytes 1179656 | tf_op jit(solution)/shard_map/ppermute | solution.py:81
  232.1 14.3 %collective-permute-done.11 = bf16[2,3,2,1,128,128]{4,5,1,2,3,0:T(8,128)(2,1)S(1)} collective-permute-done((bf16[2,3,2,1,128,128]{4,5,1,2,3,0:T(8,128)(2,1)S(1)}, bf16[2,3,2,1,128,128]{4,5,1,2,3,0:T(8,128)(2,1)S(1)}, u32[]{:S(2)}, u32[]{:S(2)}) %collective-permute-start.11) | collective-permute-done | bytes 393248 | tf_op jit(solution)/shard_map/ppermute | solution.py:81
  (139 shorter events, 53.7 us)
Async XLA Ops:
  7.2 124.5 %all-gather.2.cloned.1.call-start = ((), (), s32[]{:S(2)}) async-start(), calls=%async_computation.1 | async-start | bytes 3538944 | tf_op jit(solution)/shard_map/all_gather | solution.py:92
  7.9 23.6 %copy-start.13 = (bf16[96,384]{1,0:T(8,128)(2,1)S(1)}, bf16[96,384]{1,0:T(8,128)(2,1)}, u32[]{:S(2)}) copy-start(bf16[96,384]{1,0:T(8,128)(2,1)} %param.41) | copy-start | bytes 221188
  11.3 36.8 %collective-permute-start = (bf16[2,3,1,1,128,128]{4,5,1,3,2,0:T(8,128)(2,1)}, bf16[2,3,1,1,128,128]{4,5,1,3,2,0:T(8,128)(2,1)}, u32[]{:S(2)}, u32[]{:S(2)}) collective-permute-start(bf16[2,3,1,1,128,128]{4,5,1,3,2,0:T(8,128)(2,1)} %get-tuple-element.223), channel_id=1, source_target_pairs={{0,5},{1,6},{2,7},{4,9},{5,10},{6,11},{8,13},{9,14},{10,15},{12,17... | collective-permute-start | bytes 589832 | tf_op jit(solution)/shard_map/ppermute | solution.py:62
  17.8 34.7 %collective-permute-start.1 = (bf16[2,3,1,2,128,128]{4,5,1,3,2,0:T(8,128)(2,1)}, bf16[2,3,1,2,128,128]{4,5,1,3,2,0:T(8,128)(2,1)S(1)}, u32[]{:S(2)}, u32[]{:S(2)}) collective-permute-start(bf16[2,3,1,2,128,128]{4,5,1,3,2,0:T(8,128)(2,1)} %get-tuple-element.227), channel_id=1, source_target_pairs={{0,4},{1,5},{2,6},{3,7},{4,8},{5,9},{6,10},{7,11},{8,12},{9,13},{1... | collective-permute-start | bytes 1179656 | tf_op jit(solution)/shard_map/ppermute | solution.py:62
  22.5 32.0 %collective-permute-start.2 = (bf16[2,3,1,1,128,128]{4,5,1,3,2,0:T(8,128)(2,1)}, bf16[2,3,1,1,128,128]{4,5,1,3,2,0:T(8,128)(2,1)}, u32[]{:S(2)}, u32[]{:S(2)}) collective-permute-start(bf16[2,3,1,1,128,128]{4,5,1,3,2,0:T(8,128)(2,1)} %get-tuple-element.224), channel_id=1, source_target_pairs={{1,4},{2,5},{3,6},{5,8},{6,9},{7,10},{9,12},{10,13},{11,14},{13,16... | collective-permute-start | bytes 589832 | tf_op jit(solution)/shard_map/ppermute | solution.py:62
  24.7 32.3 %collective-permute-start.3 = (bf16[2,3,2,1,128,128]{4,5,1,3,2,0:T(8,128)(2,1)}, bf16[2,3,2,1,128,128]{4,5,1,3,2,0:T(8,128)(2,1)S(1)}, u32[]{:S(2)}, u32[]{:S(2)}) collective-permute-start(bf16[2,3,2,1,128,128]{4,5,1,3,2,0:T(8,128)(2,1)} %get-tuple-element.229), channel_id=1, source_target_pairs={{0,1},{1,2},{2,3},{4,5},{5,6},{6,7},{8,9},{9,10},{10,11},{12,13},{... | collective-permute-start | bytes 1179656 | tf_op jit(solution)/shard_map/ppermute | solution.py:62
  30.2 31.1 %collective-permute-start.4 = (bf16[2,3,2,1,128,128]{4,5,1,3,2,0:T(8,128)(2,1)}, bf16[2,3,2,1,128,128]{4,5,1,3,2,0:T(8,128)(2,1)S(1)}, u32[]{:S(2)}, u32[]{:S(2)}) collective-permute-start(bf16[2,3,2,1,128,128]{4,5,1,3,2,0:T(8,128)(2,1)} %get-tuple-element.228), channel_id=1, source_target_pairs={{1,0},{2,1},{3,2},{5,4},{6,5},{7,6},{9,8},{10,9},{11,10},{13,12},{... | collective-permute-start | bytes 1179656 | tf_op jit(solution)/shard_map/ppermute | solution.py:62
  33.2 14.0 %copy-start.9 = (bf16[1,2,2,128,384]{4,3,2,1,0:T(8,128)(2,1)S(1)}, bf16[1,2,2,128,384]{4,3,2,1,0:T(8,128)(2,1)}, u32[]{:S(2)}) copy-start(bf16[1,2,2,128,384]{4,3,2,1,0:T(8,128)(2,1)} %param.37) | copy-start | bytes 1179652
  33.2 98.4 %all-to-all-start = ((bf16[32,96,384]{2,1,0:T(8,128)(2,1)}), bf16[32,96,384]{2,1,0:T(8,128)(2,1)}, u32[]{:S(2)}, u32[]{:S(2)}) async-start(bf16[32,96,384]{2,1,0:T(8,128)(2,1)} %broadcast_in_dim.18), calls=%async_computation | async-start | bytes 4718592 | tf_op jit(solution)/shard_map/all_to_all | solution.py:95
  46.6 8.0 %copy-start.11 = (bf16[2,3,1,1,128,128]{4,5,1,3,2,0:T(8,128)(2,1)S(1)}, bf16[2,3,1,1,128,128]{4,5,1,3,2,0:T(8,128)(2,1)}, u32[]{:S(2)}) copy-start(bf16[2,3,1,1,128,128]{4,5,1,3,2,0:T(8,128)(2,1)} %get-tuple-element.222) | copy-start | bytes 589828
  48.2 53.3 %collective-permute-start.5 = (bf16[2,3,1,1,128,128]{4,5,1,3,2,0:T(8,128)(2,1)S(1)}, bf16[2,3,1,1,128,128]{4,5,1,3,2,0:T(8,128)(2,1)S(1)}, u32[]{:S(2)}, u32[]{:S(2)}) collective-permute-start(bf16[2,3,1,1,128,128]{4,5,1,3,2,0:T(8,128)(2,1)S(1)} %copy-done.12), channel_id=1, source_target_pairs={{4,1},{5,2},{6,3},{8,5},{9,6},{10,7},{12,9},{13,10},{14,11},{16,13... | collective-permute-start | bytes 589832 | tf_op jit(solution)/shard_map/ppermute | solution.py:62
  52.5 59.7 %collective-permute-start.6 = (bf16[2,3,1,2,128,128]{4,5,1,3,2,0:T(8,128)(2,1)S(1)}, bf16[2,3,1,2,128,128]{4,5,1,3,2,0:T(8,128)(2,1)S(1)}, u32[]{:S(2)}, u32[]{:S(2)}) collective-permute-start(bf16[2,3,1,2,128,128]{4,5,1,3,2,0:T(8,128)(2,1)S(1)} %copy-done.10), channel_id=1, source_target_pairs={{4,0},{5,1},{6,2},{7,3},{8,4},{9,5},{10,6},{11,7},{12,8},{13,9},{1... | collective-permute-start | bytes 1179656 | tf_op jit(solution)/shard_map/ppermute | solution.py:62
  54.5 57.8 %collective-permute-start.7 = (bf16[2,3,1,1,128,128]{4,5,1,3,2,0:T(8,128)(2,1)S(1)}, bf16[2,3,1,1,128,128]{4,5,1,3,2,0:T(8,128)(2,1)S(1)}, u32[]{:S(2)}, u32[]{:S(2)}) collective-permute-start(bf16[2,3,1,1,128,128]{4,5,1,3,2,0:T(8,128)(2,1)S(1)} %copy-done.11), channel_id=1, source_target_pairs={{5,0},{6,1},{7,2},{9,4},{10,5},{11,6},{13,8},{14,9},{15,10},{17,12... | collective-permute-start | bytes 589832 | tf_op jit(solution)/shard_map/ppermute | solution.py:62
  136.4 9.7 %copy-start = (f32[3,4,128,2048]{2,3,1,0:T(8,128)S(1)}, f32[3,4,128,2048]{2,3,1,0:T(8,128)}, u32[]{:S(2)}) copy-start(f32[3,4,128,2048]{2,3,1,0:T(8,128)} %get-tuple-element.239) | copy-start | bytes 37748740
  171.0 59.7 %collective-permute-start.9 = (bf16[2,3,1,2,128,128]{4,5,1,3,2,0:T(8,128)(2,1)}, bf16[2,3,1,2,128,128]{4,5,1,3,2,0:T(8,128)(2,1)}, u32[]{:S(2)}, u32[]{:S(2)}) collective-permute-start(bf16[2,3,1,2,128,128]{4,5,1,3,2,0:T(8,128)(2,1)} %pad_maximum_fusion.1), channel_id=1, source_target_pairs={{4,0},{5,1},{6,2},{7,3},{8,4},{9,5},{10,6},{11,7},{12,8},{13,9},{1... | collective-permute-start | bytes 1179656 | tf_op jit(solution)/shard_map/ppermute | solution.py:81
  186.3 26.9 %collective-permute-start.8 = (bf16[2,3,1,1,128,128]{4,5,1,3,2,0:T(8,128)(2,1)}, bf16[2,3,1,1,128,128]{4,5,1,3,2,0:T(8,128)(2,1)}, u32[]{:S(2)}, u32[]{:S(2)}) collective-permute-start(bf16[2,3,1,1,128,128]{4,5,1,3,2,0:T(8,128)(2,1)} %pad_maximum_fusion.5), channel_id=1, source_target_pairs={{5,0},{6,1},{7,2},{9,4},{10,5},{11,6},{13,8},{14,9},{15,10},{17,12... | collective-permute-start | bytes 589832 | tf_op jit(solution)/shard_map/ppermute | solution.py:81
  188.3 31.8 %collective-permute-start.10 = (bf16[2,3,1,1,128,128]{4,5,1,3,2,0:T(8,128)(2,1)}, bf16[2,3,1,1,128,128]{4,5,1,3,2,0:T(8,128)(2,1)}, u32[]{:S(2)}, u32[]{:S(2)}) collective-permute-start(bf16[2,3,1,1,128,128]{4,5,1,3,2,0:T(8,128)(2,1)} %pad_maximum_fusion.6), channel_id=1, source_target_pairs={{4,1},{5,2},{6,3},{8,5},{9,6},{10,7},{12,9},{13,10},{14,11},{16,13... | collective-permute-start | bytes 589832 | tf_op jit(solution)/shard_map/ppermute | solution.py:81
  195.4 31.0 %collective-permute-start.13 = (bf16[2,3,1,1,128,128]{4,5,1,3,2,0:T(8,128)(2,1)}, bf16[2,3,1,1,128,128]{4,5,1,3,2,0:T(8,128)(2,1)}, u32[]{:S(2)}, u32[]{:S(2)}) collective-permute-start(bf16[2,3,1,1,128,128]{4,5,1,3,2,0:T(8,128)(2,1)} %pad_maximum_fusion.7), channel_id=1, source_target_pairs={{1,4},{2,5},{3,6},{5,8},{6,9},{7,10},{9,12},{10,13},{11,14},{13,16... | collective-permute-start | bytes 589832 | tf_op jit(solution)/shard_map/ppermute | solution.py:81
  197.4 31.3 %collective-permute-start.15 = (bf16[2,3,1,1,128,128]{4,5,1,3,2,0:T(8,128)(2,1)}, bf16[2,3,1,1,128,128]{4,5,1,3,2,0:T(8,128)(2,1)}, u32[]{:S(2)}, u32[]{:S(2)}) collective-permute-start(bf16[2,3,1,1,128,128]{4,5,1,3,2,0:T(8,128)(2,1)} %pad_maximum_fusion.8), channel_id=1, source_target_pairs={{0,5},{1,6},{2,7},{4,9},{5,10},{6,11},{8,13},{9,14},{10,15},{12,17... | collective-permute-start | bytes 589832 | tf_op jit(solution)/shard_map/ppermute | solution.py:81
  212.0 17.6 %copy-start.1 = (f32[3,2,2,128,128]{3,4,0,2,1:T(8,128)S(1)}, f32[3,2,2,128,128]{3,4,0,2,1:T(8,128)}, u32[]{:S(2)}) copy-start(f32[3,2,2,128,128]{3,4,0,2,1:T(8,128)} %slice.811) | copy-start | bytes 2359300
  212.0 17.6 %copy-start.3 = (f32[3,2,2,128,128]{3,4,0,2,1:T(8,128)S(1)}, f32[3,2,2,128,128]{3,4,0,2,1:T(8,128)}, u32[]{:S(2)}) copy-start(f32[3,2,2,128,128]{3,4,0,2,1:T(8,128)} %slice.843) | copy-start | bytes 2359300
  213.2 35.0 %collective-permute-start.14 = (bf16[2,3,1,2,128,128]{4,5,1,3,2,0:T(8,128)(2,1)}, bf16[2,3,1,2,128,128]{4,5,1,3,2,0:T(8,128)(2,1)S(1)}, u32[]{:S(2)}, u32[]{:S(2)}) collective-permute-start(bf16[2,3,1,2,128,128]{4,5,1,3,2,0:T(8,128)(2,1)} %pad_maximum_fusion.4), channel_id=1, source_target_pairs={{0,4},{1,5},{2,6},{3,7},{4,8},{5,9},{6,10},{7,11},{8,12},{9,13},{1... | collective-permute-start | bytes 1179656 | tf_op jit(solution)/shard_map/ppermute | solution.py:81
  220.1 26.5 %collective-permute-start.12 = (bf16[2,3,2,1,128,128]{4,5,1,2,3,0:T(8,128)(2,1)}, bf16[2,3,2,1,128,128]{4,5,1,2,3,0:T(8,128)(2,1)S(1)}, u32[]{:S(2)}, u32[]{:S(2)}) collective-permute-start(bf16[2,3,2,1,128,128]{4,5,1,2,3,0:T(8,128)(2,1)} %pad_maximum_fusion.3), channel_id=1, source_target_pairs={{0,1},{1,2},{2,3},{4,5},{5,6},{6,7},{8,9},{9,10},{10,11},{12,13},{... | collective-permute-start | bytes 1179656 | tf_op jit(solution)/shard_map/ppermute | solution.py:81
  226.4 19.9 %collective-permute-start.11 = (bf16[2,3,2,1,128,128]{4,5,1,2,3,0:T(8,128)(2,1)S(1)}, bf16[2,3,2,1,128,128]{4,5,1,2,3,0:T(8,128)(2,1)S(1)}, u32[]{:S(2)}, u32[]{:S(2)}) collective-permute-start(bf16[2,3,2,1,128,128]{4,5,1,2,3,0:T(8,128)(2,1)S(1)} %pad_maximum_fusion.2), channel_id=1, source_target_pairs={{1,0},{2,1},{3,2},{5,4},{6,5},{7,6},{9,8},{10,9},{11,10},{13,12},{... | collective-permute-start | bytes 1179656 | tf_op jit(solution)/shard_map/ppermute | solution.py:81
  (10 other events, 41.9 us)
Sparse Core Ops, SparseCore 0:
  9.8 31.9 all-gather.1

commit v6 on v4

--- a/solution.py
+++ b/solution.py
@@ -66,23 +66,35 @@
     return out
 
 
+def passed_along(value, axis, steps):
+    count = lax.axis_size(axis)
+    first, last = (max(0, -steps), min(count, count - steps))
+    return lax.ppermute(value, axis, [(source, source + steps) for source in range(first, last)])
+
+
+def sent_back(pieces, axis, steps):
+    got = passed_along(jnp.stack(pieces).astype(jnp.bfloat16), axis, steps)
+    return got.astype(jnp.float32)
+
+
 def folded(grad_k, grad_v):
-    rows, cols = grad_k.shape[1] - 2, grad_k.shape[2] - 2
-    own_k = grad_k[:, 1:-1, 1:-1]
-    own_v = grad_v[:, 1:-1, 1:-1]
-    for d_r, d_c in DIRS:
-        r0 = 0 if d_r < 0 else (rows + 1 if d_r > 0 else 1)
-        c0 = 0 if d_c < 0 else (cols + 1 if d_c > 0 else 1)
-        nr = rows if d_r == 0 else 1
-        nc = cols if d_c == 0 else 1
-        piece = jnp.stack(
-            [grad_k[:, r0 : r0 + nr, c0 : c0 + nc], grad_v[:, r0 : r0 + nr, c0 : c0 + nc]]
-        ).astype(jnp.bfloat16)
-        got = lax.ppermute(piece, ("ha", "wa"), neighbour_pairs(-d_r, -d_c)).astype(jnp.float32)
-        rs, cs = pick(rows, d_r), pick(cols, d_c)
-        own_k = own_k.at[:, rs, cs].add(got[0])
-        own_v = own_v.at[:, rs, cs].add(got[1])
-    return own_k, own_v
+    from_right = sent_back([grad_k[:, :, 0], grad_v[:, :, 0]], "wa", -1)
+    from_left = sent_back([grad_k[:, :, -1], grad_v[:, :, -1]], "wa", 1)
+    own = []
+    for n, part in enumerate((grad_k, grad_v)):
+        inner = part[:, :, 1:-1]
+        inner = inner.at[:, :, 0:1].add(from_left[n][:, :, None])
+        inner = inner.at[:, :, -1:].add(from_right[n][:, :, None])
+        own.append(inner)
+    from_below = sent_back([own[0][:, 0], own[1][:, 0]], "ha", -1)
+    from_above = sent_back([own[0][:, -1], own[1][:, -1]], "ha", 1)
+    result = []
+    for n, part in enumerate(own):
+        inner = part[:, 1:-1]
+        inner = inner.at[:, 0:1].add(from_above[n][:, None])
+        inner = inner.at[:, -1:].add(from_below[n][:, None])
+        result.append(inner)
+    return result[0], result[1]
 
 
 def local(queries, keys, values, grad_out, out_proj):

time: 253 us -> 245 us (0.968)
  starting transfers between devices: 70.3 us -> 61.4 us
  waiting for transfers between devices: 74.7 us -> 77.4 us
    ppermute x5, waiting for transfers between devices: 49.3 us -> 22.5 us  [doubling_gather(): other = lax.ppermute(buf, axis, [(i, i ^ bit) for i in range(count)])]
    ppermute x8 -> x4, waiting for transfers between devices: 10.8 us -> 34.2 us  [passed_along(): lax.ppermute(value, axis, [(source, source + steps) for source in range(f...]
    ppermute x8 -> x4, starting transfers between devices: 30.8 us -> 15.7 us  [passed_along(): lax.ppermute(value, axis, [(source, source + steps) for source in range(f...]
    ppermute x5, starting transfers between devices: 12.4 us -> 20 us  [doubling_gather(): other = lax.ppermute(buf, axis, [(i, i ^ bit) for i in range(count)])]
    ppermute x8, waiting for transfers between devices: 14.6 us -> 20 us  [extended(): got = lax.ppermute(piece, ('ha', 'wa'), neighbour_pairs(d_r, d_c))]
    unnamed x40 -> x45, local copies, waits for them, and re-layouts: 6.73 us -> 9.74 us
    another operation x8 -> x4, local copies, waits for them, and re-layouts: 3.92 us -> 1.18 us  [sent_back(): got = passed_along(jnp.stack(pieces).astype(jnp.bfloat16), axis, steps)]
    another operation x10 -> x8, other arithmetic: 8.72 us -> 6.23 us  [the longest x4 3.5 us: sent_back(): got = passed_along(jnp.stack(pieces).astype(jnp.bfloat16), axis, steps)]
  transfers between devices with their start and end apart: 22 -> 18, of which waited for: 8 -> 9; matrix products, arithmetic and copies ran while one was open for 19% -> 19% of each run, Pallas kernels for 0% -> 0%
where the time goes in v6:
time: 245 us; the launch traced here: 241 us
  waiting for transfers between devices  77.4 us (32%)
  starting transfers between devices  61.4 us (25%)
  other arithmetic  31.5 us (13%)
  matrix products  29.4 us (12%)
  local copies, waits for them, and re-layouts  26 us (11%)
  between operations  14.8 us (6%)
    ppermute x4, waiting for transfers between devices, passed_along(): lax.ppermute(value, axis, [(source, source + steps) for source in range(f...  34.2 us
    ppermute x8, starting transfers between devices, extended(): got = lax.ppermute(piece, ('ha', 'wa'), neighbour_pairs(d_r, d_c))  25.7 us
    ppermute x5, waiting for transfers between devices, doubling_gather(): other = lax.ppermute(buf, axis, [(i, i ^ bit) for i in range(count)])  22.5 us
    ppermute x8, waiting for transfers between devices, extended(): got = lax.ppermute(piece, ('ha', 'wa'), neighbour_pairs(d_r, d_c))  20 us
    ppermute x5, starting transfers between devices, doubling_gather(): other = lax.ppermute(buf, axis, [(i, i ^ bit) for i in range(count)])  20 us
    ppermute x4, starting transfers between devices, passed_along(): lax.ppermute(value, axis, [(source, source + steps) for source in range(f...  15.7 us
    unnamed x45, local copies, waits for them, and re-layouts  9.74 us
    convert_element_type x1, other arithmetic, local(): probs_lo = probs.astype(bf16)  8.48 us
  transfers between devices with their start and end apart: 18, of which 9 were waited for; matrix products, arithmetic and copies ran while one was open for 19% of the time, Pallas kernels for 0%

profile of v6, /device:TPU:64, one launch (start us, length us, event | category | flops | bytes accessed | tf_op | source)
XLA Modules:
  0.0 240.6 jit_solution(13821209474071089941)
XLA Ops:
  7.9 5.5 %collective-permute-start.8 = (bf16[96,384]{1,0:T(8,128)(2,1)}, bf16[96,384]{1,0:T(8,128)(2,1)S(1)}, u32[]{:S(2)}, u32[]{:S(2)}) collective-permute-start(bf16[96,384]{1,0:T(8,128)(2,1)} %param.25), channel_id=1, source_target_pairs={{0,2},{1,3},{2,0},{3,1},{4,6},{5,7},{6,4},{7,5},{8,10},{9,11},{10,... | collective-permute-start | bytes 221192 | tf_op jit(solution)/shard_map/ppermute | solution.py:15
  17.9 7.6 %collective-permute-start = (bf16[2,3,1,1,128,128]{4,5,1,3,2,0:T(8,128)(2,1)S(1)}, bf16[2,3,1,1,128,128]{4,5,1,3,2,0:T(8,128)(2,1)S(1)}, u32[]{:S(2)}, u32[]{:S(2)}) collective-permute-start(bf16[2,3,1,1,128,128]{4,5,1,3,2,0:T(8,128)(2,1)S(1)} %get-tuple-element.122), channel_id=1, source_target_pairs={{0,5},{1,6},{2,7},{4,9},{5,10},{6,11},{8,13},{9,14},{10,15},{12,17... | collective-permute-start | bytes 589832 | tf_op jit(solution)/shard_map/ppermute | solution.py:62
  28.4 4.6 %collective-permute-start.1 = (bf16[2,3,1,2,128,128]{4,5,1,3,2,0:T(8,128)(2,1)}, bf16[2,3,1,2,128,128]{4,5,1,3,2,0:T(8,128)(2,1)S(1)}, u32[]{:S(2)}, u32[]{:S(2)}) collective-permute-start(bf16[2,3,1,2,128,128]{4,5,1,3,2,0:T(8,128)(2,1)} %get-tuple-element.126), channel_id=1, source_target_pairs={{0,4},{1,5},{2,6},{3,7},{4,8},{5,9},{6,10},{7,11},{8,12},{9,13},{1... | collective-permute-start | bytes 1179656 | tf_op jit(solution)/shard_map/ppermute | solution.py:62
  35.6 5.8 %collective-permute-start.3 = (bf16[2,3,2,1,128,128]{4,5,1,3,2,0:T(8,128)(2,1)}, bf16[2,3,2,1,128,128]{4,5,1,3,2,0:T(8,128)(2,1)S(1)}, u32[]{:S(2)}, u32[]{:S(2)}) collective-permute-start(bf16[2,3,2,1,128,128]{4,5,1,3,2,0:T(8,128)(2,1)} %get-tuple-element.128), channel_id=1, source_target_pairs={{0,1},{1,2},{2,3},{4,5},{5,6},{6,7},{8,9},{9,10},{10,11},{12,13},{... | collective-permute-start | bytes 1179656 | tf_op jit(solution)/shard_map/ppermute | solution.py:62
  50.8 10.9 %collective-permute-done.3 = bf16[2,3,2,1,128,128]{4,5,1,3,2,0:T(8,128)(2,1)S(1)} collective-permute-done((bf16[2,3,2,1,128,128]{4,5,1,3,2,0:T(8,128)(2,1)}, bf16[2,3,2,1,128,128]{4,5,1,3,2,0:T(8,128)(2,1)S(1)}, u32[]{:S(2)}, u32[]{:S(2)}) %collective-permute-start.3) | collective-permute-done | bytes 393248 | tf_op jit(solution)/shard_map/ppermute | solution.py:62
  61.7 8.8 %collective-permute-start.10 = (bf16[384,384]{1,0:T(8,128)(2,1)}, bf16[384,384]{1,0:T(8,128)(2,1)}, u32[]{:S(2)}, u32[]{:S(2)}) collective-permute-start(bf16[384,384]{1,0:T(8,128)(2,1)} %maximum_select_fusion.3), channel_id=1, source_target_pairs={{0,16},{4,20},{8,24},{12,28},{16,0},{20,4},{24,8},{28,12},{1,17},{... | collective-permute-start | bytes 884744 | tf_op jit(solution)/shard_map/ppermute | solution.py:15
  70.7 9.1 %collective-permute-done.6 = bf16[2,3,1,2,128,128]{4,5,1,3,2,0:T(8,128)(2,1)S(1)} collective-permute-done((bf16[2,3,1,2,128,128]{4,5,1,3,2,0:T(8,128)(2,1)S(1)}, bf16[2,3,1,2,128,128]{4,5,1,3,2,0:T(8,128)(2,1)S(1)}, u32[]{:S(2)}, u32[]{:S(2)}) %collective-permute-start.6) | collective-permute-done | bytes 393248 | tf_op jit(solution)/shard_map/ppermute | solution.py:62
  87.5 7.1 %fusion.48 = (f32[3,4,128]{2,1,0:T(4,128)S(1)}, f32[3,4,128,2048]{2,3,1,0:T(8,128)}) fusion(pred[4,2048]{1,0:T(4,128)(4,1)S(1)} %bitcast.200, bf16[3,2048,128,1]{2,1,3,0:T(8,128)(2,1)S(1)} %bitcast.191, bf16[3,4,128,128]{2,3,0,1:T(8,128)(2,1)S(1)} %bitcast.186), kind=kOutput, calls=%fused_computation.111 | convolution fusion | flops 817891328 | bytes 14563328 | tf_op jit(solution)/shard_map/sub | solution.py:142
  94.6 4.4 %collective-permute-done.11 = bf16[768,384]{1,0:T(8,128)(2,1)S(1)} collective-permute-done((bf16[768,384]{1,0:T(8,128)(2,1)S(1)}, bf16[768,384]{1,0:T(8,128)(2,1)S(1)}, u32[]{:S(2)}, u32[]{:S(2)}) %collective-permute-start.11) | collective-permute-done | bytes 589856 | tf_op jit(solution)/shard_map/ppermute | solution.py:15
  99.4 3.9 %collective-permute-start.12 = (bf16[1536,384]{1,0:T(8,128)(2,1)S(1)}, bf16[1536,384]{1,0:T(8,128)(2,1)S(1)}, u32[]{:S(2)}, u32[]{:S(2)}) collective-permute-start(bf16[1536,384]{1,0:T(8,128)(2,1)S(1)} %maximum_select_fusion.1), channel_id=1, source_target_pairs={{0,4},{4,0},{8,12},{12,8},{16,20},{20,16},{24,28},{28,24},{1,5},{5... | collective-permute-start | bytes 3538952 | tf_op jit(solution)/shard_map/ppermute | solution.py:15
  103.3 8.5 %fusion.5 = bf16[3,4,128,2048]{2,3,1,0:T(8,128)(2,1)} fusion(f32[3,4,128,2048]{2,3,1,0:T(8,128)} %get-tuple-element.130, f32[3,4,128]{2,1,0:T(4,128)S(1)} %get-tuple-element.129), kind=kLoop, calls=%fused_computation.9 | loop fusion | flops 6291456 | bytes 18880512 | tf_op jit(solution)/shard_map/convert_element_type | solution.py:145
  111.8 16.1 %collective-permute-done.12 = bf16[1536,384]{1,0:T(8,128)(2,1)S(1)} collective-permute-done((bf16[1536,384]{1,0:T(8,128)(2,1)S(1)}, bf16[1536,384]{1,0:T(8,128)(2,1)S(1)}, u32[]{:S(2)}, u32[]{:S(2)}) %collective-permute-start.12) | collective-permute-done | bytes 1179680 | tf_op jit(solution)/shard_map/ppermute | solution.py:15
  128.9 4.1 %fusion.9 = bf16[512,384]{0,1:T(8,128)(2,1)} fusion(bf16[3072,384]{1,0:T(8,128)(2,1)S(1)} %bitcast.185, bf16[512,3072]{1,0:T(8,128)(2,1)} %bitcast.201), kind=kOutput, calls=%fused_computation.33 | convolution fusion | flops 1208156160 | bytes 5898240 | tf_op jit(solution)/shard_map/dot_general | solution.py:147
  134.3 6.4 %fusion.53 = f32[3,2048,128,1]{2,1,3,0:T(8,128)} fusion(bf16[3,4,128,2048]{2,3,1,0:T(8,128)(2,1)} %fusion.5, bf16[3,4,128,128]{2,3,1,0:T(8,128)(2,1)S(1)} %bitcast.188), kind=kOutput, calls=%fused_computation.112 | convolution fusion | flops 805306368 | bytes 9830400 | tf_op jit(solution)/shard_map/hqtl,hqtd->hld/dot_general | solution.py:158
  141.9 5.9 %multiply_convert_fusion = bf16[3,4,128,2048]{2,3,1,0:T(8,128)(2,1)S(1)} fusion(f32[3,4,128]{2,1,0:T(4,128)S(1)} %fusion.8, bf16[3,2048,128,1]{2,1,3,0:T(8,128)(2,1)S(1)} %bitcast.194, bf16[3,4,128,128]{2,3,1,0:T(8,128)(2,1)S(1)} %bitcast.190, f32[3,4,128,2048]{2,3,1,0:T(8,128)} %get-tuple-element.130, f32[3,4,128]{2,1,0:T(4,128)S(1)} %get-tuple-element.129), kind=kOutput, calls=%fused_computation.2 | convolution fusion | flops 821035008 | bytes 20852736 | tf_op jit(solution)/shard_map/hqtd,hld->hqtl/dot_general | solution.py:154
  147.8 3.6 %fusion.35 = f32[3,2048,128,1]{2,1,3,0:T(8,128)} fusion(bf16[3,4,128,2048]{2,3,1,0:T(8,128)(2,1)S(1)} %multiply_convert_fusion, bf16[3,4,128,128]{2,3,0,1:T(8,128)(2,1)S(1)} %bitcast.187), kind=kOutput, calls=%fused_computation.75 | convolution fusion | flops 805306368 | bytes 9830400 | tf_op jit(solution)/shard_map/hqtl,hqtd->hld/dot_general | solution.py:157
  155.2 3.6 %copy.82 = f32[3,4,4,128,128]{3,4,0,1,2:T(8,128)} copy(f32[3,4,4,128,128]{4,3,2,1,0:T(8,128)} %bitcast.171) | data formatting | bytes 6291456 | tf_op jit(solution)/shard_map/reshape | solution.py:162
  162.0 2.6 %collective-permute-start.13 = (bf16[2,3,4,128,128]{3,4,1,2,0:T(8,128)(2,1)}, bf16[2,3,4,128,128]{3,4,1,2,0:T(8,128)(2,1)}, u32[]{:S(2)}, u32[]{:S(2)}) collective-permute-start(bf16[2,3,4,128,128]{3,4,1,2,0:T(8,128)(2,1)} %pad_maximum_fusion.1), channel_id=1, source_target_pairs={{0,1},{1,2},{2,3},{4,5},{5,6},{6,7},{8,9},{9,10},{10,11},{12,13},{... | collective-permute-start | bytes 2359304 | tf_op jit(solution)/shard_map/ppermute | solution.py:72
  165.6 5.4 %collective-permute-start.14 = (bf16[2,3,4,128,128]{3,4,1,2,0:T(8,128)(2,1)}, bf16[2,3,4,128,128]{3,4,1,2,0:T(8,128)(2,1)}, u32[]{:S(2)}, u32[]{:S(2)}) collective-permute-start(bf16[2,3,4,128,128]{3,4,1,2,0:T(8,128)(2,1)} %pad_maximum_fusion.2), channel_id=1, source_target_pairs={{1,0},{2,1},{3,2},{5,4},{6,5},{7,6},{9,8},{10,9},{11,10},{13,12},{... | collective-permute-start | bytes 2359304 | tf_op jit(solution)/shard_map/ppermute | solution.py:72
  174.3 8.4 %collective-permute-done.13 = bf16[2,3,4,128,128]{3,4,1,2,0:T(8,128)(2,1)} collective-permute-done((bf16[2,3,4,128,128]{3,4,1,2,0:T(8,128)(2,1)}, bf16[2,3,4,128,128]{3,4,1,2,0:T(8,128)(2,1)}, u32[]{:S(2)}, u32[]{:S(2)}) %collective-permute-start.13) | collective-permute-done | bytes 786464 | tf_op jit(solution)/shard_map/ppermute | solution.py:72
  186.6 14.5 %collective-permute-done.14 = bf16[2,3,4,128,128]{3,4,1,2,0:T(8,128)(2,1)} collective-permute-done((bf16[2,3,4,128,128]{3,4,1,2,0:T(8,128)(2,1)}, bf16[2,3,4,128,128]{3,4,1,2,0:T(8,128)(2,1)}, u32[]{:S(2)}, u32[]{:S(2)}) %collective-permute-start.14) | collective-permute-done | bytes 786464 | tf_op jit(solution)/shard_map/ppermute | solution.py:72
  204.8 6.5 %collective-permute-start.15 = (bf16[2,3,2,128,128]{3,4,1,2,0:T(8,128)(2,1)}, bf16[2,3,2,128,128]{3,4,1,2,0:T(8,128)(2,1)}, u32[]{:S(2)}, u32[]{:S(2)}) collective-permute-start(bf16[2,3,2,128,128]{3,4,1,2,0:T(8,128)(2,1)} %pad_maximum_fusion.3), channel_id=1, source_target_pairs={{0,4},{4,8},{8,12},{12,16},{16,20},{20,24},{24,28},{1,5},{5,9},{9,... | collective-permute-start | bytes 1179656 | tf_op jit(solution)/shard_map/ppermute | solution.py:72
  216.1 3.2 %collective-permute-done.15 = bf16[2,3,2,128,128]{3,4,1,2,0:T(8,128)(2,1)} collective-permute-done((bf16[2,3,2,128,128]{3,4,1,2,0:T(8,128)(2,1)}, bf16[2,3,2,128,128]{3,4,1,2,0:T(8,128)(2,1)}, u32[]{:S(2)}, u32[]{:S(2)}) %collective-permute-start.15) | collective-permute-done | bytes 393248 | tf_op jit(solution)/shard_map/ppermute | solution.py:72
  220.5 8.0 %collective-permute-done.16 = bf16[2,3,2,128,128]{3,4,1,2,0:T(8,128)(2,1)} collective-permute-done((bf16[2,3,2,128,128]{3,4,1,2,0:T(8,128)(2,1)}, bf16[2,3,2,128,128]{3,4,1,2,0:T(8,128)(2,1)}, u32[]{:S(2)}, u32[]{:S(2)}) %collective-permute-start.16) | collective-permute-done | bytes 393248 | tf_op jit(solution)/shard_map/ppermute | solution.py:72
  (130 shorter events, 61.3 us)
Async XLA Ops:
  7.2 121.7 %all-gather.2.cloned.1.call-start = ((), (), s32[]{:S(2)}) async-start(), calls=%async_computation | async-start | bytes 3538944 | tf_op jit(solution)/shard_map/all_gather | solution.py:104
  7.9 25.7 %copy-start.13 = (bf16[96,384]{1,0:T(8,128)(2,1)S(1)}, bf16[96,384]{1,0:T(8,128)(2,1)}, u32[]{:S(2)}) copy-start(bf16[96,384]{1,0:T(8,128)(2,1)} %param.25) | copy-start | bytes 221188
  7.9 25.7 %collective-permute-start.8 = (bf16[96,384]{1,0:T(8,128)(2,1)}, bf16[96,384]{1,0:T(8,128)(2,1)S(1)}, u32[]{:S(2)}, u32[]{:S(2)}) collective-permute-start(bf16[96,384]{1,0:T(8,128)(2,1)} %param.25), channel_id=1, source_target_pairs={{0,2},{1,3},{2,0},{3,1},{4,6},{5,7},{6,4},{7,5},{8,10},{9,11},{10,... | collective-permute-start | bytes 221192 | tf_op jit(solution)/shard_map/ppermute | solution.py:15
  15.8 18.9 %copy-start.10 = (bf16[1,2,2,128,384]{4,3,2,1,0:T(8,128)(2,1)S(1)}, bf16[1,2,2,128,384]{4,3,2,1,0:T(8,128)(2,1)}, u32[]{:S(2)}) copy-start(bf16[1,2,2,128,384]{4,3,2,1,0:T(8,128)(2,1)} %param.21) | copy-start | bytes 1179652
  16.7 63.2 %collective-permute-start.7 = (bf16[2,3,1,1,128,128]{4,5,1,3,2,0:T(8,128)(2,1)S(1)}, bf16[2,3,1,1,128,128]{4,5,1,3,2,0:T(8,128)(2,1)}, u32[]{:S(2)}, u32[]{:S(2)}) collective-permute-start(bf16[2,3,1,1,128,128]{4,5,1,3,2,0:T(8,128)(2,1)S(1)} %get-tuple-element.121), channel_id=1, source_target_pairs={{5,0},{6,1},{7,2},{9,4},{10,5},{11,6},{13,8},{14,9},{15,10},{17,12... | collective-permute-start | bytes 589832 | tf_op jit(solution)/shard_map/ppermute | solution.py:62
  17.9 17.7 %collective-permute-start = (bf16[2,3,1,1,128,128]{4,5,1,3,2,0:T(8,128)(2,1)S(1)}, bf16[2,3,1,1,128,128]{4,5,1,3,2,0:T(8,128)(2,1)S(1)}, u32[]{:S(2)}, u32[]{:S(2)}) collective-permute-start(bf16[2,3,1,1,128,128]{4,5,1,3,2,0:T(8,128)(2,1)S(1)} %get-tuple-element.122), channel_id=1, source_target_pairs={{0,5},{1,6},{2,7},{4,9},{5,10},{6,11},{8,13},{9,14},{10,15},{12,17... | collective-permute-start | bytes 589832 | tf_op jit(solution)/shard_map/ppermute | solution.py:62
  25.5 23.0 %collective-permute-start.2 = (bf16[2,3,1,1,128,128]{4,5,1,3,2,0:T(8,128)(2,1)}, bf16[2,3,1,1,128,128]{4,5,1,3,2,0:T(8,128)(2,1)}, u32[]{:S(2)}, u32[]{:S(2)}) collective-permute-start(bf16[2,3,1,1,128,128]{4,5,1,3,2,0:T(8,128)(2,1)} %get-tuple-element.123), channel_id=1, source_target_pairs={{1,4},{2,5},{3,6},{5,8},{6,9},{7,10},{9,12},{10,13},{11,14},{13,16... | collective-permute-start | bytes 589832 | tf_op jit(solution)/shard_map/ppermute | solution.py:62
  28.4 18.7 %collective-permute-start.1 = (bf16[2,3,1,2,128,128]{4,5,1,3,2,0:T(8,128)(2,1)}, bf16[2,3,1,2,128,128]{4,5,1,3,2,0:T(8,128)(2,1)S(1)}, u32[]{:S(2)}, u32[]{:S(2)}) collective-permute-start(bf16[2,3,1,2,128,128]{4,5,1,3,2,0:T(8,128)(2,1)} %get-tuple-element.126), channel_id=1, source_target_pairs={{0,4},{1,5},{2,6},{3,7},{4,8},{5,9},{6,10},{7,11},{8,12},{9,13},{1... | collective-permute-start | bytes 1179656 | tf_op jit(solution)/shard_map/ppermute | solution.py:62
  33.6 9.8 %collective-permute-start.9 = (bf16[192,384]{1,0:T(8,128)(2,1)S(1)}, bf16[192,384]{1,0:T(8,128)(2,1)}, u32[]{:S(2)}, u32[]{:S(2)}) collective-permute-start(bf16[192,384]{1,0:T(8,128)(2,1)S(1)} %maximum_select_fusion.4), channel_id=1, source_target_pairs={{0,1},{1,0},{2,3},{3,2},{4,5},{5,4},{6,7},{7,6},{8,9},{9,8},{10,11... | collective-permute-start | bytes 442376 | tf_op jit(solution)/shard_map/ppermute | solution.py:15
  34.7 13.8 %copy-start.11 = (bf16[2,3,1,2,128,128]{4,5,1,3,2,0:T(8,128)(2,1)S(1)}, bf16[2,3,1,2,128,128]{4,5,1,3,2,0:T(8,128)(2,1)}, u32[]{:S(2)}) copy-start(bf16[2,3,1,2,128,128]{4,5,1,3,2,0:T(8,128)(2,1)} %get-tuple-element.125) | copy-start | bytes 1179652
  35.6 26.1 %collective-permute-start.3 = (bf16[2,3,2,1,128,128]{4,5,1,3,2,0:T(8,128)(2,1)}, bf16[2,3,2,1,128,128]{4,5,1,3,2,0:T(8,128)(2,1)S(1)}, u32[]{:S(2)}, u32[]{:S(2)}) collective-permute-start(bf16[2,3,2,1,128,128]{4,5,1,3,2,0:T(8,128)(2,1)} %get-tuple-element.128), channel_id=1, source_target_pairs={{0,1},{1,2},{2,3},{4,5},{5,6},{6,7},{8,9},{9,10},{10,11},{12,13},{... | collective-permute-start | bytes 1179656 | tf_op jit(solution)/shard_map/ppermute | solution.py:62
  43.5 27.1 %collective-permute-start.4 = (bf16[2,3,2,1,128,128]{4,5,1,3,2,0:T(8,128)(2,1)S(1)}, bf16[2,3,2,1,128,128]{4,5,1,3,2,0:T(8,128)(2,1)S(1)}, u32[]{:S(2)}, u32[]{:S(2)}) collective-permute-start(bf16[2,3,2,1,128,128]{4,5,1,3,2,0:T(8,128)(2,1)S(1)} %copy-done.12), channel_id=1, source_target_pairs={{1,0},{2,1},{3,2},{5,4},{6,5},{7,6},{9,8},{10,9},{11,10},{13,12},{... | collective-permute-start | bytes 1179656 | tf_op jit(solution)/shard_map/ppermute | solution.py:62
  47.2 23.4 %collective-permute-start.5 = (bf16[2,3,1,1,128,128]{4,5,1,3,2,0:T(8,128)(2,1)}, bf16[2,3,1,1,128,128]{4,5,1,3,2,0:T(8,128)(2,1)S(1)}, u32[]{:S(2)}, u32[]{:S(2)}) collective-permute-start(bf16[2,3,1,1,128,128]{4,5,1,3,2,0:T(8,128)(2,1)} %get-tuple-element.124), channel_id=1, source_target_pairs={{4,1},{5,2},{6,3},{8,5},{9,6},{10,7},{12,9},{13,10},{14,11},{16,13... | collective-permute-start | bytes 589832 | tf_op jit(solution)/shard_map/ppermute | solution.py:62
  48.6 31.2 %collective-permute-start.6 = (bf16[2,3,1,2,128,128]{4,5,1,3,2,0:T(8,128)(2,1)S(1)}, bf16[2,3,1,2,128,128]{4,5,1,3,2,0:T(8,128)(2,1)S(1)}, u32[]{:S(2)}, u32[]{:S(2)}) collective-permute-start(bf16[2,3,1,2,128,128]{4,5,1,3,2,0:T(8,128)(2,1)S(1)} %copy-done.11), channel_id=1, source_target_pairs={{4,0},{5,1},{6,2},{7,3},{8,4},{9,5},{10,6},{11,7},{12,8},{13,9},{1... | collective-permute-start | bytes 1179656 | tf_op jit(solution)/shard_map/ppermute | solution.py:62
  61.7 22.0 %collective-permute-start.10 = (bf16[384,384]{1,0:T(8,128)(2,1)}, bf16[384,384]{1,0:T(8,128)(2,1)}, u32[]{:S(2)}, u32[]{:S(2)}) collective-permute-start(bf16[384,384]{1,0:T(8,128)(2,1)} %maximum_select_fusion.3), channel_id=1, source_target_pairs={{0,16},{4,20},{8,24},{12,28},{16,0},{20,4},{24,8},{28,12},{1,17},{... | collective-permute-start | bytes 884744 | tf_op jit(solution)/shard_map/ppermute | solution.py:15
  85.7 13.3 %collective-permute-start.11 = (bf16[768,384]{1,0:T(8,128)(2,1)S(1)}, bf16[768,384]{1,0:T(8,128)(2,1)S(1)}, u32[]{:S(2)}, u32[]{:S(2)}) collective-permute-start(bf16[768,384]{1,0:T(8,128)(2,1)S(1)} %maximum_select_fusion.2), channel_id=1, source_target_pairs={{0,8},{4,12},{8,0},{12,4},{16,24},{20,28},{24,16},{28,20},{1,9},{5... | collective-permute-start | bytes 1769480 | tf_op jit(solution)/shard_map/ppermute | solution.py:15
  99.4 28.5 %collective-permute-start.12 = (bf16[1536,384]{1,0:T(8,128)(2,1)S(1)}, bf16[1536,384]{1,0:T(8,128)(2,1)S(1)}, u32[]{:S(2)}, u32[]{:S(2)}) collective-permute-start(bf16[1536,384]{1,0:T(8,128)(2,1)S(1)} %maximum_select_fusion.1), channel_id=1, source_target_pairs={{0,4},{4,0},{8,12},{12,8},{16,20},{20,16},{24,28},{28,24},{1,5},{5... | collective-permute-start | bytes 3538952 | tf_op jit(solution)/shard_map/ppermute | solution.py:15
  153.9 17.2 %copy-start = (f32[3,4,4,128,128]{3,4,0,1,2:T(8,128)}, f32[3,4,4,128,128]{3,4,0,1,2:T(8,128)S(1)}, u32[]{:S(2)}) copy-start(f32[3,4,4,128,128]{3,4,0,1,2:T(8,128)S(1)} %copy.78) | copy-start | bytes 9437188
  162.0 20.6 %collective-permute-start.13 = (bf16[2,3,4,128,128]{3,4,1,2,0:T(8,128)(2,1)}, bf16[2,3,4,128,128]{3,4,1,2,0:T(8,128)(2,1)}, u32[]{:S(2)}, u32[]{:S(2)}) collective-permute-start(bf16[2,3,4,128,128]{3,4,1,2,0:T(8,128)(2,1)} %pad_maximum_fusion.1), channel_id=1, source_target_pairs={{0,1},{1,2},{2,3},{4,5},{5,6},{6,7},{8,9},{9,10},{10,11},{12,13},{... | collective-permute-start | bytes 2359304 | tf_op jit(solution)/shard_map/ppermute | solution.py:72
  165.6 35.5 %collective-permute-start.14 = (bf16[2,3,4,128,128]{3,4,1,2,0:T(8,128)(2,1)}, bf16[2,3,4,128,128]{3,4,1,2,0:T(8,128)(2,1)}, u32[]{:S(2)}, u32[]{:S(2)}) collective-permute-start(bf16[2,3,4,128,128]{3,4,1,2,0:T(8,128)(2,1)} %pad_maximum_fusion.2), channel_id=1, source_target_pairs={{1,0},{2,1},{3,2},{5,4},{6,5},{7,6},{9,8},{10,9},{11,10},{13,12},{... | collective-permute-start | bytes 2359304 | tf_op jit(solution)/shard_map/ppermute | solution.py:72
  172.3 11.7 %slice-start.2 = ((f32[3,4,4,128,128]{3,4,0,1,2:T(8,128)}), f32[3,4,2,128,128]{3,4,0,1,2:T(8,128)S(1)}, s32[]{:S(2)}) async-start(f32[3,4,4,128,128]{3,4,0,1,2:T(8,128)} %copy-done), calls=%async_computation.3 | async-start | bytes 3145728 | tf_op jit(solution)/shard_map/slice | solution.py:85
  202.4 10.9 %slice-start.3 = ((s8[6291456]{0:T(1024)(128)(4,1)}), s8[4194304]{0:T(1024)(128)(4,1)S(1)}, s32[]{:S(2)}) async-start(s8[6291456]{0:T(1024)(128)(4,1)} %bitcast.183), calls=%async_computation.4 | async-start | bytes 8388608
  204.8 14.5 %collective-permute-start.15 = (bf16[2,3,2,128,128]{3,4,1,2,0:T(8,128)(2,1)}, bf16[2,3,2,128,128]{3,4,1,2,0:T(8,128)(2,1)}, u32[]{:S(2)}, u32[]{:S(2)}) collective-permute-start(bf16[2,3,2,128,128]{3,4,1,2,0:T(8,128)(2,1)} %pad_maximum_fusion.3), channel_id=1, source_target_pairs={{0,4},{4,8},{8,12},{12,16},{16,20},{20,24},{24,28},{1,5},{5,9},{9,... | collective-permute-start | bytes 1179656 | tf_op jit(solution)/shard_map/ppermute | solution.py:72
  212.1 16.5 %collective-permute-start.16 = (bf16[2,3,2,128,128]{3,4,1,2,0:T(8,128)(2,1)}, bf16[2,3,2,128,128]{3,4,1,2,0:T(8,128)(2,1)}, u32[]{:S(2)}, u32[]{:S(2)}) collective-permute-start(bf16[2,3,2,128,128]{3,4,1,2,0:T(8,128)(2,1)} %pad_maximum_fusion.4), channel_id=1, source_target_pairs={{4,0},{8,4},{12,8},{16,12},{20,16},{24,20},{28,24},{5,1},{9,5},{13... | collective-permute-start | bytes 1179656 | tf_op jit(solution)/shard_map/ppermute | solution.py:72
  (13 other events, 80.8 us)
Sparse Core Ops, SparseCore 0:
  9.8 32.4 all-gather.1

commit v7 on v6

--- a/solution.py
+++ b/solution.py
@@ -77,6 +77,19 @@
     return got.astype(jnp.float32)
 
 
+def extended_2(array, sides, width):
+    for axis, dim in sides:
+        peers, length = (lax.axis_size(axis), array.shape[dim])
+        up = [(i, (i + 1) % peers) for i in range(peers - 1)]
+        down = [(j, i) for i, j in up]
+        last = lax.slice_in_dim(array, length - width, length, axis=dim)
+        first = lax.slice_in_dim(array, 0, width, axis=dim)
+        before = lax.ppermute(last, axis, up)
+        after = lax.ppermute(first, axis, down)
+        array = jnp.concatenate([before, array, after], axis=dim)
+    return array
+
+
 def folded(grad_k, grad_v):
     from_right = sent_back([grad_k[:, :, 0], grad_v[:, :, 0]], "wa", -1)
     from_left = sent_back([grad_k[:, :, -1], grad_v[:, :, -1]], "wa", 1)
@@ -111,7 +124,7 @@
     def head_minor(array):
         return jnp.transpose(array, (1, 2, 3, 0, 4)).reshape(queries.shape)
 
-    ext = extended(jnp.stack([head_major(keys), head_major(values)]))
+    ext = extended_2(jnp.stack([head_major(keys), head_major(values)]), (("ha", 2), ("wa", 3)), 1)
     ext_r, ext_c = tile_rows + 2, tile_cols + 2
     row_base = lax.axis_index("ha") * tile_rows
     col_base = lax.axis_index("wa") * tile_cols

time: 245 us -> 230 us (0.939)
  starting transfers between devices: 61.4 us -> 44.3 us
  waiting for transfers between devices: 77.4 us -> 80.9 us
    ppermute x8 -> x4, starting transfers between devices: 25.7 us -> 11 us  [the longest x2 6.16 us: extended_2(): after = lax.ppermute(first, axis, down)]
    ppermute x5, waiting for transfers between devices: 22.5 us -> 26.2 us  [doubling_gather(): other = lax.ppermute(buf, axis, [(i, i ^ bit) for i in range(count)])]
    ppermute x8 -> x4, waiting for transfers between devices: 20 us -> 16.7 us  [the longest x2 16.7 us: extended_2(): after = lax.ppermute(first, axis, down)]
    ppermute x4, waiting for transfers between devices: 34.2 us -> 37.3 us  [passed_along(): lax.ppermute(value, axis, [(source, source + steps) for source in range(f...]
    another operation x8 -> x5, other arithmetic: 5.5 us -> 2.8 us  [the longest x4 2.78 us: local(): ext = extended(jnp.stack([head_major(keys), head_major(values)]))]
    unnamed x45 -> x39, local copies, waits for them, and re-layouts: 9.74 us -> 10.7 us
  transfers between devices with their start and end apart: 18 -> 14, of which waited for: 9 -> 8; matrix products, arithmetic and copies ran while one was open for 19% -> 20% of each run, Pallas kernels for 0% -> 0%
where the time goes in v7:
time: 230 us; the launch traced here: 227 us
  waiting for transfers between devices  80.9 us (35%)
  starting transfers between devices  44.3 us (19%)
  other arithmetic  31.9 us (14%)
  matrix products  29.5 us (13%)
  local copies, waits for them, and re-layouts  25.4 us (11%)
  between operations  14.6 us (6%)
    ppermute x4, waiting for transfers between devices, passed_along(): lax.ppermute(value, axis, [(source, source + steps) for source in range(f...  37.3 us
    ppermute x5, waiting for transfers between devices, doubling_gather(): other = lax.ppermute(buf, axis, [(i, i ^ bit) for i in range(count)])  26.2 us
    ppermute x5, starting transfers between devices, doubling_gather(): other = lax.ppermute(buf, axis, [(i, i ^ bit) for i in range(count)])  19.5 us
    ppermute x2, waiting for transfers between devices, extended_2(): after = lax.ppermute(first, axis, down)  16.7 us
    ppermute x4, starting transfers between devices, passed_along(): lax.ppermute(value, axis, [(source, source + steps) for source in range(f...  13.8 us
    unnamed x39, local copies, waits for them, and re-layouts  10.7 us
    convert_element_type x1, other arithmetic, local(): probs_lo = probs.astype(bf16)  8.48 us
    sub x1, matrix products, local(): scores = scores - jnp.max(scores, axis=-1, keepdims=True)  7.22 us
  transfers between devices with their start and end apart: 14, of which 8 were waited for; matrix products, arithmetic and copies ran while one was open for 20% of the time, Pallas kernels for 0%

profile of v7, /device:TPU:64, one launch (start us, length us, event | category | flops | bytes accessed | tf_op | source)
XLA Modules:
  0.0 226.6 jit_solution(7804117029866870620)
XLA Ops:
  7.9 5.5 %collective-permute-start.4 = (bf16[96,384]{1,0:T(8,128)(2,1)}, bf16[96,384]{1,0:T(8,128)(2,1)S(1)}, u32[]{:S(2)}, u32[]{:S(2)}) collective-permute-start(bf16[96,384]{1,0:T(8,128)(2,1)} %param.25), channel_id=1, source_target_pairs={{0,2},{1,3},{2,0},{3,1},{4,6},{5,7},{6,4},{7,5},{8,10},{9,11},{10,... | collective-permute-start | bytes 221192 | tf_op jit(solution)/shard_map/ppermute | solution.py:15
  15.9 2.9 %collective-permute-start = (bf16[2,3,1,2,128,128]{4,5,1,3,2,0:T(8,128)(2,1)S(1)}, bf16[2,3,1,2,128,128]{4,5,1,3,2,0:T(8,128)(2,1)S(1)}, u32[]{:S(2)}, u32[]{:S(2)}) collective-permute-start(bf16[2,3,1,2,128,128]{4,5,1,3,2,0:T(8,128)(2,1)S(1)} %get-tuple-element.123), channel_id=1, source_target_pairs={{0,4},{4,8},{8,12},{12,16},{16,20},{20,24},{24,28},{1,5},{5,9},{9,... | collective-permute-start | bytes 1179656 | tf_op jit(solution)/shard_map/ppermute | solution.py:87
  21.9 10.1 %collective-permute-done.5 = bf16[192,384]{1,0:T(8,128)(2,1)S(1)} collective-permute-done((bf16[192,384]{1,0:T(8,128)(2,1)S(1)}, bf16[192,384]{1,0:T(8,128)(2,1)S(1)}, u32[]{:S(2)}, u32[]{:S(2)}) %collective-permute-start.5) | collective-permute-done | bytes 147488 | tf_op jit(solution)/shard_map/ppermute | solution.py:15
  32.1 11.7 %collective-permute-start.6 = (bf16[384,384]{1,0:T(8,128)(2,1)S(1)}, bf16[384,384]{1,0:T(8,128)(2,1)S(1)}, u32[]{:S(2)}, u32[]{:S(2)}) collective-permute-start(bf16[384,384]{1,0:T(8,128)(2,1)S(1)} %maximum_select_fusion.3), channel_id=1, source_target_pairs={{0,16},{4,20},{8,24},{12,28},{16,0},{20,4},{24,8},{28,12},{1,17},{... | collective-permute-start | bytes 884744 | tf_op jit(solution)/shard_map/ppermute | solution.py:15
  47.2 4.9 %collective-permute-start.3 = (bf16[2,3,4,1,128,128]{4,5,1,3,2,0:T(8,128)(2,1)}, bf16[2,3,4,1,128,128]{4,5,1,3,2,0:T(8,128)(2,1)}, u32[]{:S(2)}, u32[]{:S(2)}) collective-permute-start(bf16[2,3,4,1,128,128]{4,5,1,3,2,0:T(8,128)(2,1)} %get-tuple-element.114), channel_id=1, source_target_pairs={{1,0},{2,1},{3,2},{5,4},{6,5},{7,6},{9,8},{10,9},{11,10},{13,12},{... | collective-permute-start | bytes 2359304 | tf_op jit(solution)/shard_map/ppermute | solution.py:88
  54.6 11.1 %collective-permute-done.7 = bf16[768,384]{1,0:T(8,128)(2,1)} collective-permute-done((bf16[768,384]{1,0:T(8,128)(2,1)S(1)}, bf16[768,384]{1,0:T(8,128)(2,1)}, u32[]{:S(2)}, u32[]{:S(2)}) %collective-permute-start.7) | collective-permute-done | bytes 589856 | tf_op jit(solution)/shard_map/ppermute | solution.py:15
  65.7 2.8 %maximum_select_fusion.1 = bf16[1536,384]{1,0:T(8,128)(2,1)} fusion(bf16[768,384]{1,0:T(8,128)(2,1)} %collective-permute-done.7, bf16[768,384]{1,0:T(8,128)(2,1)S(1)} %maximum_select_fusion.2, pred[]{:T(512)S(6)} %eq.22), kind=kLoop, calls=%fused_computation.19 | loop fusion | flops 5308416 | bytes 2359297 | tf_op jit(solution)/shard_map/jit(_where)/select_n | solution.py:17
  68.4 16.7 %collective-permute-done.3 = bf16[2,3,4,1,128,128]{4,5,1,3,2,0:T(8,128)(2,1)} collective-permute-done((bf16[2,3,4,1,128,128]{4,5,1,3,2,0:T(8,128)(2,1)}, bf16[2,3,4,1,128,128]{4,5,1,3,2,0:T(8,128)(2,1)}, u32[]{:S(2)}, u32[]{:S(2)}) %collective-permute-start.3) | collective-permute-done | bytes 786464 | tf_op jit(solution)/shard_map/ppermute | solution.py:88
  89.4 7.2 %fusion.42 = (f32[3,4,128]{2,1,0:T(4,128)S(1)}, f32[3,4,128,2048]{2,3,1,0:T(8,128)}) fusion(pred[4,2048]{1,0:T(4,128)(4,1)S(1)} %bitcast.198, bf16[3,2048,128,1]{2,1,3,0:T(8,128)(2,1)S(1)} %bitcast.189, bf16[3,4,128,128]{2,3,0,1:T(8,128)(2,1)S(1)} %bitcast.184), kind=kOutput, calls=%fused_computation.85 | convolution fusion | flops 817891328 | bytes 14563328 | tf_op jit(solution)/shard_map/sub | solution.py:155
  96.6 8.5 %fusion.5 = bf16[3,4,128,2048]{2,3,1,0:T(8,128)(2,1)} fusion(f32[3,4,128,2048]{2,3,1,0:T(8,128)} %get-tuple-element.126, f32[3,4,128]{2,1,0:T(4,128)S(1)} %get-tuple-element.125), kind=kLoop, calls=%fused_computation.9 | loop fusion | flops 6291456 | bytes 18880512 | tf_op jit(solution)/shard_map/convert_element_type | solution.py:158
  105.1 5.0 %collective-permute-done.8 = bf16[1536,384]{1,0:T(8,128)(2,1)} collective-permute-done((bf16[1536,384]{1,0:T(8,128)(2,1)}, bf16[1536,384]{1,0:T(8,128)(2,1)}, u32[]{:S(2)}, u32[]{:S(2)}) %collective-permute-start.8) | collective-permute-done | bytes 1179680 | tf_op jit(solution)/shard_map/ppermute | solution.py:15
  110.1 3.1 %maximum_select_fusion = bf16[3072,384]{1,0:T(8,128)(2,1)S(1)} fusion(bf16[1536,384]{1,0:T(8,128)(2,1)} %collective-permute-done.8, bf16[1536,384]{1,0:T(8,128)(2,1)} %maximum_select_fusion.1, pred[]{:T(512)S(6)} %eq.21), kind=kLoop, calls=%fused_computation.11 | loop fusion | flops 10616832 | bytes 4718593 | tf_op jit(solution)/shard_map/jit(_where)/select_n | solution.py:17
  113.6 4.1 %fusion.9 = bf16[512,384]{0,1:T(8,128)(2,1)} fusion(bf16[3072,384]{1,0:T(8,128)(2,1)S(1)} %bitcast.183, bf16[512,3072]{1,0:T(8,128)(2,1)} %bitcast.199), kind=kOutput, calls=%fused_computation.18 | convolution fusion | flops 1208156160 | bytes 5898240 | tf_op jit(solution)/shard_map/dot_general | solution.py:160
  119.0 6.4 %fusion.47 = f32[3,2048,128,1]{2,1,3,0:T(8,128)} fusion(bf16[3,4,128,2048]{2,3,1,0:T(8,128)(2,1)} %fusion.5, bf16[3,4,128,128]{2,3,1,0:T(8,128)(2,1)S(1)} %bitcast.186), kind=kOutput, calls=%fused_computation.86 | convolution fusion | flops 805306368 | bytes 9830400 | tf_op jit(solution)/shard_map/hqtl,hqtd->hld/dot_general | solution.py:171
  126.6 5.9 %multiply_convert_fusion = bf16[3,4,128,2048]{2,3,1,0:T(8,128)(2,1)S(1)} fusion(f32[3,4,128]{2,1,0:T(4,128)S(1)} %fusion.8, bf16[3,2048,128,1]{2,1,3,0:T(8,128)(2,1)S(1)} %bitcast.192, bf16[3,4,128,128]{2,3,1,0:T(8,128)(2,1)S(1)} %bitcast.188, f32[3,4,128,2048]{2,3,1,0:T(8,128)} %get-tuple-element.126, f32[3,4,128]{2,1,0:T(4,128)S(1)} %get-tuple-element.125), kind=kOutput, calls=%fused_computation.2 | convolution fusion | flops 821035008 | bytes 20852736 | tf_op jit(solution)/shard_map/hqtd,hld->hqtl/dot_general | solution.py:167
  132.5 3.6 %fusion.32 = f32[3,2048,128,1]{2,1,3,0:T(8,128)} fusion(bf16[3,4,128,2048]{2,3,1,0:T(8,128)(2,1)S(1)} %multiply_convert_fusion, bf16[3,4,128,128]{2,3,0,1:T(8,128)(2,1)S(1)} %bitcast.185), kind=kOutput, calls=%fused_computation.60 | convolution fusion | flops 805306368 | bytes 9830400 | tf_op jit(solution)/shard_map/hqtl,hqtd->hld/dot_general | solution.py:170
  136.2 2.6 %copy.78 = f32[3,4,4,128,128]{3,4,0,1,2:T(8,128)S(1)} copy(f32[3,4,4,128,128]{4,3,2,1,0:T(8,128)} %bitcast.173) | data formatting | bytes 6291456 | tf_op jit(solution)/shard_map/reshape | solution.py:175
  140.1 3.6 %copy.82 = f32[3,4,4,128,128]{3,4,0,1,2:T(8,128)} copy(f32[3,4,4,128,128]{4,3,2,1,0:T(8,128)} %bitcast.171) | data formatting | bytes 6291456 | tf_op jit(solution)/shard_map/reshape | solution.py:175
  146.9 4.9 %collective-permute-start.9 = (bf16[2,3,4,128,128]{3,4,1,2,0:T(8,128)(2,1)}, bf16[2,3,4,128,128]{3,4,1,2,0:T(8,128)(2,1)}, u32[]{:S(2)}, u32[]{:S(2)}) collective-permute-start(bf16[2,3,4,128,128]{3,4,1,2,0:T(8,128)(2,1)} %pad_maximum_fusion.2), channel_id=1, source_target_pairs={{0,1},{1,2},{2,3},{4,5},{5,6},{6,7},{8,9},{9,10},{10,11},{12,13},{... | collective-permute-start | bytes 2359304 | tf_op jit(solution)/shard_map/ppermute | solution.py:72
  152.7 2.9 %collective-permute-start.10 = (bf16[2,3,4,128,128]{3,4,1,2,0:T(8,128)(2,1)}, bf16[2,3,4,128,128]{3,4,1,2,0:T(8,128)(2,1)}, u32[]{:S(2)}, u32[]{:S(2)}) collective-permute-start(bf16[2,3,4,128,128]{3,4,1,2,0:T(8,128)(2,1)} %pad_maximum_fusion.3), channel_id=1, source_target_pairs={{1,0},{2,1},{3,2},{5,4},{6,5},{7,6},{9,8},{10,9},{11,10},{13,12},{... | collective-permute-start | bytes 2359304 | tf_op jit(solution)/shard_map/ppermute | solution.py:72
  158.9 10.2 %collective-permute-done.9 = bf16[2,3,4,128,128]{3,4,1,2,0:T(8,128)(2,1)} collective-permute-done((bf16[2,3,4,128,128]{3,4,1,2,0:T(8,128)(2,1)}, bf16[2,3,4,128,128]{3,4,1,2,0:T(8,128)(2,1)}, u32[]{:S(2)}, u32[]{:S(2)}) %collective-permute-start.9) | collective-permute-done | bytes 786464 | tf_op jit(solution)/shard_map/ppermute | solution.py:72
  173.0 16.7 %collective-permute-done.10 = bf16[2,3,4,128,128]{3,4,1,2,0:T(8,128)(2,1)} collective-permute-done((bf16[2,3,4,128,128]{3,4,1,2,0:T(8,128)(2,1)}, bf16[2,3,4,128,128]{3,4,1,2,0:T(8,128)(2,1)}, u32[]{:S(2)}, u32[]{:S(2)}) %collective-permute-start.10) | collective-permute-done | bytes 786464 | tf_op jit(solution)/shard_map/ppermute | solution.py:72
  193.4 4.8 %collective-permute-start.11 = (bf16[2,3,2,128,128]{3,4,1,2,0:T(8,128)(2,1)}, bf16[2,3,2,128,128]{3,4,1,2,0:T(8,128)(2,1)}, u32[]{:S(2)}, u32[]{:S(2)}) collective-permute-start(bf16[2,3,2,128,128]{3,4,1,2,0:T(8,128)(2,1)} %pad_maximum_fusion.5), channel_id=1, source_target_pairs={{0,4},{4,8},{8,12},{12,16},{16,20},{20,24},{24,28},{1,5},{5,9},{9,... | collective-permute-start | bytes 1179656 | tf_op jit(solution)/shard_map/ppermute | solution.py:72
  205.1 9.5 %collective-permute-done.12 = bf16[2,3,2,128,128]{3,4,1,2,0:T(8,128)(2,1)} collective-permute-done((bf16[2,3,2,128,128]{3,4,1,2,0:T(8,128)(2,1)}, bf16[2,3,2,128,128]{3,4,1,2,0:T(8,128)(2,1)}, u32[]{:S(2)}, u32[]{:S(2)}) %collective-permute-start.12) | collective-permute-done | bytes 393248 | tf_op jit(solution)/shard_map/ppermute | solution.py:72
  (107 shorter events, 47.5 us)
Async XLA Ops:
  7.2 13.1 %copy-start.10 = (bf16[96,384]{1,0:T(8,128)(2,1)S(1)}, bf16[96,384]{1,0:T(8,128)(2,1)}, u32[]{:S(2)}) copy-start(bf16[96,384]{1,0:T(8,128)(2,1)} %param.25) | copy-start | bytes 221188
  7.2 106.5 %all-gather.2.cloned.1.call-start = ((), (), s32[]{:S(2)}) async-start(), calls=%async_computation | async-start | bytes 3538944 | tf_op jit(solution)/shard_map/all_gather | solution.py:117
  7.9 12.3 %collective-permute-start.4 = (bf16[96,384]{1,0:T(8,128)(2,1)}, bf16[96,384]{1,0:T(8,128)(2,1)S(1)}, u32[]{:S(2)}, u32[]{:S(2)}) collective-permute-start(bf16[96,384]{1,0:T(8,128)(2,1)} %param.25), channel_id=1, source_target_pairs={{0,2},{1,3},{2,0},{3,1},{4,6},{5,7},{6,4},{7,5},{8,10},{9,11},{10,... | collective-permute-start | bytes 221192 | tf_op jit(solution)/shard_map/ppermute | solution.py:15
  15.9 27.9 %collective-permute-start = (bf16[2,3,1,2,128,128]{4,5,1,3,2,0:T(8,128)(2,1)S(1)}, bf16[2,3,1,2,128,128]{4,5,1,3,2,0:T(8,128)(2,1)S(1)}, u32[]{:S(2)}, u32[]{:S(2)}) collective-permute-start(bf16[2,3,1,2,128,128]{4,5,1,3,2,0:T(8,128)(2,1)S(1)} %get-tuple-element.123), channel_id=1, source_target_pairs={{0,4},{4,8},{8,12},{12,16},{16,20},{20,24},{24,28},{1,5},{5,9},{9,... | collective-permute-start | bytes 1179656 | tf_op jit(solution)/shard_map/ppermute | solution.py:87
  18.9 24.9 %collective-permute-start.1 = (bf16[2,3,1,2,128,128]{4,5,1,3,2,0:T(8,128)(2,1)S(1)}, bf16[2,3,1,2,128,128]{4,5,1,3,2,0:T(8,128)(2,1)S(1)}, u32[]{:S(2)}, u32[]{:S(2)}) collective-permute-start(bf16[2,3,1,2,128,128]{4,5,1,3,2,0:T(8,128)(2,1)S(1)} %get-tuple-element.124), channel_id=1, source_target_pairs={{4,0},{8,4},{12,8},{16,12},{20,16},{24,20},{28,24},{5,1},{9,5},{13... | collective-permute-start | bytes 1179656 | tf_op jit(solution)/shard_map/ppermute | solution.py:88
  20.3 11.7 %collective-permute-start.5 = (bf16[192,384]{1,0:T(8,128)(2,1)S(1)}, bf16[192,384]{1,0:T(8,128)(2,1)S(1)}, u32[]{:S(2)}, u32[]{:S(2)}) collective-permute-start(bf16[192,384]{1,0:T(8,128)(2,1)S(1)} %maximum_select_fusion.4), channel_id=1, source_target_pairs={{0,1},{1,0},{2,3},{3,2},{4,5},{5,4},{6,7},{7,6},{8,9},{9,8},{10,11... | collective-permute-start | bytes 442376 | tf_op jit(solution)/shard_map/ppermute | solution.py:15
  32.1 20.0 %collective-permute-start.6 = (bf16[384,384]{1,0:T(8,128)(2,1)S(1)}, bf16[384,384]{1,0:T(8,128)(2,1)S(1)}, u32[]{:S(2)}, u32[]{:S(2)}) collective-permute-start(bf16[384,384]{1,0:T(8,128)(2,1)S(1)} %maximum_select_fusion.3), channel_id=1, source_target_pairs={{0,16},{4,20},{8,24},{12,28},{16,0},{20,4},{24,8},{28,12},{1,17},{... | collective-permute-start | bytes 884744 | tf_op jit(solution)/shard_map/ppermute | solution.py:15
  45.3 23.2 %collective-permute-start.2 = (bf16[2,3,4,1,128,128]{4,5,1,3,2,0:T(8,128)(2,1)}, bf16[2,3,4,1,128,128]{4,5,1,3,2,0:T(8,128)(2,1)S(1)}, u32[]{:S(2)}, u32[]{:S(2)}) collective-permute-start(bf16[2,3,4,1,128,128]{4,5,1,3,2,0:T(8,128)(2,1)} %get-tuple-element.113), channel_id=1, source_target_pairs={{0,1},{1,2},{2,3},{4,5},{5,6},{6,7},{8,9},{9,10},{10,11},{12,13},{... | collective-permute-start | bytes 2359304 | tf_op jit(solution)/shard_map/ppermute | solution.py:87
  47.2 37.9 %collective-permute-start.3 = (bf16[2,3,4,1,128,128]{4,5,1,3,2,0:T(8,128)(2,1)}, bf16[2,3,4,1,128,128]{4,5,1,3,2,0:T(8,128)(2,1)}, u32[]{:S(2)}, u32[]{:S(2)}) collective-permute-start(bf16[2,3,4,1,128,128]{4,5,1,3,2,0:T(8,128)(2,1)} %get-tuple-element.114), channel_id=1, source_target_pairs={{1,0},{2,1},{3,2},{5,4},{6,5},{7,6},{9,8},{10,9},{11,10},{13,12},{... | collective-permute-start | bytes 2359304 | tf_op jit(solution)/shard_map/ppermute | solution.py:88
  52.3 13.4 %collective-permute-start.7 = (bf16[768,384]{1,0:T(8,128)(2,1)S(1)}, bf16[768,384]{1,0:T(8,128)(2,1)}, u32[]{:S(2)}, u32[]{:S(2)}) collective-permute-start(bf16[768,384]{1,0:T(8,128)(2,1)S(1)} %maximum_select_fusion.2), channel_id=1, source_target_pairs={{0,8},{4,12},{8,0},{12,4},{16,24},{20,28},{24,16},{28,20},{1,9},{5... | collective-permute-start | bytes 1769480 | tf_op jit(solution)/shard_map/ppermute | solution.py:15
  68.4 41.7 %collective-permute-start.8 = (bf16[1536,384]{1,0:T(8,128)(2,1)}, bf16[1536,384]{1,0:T(8,128)(2,1)}, u32[]{:S(2)}, u32[]{:S(2)}) collective-permute-start(bf16[1536,384]{1,0:T(8,128)(2,1)} %maximum_select_fusion.1), channel_id=1, source_target_pairs={{0,4},{4,0},{8,12},{12,8},{16,20},{20,16},{24,28},{28,24},{1,5},{5... | collective-permute-start | bytes 3538952 | tf_op jit(solution)/shard_map/ppermute | solution.py:15
  89.4 7.2 %copy-start.6 = (bf16[1,3,4,4,128,128]{5,4,3,2,1,0:T(8,128)(2,1)}, bf16[1,3,4,4,128,128]{5,4,3,2,1,0:T(8,128)(2,1)S(1)}, u32[]{:S(2)}) copy-start(bf16[1,3,4,4,128,128]{5,4,3,2,1,0:T(8,128)(2,1)S(1)} %copy.64) | copy-start | bytes 4718596
  117.7 7.7 %slice-start = ((s8[6291456]{0:T(1024)(128)(4,1)}), s8[2097152]{0:T(1024)(128)(4,1)S(1)}, s32[]{:S(2)}) async-start(s8[6291456]{0:T(1024)(128)(4,1)} %bitcast.169), calls=%async_computation.1 | async-start | bytes 4194304
  119.0 6.4 %slice-start.1 = ((s8[6291456]{0:T(1024)(128)(4,1)}), s8[4194304]{0:T(1024)(128)(4,1)S(1)}, s32[]{:S(2)}) async-start(s8[6291456]{0:T(1024)(128)(4,1)} %bitcast.169), calls=%async_computation.2 | async-start | bytes 8388608
  119.0 6.4 %copy-start.8 = (bf16[1,3,4,4,128,128]{5,4,3,2,1,0:T(8,128)(2,1)S(1)}, bf16[1,3,4,4,128,128]{5,4,3,2,1,0:T(8,128)(2,1)}, u32[]{:S(2)}) copy-start(bf16[1,3,4,4,128,128]{5,4,3,2,1,0:T(8,128)(2,1)} %copy.69) | copy-start | bytes 4718596
  138.8 16.8 %copy-start = (f32[3,4,4,128,128]{3,4,0,1,2:T(8,128)}, f32[3,4,4,128,128]{3,4,0,1,2:T(8,128)S(1)}, u32[]{:S(2)}) copy-start(f32[3,4,4,128,128]{3,4,0,1,2:T(8,128)S(1)} %copy.78) | copy-start | bytes 9437188
  146.9 22.1 %collective-permute-start.9 = (bf16[2,3,4,128,128]{3,4,1,2,0:T(8,128)(2,1)}, bf16[2,3,4,128,128]{3,4,1,2,0:T(8,128)(2,1)}, u32[]{:S(2)}, u32[]{:S(2)}) collective-permute-start(bf16[2,3,4,128,128]{3,4,1,2,0:T(8,128)(2,1)} %pad_maximum_fusion.2), channel_id=1, source_target_pairs={{0,1},{1,2},{2,3},{4,5},{5,6},{6,7},{8,9},{9,10},{10,11},{12,13},{... | collective-permute-start | bytes 2359304 | tf_op jit(solution)/shard_map/ppermute | solution.py:72
  152.7 36.9 %collective-permute-start.10 = (bf16[2,3,4,128,128]{3,4,1,2,0:T(8,128)(2,1)}, bf16[2,3,4,128,128]{3,4,1,2,0:T(8,128)(2,1)}, u32[]{:S(2)}, u32[]{:S(2)}) collective-permute-start(bf16[2,3,4,128,128]{3,4,1,2,0:T(8,128)(2,1)} %pad_maximum_fusion.3), channel_id=1, source_target_pairs={{1,0},{2,1},{3,2},{5,4},{6,5},{7,6},{9,8},{10,9},{11,10},{13,12},{... | collective-permute-start | bytes 2359304 | tf_op jit(solution)/shard_map/ppermute | solution.py:72
  156.9 13.5 %slice-start.2 = ((f32[3,4,4,128,128]{3,4,0,1,2:T(8,128)}), f32[3,4,2,128,128]{3,4,0,1,2:T(8,128)S(1)}, s32[]{:S(2)}) async-start(f32[3,4,4,128,128]{3,4,0,1,2:T(8,128)} %copy-done), calls=%async_computation.3 | async-start | bytes 3145728 | tf_op jit(solution)/shard_map/slice | solution.py:98
  191.0 9.2 %slice-start.3 = ((s8[6291456]{0:T(1024)(128)(4,1)}), s8[4194304]{0:T(1024)(128)(4,1)S(1)}, s32[]{:S(2)}) async-start(s8[6291456]{0:T(1024)(128)(4,1)} %bitcast.175), calls=%async_computation.4 | async-start | bytes 8388608
  191.4 8.8 %slice-start.4 = ((s8[6291456]{0:T(1024)(128)(4,1)}), s8[2097152]{0:T(1024)(128)(4,1)S(1)}, s32[]{:S(2)}) async-start(s8[6291456]{0:T(1024)(128)(4,1)} %bitcast.175), calls=%async_computation.5 | async-start | bytes 4194304
  191.6 8.6 %copy-start.7 = (bf16[1,3,4,4,128,128]{5,4,3,2,1,0:T(8,128)(2,1)S(1)}, bf16[1,3,4,4,128,128]{5,4,3,2,1,0:T(8,128)(2,1)}, u32[]{:S(2)}) copy-start(bf16[1,3,4,4,128,128]{5,4,3,2,1,0:T(8,128)(2,1)} %copy-done.6) | copy-start | bytes 4718596
  193.4 10.5 %collective-permute-start.11 = (bf16[2,3,2,128,128]{3,4,1,2,0:T(8,128)(2,1)}, bf16[2,3,2,128,128]{3,4,1,2,0:T(8,128)(2,1)}, u32[]{:S(2)}, u32[]{:S(2)}) collective-permute-start(bf16[2,3,2,128,128]{3,4,1,2,0:T(8,128)(2,1)} %pad_maximum_fusion.5), channel_id=1, source_target_pairs={{0,4},{4,8},{8,12},{12,16},{16,20},{20,24},{24,28},{1,5},{5,9},{9,... | collective-permute-start | bytes 1179656 | tf_op jit(solution)/shard_map/ppermute | solution.py:72
  198.9 15.7 %collective-permute-start.12 = (bf16[2,3,2,128,128]{3,4,1,2,0:T(8,128)(2,1)}, bf16[2,3,2,128,128]{3,4,1,2,0:T(8,128)(2,1)}, u32[]{:S(2)}, u32[]{:S(2)}) collective-permute-start(bf16[2,3,2,128,128]{3,4,1,2,0:T(8,128)(2,1)} %pad_maximum_fusion.6), channel_id=1, source_target_pairs={{4,0},{8,4},{12,8},{16,12},{20,16},{24,20},{28,24},{5,1},{9,5},{13... | collective-permute-start | bytes 1179656 | tf_op jit(solution)/shard_map/ppermute | solution.py:72
  (6 other events, 13.4 us)
Sparse Core Ops, SparseCore 0:
  9.8 32.4 all-gather.1

commit v8 on v7

--- a/solution.py
+++ b/solution.py
@@ -91,21 +91,21 @@
 
 
 def folded(grad_k, grad_v):
-    from_right = sent_back([grad_k[:, :, 0], grad_v[:, :, 0]], "wa", -1)
-    from_left = sent_back([grad_k[:, :, -1], grad_v[:, :, -1]], "wa", 1)
+    from_below = sent_back([grad_k[:, 0], grad_v[:, 0]], "ha", -1)
+    from_above = sent_back([grad_k[:, -1], grad_v[:, -1]], "ha", 1)
     own = []
     for n, part in enumerate((grad_k, grad_v)):
+        inner = part[:, 1:-1]
+        inner = inner.at[:, 0:1].add(from_above[n][:, None])
+        inner = inner.at[:, -1:].add(from_below[n][:, None])
+        own.append(inner)
+    from_right = sent_back([own[0][:, :, 0], own[1][:, :, 0]], "wa", -1)
+    from_left = sent_back([own[0][:, :, -1], own[1][:, :, -1]], "wa", 1)
+    result = []
+    for n, part in enumerate(own):
         inner = part[:, :, 1:-1]
         inner = inner.at[:, :, 0:1].add(from_left[n][:, :, None])
         inner = inner.at[:, :, -1:].add(from_right[n][:, :, None])
-        own.append(inner)
-    from_below = sent_back([own[0][:, 0], own[1][:, 0]], "ha", -1)
-    from_above = sent_back([own[0][:, -1], own[1][:, -1]], "ha", 1)
-    result = []
-    for n, part in enumerate(own):
-        inner = part[:, 1:-1]
-        inner = inner.at[:, 0:1].add(from_above[n][:, None])
-        inner = inner.at[:, -1:].add(from_below[n][:, None])
         result.append(inner)
     return result[0], result[1]
 
@@ -124,7 +124,7 @@
     def head_minor(array):
         return jnp.transpose(array, (1, 2, 3, 0, 4)).reshape(queries.shape)
 
-    ext = extended_2(jnp.stack([head_major(keys), head_major(values)]), (("ha", 2), ("wa", 3)), 1)
+    ext = extended_2(jnp.stack([head_major(keys), head_major(values)]), (("wa", 3), ("ha", 2)), 1)
     ext_r, ext_c = tile_rows + 2, tile_cols + 2
     row_base = lax.axis_index("ha") * tile_rows
     col_base = lax.axis_index("wa") * tile_cols

time: 230 us -> 227 us (0.987)
  starting transfers between devices: 44.3 us -> 30.2 us
  waiting for transfers between devices: 80.9 us -> 92.8 us
    ppermute x5, waiting for transfers between devices: 26.2 us -> 55.5 us  [doubling_gather(): other = lax.ppermute(buf, axis, [(i, i ^ bit) for i in range(count)])]
    ppermute x2, waiting for transfers between devices: 16.7 us -> 1.61 us  [extended_2(): after = lax.ppermute(first, axis, down)]
    ppermute x5, starting transfers between devices: 19.5 us -> 8.95 us  [doubling_gather(): other = lax.ppermute(buf, axis, [(i, i ^ bit) for i in range(count)])]
    ppermute x4, waiting for transfers between devices: 37.3 us -> 34.9 us  [passed_along(): lax.ppermute(value, axis, [(source, source + steps) for source in range(f...]
    scatter-add x1 -> x2, other arithmetic: 0.09 us -> 2.44 us  [folded(): inner = inner.at[:, 0:1].add(from_above[n][:, None])]
    scatter-add x2 -> x1, other arithmetic: 2.44 us -> 0.09 us  [folded(): inner = inner.at[:, :, 0:1].add(from_left[n][:, :, None])]
    ppermute x4, starting transfers between devices: 13.8 us -> 11.4 us  [passed_along(): lax.ppermute(value, axis, [(source, source + steps) for source in range(f...]
where the time goes in v8:
time: 227 us; the launch traced here: 225 us
  waiting for transfers between devices  92.8 us (41%)
  other arithmetic  31.8 us (14%)
  starting transfers between devices  30.2 us (13%)
  matrix products  29.5 us (13%)
  local copies, waits for them, and re-layouts  25.8 us (11%)
  between operations  14.7 us (6%)
    ppermute x5, waiting for transfers between devices, doubling_gather(): other = lax.ppermute(buf, axis, [(i, i ^ bit) for i in range(count)])  55.5 us
    ppermute x4, waiting for transfers between devices, passed_along(): lax.ppermute(value, axis, [(source, source + steps) for source in range(f...  34.9 us
    ppermute x4, starting transfers between devices, passed_along(): lax.ppermute(value, axis, [(source, source + steps) for source in range(f...  11.4 us
    unnamed x39, local copies, waits for them, and re-layouts  9.91 us
    ppermute x5, starting transfers between devices, doubling_gather(): other = lax.ppermute(buf, axis, [(i, i ^ bit) for i in range(count)])  8.95 us
    convert_element_type x1, other arithmetic, local(): probs_lo = probs.astype(bf16)  8.49 us
    sub x1, matrix products, local(): scores = scores - jnp.max(scores, axis=-1, keepdims=True)  7.24 us
    dot_general x1, matrix products, local(): jnp.einsum('hqtl,hqtd->hld', probs_lo, grad, preferred_element_type=f32)  6.42 us
  transfers between devices with their start and end apart: 14, of which 8 were waited for; matrix products, arithmetic and copies ran while one was open for 20% of the time, Pallas kernels for 0%

profile of v8, /device:TPU:64, one launch (start us, length us, event | category | flops | bytes accessed | tf_op | source)
XLA Modules:
  0.0 224.7 jit_solution(4589929408401092270)
XLA Ops:
  7.9 5.5 %collective-permute-start.4 = (bf16[96,384]{1,0:T(8,128)(2,1)}, bf16[96,384]{1,0:T(8,128)(2,1)S(1)}, u32[]{:S(2)}, u32[]{:S(2)}) collective-permute-start(bf16[96,384]{1,0:T(8,128)(2,1)} %param.25), channel_id=1, source_target_pairs={{0,2},{1,3},{2,0},{3,1},{4,6},{5,7},{6,4},{7,5},{8,10},{9,11},{10,... | collective-permute-start | bytes 221192 | tf_op jit(solution)/shard_map/ppermute | solution.py:15
  17.8 4.8 %collective-permute-start.1 = (bf16[2,3,2,1,128,128]{4,5,1,3,2,0:T(8,128)(2,1)S(1)}, bf16[2,3,2,1,128,128]{4,5,1,3,2,0:T(8,128)(2,1)S(1)}, u32[]{:S(2)}, u32[]{:S(2)}) collective-permute-start(bf16[2,3,2,1,128,128]{4,5,1,3,2,0:T(8,128)(2,1)S(1)} %get-tuple-element.122), channel_id=1, source_target_pairs={{1,0},{2,1},{3,2},{5,4},{6,5},{7,6},{9,8},{10,9},{11,10},{13,12},{... | collective-permute-start | bytes 1179656 | tf_op jit(solution)/shard_map/ppermute | solution.py:88
  23.0 22.2 %collective-permute-done.5 = bf16[192,384]{1,0:T(8,128)(2,1)S(1)} collective-permute-done((bf16[192,384]{1,0:T(8,128)(2,1)S(1)}, bf16[192,384]{1,0:T(8,128)(2,1)S(1)}, u32[]{:S(2)}, u32[]{:S(2)}) %collective-permute-start.5) | collective-permute-done | bytes 147488 | tf_op jit(solution)/shard_map/ppermute | solution.py:15
  45.3 3.3 %collective-permute-start.6 = (bf16[384,384]{1,0:T(8,128)(2,1)S(1)}, bf16[384,384]{1,0:T(8,128)(2,1)S(1)}, u32[]{:S(2)}, u32[]{:S(2)}) collective-permute-start(bf16[384,384]{1,0:T(8,128)(2,1)S(1)} %maximum_select_fusion.3), channel_id=1, source_target_pairs={{0,16},{4,20},{8,24},{12,28},{16,0},{20,4},{24,8},{28,12},{1,17},{... | collective-permute-start | bytes 884744 | tf_op jit(solution)/shard_map/ppermute | solution.py:15
  53.1 19.9 %collective-permute-done.6 = bf16[384,384]{1,0:T(8,128)(2,1)S(1)} collective-permute-done((bf16[384,384]{1,0:T(8,128)(2,1)S(1)}, bf16[384,384]{1,0:T(8,128)(2,1)S(1)}, u32[]{:S(2)}, u32[]{:S(2)}) %collective-permute-start.6) | collective-permute-done | bytes 294944 | tf_op jit(solution)/shard_map/ppermute | solution.py:15
  74.9 9.0 %collective-permute-done.7 = bf16[768,384]{1,0:T(8,128)(2,1)} collective-permute-done((bf16[768,384]{1,0:T(8,128)(2,1)S(1)}, bf16[768,384]{1,0:T(8,128)(2,1)}, u32[]{:S(2)}, u32[]{:S(2)}) %collective-permute-start.7) | collective-permute-done | bytes 589856 | tf_op jit(solution)/shard_map/ppermute | solution.py:15
  83.9 2.8 %maximum_select_fusion.1 = bf16[1536,384]{1,0:T(8,128)(2,1)} fusion(bf16[768,384]{1,0:T(8,128)(2,1)} %collective-permute-done.7, bf16[768,384]{1,0:T(8,128)(2,1)S(1)} %maximum_select_fusion.2, pred[]{:T(512)S(6)} %eq.22), kind=kLoop, calls=%fused_computation.19 | loop fusion | flops 5308416 | bytes 2359297 | tf_op jit(solution)/shard_map/jit(_where)/select_n | solution.py:17
  92.6 7.2 %fusion.42 = (f32[3,4,128]{2,1,0:T(4,128)S(1)}, f32[3,4,128,2048]{2,3,1,0:T(8,128)}) fusion(pred[4,2048]{1,0:T(4,128)(4,1)S(1)} %bitcast.202, bf16[3,2048,128,1]{2,1,3,0:T(8,128)(2,1)S(1)} %bitcast.193, bf16[3,4,128,128]{2,3,0,1:T(8,128)(2,1)S(1)} %bitcast.188), kind=kOutput, calls=%fused_computation.86 | convolution fusion | flops 817891328 | bytes 14563328 | tf_op jit(solution)/shard_map/sub | solution.py:155
  99.9 8.5 %fusion.5 = bf16[3,4,128,2048]{2,3,1,0:T(8,128)(2,1)} fusion(f32[3,4,128,2048]{2,3,1,0:T(8,128)} %get-tuple-element.124, f32[3,4,128]{2,1,0:T(4,128)S(1)} %get-tuple-element.123), kind=kLoop, calls=%fused_computation.9 | loop fusion | flops 6291456 | bytes 18880512 | tf_op jit(solution)/shard_map/convert_element_type | solution.py:158
  108.3 4.4 %collective-permute-done.8 = bf16[1536,384]{1,0:T(8,128)(2,1)} collective-permute-done((bf16[1536,384]{1,0:T(8,128)(2,1)}, bf16[1536,384]{1,0:T(8,128)(2,1)}, u32[]{:S(2)}, u32[]{:S(2)}) %collective-permute-start.8) | collective-permute-done | bytes 1179680 | tf_op jit(solution)/shard_map/ppermute | solution.py:15
  112.7 3.2 %maximum_select_fusion = bf16[3072,384]{1,0:T(8,128)(2,1)S(1)} fusion(bf16[1536,384]{1,0:T(8,128)(2,1)} %collective-permute-done.8, bf16[1536,384]{1,0:T(8,128)(2,1)} %maximum_select_fusion.1, pred[]{:T(512)S(6)} %eq.21), kind=kLoop, calls=%fused_computation.11 | loop fusion | flops 10616832 | bytes 4718593 | tf_op jit(solution)/shard_map/jit(_where)/select_n | solution.py:17
  116.3 4.1 %fusion.9 = bf16[512,384]{0,1:T(8,128)(2,1)} fusion(bf16[3072,384]{1,0:T(8,128)(2,1)S(1)} %bitcast.187, bf16[512,3072]{1,0:T(8,128)(2,1)} %bitcast.203), kind=kOutput, calls=%fused_computation.18 | convolution fusion | flops 1208156160 | bytes 5898240 | tf_op jit(solution)/shard_map/dot_general | solution.py:160
  121.7 6.4 %fusion.47 = f32[3,2048,128,1]{2,1,3,0:T(8,128)} fusion(bf16[3,4,128,2048]{2,3,1,0:T(8,128)(2,1)} %fusion.5, bf16[3,4,128,128]{2,3,1,0:T(8,128)(2,1)S(1)} %bitcast.190), kind=kOutput, calls=%fused_computation.87 | convolution fusion | flops 805306368 | bytes 9830400 | tf_op jit(solution)/shard_map/hqtl,hqtd->hld/dot_general | solution.py:171
  129.3 5.9 %multiply_convert_fusion = bf16[3,4,128,2048]{2,3,1,0:T(8,128)(2,1)S(1)} fusion(f32[3,4,128]{2,1,0:T(4,128)S(1)} %fusion.8, bf16[3,2048,128,1]{2,1,3,0:T(8,128)(2,1)S(1)} %bitcast.196, bf16[3,4,128,128]{2,3,1,0:T(8,128)(2,1)S(1)} %bitcast.192, f32[3,4,128,2048]{2,3,1,0:T(8,128)} %get-tuple-element.124, f32[3,4,128]{2,1,0:T(4,128)S(1)} %get-tuple-element.123), kind=kOutput, calls=%fused_computation.2 | convolution fusion | flops 821035008 | bytes 20852736 | tf_op jit(solution)/shard_map/hqtd,hld->hqtl/dot_general | solution.py:167
  135.2 3.6 %fusion.32 = f32[3,2048,128,1]{2,1,3,0:T(8,128)} fusion(bf16[3,4,128,2048]{2,3,1,0:T(8,128)(2,1)S(1)} %multiply_convert_fusion, bf16[3,4,128,128]{2,3,0,1:T(8,128)(2,1)S(1)} %bitcast.189), kind=kOutput, calls=%fused_computation.61 | convolution fusion | flops 805306368 | bytes 9830400 | tf_op jit(solution)/shard_map/hqtl,hqtd->hld/dot_general | solution.py:170
  138.8 2.6 %copy.81 = f32[3,4,4,128,128]{3,4,0,2,1:T(8,128)S(1)} copy(f32[3,4,4,128,128]{4,3,2,1,0:T(8,128)} %bitcast.177) | data formatting | bytes 6291456 | tf_op jit(solution)/shard_map/reshape | solution.py:175
  142.8 3.6 %copy.85 = f32[3,4,4,128,128]{3,4,0,2,1:T(8,128)} copy(f32[3,4,4,128,128]{4,3,2,1,0:T(8,128)} %bitcast.175) | data formatting | bytes 6291456 | tf_op jit(solution)/shard_map/reshape | solution.py:175
  146.4 2.2 convert.33
  149.6 2.3 %collective-permute-start.9 = (bf16[2,3,4,128,128]{3,4,1,2,0:T(8,128)(2,1)}, bf16[2,3,4,128,128]{3,4,1,2,0:T(8,128)(2,1)}, u32[]{:S(2)}, u32[]{:S(2)}) collective-permute-start(bf16[2,3,4,128,128]{3,4,1,2,0:T(8,128)(2,1)} %pad_maximum_fusion.2), channel_id=1, source_target_pairs={{0,4},{4,8},{8,12},{12,16},{16,20},{20,24},{24,28},{1,5},{5,9},{9,... | collective-permute-start | bytes 2359304 | tf_op jit(solution)/shard_map/ppermute | solution.py:72
  157.6 7.8 %collective-permute-done.9 = bf16[2,3,4,128,128]{3,4,1,2,0:T(8,128)(2,1)} collective-permute-done((bf16[2,3,4,128,128]{3,4,1,2,0:T(8,128)(2,1)}, bf16[2,3,4,128,128]{3,4,1,2,0:T(8,128)(2,1)}, u32[]{:S(2)}, u32[]{:S(2)}) %collective-permute-start.9) | collective-permute-done | bytes 786464 | tf_op jit(solution)/shard_map/ppermute | solution.py:72
  169.3 16.0 %collective-permute-done.10 = bf16[2,3,4,128,128]{3,4,1,2,0:T(8,128)(2,1)} collective-permute-done((bf16[2,3,4,128,128]{3,4,1,2,0:T(8,128)(2,1)}, bf16[2,3,4,128,128]{3,4,1,2,0:T(8,128)(2,1)}, u32[]{:S(2)}, u32[]{:S(2)}) %collective-permute-start.10) | collective-permute-done | bytes 786464 | tf_op jit(solution)/shard_map/ppermute | solution.py:72
  189.0 3.2 %collective-permute-start.11 = (bf16[2,3,2,128,128]{3,4,1,2,0:T(8,128)(2,1)}, bf16[2,3,2,128,128]{3,4,1,2,0:T(8,128)(2,1)}, u32[]{:S(2)}, u32[]{:S(2)}) collective-permute-start(bf16[2,3,2,128,128]{3,4,1,2,0:T(8,128)(2,1)} %pad_maximum_fusion.5), channel_id=1, source_target_pairs={{0,1},{1,2},{2,3},{4,5},{5,6},{6,7},{8,9},{9,10},{10,11},{12,13},{... | collective-permute-start | bytes 1179656 | tf_op jit(solution)/shard_map/ppermute | solution.py:72
  193.1 4.4 %collective-permute-start.12 = (bf16[2,3,2,128,128]{3,4,1,2,0:T(8,128)(2,1)}, bf16[2,3,2,128,128]{3,4,1,2,0:T(8,128)(2,1)}, u32[]{:S(2)}, u32[]{:S(2)}) collective-permute-start(bf16[2,3,2,128,128]{3,4,1,2,0:T(8,128)(2,1)} %pad_maximum_fusion.6), channel_id=1, source_target_pairs={{1,0},{2,1},{3,2},{5,4},{6,5},{7,6},{9,8},{10,9},{11,10},{13,12},{... | collective-permute-start | bytes 1179656 | tf_op jit(solution)/shard_map/ppermute | solution.py:72
  201.4 11.1 %collective-permute-done.12 = bf16[2,3,2,128,128]{3,4,1,2,0:T(8,128)(2,1)} collective-permute-done((bf16[2,3,2,128,128]{3,4,1,2,0:T(8,128)(2,1)}, bf16[2,3,2,128,128]{3,4,1,2,0:T(8,128)(2,1)}, u32[]{:S(2)}, u32[]{:S(2)}) %collective-permute-start.12) | collective-permute-done | bytes 393248 | tf_op jit(solution)/shard_map/ppermute | solution.py:72
  (108 shorter events, 45.9 us)
Async XLA Ops:
  7.2 15.6 %copy-start.10 = (bf16[96,384]{1,0:T(8,128)(2,1)S(1)}, bf16[96,384]{1,0:T(8,128)(2,1)}, u32[]{:S(2)}) copy-start(bf16[96,384]{1,0:T(8,128)(2,1)} %param.25) | copy-start | bytes 221188
  7.2 109.1 %all-gather.2.cloned.1.call-start = ((), (), s32[]{:S(2)}) async-start(), calls=%async_computation | async-start | bytes 3538944 | tf_op jit(solution)/shard_map/all_gather | solution.py:117
  7.9 14.8 %collective-permute-start.4 = (bf16[96,384]{1,0:T(8,128)(2,1)}, bf16[96,384]{1,0:T(8,128)(2,1)S(1)}, u32[]{:S(2)}, u32[]{:S(2)}) collective-permute-start(bf16[96,384]{1,0:T(8,128)(2,1)} %param.25), channel_id=1, source_target_pairs={{0,2},{1,3},{2,0},{3,1},{4,6},{5,7},{6,4},{7,5},{8,10},{9,11},{10,... | collective-permute-start | bytes 221192 | tf_op jit(solution)/shard_map/ppermute | solution.py:15
  15.9 32.7 %collective-permute-start = (bf16[2,3,2,1,128,128]{4,5,1,3,2,0:T(8,128)(2,1)S(1)}, bf16[2,3,2,1,128,128]{4,5,1,3,2,0:T(8,128)(2,1)S(1)}, u32[]{:S(2)}, u32[]{:S(2)}) collective-permute-start(bf16[2,3,2,1,128,128]{4,5,1,3,2,0:T(8,128)(2,1)S(1)} %get-tuple-element.121), channel_id=1, source_target_pairs={{0,1},{1,2},{2,3},{4,5},{5,6},{6,7},{8,9},{9,10},{10,11},{12,13},{... | collective-permute-start | bytes 1179656 | tf_op jit(solution)/shard_map/ppermute | solution.py:87
  17.8 30.8 %collective-permute-start.1 = (bf16[2,3,2,1,128,128]{4,5,1,3,2,0:T(8,128)(2,1)S(1)}, bf16[2,3,2,1,128,128]{4,5,1,3,2,0:T(8,128)(2,1)S(1)}, u32[]{:S(2)}, u32[]{:S(2)}) collective-permute-start(bf16[2,3,2,1,128,128]{4,5,1,3,2,0:T(8,128)(2,1)S(1)} %get-tuple-element.122), channel_id=1, source_target_pairs={{1,0},{2,1},{3,2},{5,4},{6,5},{7,6},{9,8},{10,9},{11,10},{13,12},{... | collective-permute-start | bytes 1179656 | tf_op jit(solution)/shard_map/ppermute | solution.py:88
  22.8 22.4 %collective-permute-start.5 = (bf16[192,384]{1,0:T(8,128)(2,1)S(1)}, bf16[192,384]{1,0:T(8,128)(2,1)S(1)}, u32[]{:S(2)}, u32[]{:S(2)}) collective-permute-start(bf16[192,384]{1,0:T(8,128)(2,1)S(1)} %maximum_select_fusion.4), channel_id=1, source_target_pairs={{0,1},{1,0},{2,3},{3,2},{4,5},{5,4},{6,7},{7,6},{8,9},{9,8},{10,11... | collective-permute-start | bytes 442376 | tf_op jit(solution)/shard_map/ppermute | solution.py:15
  45.3 27.7 %collective-permute-start.6 = (bf16[384,384]{1,0:T(8,128)(2,1)S(1)}, bf16[384,384]{1,0:T(8,128)(2,1)S(1)}, u32[]{:S(2)}, u32[]{:S(2)}) collective-permute-start(bf16[384,384]{1,0:T(8,128)(2,1)S(1)} %maximum_select_fusion.3), channel_id=1, source_target_pairs={{0,16},{4,20},{8,24},{12,28},{16,0},{20,4},{24,8},{28,12},{1,17},{... | collective-permute-start | bytes 884744 | tf_op jit(solution)/shard_map/ppermute | solution.py:15
  50.1 36.6 %collective-permute-start.2 = (bf16[2,3,1,4,128,128]{4,5,1,3,2,0:T(8,128)(2,1)}, bf16[2,3,1,4,128,128]{4,5,1,3,2,0:T(8,128)(2,1)S(1)}, u32[]{:S(2)}, u32[]{:S(2)}) collective-permute-start(bf16[2,3,1,4,128,128]{4,5,1,3,2,0:T(8,128)(2,1)} %get-tuple-element.113), channel_id=1, source_target_pairs={{0,4},{4,8},{8,12},{12,16},{16,20},{20,24},{24,28},{1,5},{5,9},{9,... | collective-permute-start | bytes 2359304 | tf_op jit(solution)/shard_map/ppermute | solution.py:87
  51.8 36.5 %collective-permute-start.3 = (bf16[2,3,1,4,128,128]{4,5,1,3,2,0:T(8,128)(2,1)}, bf16[2,3,1,4,128,128]{4,5,1,3,2,0:T(8,128)(2,1)}, u32[]{:S(2)}, u32[]{:S(2)}) collective-permute-start(bf16[2,3,1,4,128,128]{4,5,1,3,2,0:T(8,128)(2,1)} %get-tuple-element.114), channel_id=1, source_target_pairs={{4,0},{8,4},{12,8},{16,12},{20,16},{24,20},{28,24},{5,1},{9,5},{13... | collective-permute-start | bytes 2359304 | tf_op jit(solution)/shard_map/ppermute | solution.py:88
  73.3 10.7 %collective-permute-start.7 = (bf16[768,384]{1,0:T(8,128)(2,1)S(1)}, bf16[768,384]{1,0:T(8,128)(2,1)}, u32[]{:S(2)}, u32[]{:S(2)}) collective-permute-start(bf16[768,384]{1,0:T(8,128)(2,1)S(1)} %maximum_select_fusion.2), channel_id=1, source_target_pairs={{0,8},{4,12},{8,0},{12,4},{16,24},{20,28},{24,16},{28,20},{1,9},{5... | collective-permute-start | bytes 1769480 | tf_op jit(solution)/shard_map/ppermute | solution.py:15
  86.7 26.0 %collective-permute-start.8 = (bf16[1536,384]{1,0:T(8,128)(2,1)}, bf16[1536,384]{1,0:T(8,128)(2,1)}, u32[]{:S(2)}, u32[]{:S(2)}) collective-permute-start(bf16[1536,384]{1,0:T(8,128)(2,1)} %maximum_select_fusion.1), channel_id=1, source_target_pairs={{0,4},{4,0},{8,12},{12,8},{16,20},{20,16},{24,28},{28,24},{1,5},{5... | collective-permute-start | bytes 3538952 | tf_op jit(solution)/shard_map/ppermute | solution.py:15
  92.6 7.3 %copy-start.6 = (bf16[1,3,4,4,128,128]{5,4,3,2,1,0:T(8,128)(2,1)}, bf16[1,3,4,4,128,128]{5,4,3,2,1,0:T(8,128)(2,1)S(1)}, u32[]{:S(2)}) copy-start(bf16[1,3,4,4,128,128]{5,4,3,2,1,0:T(8,128)(2,1)S(1)} %copy.67) | copy-start | bytes 4718596
  120.4 7.8 %slice-start = ((s8[6291456]{0:T(1024)(128)(4,1)}), s8[2097152]{0:T(1024)(128)(4,1)S(1)}, s32[]{:S(2)}) async-start(s8[6291456]{0:T(1024)(128)(4,1)} %bitcast.173), calls=%async_computation.1 | async-start | bytes 4194304
  121.7 6.4 %slice-start.1 = ((s8[6291456]{0:T(1024)(128)(4,1)}), s8[4194304]{0:T(1024)(128)(4,1)S(1)}, s32[]{:S(2)}) async-start(s8[6291456]{0:T(1024)(128)(4,1)} %bitcast.173), calls=%async_computation.2 | async-start | bytes 8388608
  141.5 12.8 %copy-start = (f32[3,4,4,128,128]{3,4,0,2,1:T(8,128)}, f32[3,4,4,128,128]{3,4,0,2,1:T(8,128)S(1)}, u32[]{:S(2)}) copy-start(f32[3,4,4,128,128]{3,4,0,2,1:T(8,128)S(1)} %copy.81) | copy-start | bytes 9437188
  149.6 15.8 %collective-permute-start.9 = (bf16[2,3,4,128,128]{3,4,1,2,0:T(8,128)(2,1)}, bf16[2,3,4,128,128]{3,4,1,2,0:T(8,128)(2,1)}, u32[]{:S(2)}, u32[]{:S(2)}) collective-permute-start(bf16[2,3,4,128,128]{3,4,1,2,0:T(8,128)(2,1)} %pad_maximum_fusion.2), channel_id=1, source_target_pairs={{0,4},{4,8},{8,12},{12,16},{16,20},{20,24},{24,28},{1,5},{5,9},{9,... | collective-permute-start | bytes 2359304 | tf_op jit(solution)/shard_map/ppermute | solution.py:72
  152.9 32.5 %collective-permute-start.10 = (bf16[2,3,4,128,128]{3,4,1,2,0:T(8,128)(2,1)}, bf16[2,3,4,128,128]{3,4,1,2,0:T(8,128)(2,1)}, u32[]{:S(2)}, u32[]{:S(2)}) collective-permute-start(bf16[2,3,4,128,128]{3,4,1,2,0:T(8,128)(2,1)} %pad_maximum_fusion.3), channel_id=1, source_target_pairs={{4,0},{8,4},{12,8},{16,12},{20,16},{24,20},{28,24},{5,1},{9,5},{13... | collective-permute-start | bytes 2359304 | tf_op jit(solution)/shard_map/ppermute | solution.py:72
  155.6 11.1 %slice-start.2 = ((f32[3,4,4,128,128]{3,4,0,2,1:T(8,128)}), f32[3,2,4,128,128]{3,4,0,2,1:T(8,128)S(1)}, s32[]{:S(2)}) async-start(f32[3,4,4,128,128]{3,4,0,2,1:T(8,128)} %copy-done), calls=%async_computation.3 | async-start | bytes 3145728 | tf_op jit(solution)/shard_map/slice | solution.py:98
  186.6 10.9 %slice-start.3 = ((s8[6291456]{0:T(1024)(128)(4,1)}), s8[4194304]{0:T(1024)(128)(4,1)S(1)}, s32[]{:S(2)}) async-start(s8[6291456]{0:T(1024)(128)(4,1)} %bitcast.179), calls=%async_computation.4 | async-start | bytes 8388608
  187.1 10.4 %slice-start.4 = ((s8[6291456]{0:T(1024)(128)(4,1)}), s8[2097152]{0:T(1024)(128)(4,1)S(1)}, s32[]{:S(2)}) async-start(s8[6291456]{0:T(1024)(128)(4,1)} %bitcast.179), calls=%async_computation.5 | async-start | bytes 4194304
  187.3 10.3 %copy-start.7 = (bf16[1,3,4,4,128,128]{5,4,3,2,1,0:T(8,128)(2,1)S(1)}, bf16[1,3,4,4,128,128]{5,4,3,2,1,0:T(8,128)(2,1)}, u32[]{:S(2)}) copy-start(bf16[1,3,4,4,128,128]{5,4,3,2,1,0:T(8,128)(2,1)} %copy-done.6) | copy-start | bytes 4718596
  189.0 11.2 %collective-permute-start.11 = (bf16[2,3,2,128,128]{3,4,1,2,0:T(8,128)(2,1)}, bf16[2,3,2,128,128]{3,4,1,2,0:T(8,128)(2,1)}, u32[]{:S(2)}, u32[]{:S(2)}) collective-permute-start(bf16[2,3,2,128,128]{3,4,1,2,0:T(8,128)(2,1)} %pad_maximum_fusion.5), channel_id=1, source_target_pairs={{0,1},{1,2},{2,3},{4,5},{5,6},{6,7},{8,9},{9,10},{10,11},{12,13},{... | collective-permute-start | bytes 1179656 | tf_op jit(solution)/shard_map/ppermute | solution.py:72
  193.1 19.4 %collective-permute-start.12 = (bf16[2,3,2,128,128]{3,4,1,2,0:T(8,128)(2,1)}, bf16[2,3,2,128,128]{3,4,1,2,0:T(8,128)(2,1)}, u32[]{:S(2)}, u32[]{:S(2)}) collective-permute-start(bf16[2,3,2,128,128]{3,4,1,2,0:T(8,128)(2,1)} %pad_maximum_fusion.6), channel_id=1, source_target_pairs={{1,0},{2,1},{3,2},{5,4},{6,5},{7,6},{9,8},{10,9},{11,10},{13,12},{... | collective-permute-start | bytes 1179656 | tf_op jit(solution)/shard_map/ppermute | solution.py:72
  201.4 12.3 %copy-start.5 = (f32[3,2,2,128,128]{3,4,0,1,2:T(8,128)}, f32[3,2,2,128,128]{3,4,0,1,2:T(8,128)S(1)}, u32[]{:S(2)}) copy-start(f32[3,2,2,128,128]{3,4,0,1,2:T(8,128)S(1)} %get-tuple-element.116) | copy-start | bytes 2359300
  (6 other events, 17.4 us)
Sparse Core Ops, SparseCore 0:
  9.8 32.4 all-gather.1

commit v9 on v8

--- a/solution.py
+++ b/solution.py
@@ -6,30 +6,31 @@
 HEAD = 128
 
 
-def doubling_gather(block, steps):
-    sizes = {"ha": lax.axis_size("ha"), "wa": lax.axis_size("wa")}
+def gather_rows(out_proj):
+    rows, cols = out_proj.shape
+    bits = []
+    for axis in ("ha", "wa"):
+        size = lax.axis_size(axis)
+        bits += [(axis, 1 << b) for b in reversed(range(size.bit_length() - 1))]
     index = {"ha": lax.axis_index("ha"), "wa": lax.axis_index("wa")}
-    buf = block
+    mine = [(index[axis] // bit) % 2 for axis, bit in bits]
+    zero = jnp.zeros((), jnp.int32)
+    buf = jnp.zeros([2] * len(bits) + [rows, cols], out_proj.dtype)
+    start = mine + [zero, zero]
+    buf = lax.dynamic_update_slice(buf, out_proj.reshape([1] * len(bits) + [rows, cols]), start)
+    done = []
+    steps = [b for b in bits if b[0] == "wa"] + [b for b in bits if b[0] == "ha"]
     for axis, bit in steps:
-        count = sizes[axis]
-        other = lax.ppermute(buf, axis, [(i, i ^ bit) for i in range(count)])
-        low = (index[axis] // bit) % 2 == 0
-        buf = jnp.where(low, jnp.concatenate([buf, other], 0), jnp.concatenate([other, buf], 0))
-    return buf
-
-
-def gather_rows(out_proj):
-    ha, wa = lax.axis_size("ha"), lax.axis_size("wa")
-    ha_bits = [1 << b for b in range(ha.bit_length() - 1)]
-    wa_bits = [1 << b for b in range(wa.bit_length() - 1)]
-    steps = [("wa", b) for b in reversed(wa_bits)] + [("ha", b) for b in reversed(ha_bits)]
-    buf = doubling_gather(out_proj, steps)
-    rows, cols = out_proj.shape
-    order = list(reversed(steps))
-    buf = buf.reshape([2] * len(steps) + [rows, cols])
-    natural = [("ha", b) for b in reversed(ha_bits)] + [("wa", b) for b in reversed(wa_bits)]
-    perm = [order.index(s) for s in natural] + [len(steps), len(steps) + 1]
-    return buf.transpose(perm).reshape(-1, cols)
+        k = bits.index((axis, bit))
+        sizes = [2 if n in done else 1 for n in range(len(bits))] + [rows, cols]
+        start = [zero if n in done else mine[n] for n in range(len(bits))] + [zero, zero]
+        box = lax.dynamic_slice(buf, start, sizes)
+        count = lax.axis_size(axis)
+        got = lax.ppermute(box, axis, [(i, i ^ bit) for i in range(count)])
+        start[k] = 1 - mine[k]
+        buf = lax.dynamic_update_slice(buf, got, start)
+        done.append(k)
+    return buf.reshape(-1, cols)
 
 
 def pick(length, d):

time: 227 us -> 234 us (1.031)
  waiting for transfers between devices: 92.8 us -> 74.8 us
  starting transfers between devices: 30.2 us -> 45.1 us
  local copies, waits for them, and re-layouts: 25.8 us -> 39 us
  other arithmetic: 31.8 us -> 27.8 us
    ppermute x5, waiting for transfers between devices: 55.5 us -> 40.3 us  [gather_rows(): got = lax.ppermute(box, axis, [(i, i ^ bit) for i in range(count)])]
    ppermute x2, starting transfers between devices: 3.68 us -> 12 us  [extended_2(): before = lax.ppermute(last, axis, up)]
    select_n x5 -> x0, other arithmetic: 6.25 us -> none  [doubling_gather(): jnp.where(low, jnp.concatenate([buf, other], 0), jnp.concatenate([other,...]
    ppermute x5, starting transfers between devices: 8.95 us -> 14.9 us  [gather_rows(): got = lax.ppermute(box, axis, [(i, i ^ bit) for i in range(count)])]
    dynamic_update_slice x0 -> x6, local copies, waits for them, and re-layouts: none -> 5.46 us  [the longest x5 4.55 us: gather_rows(): buf = lax.dynamic_update_slice(buf, got, start)]
    ppermute x4, starting transfers between devices: 11.4 us -> 15 us  [passed_along(): lax.ppermute(value, axis, [(source, source + steps) for source in range(f...]
    dynamic_slice x0 -> x5, local copies, waits for them, and re-layouts: none -> 3.47 us  [gather_rows(): box = lax.dynamic_slice(buf, start, sizes)]
    ppermute x2, starting transfers between devices: 6.13 us -> 3.2 us  [extended_2(): after = lax.ppermute(first, axis, down)]
  transfers between devices with their start and end apart: 14 -> 14, of which waited for: 8 -> 8; matrix products, arithmetic and copies ran while one was open for 20% -> 24% of each run, Pallas kernels for 0% -> 0%
where the time goes in v9:
time: 234 us; the launch traced here: 232 us
  waiting for transfers between devices  74.8 us (32%)
  starting transfers between devices  45.1 us (19%)
  local copies, waits for them, and re-layouts  39 us (17%)
  matrix products  30.8 us (13%)
  other arithmetic  27.8 us (12%)
  between operations  14.7 us (6%)
    ppermute x5, waiting for transfers between devices, gather_rows(): got = lax.ppermute(box, axis, [(i, i ^ bit) for i in range(count)])  40.3 us
    ppermute x4, waiting for transfers between devices, passed_along(): lax.ppermute(value, axis, [(source, source + steps) for source in range(f...  33.8 us
    ppermute x4, starting transfers between devices, passed_along(): lax.ppermute(value, axis, [(source, source + steps) for source in range(f...  15 us
    ppermute x5, starting transfers between devices, gather_rows(): got = lax.ppermute(box, axis, [(i, i ^ bit) for i in range(count)])  14.9 us
    ppermute x2, starting transfers between devices, extended_2(): before = lax.ppermute(last, axis, up)  12 us
    unnamed x39, local copies, waits for them, and re-layouts  9.91 us
    sub x1, matrix products, local(): scores = scores - jnp.max(scores, axis=-1, keepdims=True)  8.55 us
    convert_element_type x1, other arithmetic, local(): probs_lo = probs.astype(bf16)  8.49 us
  transfers between devices with their start and end apart: 14, of which 8 were waited for; matrix products, arithmetic and copies ran while one was open for 24% of the time, Pallas kernels for 0%

profile of v9, /device:TPU:64, one launch (start us, length us, event | category | flops | bytes accessed | tf_op | source)
XLA Modules:
  0.0 232.3 jit_solution(12058473326430122730)
XLA Ops:
  11.3 6.4 %collective-permute-start = (bf16[2,3,2,1,128,128]{4,5,1,3,2,0:T(8,128)(2,1)}, bf16[2,3,2,1,128,128]{4,5,1,3,2,0:T(8,128)(2,1)S(1)}, u32[]{:S(2)}, u32[]{:S(2)}) collective-permute-start(bf16[2,3,2,1,128,128]{4,5,1,3,2,0:T(8,128)(2,1)} %get-tuple-element.118), channel_id=1, source_target_pairs={{0,1},{1,2},{2,3},{4,5},{5,6},{6,7},{8,9},{9,10},{10,11},{12,13},{... | collective-permute-start | bytes 1179656 | tf_op jit(solution)/shard_map/ppermute | solution.py:88
  21.6 4.5 %collective-permute-start.4 = (bf16[1,1,1,1,1,96,384]{6,5,4,3,2,1,0:T(8,128)(2,1)}, bf16[1,1,1,1,1,96,384]{6,5,4,3,2,1,0:T(8,128)(2,1)}, u32[]{:S(2)}, u32[]{:S(2)}) collective-permute-start(bf16[1,1,1,1,1,96,384]{6,5,4,3,2,1,0:T(8,128)(2,1)} %constant_dynamic-slice_fusion.4), channel_id=1, source_target_pairs={{0,2},{1,3},{2,0},{3,1},{4,6},{5,7},{6,4},{7,5},{8,10},{9,11},{10,... | collective-permute-start | bytes 221192 | tf_op jit(solution)/shard_map/ppermute | solution.py:29
  26.1 11.8 %collective-permute-done.4 = bf16[1,1,1,1,1,96,384]{6,5,4,3,2,1,0:T(8,128)(2,1)} collective-permute-done((bf16[1,1,1,1,1,96,384]{6,5,4,3,2,1,0:T(8,128)(2,1)}, bf16[1,1,1,1,1,96,384]{6,5,4,3,2,1,0:T(8,128)(2,1)}, u32[]{:S(2)}, u32[]{:S(2)}) %collective-permute-start.4) | collective-permute-done | bytes 73760 | tf_op jit(solution)/shard_map/ppermute | solution.py:29
  39.6 6.4 %collective-permute-done.5 = bf16[1,1,1,2,1,96,384]{6,5,4,3,2,1,0:T(8,128)(2,1)} collective-permute-done((bf16[1,1,1,2,1,96,384]{6,5,4,3,2,1,0:T(8,128)(2,1)}, bf16[1,1,1,2,1,96,384]{6,5,4,3,2,1,0:T(8,128)(2,1)}, u32[]{:S(2)}, u32[]{:S(2)}) %collective-permute-start.5) | collective-permute-done | bytes 147488 | tf_op jit(solution)/shard_map/ppermute | solution.py:29
  47.0 3.3 %collective-permute-start.6 = (bf16[1,1,1,2,2,96,384]{6,5,4,3,2,1,0:T(8,128)(2,1)S(1)}, bf16[1,1,1,2,2,96,384]{6,5,4,3,2,1,0:T(8,128)(2,1)S(1)}, u32[]{:S(2)}, u32[]{:S(2)}) collective-permute-start(bf16[1,1,1,2,2,96,384]{6,5,4,3,2,1,0:T(8,128)(2,1)S(1)} %constant_dynamic-slice_fusion.2), channel_id=1, source_target_pairs={{0,16},{4,20},{8,24},{12,28},{16,0},{20,4},{24,8},{28,12},{1,17},{... | collective-permute-start | bytes 884744 | tf_op jit(solution)/shard_map/ppermute | solution.py:29
  53.0 5.6 %collective-permute-start.2 = (bf16[2,3,1,4,128,128]{4,5,1,3,2,0:T(8,128)(2,1)}, bf16[2,3,1,4,128,128]{4,5,1,3,2,0:T(8,128)(2,1)}, u32[]{:S(2)}, u32[]{:S(2)}) collective-permute-start(bf16[2,3,1,4,128,128]{4,5,1,3,2,0:T(8,128)(2,1)} %get-tuple-element.110), channel_id=1, source_target_pairs={{0,4},{4,8},{8,12},{12,16},{16,20},{20,24},{24,28},{1,5},{5,9},{9,... | collective-permute-start | bytes 2359304 | tf_op jit(solution)/shard_map/ppermute | solution.py:88
  59.9 8.3 %collective-permute-done.6 = bf16[1,1,1,2,2,96,384]{6,5,4,3,2,1,0:T(8,128)(2,1)S(1)} collective-permute-done((bf16[1,1,1,2,2,96,384]{6,5,4,3,2,1,0:T(8,128)(2,1)S(1)}, bf16[1,1,1,2,2,96,384]{6,5,4,3,2,1,0:T(8,128)(2,1)S(1)}, u32[]{:S(2)}, u32[]{:S(2)}) %collective-permute-start.6) | collective-permute-done | bytes 294944 | tf_op jit(solution)/shard_map/ppermute | solution.py:29
  70.7 13.7 %collective-permute-done.7 = bf16[2,1,1,2,2,96,384]{6,5,4,3,2,1,0:T(8,128)(2,1)} collective-permute-done((bf16[2,1,1,2,2,96,384]{6,5,4,3,2,1,0:T(8,128)(2,1)}, bf16[2,1,1,2,2,96,384]{6,5,4,3,2,1,0:T(8,128)(2,1)}, u32[]{:S(2)}, u32[]{:S(2)}) %collective-permute-start.7) | collective-permute-done | bytes 589856 | tf_op jit(solution)/shard_map/ppermute | solution.py:29
  86.8 7.2 %collective-permute-start.8 = (bf16[2,2,1,2,2,96,384]{6,5,4,3,2,1,0:T(8,128)(2,1)}, bf16[2,2,1,2,2,96,384]{6,5,4,3,2,1,0:T(8,128)(2,1)}, u32[]{:S(2)}, u32[]{:S(2)}) collective-permute-start(bf16[2,2,1,2,2,96,384]{6,5,4,3,2,1,0:T(8,128)(2,1)} %constant_dynamic-slice_fusion), channel_id=1, source_target_pairs={{0,4},{4,0},{8,12},{12,8},{16,20},{20,16},{24,28},{28,24},{1,5},{5... | collective-permute-start | bytes 3538952 | tf_op jit(solution)/shard_map/ppermute | solution.py:29
  97.9 2.7 %copy.40 = bf16[1,3,4,4,128,128]{5,4,3,2,1,0:T(8,128)(2,1)} copy(bf16[1,3,4,4,128,128]{4,5,1,3,2,0:T(8,128)(2,1)} %get-tuple-element.102) | data formatting | bytes 3145728 | tf_op jit(solution)/shard_map/slice | solution.py:151
  100.5 2.6 %copy.36 = bf16[1,3,4,4,128,128]{5,4,3,2,1,0:T(8,128)(2,1)} copy(bf16[1,3,4,4,128,128]{4,5,1,3,2,0:T(8,128)(2,1)} %get-tuple-element.103) | data formatting | bytes 3145728 | tf_op jit(solution)/shard_map/slice | solution.py:150
  103.1 8.6 %fusion.42 = (f32[3,4,128]{2,1,0:T(4,128)S(1)}, f32[3,4,128,2048]{2,3,1,0:T(8,128)}) fusion(pred[4,2048]{1,0:T(4,128)(4,1)S(1)} %bitcast.200, bf16[3,2048,128,1]{2,1,3,0:T(8,128)(2,1)} %bitcast.191, bf16[3,4,128,128]{2,3,0,1:T(8,128)(2,1)S(1)} %bitcast.186), kind=kOutput, calls=%fused_computation.92 | convolution fusion | flops 817891328 | bytes 14563328 | tf_op jit(solution)/shard_map/sub | solution.py:156
  111.7 8.5 %fusion.5 = bf16[3,4,128,2048]{2,3,1,0:T(8,128)(2,1)} fusion(f32[3,4,128,2048]{2,3,1,0:T(8,128)} %get-tuple-element.121, f32[3,4,128]{2,1,0:T(4,128)S(1)} %get-tuple-element.120), kind=kLoop, calls=%fused_computation.9 | loop fusion | flops 6291456 | bytes 18880512 | tf_op jit(solution)/shard_map/convert_element_type | solution.py:159
  121.7 4.1 %fusion.9 = bf16[512,384]{0,1:T(8,128)(2,1)} fusion(bf16[3072,384]{1,0:T(8,128)(2,1)S(1)} %bitcast.177, bf16[512,3072]{1,0:T(8,128)(2,1)} %bitcast.201), kind=kOutput, calls=%fused_computation.17 | convolution fusion | flops 1208156160 | bytes 5898240 | tf_op jit(solution)/shard_map/dot_general | solution.py:161
  127.1 6.4 %fusion.47 = f32[3,2048,128,1]{2,1,3,0:T(8,128)} fusion(bf16[3,4,128,2048]{2,3,1,0:T(8,128)(2,1)} %fusion.5, bf16[3,4,128,128]{2,3,1,0:T(8,128)(2,1)S(1)} %bitcast.188), kind=kOutput, calls=%fused_computation.93 | convolution fusion | flops 805306368 | bytes 9830400 | tf_op jit(solution)/shard_map/hqtl,hqtd->hld/dot_general | solution.py:172
  134.7 5.9 %multiply_convert_fusion = bf16[3,4,128,2048]{2,3,1,0:T(8,128)(2,1)S(1)} fusion(f32[3,4,128]{2,1,0:T(4,128)S(1)} %fusion.8, bf16[3,2048,128,1]{2,1,3,0:T(8,128)(2,1)S(1)} %bitcast.194, bf16[3,4,128,128]{2,3,1,0:T(8,128)(2,1)S(1)} %bitcast.190, f32[3,4,128,2048]{2,3,1,0:T(8,128)} %get-tuple-element.121, f32[3,4,128]{2,1,0:T(4,128)S(1)} %get-tuple-element.120), kind=kOutput, calls=%fused_computation.2 | convolution fusion | flops 821035008 | bytes 20852736 | tf_op jit(solution)/shard_map/hqtd,hld->hqtl/dot_general | solution.py:168
  140.6 3.6 %fusion.32 = f32[3,2048,128,1]{2,1,3,0:T(8,128)} fusion(bf16[3,4,128,2048]{2,3,1,0:T(8,128)(2,1)S(1)} %multiply_convert_fusion, bf16[3,4,128,128]{2,3,0,1:T(8,128)(2,1)S(1)} %bitcast.187), kind=kOutput, calls=%fused_computation.58 | convolution fusion | flops 805306368 | bytes 9830400 | tf_op jit(solution)/shard_map/hqtl,hqtd->hld/dot_general | solution.py:171
  148.0 3.6 %copy.53 = f32[3,4,4,128,128]{3,4,0,2,1:T(8,128)} copy(f32[3,4,4,128,128]{4,3,2,1,0:T(8,128)} %bitcast.174) | data formatting | bytes 6291456 | tf_op jit(solution)/shard_map/reshape | solution.py:176
  154.8 2.8 %collective-permute-start.9 = (bf16[2,3,4,128,128]{3,4,1,2,0:T(8,128)(2,1)}, bf16[2,3,4,128,128]{3,4,1,2,0:T(8,128)(2,1)}, u32[]{:S(2)}, u32[]{:S(2)}) collective-permute-start(bf16[2,3,4,128,128]{3,4,1,2,0:T(8,128)(2,1)} %pad_maximum_fusion.2), channel_id=1, source_target_pairs={{0,4},{4,8},{8,12},{12,16},{16,20},{20,24},{24,28},{1,5},{5,9},{9,... | collective-permute-start | bytes 2359304 | tf_op jit(solution)/shard_map/ppermute | solution.py:73
  163.2 4.3 %collective-permute-done.9 = bf16[2,3,4,128,128]{3,4,1,2,0:T(8,128)(2,1)} collective-permute-done((bf16[2,3,4,128,128]{3,4,1,2,0:T(8,128)(2,1)}, bf16[2,3,4,128,128]{3,4,1,2,0:T(8,128)(2,1)}, u32[]{:S(2)}, u32[]{:S(2)}) %collective-permute-start.9) | collective-permute-done | bytes 786464 | tf_op jit(solution)/shard_map/ppermute | solution.py:73
  171.4 15.6 %collective-permute-done.10 = bf16[2,3,4,128,128]{3,4,1,2,0:T(8,128)(2,1)} collective-permute-done((bf16[2,3,4,128,128]{3,4,1,2,0:T(8,128)(2,1)}, bf16[2,3,4,128,128]{3,4,1,2,0:T(8,128)(2,1)}, u32[]{:S(2)}, u32[]{:S(2)}) %collective-permute-start.10) | collective-permute-done | bytes 786464 | tf_op jit(solution)/shard_map/ppermute | solution.py:73
  190.7 8.8 %collective-permute-start.11 = (bf16[2,3,2,128,128]{3,4,1,2,0:T(8,128)(2,1)}, bf16[2,3,2,128,128]{3,4,1,2,0:T(8,128)(2,1)}, u32[]{:S(2)}, u32[]{:S(2)}) collective-permute-start(bf16[2,3,2,128,128]{3,4,1,2,0:T(8,128)(2,1)} %pad_maximum_fusion.5), channel_id=1, source_target_pairs={{0,1},{1,2},{2,3},{4,5},{5,6},{6,7},{8,9},{9,10},{10,11},{12,13},{... | collective-permute-start | bytes 1179656 | tf_op jit(solution)/shard_map/ppermute | solution.py:73
  205.0 6.1 %collective-permute-done.11 = bf16[2,3,2,128,128]{3,4,1,2,0:T(8,128)(2,1)} collective-permute-done((bf16[2,3,2,128,128]{3,4,1,2,0:T(8,128)(2,1)}, bf16[2,3,2,128,128]{3,4,1,2,0:T(8,128)(2,1)}, u32[]{:S(2)}, u32[]{:S(2)}) %collective-permute-start.11) | collective-permute-done | bytes 393248 | tf_op jit(solution)/shard_map/ppermute | solution.py:73
  212.3 7.8 %collective-permute-done.12 = bf16[2,3,2,128,128]{3,4,1,2,0:T(8,128)(2,1)} collective-permute-done((bf16[2,3,2,128,128]{3,4,1,2,0:T(8,128)(2,1)}, bf16[2,3,2,128,128]{3,4,1,2,0:T(8,128)(2,1)}, u32[]{:S(2)}, u32[]{:S(2)}) %collective-permute-start.12) | collective-permute-done | bytes 393248 | tf_op jit(solution)/shard_map/ppermute | solution.py:73
  (114 shorter events, 59.1 us)
Async XLA Ops:
  7.2 114.5 %all-gather.2.cloned.1.call-start = ((), (), s32[]{:S(2)}) async-start(), calls=%async_computation | async-start | bytes 3538944 | tf_op jit(solution)/shard_map/all_gather | solution.py:118
  11.3 39.0 %collective-permute-start = (bf16[2,3,2,1,128,128]{4,5,1,3,2,0:T(8,128)(2,1)}, bf16[2,3,2,1,128,128]{4,5,1,3,2,0:T(8,128)(2,1)S(1)}, u32[]{:S(2)}, u32[]{:S(2)}) collective-permute-start(bf16[2,3,2,1,128,128]{4,5,1,3,2,0:T(8,128)(2,1)} %get-tuple-element.118), channel_id=1, source_target_pairs={{0,1},{1,2},{2,3},{4,5},{5,6},{6,7},{8,9},{9,10},{10,11},{12,13},{... | collective-permute-start | bytes 1179656 | tf_op jit(solution)/shard_map/ppermute | solution.py:88
  17.7 32.6 %collective-permute-start.1 = (bf16[2,3,2,1,128,128]{4,5,1,3,2,0:T(8,128)(2,1)}, bf16[2,3,2,1,128,128]{4,5,1,3,2,0:T(8,128)(2,1)}, u32[]{:S(2)}, u32[]{:S(2)}) collective-permute-start(bf16[2,3,2,1,128,128]{4,5,1,3,2,0:T(8,128)(2,1)} %get-tuple-element.119), channel_id=1, source_target_pairs={{1,0},{2,1},{3,2},{5,4},{6,5},{7,6},{9,8},{10,9},{11,10},{13,12},{... | collective-permute-start | bytes 1179656 | tf_op jit(solution)/shard_map/ppermute | solution.py:89
  21.6 16.3 %collective-permute-start.4 = (bf16[1,1,1,1,1,96,384]{6,5,4,3,2,1,0:T(8,128)(2,1)}, bf16[1,1,1,1,1,96,384]{6,5,4,3,2,1,0:T(8,128)(2,1)}, u32[]{:S(2)}, u32[]{:S(2)}) collective-permute-start(bf16[1,1,1,1,1,96,384]{6,5,4,3,2,1,0:T(8,128)(2,1)} %constant_dynamic-slice_fusion.4), channel_id=1, source_target_pairs={{0,2},{1,3},{2,0},{3,1},{4,6},{5,7},{6,4},{7,5},{8,10},{9,11},{10,... | collective-permute-start | bytes 221192 | tf_op jit(solution)/shard_map/ppermute | solution.py:29
  39.5 6.5 %collective-permute-start.5 = (bf16[1,1,1,2,1,96,384]{6,5,4,3,2,1,0:T(8,128)(2,1)}, bf16[1,1,1,2,1,96,384]{6,5,4,3,2,1,0:T(8,128)(2,1)}, u32[]{:S(2)}, u32[]{:S(2)}) collective-permute-start(bf16[1,1,1,2,1,96,384]{6,5,4,3,2,1,0:T(8,128)(2,1)} %constant_dynamic-slice_fusion.3), channel_id=1, source_target_pairs={{0,1},{1,0},{2,3},{3,2},{4,5},{5,4},{6,7},{7,6},{8,9},{9,8},{10,11... | collective-permute-start | bytes 442376 | tf_op jit(solution)/shard_map/ppermute | solution.py:29
  47.0 21.2 %collective-permute-start.6 = (bf16[1,1,1,2,2,96,384]{6,5,4,3,2,1,0:T(8,128)(2,1)S(1)}, bf16[1,1,1,2,2,96,384]{6,5,4,3,2,1,0:T(8,128)(2,1)S(1)}, u32[]{:S(2)}, u32[]{:S(2)}) collective-permute-start(bf16[1,1,1,2,2,96,384]{6,5,4,3,2,1,0:T(8,128)(2,1)S(1)} %constant_dynamic-slice_fusion.2), channel_id=1, source_target_pairs={{0,16},{4,20},{8,24},{12,28},{16,0},{20,4},{24,8},{28,12},{1,17},{... | collective-permute-start | bytes 884744 | tf_op jit(solution)/shard_map/ppermute | solution.py:29
  53.0 41.0 %collective-permute-start.2 = (bf16[2,3,1,4,128,128]{4,5,1,3,2,0:T(8,128)(2,1)}, bf16[2,3,1,4,128,128]{4,5,1,3,2,0:T(8,128)(2,1)}, u32[]{:S(2)}, u32[]{:S(2)}) collective-permute-start(bf16[2,3,1,4,128,128]{4,5,1,3,2,0:T(8,128)(2,1)} %get-tuple-element.110), channel_id=1, source_target_pairs={{0,4},{4,8},{8,12},{12,16},{16,20},{20,24},{24,28},{1,5},{5,9},{9,... | collective-permute-start | bytes 2359304 | tf_op jit(solution)/shard_map/ppermute | solution.py:88
  58.6 35.4 %collective-permute-start.3 = (bf16[2,3,1,4,128,128]{4,5,1,3,2,0:T(8,128)(2,1)}, bf16[2,3,1,4,128,128]{4,5,1,3,2,0:T(8,128)(2,1)}, u32[]{:S(2)}, u32[]{:S(2)}) collective-permute-start(bf16[2,3,1,4,128,128]{4,5,1,3,2,0:T(8,128)(2,1)} %get-tuple-element.111), channel_id=1, source_target_pairs={{4,0},{8,4},{12,8},{16,12},{20,16},{24,20},{28,24},{5,1},{9,5},{13... | collective-permute-start | bytes 2359304 | tf_op jit(solution)/shard_map/ppermute | solution.py:89
  69.1 15.3 %collective-permute-start.7 = (bf16[2,1,1,2,2,96,384]{6,5,4,3,2,1,0:T(8,128)(2,1)}, bf16[2,1,1,2,2,96,384]{6,5,4,3,2,1,0:T(8,128)(2,1)}, u32[]{:S(2)}, u32[]{:S(2)}) collective-permute-start(bf16[2,1,1,2,2,96,384]{6,5,4,3,2,1,0:T(8,128)(2,1)} %constant_dynamic-slice_fusion.1), channel_id=1, source_target_pairs={{0,8},{4,12},{8,0},{12,4},{16,24},{20,28},{24,16},{28,20},{1,9},{5... | collective-permute-start | bytes 1769480 | tf_op jit(solution)/shard_map/ppermute | solution.py:29
  70.7 23.3 %copy-start.7 = (bf16[2,3,2,1,128,128]{4,5,1,3,2,0:T(8,128)(2,1)S(1)}, bf16[2,3,2,1,128,128]{4,5,1,3,2,0:T(8,128)(2,1)}, u32[]{:S(2)}) copy-start(bf16[2,3,2,1,128,128]{4,5,1,3,2,0:T(8,128)(2,1)} %copy-done.6) | copy-start | bytes 1179652
  86.8 33.3 %collective-permute-start.8 = (bf16[2,2,1,2,2,96,384]{6,5,4,3,2,1,0:T(8,128)(2,1)}, bf16[2,2,1,2,2,96,384]{6,5,4,3,2,1,0:T(8,128)(2,1)}, u32[]{:S(2)}, u32[]{:S(2)}) collective-permute-start(bf16[2,2,1,2,2,96,384]{6,5,4,3,2,1,0:T(8,128)(2,1)} %constant_dynamic-slice_fusion), channel_id=1, source_target_pairs={{0,4},{4,0},{8,12},{12,8},{16,20},{20,16},{24,28},{28,24},{1,5},{5... | collective-permute-start | bytes 3538952 | tf_op jit(solution)/shard_map/ppermute | solution.py:29
  125.8 7.8 %slice-start = ((s8[6291456]{0:T(1024)(128)(4,1)}), s8[2097152]{0:T(1024)(128)(4,1)S(1)}, s32[]{:S(2)}) async-start(s8[6291456]{0:T(1024)(128)(4,1)} %bitcast.172), calls=%async_computation.1 | async-start | bytes 4194304
  127.1 6.4 %slice-start.1 = ((s8[6291456]{0:T(1024)(128)(4,1)}), s8[4194304]{0:T(1024)(128)(4,1)S(1)}, s32[]{:S(2)}) async-start(s8[6291456]{0:T(1024)(128)(4,1)} %bitcast.172), calls=%async_computation.2 | async-start | bytes 8388608
  127.1 6.4 %copy-start.9 = (bf16[1,3,4,4,128,128]{5,4,3,2,1,0:T(8,128)(2,1)S(1)}, bf16[1,3,4,4,128,128]{5,4,3,2,1,0:T(8,128)(2,1)}, u32[]{:S(2)}) copy-start(bf16[1,3,4,4,128,128]{5,4,3,2,1,0:T(8,128)(2,1)} %copy.40) | copy-start | bytes 4718596
  146.6 13.3 %copy-start = (f32[3,4,4,128,128]{3,4,0,2,1:T(8,128)}, f32[3,4,4,128,128]{3,4,0,2,1:T(8,128)S(1)}, u32[]{:S(2)}) copy-start(f32[3,4,4,128,128]{3,4,0,2,1:T(8,128)S(1)} %copy.49) | copy-start | bytes 9437188
  154.8 12.7 %collective-permute-start.9 = (bf16[2,3,4,128,128]{3,4,1,2,0:T(8,128)(2,1)}, bf16[2,3,4,128,128]{3,4,1,2,0:T(8,128)(2,1)}, u32[]{:S(2)}, u32[]{:S(2)}) collective-permute-start(bf16[2,3,4,128,128]{3,4,1,2,0:T(8,128)(2,1)} %pad_maximum_fusion.2), channel_id=1, source_target_pairs={{0,4},{4,8},{8,12},{12,16},{16,20},{20,24},{24,28},{1,5},{5,9},{9,... | collective-permute-start | bytes 2359304 | tf_op jit(solution)/shard_map/ppermute | solution.py:73
  158.5 28.5 %collective-permute-start.10 = (bf16[2,3,4,128,128]{3,4,1,2,0:T(8,128)(2,1)}, bf16[2,3,4,128,128]{3,4,1,2,0:T(8,128)(2,1)}, u32[]{:S(2)}, u32[]{:S(2)}) collective-permute-start(bf16[2,3,4,128,128]{3,4,1,2,0:T(8,128)(2,1)} %pad_maximum_fusion.3), channel_id=1, source_target_pairs={{4,0},{8,4},{12,8},{16,12},{20,16},{24,20},{28,24},{5,1},{9,5},{13... | collective-permute-start | bytes 2359304 | tf_op jit(solution)/shard_map/ppermute | solution.py:73
  161.2 7.6 %slice-start.2 = ((f32[3,4,4,128,128]{3,4,0,2,1:T(8,128)}), f32[3,2,4,128,128]{3,4,0,2,1:T(8,128)S(1)}, s32[]{:S(2)}) async-start(f32[3,4,4,128,128]{3,4,0,2,1:T(8,128)} %copy-done), calls=%async_computation.3 | async-start | bytes 3145728 | tf_op jit(solution)/shard_map/slice | solution.py:99
  188.3 14.0 %slice-start.3 = ((s8[6291456]{0:T(1024)(128)(4,1)}), s8[4194304]{0:T(1024)(128)(4,1)S(1)}, s32[]{:S(2)}) async-start(s8[6291456]{0:T(1024)(128)(4,1)} %bitcast.178), calls=%async_computation.4 | async-start | bytes 8388608
  188.8 13.5 %slice-start.4 = ((s8[6291456]{0:T(1024)(128)(4,1)}), s8[2097152]{0:T(1024)(128)(4,1)S(1)}, s32[]{:S(2)}) async-start(s8[6291456]{0:T(1024)(128)(4,1)} %bitcast.178), calls=%async_computation.5 | async-start | bytes 4194304
  188.9 13.4 %copy-start.8 = (bf16[1,3,4,4,128,128]{5,4,3,2,1,0:T(8,128)(2,1)S(1)}, bf16[1,3,4,4,128,128]{5,4,3,2,1,0:T(8,128)(2,1)}, u32[]{:S(2)}) copy-start(bf16[1,3,4,4,128,128]{5,4,3,2,1,0:T(8,128)(2,1)} %copy.36) | copy-start | bytes 4718596
  190.7 20.4 %collective-permute-start.11 = (bf16[2,3,2,128,128]{3,4,1,2,0:T(8,128)(2,1)}, bf16[2,3,2,128,128]{3,4,1,2,0:T(8,128)(2,1)}, u32[]{:S(2)}, u32[]{:S(2)}) collective-permute-start(bf16[2,3,2,128,128]{3,4,1,2,0:T(8,128)(2,1)} %pad_maximum_fusion.5), channel_id=1, source_target_pairs={{0,1},{1,2},{2,3},{4,5},{5,6},{6,7},{8,9},{9,10},{10,11},{12,13},{... | collective-permute-start | bytes 1179656 | tf_op jit(solution)/shard_map/ppermute | solution.py:73
  200.4 19.8 %collective-permute-start.12 = (bf16[2,3,2,128,128]{3,4,1,2,0:T(8,128)(2,1)}, bf16[2,3,2,128,128]{3,4,1,2,0:T(8,128)(2,1)}, u32[]{:S(2)}, u32[]{:S(2)}) collective-permute-start(bf16[2,3,2,128,128]{3,4,1,2,0:T(8,128)(2,1)} %pad_maximum_fusion.6), channel_id=1, source_target_pairs={{1,0},{2,1},{3,2},{5,4},{6,5},{7,6},{9,8},{10,9},{11,10},{13,12},{... | collective-permute-start | bytes 1179656 | tf_op jit(solution)/shard_map/ppermute | solution.py:73
  212.3 9.1 %copy-start.5 = (f32[3,2,2,128,128]{3,4,0,1,2:T(8,128)}, f32[3,2,2,128,128]{3,4,0,1,2:T(8,128)S(1)}, u32[]{:S(2)}) copy-start(f32[3,2,2,128,128]{3,4,0,1,2:T(8,128)S(1)} %get-tuple-element.113) | copy-start | bytes 2359300
  (6 other events, 13.7 us)
Sparse Core Ops, SparseCore 0:
  9.8 32.4 all-gather.1

commit v10 on v8

--- a/solution.py
+++ b/solution.py
@@ -115,7 +115,6 @@
     heads = columns // HEAD
     f32, bf16 = jnp.float32, jnp.bfloat16
     whole = lax.all_gather(grad_out, "tp", axis=4, tiled=True)
-    weight = gather_rows(out_proj)
 
     def head_major(array):
         split = array.reshape(frames * tile_rows, tile_cols, tile_len, heads, HEAD)
@@ -125,6 +124,8 @@
         return jnp.transpose(array, (1, 2, 3, 0, 4)).reshape(queries.shape)
 
     ext = extended_2(jnp.stack([head_major(keys), head_major(values)]), (("wa", 3), ("ha", 2)), 1)
+    ext, out_proj = lax.optimization_barrier((ext, out_proj))
+    weight = gather_rows(out_proj)
     ext_r, ext_c = tile_rows + 2, tile_cols + 2
     row_base = lax.axis_index("ha") * tile_rows
     col_base = lax.axis_index("wa") * tile_cols

time: 227 us -> 259 us (1.14)
  the two profiles are of different devices: /device:TPU:64 before, /device:TPU:54 now
where the time goes in v10:
time: 259 us; the launch traced here: 258 us
  waiting for transfers between devices  108 us (42%)
  starting transfers between devices  45.5 us (18%)
  other arithmetic  32.1 us (12%)
  matrix products  29.5 us (11%)
  local copies, waits for them, and re-layouts  28.6 us (11%)
  between operations  14.7 us (6%)
    ppermute x4, waiting for transfers between devices, passed_along(): lax.ppermute(value, axis, [(source, source + steps) for source in range(f...  34.8 us
    ppermute x2, waiting for transfers between devices, extended_2(): before = lax.ppermute(last, axis, up)  30.8 us
    ppermute x5, waiting for transfers between devices, doubling_gather(): other = lax.ppermute(buf, axis, [(i, i ^ bit) for i in range(count)])  26.6 us
    ppermute x4, starting transfers between devices, passed_along(): lax.ppermute(value, axis, [(source, source + steps) for source in range(f...  16.4 us
    ppermute x2, waiting for transfers between devices, extended_2(): after = lax.ppermute(first, axis, down)  15.5 us
    ppermute x2, starting transfers between devices, extended_2(): before = lax.ppermute(last, axis, up)  15.1 us
    unnamed x47, local copies, waits for them, and re-layouts  11.4 us
    ppermute x5, starting transfers between devices, doubling_gather(): other = lax.ppermute(buf, axis, [(i, i ^ bit) for i in range(count)])  10.8 us
  transfers between devices with their start and end apart: 14, of which 12 were waited for; matrix products, arithmetic and copies ran while one was open for 17% of the time, Pallas kernels for 0%

profile of v10, /device:TPU:54, one launch (start us, length us, event | category | flops | bytes accessed | tf_op | source)
XLA Modules:
  0.0 258.2 jit_solution(18259987673733662899)
XLA Ops:
  9.7 5.2 %collective-permute-start = (bf16[2,3,2,1,128,128]{4,5,1,3,2,0:T(8,128)(2,1)S(1)}, bf16[2,3,2,1,128,128]{4,5,1,3,2,0:T(8,128)(2,1)S(1)}, u32[]{:S(2)}, u32[]{:S(2)}) collective-permute-start(bf16[2,3,2,1,128,128]{4,5,1,3,2,0:T(8,128)(2,1)S(1)} %get-tuple-element.125), channel_id=1, source_target_pairs={{0,1},{1,2},{2,3},{4,5},{5,6},{6,7},{8,9},{9,10},{10,11},{12,13},{... | collective-permute-start | bytes 1179656 | tf_op jit(solution)/shard_map/ppermute | solution.py:87
  16.3 15.0 %collective-permute-done = bf16[2,3,2,1,128,128]{4,5,1,3,2,0:T(8,128)(2,1)S(1)} collective-permute-done((bf16[2,3,2,1,128,128]{4,5,1,3,2,0:T(8,128)(2,1)S(1)}, bf16[2,3,2,1,128,128]{4,5,1,3,2,0:T(8,128)(2,1)S(1)}, u32[]{:S(2)}, u32[]{:S(2)}) %collective-permute-start) | collective-permute-done | bytes 393248 | tf_op jit(solution)/shard_map/ppermute | solution.py:87
  32.2 9.9 %collective-permute-start.2 = (bf16[2,3,1,4,128,128]{4,5,1,3,2,0:T(8,128)(2,1)S(1)}, bf16[2,3,1,4,128,128]{4,5,1,3,2,0:T(8,128)(2,1)S(1)}, u32[]{:S(2)}, u32[]{:S(2)}) collective-permute-start(bf16[2,3,1,4,128,128]{4,5,1,3,2,0:T(8,128)(2,1)S(1)} %get-tuple-element.117), channel_id=1, source_target_pairs={{0,4},{4,8},{8,12},{12,16},{16,20},{20,24},{24,28},{1,5},{5,9},{9,... | collective-permute-start | bytes 2359304 | tf_op jit(solution)/shard_map/ppermute | solution.py:87
  44.2 15.8 %collective-permute-done.2 = bf16[2,3,1,4,128,128]{4,5,1,3,2,0:T(8,128)(2,1)S(1)} collective-permute-done((bf16[2,3,1,4,128,128]{4,5,1,3,2,0:T(8,128)(2,1)S(1)}, bf16[2,3,1,4,128,128]{4,5,1,3,2,0:T(8,128)(2,1)S(1)}, u32[]{:S(2)}, u32[]{:S(2)}) %collective-permute-start.2) | collective-permute-done | bytes 786464 | tf_op jit(solution)/shard_map/ppermute | solution.py:87
  60.9 15.5 %collective-permute-done.3 = bf16[2,3,1,4,128,128]{4,5,1,3,2,0:T(8,128)(2,1)} collective-permute-done((bf16[2,3,1,4,128,128]{4,5,1,3,2,0:T(8,128)(2,1)S(1)}, bf16[2,3,1,4,128,128]{4,5,1,3,2,0:T(8,128)(2,1)}, u32[]{:S(2)}, u32[]{:S(2)}) %collective-permute-start.3) | collective-permute-done | bytes 786464 | tf_op jit(solution)/shard_map/ppermute | solution.py:88
  78.4 3.7 %collective-permute-start.4 = (bf16[96,384]{1,0:T(8,128)(2,1)}, bf16[96,384]{1,0:T(8,128)(2,1)S(1)}, u32[]{:S(2)}, u32[]{:S(2)}) collective-permute-start(bf16[96,384]{1,0:T(8,128)(2,1)} %param.25), channel_id=1, source_target_pairs={{0,2},{1,3},{2,0},{3,1},{4,6},{5,7},{6,4},{7,5},{8,10},{9,11},{10,... | collective-permute-start | bytes 221192 | tf_op jit(solution)/shard_map/ppermute | solution.py:15
  82.3 4.7 %collective-permute-done.4 = bf16[96,384]{1,0:T(8,128)(2,1)S(1)} collective-permute-done((bf16[96,384]{1,0:T(8,128)(2,1)}, bf16[96,384]{1,0:T(8,128)(2,1)S(1)}, u32[]{:S(2)}, u32[]{:S(2)}) %collective-permute-start.4) | collective-permute-done | bytes 73760 | tf_op jit(solution)/shard_map/ppermute | solution.py:15
  88.7 5.1 %collective-permute-start.5 = (bf16[192,384]{1,0:T(8,128)(2,1)}, bf16[192,384]{1,0:T(8,128)(2,1)}, u32[]{:S(2)}, u32[]{:S(2)}) collective-permute-start(bf16[192,384]{1,0:T(8,128)(2,1)} %maximum_select_fusion.4), channel_id=1, source_target_pairs={{0,1},{1,0},{2,3},{3,2},{4,5},{5,4},{6,7},{7,6},{8,9},{9,8},{10,11... | collective-permute-start | bytes 442376 | tf_op jit(solution)/shard_map/ppermute | solution.py:15
  95.1 2.8 %collective-permute-done.5 = bf16[192,384]{1,0:T(8,128)(2,1)} collective-permute-done((bf16[192,384]{1,0:T(8,128)(2,1)}, bf16[192,384]{1,0:T(8,128)(2,1)}, u32[]{:S(2)}, u32[]{:S(2)}) %collective-permute-start.5) | collective-permute-done | bytes 147488 | tf_op jit(solution)/shard_map/ppermute | solution.py:15
  110.0 7.2 %fusion.42 = (f32[3,4,128]{2,1,0:T(4,128)S(1)}, f32[3,4,128,2048]{2,3,1,0:T(8,128)}) fusion(pred[4,2048]{1,0:T(4,128)(4,1)S(1)} %bitcast.202, bf16[3,2048,128,1]{2,1,3,0:T(8,128)(2,1)S(1)} %bitcast.193, bf16[3,4,128,128]{2,3,0,1:T(8,128)(2,1)S(1)} %bitcast.188), kind=kOutput, calls=%fused_computation.86 | convolution fusion | flops 817891328 | bytes 14563328 | tf_op jit(solution)/shard_map/sub | solution.py:156
  117.2 3.6 %collective-permute-done.7 = bf16[768,384]{1,0:T(8,128)(2,1)S(1)} collective-permute-done((bf16[768,384]{1,0:T(8,128)(2,1)S(1)}, bf16[768,384]{1,0:T(8,128)(2,1)S(1)}, u32[]{:S(2)}, u32[]{:S(2)}) %collective-permute-start.7) | collective-permute-done | bytes 589856 | tf_op jit(solution)/shard_map/ppermute | solution.py:15
  122.9 8.5 %fusion.5 = bf16[3,4,128,2048]{2,3,1,0:T(8,128)(2,1)} fusion(f32[3,4,128,2048]{2,3,1,0:T(8,128)} %get-tuple-element.128, f32[3,4,128]{2,1,0:T(4,128)S(1)} %get-tuple-element.127), kind=kLoop, calls=%fused_computation.9 | loop fusion | flops 6291456 | bytes 18880512 | tf_op jit(solution)/shard_map/convert_element_type | solution.py:159
  131.4 12.8 %collective-permute-done.8 = bf16[1536,384]{1,0:T(8,128)(2,1)S(1)} collective-permute-done((bf16[1536,384]{1,0:T(8,128)(2,1)S(1)}, bf16[1536,384]{1,0:T(8,128)(2,1)S(1)}, u32[]{:S(2)}, u32[]{:S(2)}) %collective-permute-start.8) | collective-permute-done | bytes 1179680 | tf_op jit(solution)/shard_map/ppermute | solution.py:15
  145.1 4.1 %fusion.9 = bf16[512,384]{0,1:T(8,128)(2,1)} fusion(bf16[3072,384]{1,0:T(8,128)(2,1)S(1)} %bitcast.187, bf16[512,3072]{1,0:T(8,128)(2,1)} %bitcast.203), kind=kOutput, calls=%fused_computation.18 | convolution fusion | flops 1208156160 | bytes 5898240 | tf_op jit(solution)/shard_map/dot_general | solution.py:161
  150.5 6.4 %fusion.47 = f32[3,2048,128,1]{2,1,3,0:T(8,128)} fusion(bf16[3,4,128,2048]{2,3,1,0:T(8,128)(2,1)} %fusion.5, bf16[3,4,128,128]{2,3,1,0:T(8,128)(2,1)S(1)} %bitcast.190), kind=kOutput, calls=%fused_computation.87 | convolution fusion | flops 805306368 | bytes 9830400 | tf_op jit(solution)/shard_map/hqtl,hqtd->hld/dot_general | solution.py:172
  158.1 5.9 %multiply_convert_fusion = bf16[3,4,128,2048]{2,3,1,0:T(8,128)(2,1)S(1)} fusion(f32[3,4,128]{2,1,0:T(4,128)S(1)} %fusion.8, bf16[3,2048,128,1]{2,1,3,0:T(8,128)(2,1)S(1)} %bitcast.196, bf16[3,4,128,128]{2,3,1,0:T(8,128)(2,1)S(1)} %bitcast.192, f32[3,4,128,2048]{2,3,1,0:T(8,128)} %get-tuple-element.128, f32[3,4,128]{2,1,0:T(4,128)S(1)} %get-tuple-element.127), kind=kOutput, calls=%fused_computation.2 | convolution fusion | flops 821035008 | bytes 20852736 | tf_op jit(solution)/shard_map/hqtd,hld->hqtl/dot_general | solution.py:168
  164.0 3.6 %fusion.32 = f32[3,2048,128,1]{2,1,3,0:T(8,128)} fusion(bf16[3,4,128,2048]{2,3,1,0:T(8,128)(2,1)S(1)} %multiply_convert_fusion, bf16[3,4,128,128]{2,3,0,1:T(8,128)(2,1)S(1)} %bitcast.189), kind=kOutput, calls=%fused_computation.61 | convolution fusion | flops 805306368 | bytes 9830400 | tf_op jit(solution)/shard_map/hqtl,hqtd->hld/dot_general | solution.py:171
  171.4 3.6 %copy.85 = f32[3,4,4,128,128]{3,4,0,2,1:T(8,128)} copy(f32[3,4,4,128,128]{4,3,2,1,0:T(8,128)} %bitcast.175) | data formatting | bytes 6291456 | tf_op jit(solution)/shard_map/reshape | solution.py:176
  178.2 3.3 %collective-permute-start.9 = (bf16[2,3,4,128,128]{3,4,1,2,0:T(8,128)(2,1)}, bf16[2,3,4,128,128]{3,4,1,2,0:T(8,128)(2,1)}, u32[]{:S(2)}, u32[]{:S(2)}) collective-permute-start(bf16[2,3,4,128,128]{3,4,1,2,0:T(8,128)(2,1)} %pad_maximum_fusion.2), channel_id=1, source_target_pairs={{0,4},{4,8},{8,12},{12,16},{16,20},{20,24},{24,28},{1,5},{5,9},{9,... | collective-permute-start | bytes 2359304 | tf_op jit(solution)/shard_map/ppermute | solution.py:72
  182.5 2.8 %collective-permute-start.10 = (bf16[2,3,4,128,128]{3,4,1,2,0:T(8,128)(2,1)}, bf16[2,3,4,128,128]{3,4,1,2,0:T(8,128)(2,1)}, u32[]{:S(2)}, u32[]{:S(2)}) collective-permute-start(bf16[2,3,4,128,128]{3,4,1,2,0:T(8,128)(2,1)} %pad_maximum_fusion.3), channel_id=1, source_target_pairs={{4,0},{8,4},{12,8},{16,12},{20,16},{24,20},{28,24},{5,1},{9,5},{13... | collective-permute-start | bytes 2359304 | tf_op jit(solution)/shard_map/ppermute | solution.py:72
  188.6 12.2 %collective-permute-done.9 = bf16[2,3,4,128,128]{3,4,1,2,0:T(8,128)(2,1)} collective-permute-done((bf16[2,3,4,128,128]{3,4,1,2,0:T(8,128)(2,1)}, bf16[2,3,4,128,128]{3,4,1,2,0:T(8,128)(2,1)}, u32[]{:S(2)}, u32[]{:S(2)}) %collective-permute-start.9) | collective-permute-done | bytes 786464 | tf_op jit(solution)/shard_map/ppermute | solution.py:72
  204.7 6.1 %collective-permute-done.10 = bf16[2,3,4,128,128]{3,4,1,2,0:T(8,128)(2,1)} collective-permute-done((bf16[2,3,4,128,128]{3,4,1,2,0:T(8,128)(2,1)}, bf16[2,3,4,128,128]{3,4,1,2,0:T(8,128)(2,1)}, u32[]{:S(2)}, u32[]{:S(2)}) %collective-permute-start.10) | collective-permute-done | bytes 786464 | tf_op jit(solution)/shard_map/ppermute | solution.py:72
  214.6 9.0 %collective-permute-start.11 = (bf16[2,3,2,128,128]{3,4,1,2,0:T(8,128)(2,1)}, bf16[2,3,2,128,128]{3,4,1,2,0:T(8,128)(2,1)}, u32[]{:S(2)}, u32[]{:S(2)}) collective-permute-start(bf16[2,3,2,128,128]{3,4,1,2,0:T(8,128)(2,1)} %pad_maximum_fusion.5), channel_id=1, source_target_pairs={{0,1},{1,2},{2,3},{4,5},{5,6},{6,7},{8,9},{9,10},{10,11},{12,13},{... | collective-permute-start | bytes 1179656 | tf_op jit(solution)/shard_map/ppermute | solution.py:72
  231.3 14.7 %collective-permute-done.12 = bf16[2,3,2,128,128]{3,4,1,2,0:T(8,128)(2,1)} collective-permute-done((bf16[2,3,2,128,128]{3,4,1,2,0:T(8,128)(2,1)}, bf16[2,3,2,128,128]{3,4,1,2,0:T(8,128)(2,1)}, u32[]{:S(2)}, u32[]{:S(2)}) %collective-permute-start.12) | collective-permute-done | bytes 393248 | tf_op jit(solution)/shard_map/ppermute | solution.py:72
  (116 shorter events, 62.0 us)
Async XLA Ops:
  7.2 137.9 %all-gather.2.cloned.1.call-start = ((), (), s32[]{:S(2)}) async-start(), calls=%async_computation | async-start | bytes 3538944 | tf_op jit(solution)/shard_map/all_gather | solution.py:117
  9.7 21.9 %copy-start.5 = (bf16[1,2,2,128,384]{3,4,2,1,0:T(8,128)(2,1)}, bf16[1,2,2,128,384]{3,4,2,1,0:T(8,128)(2,1)S(1)}, u32[]{:S(2)}) copy-start(bf16[1,2,2,128,384]{3,4,2,1,0:T(8,128)(2,1)S(1)} %copy.66) | copy-start | bytes 1179652
  9.7 21.6 %collective-permute-start = (bf16[2,3,2,1,128,128]{4,5,1,3,2,0:T(8,128)(2,1)S(1)}, bf16[2,3,2,1,128,128]{4,5,1,3,2,0:T(8,128)(2,1)S(1)}, u32[]{:S(2)}, u32[]{:S(2)}) collective-permute-start(bf16[2,3,2,1,128,128]{4,5,1,3,2,0:T(8,128)(2,1)S(1)} %get-tuple-element.125), channel_id=1, source_target_pairs={{0,1},{1,2},{2,3},{4,5},{5,6},{6,7},{8,9},{9,10},{10,11},{12,13},{... | collective-permute-start | bytes 1179656 | tf_op jit(solution)/shard_map/ppermute | solution.py:87
  15.0 16.4 %collective-permute-start.1 = (bf16[2,3,2,1,128,128]{4,5,1,3,2,0:T(8,128)(2,1)S(1)}, bf16[2,3,2,1,128,128]{4,5,1,3,2,0:T(8,128)(2,1)S(1)}, u32[]{:S(2)}, u32[]{:S(2)}) collective-permute-start(bf16[2,3,2,1,128,128]{4,5,1,3,2,0:T(8,128)(2,1)S(1)} %get-tuple-element.126), channel_id=1, source_target_pairs={{1,0},{2,1},{3,2},{5,4},{6,5},{7,6},{9,8},{10,9},{11,10},{13,12},{... | collective-permute-start | bytes 1179656 | tf_op jit(solution)/shard_map/ppermute | solution.py:88
  32.2 27.8 %collective-permute-start.2 = (bf16[2,3,1,4,128,128]{4,5,1,3,2,0:T(8,128)(2,1)S(1)}, bf16[2,3,1,4,128,128]{4,5,1,3,2,0:T(8,128)(2,1)S(1)}, u32[]{:S(2)}, u32[]{:S(2)}) collective-permute-start(bf16[2,3,1,4,128,128]{4,5,1,3,2,0:T(8,128)(2,1)S(1)} %get-tuple-element.117), channel_id=1, source_target_pairs={{0,4},{4,8},{8,12},{12,16},{16,20},{20,24},{24,28},{1,5},{5,9},{9,... | collective-permute-start | bytes 2359304 | tf_op jit(solution)/shard_map/ppermute | solution.py:87
  42.1 34.3 %collective-permute-start.3 = (bf16[2,3,1,4,128,128]{4,5,1,3,2,0:T(8,128)(2,1)S(1)}, bf16[2,3,1,4,128,128]{4,5,1,3,2,0:T(8,128)(2,1)}, u32[]{:S(2)}, u32[]{:S(2)}) collective-permute-start(bf16[2,3,1,4,128,128]{4,5,1,3,2,0:T(8,128)(2,1)S(1)} %get-tuple-element.118), channel_id=1, source_target_pairs={{4,0},{8,4},{12,8},{16,12},{20,16},{24,20},{28,24},{5,1},{9,5},{13... | collective-permute-start | bytes 2359304 | tf_op jit(solution)/shard_map/ppermute | solution.py:88
  78.4 8.6 %collective-permute-start.4 = (bf16[96,384]{1,0:T(8,128)(2,1)}, bf16[96,384]{1,0:T(8,128)(2,1)S(1)}, u32[]{:S(2)}, u32[]{:S(2)}) collective-permute-start(bf16[96,384]{1,0:T(8,128)(2,1)} %param.25), channel_id=1, source_target_pairs={{0,2},{1,3},{2,0},{3,1},{4,6},{5,7},{6,4},{7,5},{8,10},{9,11},{10,... | collective-permute-start | bytes 221192 | tf_op jit(solution)/shard_map/ppermute | solution.py:15
  88.7 9.3 %collective-permute-start.5 = (bf16[192,384]{1,0:T(8,128)(2,1)}, bf16[192,384]{1,0:T(8,128)(2,1)}, u32[]{:S(2)}, u32[]{:S(2)}) collective-permute-start(bf16[192,384]{1,0:T(8,128)(2,1)} %maximum_select_fusion.4), channel_id=1, source_target_pairs={{0,1},{1,0},{2,3},{3,2},{4,5},{5,4},{6,7},{7,6},{8,9},{9,8},{10,11... | collective-permute-start | bytes 442376 | tf_op jit(solution)/shard_map/ppermute | solution.py:15
  99.8 8.5 %collective-permute-start.6 = (bf16[384,384]{1,0:T(8,128)(2,1)}, bf16[384,384]{1,0:T(8,128)(2,1)}, u32[]{:S(2)}, u32[]{:S(2)}) collective-permute-start(bf16[384,384]{1,0:T(8,128)(2,1)} %maximum_select_fusion.3), channel_id=1, source_target_pairs={{0,16},{4,20},{8,24},{12,28},{16,0},{20,4},{24,8},{28,12},{1,17},{... | collective-permute-start | bytes 884744 | tf_op jit(solution)/shard_map/ppermute | solution.py:15
  105.7 11.6 %copy-start.10 = (bf16[1,3,4,4,128,128]{5,4,3,2,1,0:T(8,128)(2,1)}, bf16[1,3,4,4,128,128]{5,4,3,2,1,0:T(8,128)(2,1)S(1)}, u32[]{:S(2)}) copy-start(bf16[1,3,4,4,128,128]{5,4,3,2,1,0:T(8,128)(2,1)S(1)} %copy.67) | copy-start | bytes 4718596
  109.9 10.9 %collective-permute-start.7 = (bf16[768,384]{1,0:T(8,128)(2,1)S(1)}, bf16[768,384]{1,0:T(8,128)(2,1)S(1)}, u32[]{:S(2)}, u32[]{:S(2)}) collective-permute-start(bf16[768,384]{1,0:T(8,128)(2,1)S(1)} %maximum_select_fusion.2), channel_id=1, source_target_pairs={{0,8},{4,12},{8,0},{12,4},{16,24},{20,28},{24,16},{28,20},{1,9},{5... | collective-permute-start | bytes 1769480 | tf_op jit(solution)/shard_map/ppermute | solution.py:15
  121.2 22.9 %collective-permute-start.8 = (bf16[1536,384]{1,0:T(8,128)(2,1)S(1)}, bf16[1536,384]{1,0:T(8,128)(2,1)S(1)}, u32[]{:S(2)}, u32[]{:S(2)}) collective-permute-start(bf16[1536,384]{1,0:T(8,128)(2,1)S(1)} %maximum_select_fusion.1), channel_id=1, source_target_pairs={{0,4},{4,0},{8,12},{12,8},{16,20},{20,16},{24,28},{28,24},{1,5},{5... | collective-permute-start | bytes 3538952 | tf_op jit(solution)/shard_map/ppermute | solution.py:15
  149.1 7.8 %slice-start = ((s8[6291456]{0:T(1024)(128)(4,1)}), s8[2097152]{0:T(1024)(128)(4,1)S(1)}, s32[]{:S(2)}) async-start(s8[6291456]{0:T(1024)(128)(4,1)} %bitcast.173), calls=%async_computation.1 | async-start | bytes 4194304
  150.5 6.4 %slice-start.1 = ((s8[6291456]{0:T(1024)(128)(4,1)}), s8[4194304]{0:T(1024)(128)(4,1)S(1)}, s32[]{:S(2)}) async-start(s8[6291456]{0:T(1024)(128)(4,1)} %bitcast.173), calls=%async_computation.2 | async-start | bytes 8388608
  170.0 15.3 %copy-start = (f32[3,4,4,128,128]{3,4,0,2,1:T(8,128)}, f32[3,4,4,128,128]{3,4,0,2,1:T(8,128)S(1)}, u32[]{:S(2)}) copy-start(f32[3,4,4,128,128]{3,4,0,2,1:T(8,128)S(1)} %copy.81) | copy-start | bytes 9437188
  178.2 22.6 %collective-permute-start.9 = (bf16[2,3,4,128,128]{3,4,1,2,0:T(8,128)(2,1)}, bf16[2,3,4,128,128]{3,4,1,2,0:T(8,128)(2,1)}, u32[]{:S(2)}, u32[]{:S(2)}) collective-permute-start(bf16[2,3,4,128,128]{3,4,1,2,0:T(8,128)(2,1)} %pad_maximum_fusion.2), channel_id=1, source_target_pairs={{0,4},{4,8},{8,12},{12,16},{16,20},{20,24},{24,28},{1,5},{5,9},{9,... | collective-permute-start | bytes 2359304 | tf_op jit(solution)/shard_map/ppermute | solution.py:72
  182.5 28.3 %collective-permute-start.10 = (bf16[2,3,4,128,128]{3,4,1,2,0:T(8,128)(2,1)}, bf16[2,3,4,128,128]{3,4,1,2,0:T(8,128)(2,1)}, u32[]{:S(2)}, u32[]{:S(2)}) collective-permute-start(bf16[2,3,4,128,128]{3,4,1,2,0:T(8,128)(2,1)} %pad_maximum_fusion.3), channel_id=1, source_target_pairs={{4,0},{8,4},{12,8},{16,12},{20,16},{24,20},{28,24},{5,1},{9,5},{13... | collective-permute-start | bytes 2359304 | tf_op jit(solution)/shard_map/ppermute | solution.py:72
  186.6 15.5 %slice-start.2 = ((f32[3,4,4,128,128]{3,4,0,2,1:T(8,128)}), f32[3,2,4,128,128]{3,4,0,2,1:T(8,128)S(1)}, s32[]{:S(2)}) async-start(f32[3,4,4,128,128]{3,4,0,2,1:T(8,128)} %copy-done), calls=%async_computation.3 | async-start | bytes 3145728 | tf_op jit(solution)/shard_map/slice | solution.py:98
  212.1 13.5 %slice-start.3 = ((s8[6291456]{0:T(1024)(128)(4,1)}), s8[4194304]{0:T(1024)(128)(4,1)S(1)}, s32[]{:S(2)}) async-start(s8[6291456]{0:T(1024)(128)(4,1)} %bitcast.179), calls=%async_computation.4 | async-start | bytes 8388608
  212.6 13.0 %slice-start.4 = ((s8[6291456]{0:T(1024)(128)(4,1)}), s8[2097152]{0:T(1024)(128)(4,1)S(1)}, s32[]{:S(2)}) async-start(s8[6291456]{0:T(1024)(128)(4,1)} %bitcast.179), calls=%async_computation.5 | async-start | bytes 4194304
  212.8 12.9 %copy-start.11 = (bf16[1,3,4,4,128,128]{5,4,3,2,1,0:T(8,128)(2,1)S(1)}, bf16[1,3,4,4,128,128]{5,4,3,2,1,0:T(8,128)(2,1)}, u32[]{:S(2)}) copy-start(bf16[1,3,4,4,128,128]{5,4,3,2,1,0:T(8,128)(2,1)} %copy-done.10) | copy-start | bytes 4718596
  214.6 15.6 %collective-permute-start.11 = (bf16[2,3,2,128,128]{3,4,1,2,0:T(8,128)(2,1)}, bf16[2,3,2,128,128]{3,4,1,2,0:T(8,128)(2,1)}, u32[]{:S(2)}, u32[]{:S(2)}) collective-permute-start(bf16[2,3,2,128,128]{3,4,1,2,0:T(8,128)(2,1)} %pad_maximum_fusion.5), channel_id=1, source_target_pairs={{0,1},{1,2},{2,3},{4,5},{5,6},{6,7},{8,9},{9,10},{10,11},{12,13},{... | collective-permute-start | bytes 1179656 | tf_op jit(solution)/shard_map/ppermute | solution.py:72
  224.3 21.7 %collective-permute-start.12 = (bf16[2,3,2,128,128]{3,4,1,2,0:T(8,128)(2,1)}, bf16[2,3,2,128,128]{3,4,1,2,0:T(8,128)(2,1)}, u32[]{:S(2)}, u32[]{:S(2)}) collective-permute-start(bf16[2,3,2,128,128]{3,4,1,2,0:T(8,128)(2,1)} %pad_maximum_fusion.6), channel_id=1, source_target_pairs={{1,0},{2,1},{3,2},{5,4},{6,5},{7,6},{9,8},{10,9},{11,10},{13,12},{... | collective-permute-start | bytes 1179656 | tf_op jit(solution)/shard_map/ppermute | solution.py:72
  231.3 15.9 %copy-start.7 = (f32[3,2,2,128,128]{3,4,0,1,2:T(8,128)}, f32[3,2,2,128,128]{3,4,0,1,2:T(8,128)S(1)}, u32[]{:S(2)}) copy-start(f32[3,2,2,128,128]{3,4,0,1,2:T(8,128)S(1)} %get-tuple-element.120) | copy-start | bytes 2359300
  (10 other events, 24.2 us)
Sparse Core Ops, SparseCore 0:
  16.4 33.1 all-gather.1

commit v11 on v8

--- a/solution.py
+++ b/solution.py
@@ -124,7 +124,7 @@
     def head_minor(array):
         return jnp.transpose(array, (1, 2, 3, 0, 4)).reshape(queries.shape)
 
-    ext = extended_2(jnp.stack([head_major(keys), head_major(values)]), (("wa", 3), ("ha", 2)), 1)
+    ext = extended_2(jnp.stack([head_major(keys), head_major(values)]), (("ha", 2), ("wa", 3)), 1)
     ext_r, ext_c = tile_rows + 2, tile_cols + 2
     row_base = lax.axis_index("ha") * tile_rows
     col_base = lax.axis_index("wa") * tile_cols

time: 227 us -> 231 us (1.018); the launches traced: 225 us -> 226 us
  starting transfers between devices: 30.2 us -> 42 us
  waiting for transfers between devices: 92.8 us -> 82.5 us
    ppermute x5, waiting for transfers between devices: 55.5 us -> 26.2 us  [doubling_gather(): other = lax.ppermute(buf, axis, [(i, i ^ bit) for i in range(count)])]
    ppermute x2, waiting for transfers between devices: 1.61 us -> 16.7 us  [extended_2(): after = lax.ppermute(first, axis, down)]
    ppermute x5, starting transfers between devices: 8.95 us -> 19.5 us  [doubling_gather(): other = lax.ppermute(buf, axis, [(i, i ^ bit) for i in range(count)])]
    ppermute x4, waiting for transfers between devices: 34.9 us -> 39 us  [passed_along(): lax.ppermute(value, axis, [(source, source + steps) for source in range(f...]
where the time goes in v11:
time: 231 us; the launch traced here: 226 us
  waiting for transfers between devices  82.5 us (36%)
  starting transfers between devices  42 us (18%)
  other arithmetic  31.8 us (14%)
  matrix products  29.5 us (13%)
  local copies, waits for them, and re-layouts  25.8 us (11%)
  between operations  14.6 us (6%)
    ppermute x4, waiting for transfers between devices, passed_along(): lax.ppermute(value, axis, [(source, source + steps) for source in range(f...  39 us
    ppermute x5, waiting for transfers between devices, doubling_gather(): other = lax.ppermute(buf, axis, [(i, i ^ bit) for i in range(count)])  26.2 us
    ppermute x5, starting transfers between devices, doubling_gather(): other = lax.ppermute(buf, axis, [(i, i ^ bit) for i in range(count)])  19.5 us
    ppermute x2, waiting for transfers between devices, extended_2(): after = lax.ppermute(first, axis, down)  16.7 us
    ppermute x4, starting transfers between devices, passed_along(): lax.ppermute(value, axis, [(source, source + steps) for source in range(f...  11.4 us
    unnamed x39, local copies, waits for them, and re-layouts  9.91 us
    convert_element_type x1, other arithmetic, local(): probs_lo = probs.astype(bf16)  8.49 us
    sub x1, matrix products, local(): scores = scores - jnp.max(scores, axis=-1, keepdims=True)  7.25 us
  transfers between devices with their start and end apart: 14, of which 8 were waited for; matrix products, arithmetic and copies ran while one was open for 20% of the time, Pallas kernels for 0%

profile of v11, /device:TPU:64, one launch (start us, length us, event | category | flops | bytes accessed | tf_op | source)
XLA Modules:
  0.0 226.1 jit_solution(8155571330631887746)
XLA Ops:
  7.9 5.5 %collective-permute-start.4 = (bf16[96,384]{1,0:T(8,128)(2,1)}, bf16[96,384]{1,0:T(8,128)(2,1)S(1)}, u32[]{:S(2)}, u32[]{:S(2)}) collective-permute-start(bf16[96,384]{1,0:T(8,128)(2,1)} %param.25), channel_id=1, source_target_pairs={{0,2},{1,3},{2,0},{3,1},{4,6},{5,7},{6,4},{7,5},{8,10},{9,11},{10,... | collective-permute-start | bytes 221192 | tf_op jit(solution)/shard_map/ppermute | solution.py:15
  15.9 2.9 %collective-permute-start = (bf16[2,3,1,2,128,128]{4,5,1,3,2,0:T(8,128)(2,1)S(1)}, bf16[2,3,1,2,128,128]{4,5,1,3,2,0:T(8,128)(2,1)S(1)}, u32[]{:S(2)}, u32[]{:S(2)}) collective-permute-start(bf16[2,3,1,2,128,128]{4,5,1,3,2,0:T(8,128)(2,1)S(1)} %get-tuple-element.121), channel_id=1, source_target_pairs={{0,4},{4,8},{8,12},{12,16},{16,20},{20,24},{24,28},{1,5},{5,9},{9,... | collective-permute-start | bytes 1179656 | tf_op jit(solution)/shard_map/ppermute | solution.py:87
  21.9 10.1 %collective-permute-done.5 = bf16[192,384]{1,0:T(8,128)(2,1)S(1)} collective-permute-done((bf16[192,384]{1,0:T(8,128)(2,1)S(1)}, bf16[192,384]{1,0:T(8,128)(2,1)S(1)}, u32[]{:S(2)}, u32[]{:S(2)}) %collective-permute-start.5) | collective-permute-done | bytes 147488 | tf_op jit(solution)/shard_map/ppermute | solution.py:15
  32.1 11.7 %collective-permute-start.6 = (bf16[384,384]{1,0:T(8,128)(2,1)S(1)}, bf16[384,384]{1,0:T(8,128)(2,1)S(1)}, u32[]{:S(2)}, u32[]{:S(2)}) collective-permute-start(bf16[384,384]{1,0:T(8,128)(2,1)S(1)} %maximum_select_fusion.3), channel_id=1, source_target_pairs={{0,16},{4,20},{8,24},{12,28},{16,0},{20,4},{24,8},{28,12},{1,17},{... | collective-permute-start | bytes 884744 | tf_op jit(solution)/shard_map/ppermute | solution.py:15
  47.2 4.9 %collective-permute-start.3 = (bf16[2,3,4,1,128,128]{4,5,1,3,2,0:T(8,128)(2,1)}, bf16[2,3,4,1,128,128]{4,5,1,3,2,0:T(8,128)(2,1)}, u32[]{:S(2)}, u32[]{:S(2)}) collective-permute-start(bf16[2,3,4,1,128,128]{4,5,1,3,2,0:T(8,128)(2,1)} %get-tuple-element.114), channel_id=1, source_target_pairs={{1,0},{2,1},{3,2},{5,4},{6,5},{7,6},{9,8},{10,9},{11,10},{13,12},{... | collective-permute-start | bytes 2359304 | tf_op jit(solution)/shard_map/ppermute | solution.py:88
  54.6 11.1 %collective-permute-done.7 = bf16[768,384]{1,0:T(8,128)(2,1)} collective-permute-done((bf16[768,384]{1,0:T(8,128)(2,1)S(1)}, bf16[768,384]{1,0:T(8,128)(2,1)}, u32[]{:S(2)}, u32[]{:S(2)}) %collective-permute-start.7) | collective-permute-done | bytes 589856 | tf_op jit(solution)/shard_map/ppermute | solution.py:15
  65.7 2.8 %maximum_select_fusion.1 = bf16[1536,384]{1,0:T(8,128)(2,1)} fusion(bf16[768,384]{1,0:T(8,128)(2,1)} %collective-permute-done.7, bf16[768,384]{1,0:T(8,128)(2,1)S(1)} %maximum_select_fusion.2, pred[]{:T(512)S(6)} %eq.22), kind=kLoop, calls=%fused_computation.19 | loop fusion | flops 5308416 | bytes 2359297 | tf_op jit(solution)/shard_map/jit(_where)/select_n | solution.py:17
  68.4 16.7 %collective-permute-done.3 = bf16[2,3,4,1,128,128]{4,5,1,3,2,0:T(8,128)(2,1)} collective-permute-done((bf16[2,3,4,1,128,128]{4,5,1,3,2,0:T(8,128)(2,1)}, bf16[2,3,4,1,128,128]{4,5,1,3,2,0:T(8,128)(2,1)}, u32[]{:S(2)}, u32[]{:S(2)}) %collective-permute-start.3) | collective-permute-done | bytes 786464 | tf_op jit(solution)/shard_map/ppermute | solution.py:88
  89.4 7.2 %fusion.42 = (f32[3,4,128]{2,1,0:T(4,128)S(1)}, f32[3,4,128,2048]{2,3,1,0:T(8,128)}) fusion(pred[4,2048]{1,0:T(4,128)(4,1)S(1)} %bitcast.202, bf16[3,2048,128,1]{2,1,3,0:T(8,128)(2,1)S(1)} %bitcast.193, bf16[3,4,128,128]{2,3,0,1:T(8,128)(2,1)S(1)} %bitcast.188), kind=kOutput, calls=%fused_computation.86 | convolution fusion | flops 817891328 | bytes 14563328 | tf_op jit(solution)/shard_map/sub | solution.py:155
  96.6 8.5 %fusion.5 = bf16[3,4,128,2048]{2,3,1,0:T(8,128)(2,1)} fusion(f32[3,4,128,2048]{2,3,1,0:T(8,128)} %get-tuple-element.124, f32[3,4,128]{2,1,0:T(4,128)S(1)} %get-tuple-element.123), kind=kLoop, calls=%fused_computation.9 | loop fusion | flops 6291456 | bytes 18880512 | tf_op jit(solution)/shard_map/convert_element_type | solution.py:158
  105.1 5.0 %collective-permute-done.8 = bf16[1536,384]{1,0:T(8,128)(2,1)} collective-permute-done((bf16[1536,384]{1,0:T(8,128)(2,1)}, bf16[1536,384]{1,0:T(8,128)(2,1)}, u32[]{:S(2)}, u32[]{:S(2)}) %collective-permute-start.8) | collective-permute-done | bytes 1179680 | tf_op jit(solution)/shard_map/ppermute | solution.py:15
  110.1 3.2 %maximum_select_fusion = bf16[3072,384]{1,0:T(8,128)(2,1)S(1)} fusion(bf16[1536,384]{1,0:T(8,128)(2,1)} %collective-permute-done.8, bf16[1536,384]{1,0:T(8,128)(2,1)} %maximum_select_fusion.1, pred[]{:T(512)S(6)} %eq.21), kind=kLoop, calls=%fused_computation.11 | loop fusion | flops 10616832 | bytes 4718593 | tf_op jit(solution)/shard_map/jit(_where)/select_n | solution.py:17
  113.7 4.1 %fusion.9 = bf16[512,384]{0,1:T(8,128)(2,1)} fusion(bf16[3072,384]{1,0:T(8,128)(2,1)S(1)} %bitcast.187, bf16[512,3072]{1,0:T(8,128)(2,1)} %bitcast.203), kind=kOutput, calls=%fused_computation.18 | convolution fusion | flops 1208156160 | bytes 5898240 | tf_op jit(solution)/shard_map/dot_general | solution.py:160
  119.1 6.4 %fusion.47 = f32[3,2048,128,1]{2,1,3,0:T(8,128)} fusion(bf16[3,4,128,2048]{2,3,1,0:T(8,128)(2,1)} %fusion.5, bf16[3,4,128,128]{2,3,1,0:T(8,128)(2,1)S(1)} %bitcast.190), kind=kOutput, calls=%fused_computation.87 | convolution fusion | flops 805306368 | bytes 9830400 | tf_op jit(solution)/shard_map/hqtl,hqtd->hld/dot_general | solution.py:171
  126.7 5.9 %multiply_convert_fusion = bf16[3,4,128,2048]{2,3,1,0:T(8,128)(2,1)S(1)} fusion(f32[3,4,128]{2,1,0:T(4,128)S(1)} %fusion.8, bf16[3,2048,128,1]{2,1,3,0:T(8,128)(2,1)S(1)} %bitcast.196, bf16[3,4,128,128]{2,3,1,0:T(8,128)(2,1)S(1)} %bitcast.192, f32[3,4,128,2048]{2,3,1,0:T(8,128)} %get-tuple-element.124, f32[3,4,128]{2,1,0:T(4,128)S(1)} %get-tuple-element.123), kind=kOutput, calls=%fused_computation.2 | convolution fusion | flops 821035008 | bytes 20852736 | tf_op jit(solution)/shard_map/hqtd,hld->hqtl/dot_general | solution.py:167
  132.6 3.6 %fusion.32 = f32[3,2048,128,1]{2,1,3,0:T(8,128)} fusion(bf16[3,4,128,2048]{2,3,1,0:T(8,128)(2,1)S(1)} %multiply_convert_fusion, bf16[3,4,128,128]{2,3,0,1:T(8,128)(2,1)S(1)} %bitcast.189), kind=kOutput, calls=%fused_computation.61 | convolution fusion | flops 805306368 | bytes 9830400 | tf_op jit(solution)/shard_map/hqtl,hqtd->hld/dot_general | solution.py:170
  136.2 2.6 %copy.81 = f32[3,4,4,128,128]{3,4,0,2,1:T(8,128)S(1)} copy(f32[3,4,4,128,128]{4,3,2,1,0:T(8,128)} %bitcast.177) | data formatting | bytes 6291456 | tf_op jit(solution)/shard_map/reshape | solution.py:175
  140.2 3.6 %copy.85 = f32[3,4,4,128,128]{3,4,0,2,1:T(8,128)} copy(f32[3,4,4,128,128]{4,3,2,1,0:T(8,128)} %bitcast.175) | data formatting | bytes 6291456 | tf_op jit(solution)/shard_map/reshape | solution.py:175
  147.0 2.3 %collective-permute-start.9 = (bf16[2,3,4,128,128]{3,4,1,2,0:T(8,128)(2,1)}, bf16[2,3,4,128,128]{3,4,1,2,0:T(8,128)(2,1)}, u32[]{:S(2)}, u32[]{:S(2)}) collective-permute-start(bf16[2,3,4,128,128]{3,4,1,2,0:T(8,128)(2,1)} %pad_maximum_fusion.2), channel_id=1, source_target_pairs={{0,4},{4,8},{8,12},{12,16},{16,20},{20,24},{24,28},{1,5},{5,9},{9,... | collective-permute-start | bytes 2359304 | tf_op jit(solution)/shard_map/ppermute | solution.py:72
  155.0 10.3 %collective-permute-done.9 = bf16[2,3,4,128,128]{3,4,1,2,0:T(8,128)(2,1)} collective-permute-done((bf16[2,3,4,128,128]{3,4,1,2,0:T(8,128)(2,1)}, bf16[2,3,4,128,128]{3,4,1,2,0:T(8,128)(2,1)}, u32[]{:S(2)}, u32[]{:S(2)}) %collective-permute-start.9) | collective-permute-done | bytes 786464 | tf_op jit(solution)/shard_map/ppermute | solution.py:72
  169.2 16.7 %collective-permute-done.10 = bf16[2,3,4,128,128]{3,4,1,2,0:T(8,128)(2,1)} collective-permute-done((bf16[2,3,4,128,128]{3,4,1,2,0:T(8,128)(2,1)}, bf16[2,3,4,128,128]{3,4,1,2,0:T(8,128)(2,1)}, u32[]{:S(2)}, u32[]{:S(2)}) %collective-permute-start.10) | collective-permute-done | bytes 786464 | tf_op jit(solution)/shard_map/ppermute | solution.py:72
  189.7 2.7 %collective-permute-start.11 = (bf16[2,3,2,128,128]{3,4,1,2,0:T(8,128)(2,1)}, bf16[2,3,2,128,128]{3,4,1,2,0:T(8,128)(2,1)}, u32[]{:S(2)}, u32[]{:S(2)}) collective-permute-start(bf16[2,3,2,128,128]{3,4,1,2,0:T(8,128)(2,1)} %pad_maximum_fusion.5), channel_id=1, source_target_pairs={{0,1},{1,2},{2,3},{4,5},{5,6},{6,7},{8,9},{9,10},{10,11},{12,13},{... | collective-permute-start | bytes 1179656 | tf_op jit(solution)/shard_map/ppermute | solution.py:72
  193.1 5.0 %collective-permute-start.12 = (bf16[2,3,2,128,128]{3,4,1,2,0:T(8,128)(2,1)}, bf16[2,3,2,128,128]{3,4,1,2,0:T(8,128)(2,1)}, u32[]{:S(2)}, u32[]{:S(2)}) collective-permute-start(bf16[2,3,2,128,128]{3,4,1,2,0:T(8,128)(2,1)} %pad_maximum_fusion.6), channel_id=1, source_target_pairs={{1,0},{2,1},{3,2},{5,4},{6,5},{7,6},{9,8},{10,9},{11,10},{13,12},{... | collective-permute-start | bytes 1179656 | tf_op jit(solution)/shard_map/ppermute | solution.py:72
  204.4 9.6 %collective-permute-done.12 = bf16[2,3,2,128,128]{3,4,1,2,0:T(8,128)(2,1)} collective-permute-done((bf16[2,3,2,128,128]{3,4,1,2,0:T(8,128)(2,1)}, bf16[2,3,2,128,128]{3,4,1,2,0:T(8,128)(2,1)}, u32[]{:S(2)}, u32[]{:S(2)}) %collective-permute-start.12) | collective-permute-done | bytes 393248 | tf_op jit(solution)/shard_map/ppermute | solution.py:72
  (108 shorter events, 49.2 us)
Async XLA Ops:
  7.2 13.1 %copy-start.10 = (bf16[96,384]{1,0:T(8,128)(2,1)S(1)}, bf16[96,384]{1,0:T(8,128)(2,1)}, u32[]{:S(2)}) copy-start(bf16[96,384]{1,0:T(8,128)(2,1)} %param.25) | copy-start | bytes 221188
  7.2 106.5 %all-gather.2.cloned.1.call-start = ((), (), s32[]{:S(2)}) async-start(), calls=%async_computation | async-start | bytes 3538944 | tf_op jit(solution)/shard_map/all_gather | solution.py:117
  7.9 12.3 %collective-permute-start.4 = (bf16[96,384]{1,0:T(8,128)(2,1)}, bf16[96,384]{1,0:T(8,128)(2,1)S(1)}, u32[]{:S(2)}, u32[]{:S(2)}) collective-permute-start(bf16[96,384]{1,0:T(8,128)(2,1)} %param.25), channel_id=1, source_target_pairs={{0,2},{1,3},{2,0},{3,1},{4,6},{5,7},{6,4},{7,5},{8,10},{9,11},{10,... | collective-permute-start | bytes 221192 | tf_op jit(solution)/shard_map/ppermute | solution.py:15
  15.9 27.9 %collective-permute-start = (bf16[2,3,1,2,128,128]{4,5,1,3,2,0:T(8,128)(2,1)S(1)}, bf16[2,3,1,2,128,128]{4,5,1,3,2,0:T(8,128)(2,1)S(1)}, u32[]{:S(2)}, u32[]{:S(2)}) collective-permute-start(bf16[2,3,1,2,128,128]{4,5,1,3,2,0:T(8,128)(2,1)S(1)} %get-tuple-element.121), channel_id=1, source_target_pairs={{0,4},{4,8},{8,12},{12,16},{16,20},{20,24},{24,28},{1,5},{5,9},{9,... | collective-permute-start | bytes 1179656 | tf_op jit(solution)/shard_map/ppermute | solution.py:87
  18.9 24.9 %collective-permute-start.1 = (bf16[2,3,1,2,128,128]{4,5,1,3,2,0:T(8,128)(2,1)S(1)}, bf16[2,3,1,2,128,128]{4,5,1,3,2,0:T(8,128)(2,1)S(1)}, u32[]{:S(2)}, u32[]{:S(2)}) collective-permute-start(bf16[2,3,1,2,128,128]{4,5,1,3,2,0:T(8,128)(2,1)S(1)} %get-tuple-element.122), channel_id=1, source_target_pairs={{4,0},{8,4},{12,8},{16,12},{20,16},{24,20},{28,24},{5,1},{9,5},{13... | collective-permute-start | bytes 1179656 | tf_op jit(solution)/shard_map/ppermute | solution.py:88
  20.3 11.7 %collective-permute-start.5 = (bf16[192,384]{1,0:T(8,128)(2,1)S(1)}, bf16[192,384]{1,0:T(8,128)(2,1)S(1)}, u32[]{:S(2)}, u32[]{:S(2)}) collective-permute-start(bf16[192,384]{1,0:T(8,128)(2,1)S(1)} %maximum_select_fusion.4), channel_id=1, source_target_pairs={{0,1},{1,0},{2,3},{3,2},{4,5},{5,4},{6,7},{7,6},{8,9},{9,8},{10,11... | collective-permute-start | bytes 442376 | tf_op jit(solution)/shard_map/ppermute | solution.py:15
  32.1 20.0 %collective-permute-start.6 = (bf16[384,384]{1,0:T(8,128)(2,1)S(1)}, bf16[384,384]{1,0:T(8,128)(2,1)S(1)}, u32[]{:S(2)}, u32[]{:S(2)}) collective-permute-start(bf16[384,384]{1,0:T(8,128)(2,1)S(1)} %maximum_select_fusion.3), channel_id=1, source_target_pairs={{0,16},{4,20},{8,24},{12,28},{16,0},{20,4},{24,8},{28,12},{1,17},{... | collective-permute-start | bytes 884744 | tf_op jit(solution)/shard_map/ppermute | solution.py:15
  45.3 23.2 %collective-permute-start.2 = (bf16[2,3,4,1,128,128]{4,5,1,3,2,0:T(8,128)(2,1)}, bf16[2,3,4,1,128,128]{4,5,1,3,2,0:T(8,128)(2,1)S(1)}, u32[]{:S(2)}, u32[]{:S(2)}) collective-permute-start(bf16[2,3,4,1,128,128]{4,5,1,3,2,0:T(8,128)(2,1)} %get-tuple-element.113), channel_id=1, source_target_pairs={{0,1},{1,2},{2,3},{4,5},{5,6},{6,7},{8,9},{9,10},{10,11},{12,13},{... | collective-permute-start | bytes 2359304 | tf_op jit(solution)/shard_map/ppermute | solution.py:87
  47.2 37.9 %collective-permute-start.3 = (bf16[2,3,4,1,128,128]{4,5,1,3,2,0:T(8,128)(2,1)}, bf16[2,3,4,1,128,128]{4,5,1,3,2,0:T(8,128)(2,1)}, u32[]{:S(2)}, u32[]{:S(2)}) collective-permute-start(bf16[2,3,4,1,128,128]{4,5,1,3,2,0:T(8,128)(2,1)} %get-tuple-element.114), channel_id=1, source_target_pairs={{1,0},{2,1},{3,2},{5,4},{6,5},{7,6},{9,8},{10,9},{11,10},{13,12},{... | collective-permute-start | bytes 2359304 | tf_op jit(solution)/shard_map/ppermute | solution.py:88
  52.3 13.4 %collective-permute-start.7 = (bf16[768,384]{1,0:T(8,128)(2,1)S(1)}, bf16[768,384]{1,0:T(8,128)(2,1)}, u32[]{:S(2)}, u32[]{:S(2)}) collective-permute-start(bf16[768,384]{1,0:T(8,128)(2,1)S(1)} %maximum_select_fusion.2), channel_id=1, source_target_pairs={{0,8},{4,12},{8,0},{12,4},{16,24},{20,28},{24,16},{28,20},{1,9},{5... | collective-permute-start | bytes 1769480 | tf_op jit(solution)/shard_map/ppermute | solution.py:15
  68.4 41.7 %collective-permute-start.8 = (bf16[1536,384]{1,0:T(8,128)(2,1)}, bf16[1536,384]{1,0:T(8,128)(2,1)}, u32[]{:S(2)}, u32[]{:S(2)}) collective-permute-start(bf16[1536,384]{1,0:T(8,128)(2,1)} %maximum_select_fusion.1), channel_id=1, source_target_pairs={{0,4},{4,0},{8,12},{12,8},{16,20},{20,16},{24,28},{28,24},{1,5},{5... | collective-permute-start | bytes 3538952 | tf_op jit(solution)/shard_map/ppermute | solution.py:15
  89.4 7.3 %copy-start.6 = (bf16[1,3,4,4,128,128]{5,4,3,2,1,0:T(8,128)(2,1)}, bf16[1,3,4,4,128,128]{5,4,3,2,1,0:T(8,128)(2,1)S(1)}, u32[]{:S(2)}) copy-start(bf16[1,3,4,4,128,128]{5,4,3,2,1,0:T(8,128)(2,1)S(1)} %copy.67) | copy-start | bytes 4718596
  117.8 7.8 %slice-start = ((s8[6291456]{0:T(1024)(128)(4,1)}), s8[2097152]{0:T(1024)(128)(4,1)S(1)}, s32[]{:S(2)}) async-start(s8[6291456]{0:T(1024)(128)(4,1)} %bitcast.173), calls=%async_computation.1 | async-start | bytes 4194304
  119.1 6.4 %slice-start.1 = ((s8[6291456]{0:T(1024)(128)(4,1)}), s8[4194304]{0:T(1024)(128)(4,1)S(1)}, s32[]{:S(2)}) async-start(s8[6291456]{0:T(1024)(128)(4,1)} %bitcast.173), calls=%async_computation.2 | async-start | bytes 8388608
  138.9 12.8 %copy-start = (f32[3,4,4,128,128]{3,4,0,2,1:T(8,128)}, f32[3,4,4,128,128]{3,4,0,2,1:T(8,128)S(1)}, u32[]{:S(2)}) copy-start(f32[3,4,4,128,128]{3,4,0,2,1:T(8,128)S(1)} %copy.81) | copy-start | bytes 9437188
  147.0 18.3 %collective-permute-start.9 = (bf16[2,3,4,128,128]{3,4,1,2,0:T(8,128)(2,1)}, bf16[2,3,4,128,128]{3,4,1,2,0:T(8,128)(2,1)}, u32[]{:S(2)}, u32[]{:S(2)}) collective-permute-start(bf16[2,3,4,128,128]{3,4,1,2,0:T(8,128)(2,1)} %pad_maximum_fusion.2), channel_id=1, source_target_pairs={{0,4},{4,8},{8,12},{12,16},{16,20},{20,24},{24,28},{1,5},{5,9},{9,... | collective-permute-start | bytes 2359304 | tf_op jit(solution)/shard_map/ppermute | solution.py:72
  150.3 35.7 %collective-permute-start.10 = (bf16[2,3,4,128,128]{3,4,1,2,0:T(8,128)(2,1)}, bf16[2,3,4,128,128]{3,4,1,2,0:T(8,128)(2,1)}, u32[]{:S(2)}, u32[]{:S(2)}) collective-permute-start(bf16[2,3,4,128,128]{3,4,1,2,0:T(8,128)(2,1)} %pad_maximum_fusion.3), channel_id=1, source_target_pairs={{4,0},{8,4},{12,8},{16,12},{20,16},{24,20},{28,24},{5,1},{9,5},{13... | collective-permute-start | bytes 2359304 | tf_op jit(solution)/shard_map/ppermute | solution.py:72
  153.0 13.7 %slice-start.2 = ((f32[3,4,4,128,128]{3,4,0,2,1:T(8,128)}), f32[3,2,4,128,128]{3,4,0,2,1:T(8,128)S(1)}, s32[]{:S(2)}) async-start(f32[3,4,4,128,128]{3,4,0,2,1:T(8,128)} %copy-done), calls=%async_computation.3 | async-start | bytes 3145728 | tf_op jit(solution)/shard_map/slice | solution.py:98
  187.3 10.9 %slice-start.3 = ((s8[6291456]{0:T(1024)(128)(4,1)}), s8[4194304]{0:T(1024)(128)(4,1)S(1)}, s32[]{:S(2)}) async-start(s8[6291456]{0:T(1024)(128)(4,1)} %bitcast.179), calls=%async_computation.4 | async-start | bytes 8388608
  187.7 10.4 %slice-start.4 = ((s8[6291456]{0:T(1024)(128)(4,1)}), s8[2097152]{0:T(1024)(128)(4,1)S(1)}, s32[]{:S(2)}) async-start(s8[6291456]{0:T(1024)(128)(4,1)} %bitcast.179), calls=%async_computation.5 | async-start | bytes 4194304
  187.9 10.3 %copy-start.7 = (bf16[1,3,4,4,128,128]{5,4,3,2,1,0:T(8,128)(2,1)S(1)}, bf16[1,3,4,4,128,128]{5,4,3,2,1,0:T(8,128)(2,1)}, u32[]{:S(2)}) copy-start(bf16[1,3,4,4,128,128]{5,4,3,2,1,0:T(8,128)(2,1)} %copy-done.6) | copy-start | bytes 4718596
  189.7 13.5 %collective-permute-start.11 = (bf16[2,3,2,128,128]{3,4,1,2,0:T(8,128)(2,1)}, bf16[2,3,2,128,128]{3,4,1,2,0:T(8,128)(2,1)}, u32[]{:S(2)}, u32[]{:S(2)}) collective-permute-start(bf16[2,3,2,128,128]{3,4,1,2,0:T(8,128)(2,1)} %pad_maximum_fusion.5), channel_id=1, source_target_pairs={{0,1},{1,2},{2,3},{4,5},{5,6},{6,7},{8,9},{9,10},{10,11},{12,13},{... | collective-permute-start | bytes 1179656 | tf_op jit(solution)/shard_map/ppermute | solution.py:72
  193.1 20.8 %collective-permute-start.12 = (bf16[2,3,2,128,128]{3,4,1,2,0:T(8,128)(2,1)}, bf16[2,3,2,128,128]{3,4,1,2,0:T(8,128)(2,1)}, u32[]{:S(2)}, u32[]{:S(2)}) collective-permute-start(bf16[2,3,2,128,128]{3,4,1,2,0:T(8,128)(2,1)} %pad_maximum_fusion.6), channel_id=1, source_target_pairs={{1,0},{2,1},{3,2},{5,4},{6,5},{7,6},{9,8},{10,9},{11,10},{13,12},{... | collective-permute-start | bytes 1179656 | tf_op jit(solution)/shard_map/ppermute | solution.py:72
  204.3 10.8 %copy-start.5 = (f32[3,2,2,128,128]{3,4,0,1,2:T(8,128)}, f32[3,2,2,128,128]{3,4,0,1,2:T(8,128)S(1)}, u32[]{:S(2)}) copy-start(f32[3,2,2,128,128]{3,4,0,1,2:T(8,128)S(1)} %get-tuple-element.116) | copy-start | bytes 2359300
  (6 other events, 17.5 us)
Sparse Core Ops, SparseCore 0:
  9.8 32.4 all-gather.1

commit v12 on v8

--- a/solution.py
+++ b/solution.py
@@ -9,13 +9,26 @@
 def doubling_gather(block, steps):
     sizes = {"ha": lax.axis_size("ha"), "wa": lax.axis_size("wa")}
     index = {"ha": lax.axis_index("ha"), "wa": lax.axis_index("wa")}
+
+    def swap(value, axis, bit):
+        return lax.ppermute(value, axis, [(i, i ^ bit) for i in range(sizes[axis])])
+
+    def low(axis, bit):
+        return (index[axis] // bit) % 2 == 0
+
+    def joined(axis, bit, mine, other):
+        return jnp.where(low(axis, bit), jnp.concatenate([mine, other], 0), jnp.concatenate([other, mine], 0))
+
     buf = block
-    for axis, bit in steps:
-        count = sizes[axis]
-        other = lax.ppermute(buf, axis, [(i, i ^ bit) for i in range(count)])
-        low = (index[axis] // bit) % 2 == 0
-        buf = jnp.where(low, jnp.concatenate([buf, other], 0), jnp.concatenate([other, buf], 0))
-    return buf
+    for axis, bit in steps[:-2]:
+        buf = joined(axis, bit, buf, swap(buf, axis, bit))
+    (axis_a, bit_a), (axis_b, bit_b) = steps[-2:]
+    across_a = swap(buf, axis_a, bit_a)
+    across_b = swap(buf, axis_b, bit_b)
+    diagonal = swap(across_a, axis_b, bit_b)
+    near = joined(axis_a, bit_a, buf, across_a)
+    far = joined(axis_a, bit_a, across_b, diagonal)
+    return joined(axis_b, bit_b, near, far)
 
 
 def gather_rows(out_proj):

time: 227 us -> 231 us (1.018)
    ppermute x4, waiting for transfers between devices: 34.9 us -> 38 us  [passed_along(): lax.ppermute(value, axis, [(source, source + steps) for source in range(f...]
    ppermute x5 -> x6, waiting for transfers between devices: 55.5 us -> 52.9 us  [swap(): return lax.ppermute(value, axis, [(i, i ^ bit) for i in range(sizes[axis])])]
    ppermute x5 -> x6, starting transfers between devices: 8.95 us -> 10.9 us  [swap(): return lax.ppermute(value, axis, [(i, i ^ bit) for i in range(sizes[axis])])]
    select_n x5 -> x6, other arithmetic: 6.25 us -> 6.51 us  [joined(): jnp.where(low(axis, bit), jnp.concatenate([mine, other], 0), jnp.concaten...]
  transfers between devices with their start and end apart: 14 -> 15, of which waited for: 8 -> 9; matrix products, arithmetic and copies ran while one was open for 20% -> 20% of each run, Pallas kernels for 0% -> 0%
where the time goes in v12:
time: 231 us; the launch traced here: 227 us
  waiting for transfers between devices  92 us (40%)
  starting transfers between devices  32.1 us (14%)
  other arithmetic  31 us (13%)
  matrix products  31 us (13%)
  local copies, waits for them, and re-layouts  26.3 us (11%)
  between operations  14.7 us (6%)
    ppermute x6, waiting for transfers between devices, swap(): return lax.ppermute(value, axis, [(i, i ^ bit) for i in range(sizes[axis])])  52.9 us
    ppermute x4, waiting for transfers between devices, passed_along(): lax.ppermute(value, axis, [(source, source + steps) for source in range(f...  38 us
    ppermute x4, starting transfers between devices, passed_along(): lax.ppermute(value, axis, [(source, source + steps) for source in range(f...  11.4 us
    ppermute x6, starting transfers between devices, swap(): return lax.ppermute(value, axis, [(i, i ^ bit) for i in range(sizes[axis])])  10.9 us
    unnamed x39, local copies, waits for them, and re-layouts  9.91 us
    sub x1, matrix products, local(): scores = scores - jnp.max(scores, axis=-1, keepdims=True)  8.55 us
    convert_element_type x1, other arithmetic, local(): probs_lo = probs.astype(bf16)  8.48 us
    select_n x6, other arithmetic, joined(): jnp.where(low(axis, bit), jnp.concatenate([mine, other], 0), jnp.concaten...  6.51 us
  transfers between devices with their start and end apart: 15, of which 9 were waited for; matrix products, arithmetic and copies ran while one was open for 20% of the time, Pallas kernels for 0%

profile of v12, /device:TPU:64, one launch (start us, length us, event | category | flops | bytes accessed | tf_op | source)
XLA Modules:
  0.0 227.1 jit_solution(8755218484949169706)
XLA Ops:
  7.9 5.5 %collective-permute-start.4 = (bf16[96,384]{1,0:T(8,128)(2,1)}, bf16[96,384]{1,0:T(8,128)(2,1)S(1)}, u32[]{:S(2)}, u32[]{:S(2)}) collective-permute-start(bf16[96,384]{1,0:T(8,128)(2,1)} %param.25), channel_id=1, source_target_pairs={{0,2},{1,3},{2,0},{3,1},{4,6},{5,7},{6,4},{7,5},{8,10},{9,11},{10,... | collective-permute-start | bytes 221192 | tf_op jit(solution)/shard_map/ppermute | solution.py:14
  17.8 4.8 %collective-permute-start.1 = (bf16[2,3,2,1,128,128]{4,5,1,3,2,0:T(8,128)(2,1)S(1)}, bf16[2,3,2,1,128,128]{4,5,1,3,2,0:T(8,128)(2,1)S(1)}, u32[]{:S(2)}, u32[]{:S(2)}) collective-permute-start(bf16[2,3,2,1,128,128]{4,5,1,3,2,0:T(8,128)(2,1)S(1)} %get-tuple-element.122), channel_id=1, source_target_pairs={{1,0},{2,1},{3,2},{5,4},{6,5},{7,6},{9,8},{10,9},{11,10},{13,12},{... | collective-permute-start | bytes 1179656 | tf_op jit(solution)/shard_map/ppermute | solution.py:101
  23.0 22.2 %collective-permute-done.5 = bf16[192,384]{1,0:T(8,128)(2,1)S(1)} collective-permute-done((bf16[192,384]{1,0:T(8,128)(2,1)S(1)}, bf16[192,384]{1,0:T(8,128)(2,1)S(1)}, u32[]{:S(2)}, u32[]{:S(2)}) %collective-permute-start.5) | collective-permute-done | bytes 147488 | tf_op jit(solution)/shard_map/ppermute | solution.py:14
  45.3 3.3 %collective-permute-start.6 = (bf16[384,384]{1,0:T(8,128)(2,1)S(1)}, bf16[384,384]{1,0:T(8,128)(2,1)S(1)}, u32[]{:S(2)}, u32[]{:S(2)}) collective-permute-start(bf16[384,384]{1,0:T(8,128)(2,1)S(1)} %maximum_select_fusion.4), channel_id=1, source_target_pairs={{0,16},{4,20},{8,24},{12,28},{16,0},{20,4},{24,8},{28,12},{1,17},{... | collective-permute-start | bytes 884744 | tf_op jit(solution)/shard_map/ppermute | solution.py:14
  53.1 19.9 %collective-permute-done.6 = bf16[384,384]{1,0:T(8,128)(2,1)S(1)} collective-permute-done((bf16[384,384]{1,0:T(8,128)(2,1)S(1)}, bf16[384,384]{1,0:T(8,128)(2,1)S(1)}, u32[]{:S(2)}, u32[]{:S(2)}) %collective-permute-start.6) | collective-permute-done | bytes 294944 | tf_op jit(solution)/shard_map/ppermute | solution.py:14
  75.8 8.5 %collective-permute-done.7 = bf16[768,384]{1,0:T(8,128)(2,1)} collective-permute-done((bf16[768,384]{1,0:T(8,128)(2,1)}, bf16[768,384]{1,0:T(8,128)(2,1)}, u32[]{:S(2)}, u32[]{:S(2)}) %collective-permute-start.7) | collective-permute-done | bytes 589856 | tf_op jit(solution)/shard_map/ppermute | solution.py:14
  86.2 2.9 %maximum_select_fusion.1 = bf16[1536,384]{1,0:T(8,128)(2,1)} fusion(bf16[768,384]{1,0:T(8,128)(2,1)} %collective-permute-done.7, bf16[768,384]{1,0:T(8,128)(2,1)} %maximum_select_fusion.3, pred[]{:T(512)S(6)} %eq.24), kind=kLoop, calls=%fused_computation.19 | loop fusion | flops 5308416 | bytes 2359297 | tf_op jit(solution)/shard_map/jit(_where)/select_n | solution.py:20
  91.9 8.5 %fusion.42 = (f32[3,4,128]{2,1,0:T(4,128)S(1)}, f32[3,4,128,2048]{2,3,1,0:T(8,128)}) fusion(pred[4,2048]{1,0:T(4,128)(4,1)S(1)} %bitcast.202, bf16[3,2048,128,1]{2,1,3,0:T(8,128)(2,1)} %bitcast.193, bf16[3,4,128,128]{2,3,0,1:T(8,128)(2,1)S(1)} %bitcast.188), kind=kOutput, calls=%fused_computation.87 | convolution fusion | flops 817891328 | bytes 14563328 | tf_op jit(solution)/shard_map/sub | solution.py:168
  100.4 8.5 %fusion.5 = bf16[3,4,128,2048]{2,3,1,0:T(8,128)(2,1)} fusion(f32[3,4,128,2048]{2,3,1,0:T(8,128)} %get-tuple-element.124, f32[3,4,128]{2,1,0:T(4,128)S(1)} %get-tuple-element.123), kind=kLoop, calls=%fused_computation.9 | loop fusion | flops 6291456 | bytes 18880512 | tf_op jit(solution)/shard_map/convert_element_type | solution.py:171
  110.5 2.2 collective-permute-done.9
  115.6 4.1 %fusion.9 = bf16[512,384]{0,1:T(8,128)(2,1)} fusion(bf16[3072,384]{1,0:T(8,128)(2,1)S(1)} %bitcast.187, bf16[512,3072]{1,0:T(8,128)(2,1)} %bitcast.203), kind=kOutput, calls=%fused_computation.18 | convolution fusion | flops 1208156160 | bytes 5898240 | tf_op jit(solution)/shard_map/dot_general | solution.py:173
  121.0 6.4 %fusion.47 = f32[3,2048,128,1]{2,1,3,0:T(8,128)} fusion(bf16[3,4,128,2048]{2,3,1,0:T(8,128)(2,1)} %fusion.5, bf16[3,4,128,128]{2,3,1,0:T(8,128)(2,1)S(1)} %bitcast.190), kind=kOutput, calls=%fused_computation.88 | convolution fusion | flops 805306368 | bytes 9830400 | tf_op jit(solution)/shard_map/hqtl,hqtd->hld/dot_general | solution.py:184
  128.6 6.1 %multiply_convert_fusion = bf16[3,4,128,2048]{2,3,1,0:T(8,128)(2,1)S(1)} fusion(f32[3,4,128]{2,1,0:T(4,128)S(1)} %fusion.8, bf16[3,2048,128,1]{2,1,3,0:T(8,128)(2,1)S(1)} %bitcast.196, bf16[3,4,128,128]{2,3,1,0:T(8,128)(2,1)S(1)} %bitcast.192, f32[3,4,128,2048]{2,3,1,0:T(8,128)} %get-tuple-element.124, f32[3,4,128]{2,1,0:T(4,128)S(1)} %get-tuple-element.123), kind=kOutput, calls=%fused_computation.2 | convolution fusion | flops 821035008 | bytes 20852736 | tf_op jit(solution)/shard_map/hqtd,hld->hqtl/dot_general | solution.py:180
  134.7 3.6 %fusion.32 = f32[3,2048,128,1]{2,1,3,0:T(8,128)} fusion(bf16[3,4,128,2048]{2,3,1,0:T(8,128)(2,1)S(1)} %multiply_convert_fusion, bf16[3,4,128,128]{2,3,0,1:T(8,128)(2,1)S(1)} %bitcast.189), kind=kOutput, calls=%fused_computation.62 | convolution fusion | flops 805306368 | bytes 9830400 | tf_op jit(solution)/shard_map/hqtl,hqtd->hld/dot_general | solution.py:183
  138.3 2.4 %copy.81 = f32[3,4,4,128,128]{3,4,0,2,1:T(8,128)S(1)} copy(f32[3,4,4,128,128]{4,3,2,1,0:T(8,128)} %bitcast.177) | data formatting | bytes 6291456 | tf_op jit(solution)/shard_map/reshape | solution.py:188
  142.1 3.6 %copy.85 = f32[3,4,4,128,128]{3,4,0,2,1:T(8,128)} copy(f32[3,4,4,128,128]{4,3,2,1,0:T(8,128)} %bitcast.175) | data formatting | bytes 6291456 | tf_op jit(solution)/shard_map/reshape | solution.py:188
  145.6 2.2 convert.33
  148.9 2.3 %collective-permute-start.10 = (bf16[2,3,4,128,128]{3,4,1,2,0:T(8,128)(2,1)}, bf16[2,3,4,128,128]{3,4,1,2,0:T(8,128)(2,1)}, u32[]{:S(2)}, u32[]{:S(2)}) collective-permute-start(bf16[2,3,4,128,128]{3,4,1,2,0:T(8,128)(2,1)} %pad_maximum_fusion.2), channel_id=1, source_target_pairs={{0,4},{4,8},{8,12},{12,16},{16,20},{20,24},{24,28},{1,5},{5,9},{9,... | collective-permute-start | bytes 2359304 | tf_op jit(solution)/shard_map/ppermute | solution.py:85
  154.8 2.0 copy.122
  156.8 8.8 %collective-permute-done.10 = bf16[2,3,4,128,128]{3,4,1,2,0:T(8,128)(2,1)} collective-permute-done((bf16[2,3,4,128,128]{3,4,1,2,0:T(8,128)(2,1)}, bf16[2,3,4,128,128]{3,4,1,2,0:T(8,128)(2,1)}, u32[]{:S(2)}, u32[]{:S(2)}) %collective-permute-start.10) | collective-permute-done | bytes 786464 | tf_op jit(solution)/shard_map/ppermute | solution.py:85
  169.5 16.8 %collective-permute-done.11 = bf16[2,3,4,128,128]{3,4,1,2,0:T(8,128)(2,1)} collective-permute-done((bf16[2,3,4,128,128]{3,4,1,2,0:T(8,128)(2,1)}, bf16[2,3,4,128,128]{3,4,1,2,0:T(8,128)(2,1)}, u32[]{:S(2)}, u32[]{:S(2)}) %collective-permute-start.11) | collective-permute-done | bytes 786464 | tf_op jit(solution)/shard_map/ppermute | solution.py:85
  190.1 3.1 %collective-permute-start.12 = (bf16[2,3,2,128,128]{3,4,1,2,0:T(8,128)(2,1)}, bf16[2,3,2,128,128]{3,4,1,2,0:T(8,128)(2,1)}, u32[]{:S(2)}, u32[]{:S(2)}) collective-permute-start(bf16[2,3,2,128,128]{3,4,1,2,0:T(8,128)(2,1)} %pad_maximum_fusion.5), channel_id=1, source_target_pairs={{0,1},{1,2},{2,3},{4,5},{5,6},{6,7},{8,9},{9,10},{10,11},{12,13},{... | collective-permute-start | bytes 1179656 | tf_op jit(solution)/shard_map/ppermute | solution.py:85
  193.9 4.6 %collective-permute-start.13 = (bf16[2,3,2,128,128]{3,4,1,2,0:T(8,128)(2,1)}, bf16[2,3,2,128,128]{3,4,1,2,0:T(8,128)(2,1)}, u32[]{:S(2)}, u32[]{:S(2)}) collective-permute-start(bf16[2,3,2,128,128]{3,4,1,2,0:T(8,128)(2,1)} %pad_maximum_fusion.6), channel_id=1, source_target_pairs={{1,0},{2,1},{3,2},{5,4},{6,5},{7,6},{9,8},{10,9},{11,10},{13,12},{... | collective-permute-start | bytes 1179656 | tf_op jit(solution)/shard_map/ppermute | solution.py:85
  203.3 11.5 %collective-permute-done.13 = bf16[2,3,2,128,128]{3,4,1,2,0:T(8,128)(2,1)} collective-permute-done((bf16[2,3,2,128,128]{3,4,1,2,0:T(8,128)(2,1)}, bf16[2,3,2,128,128]{3,4,1,2,0:T(8,128)(2,1)}, u32[]{:S(2)}, u32[]{:S(2)}) %collective-permute-start.13) | collective-permute-done | bytes 393248 | tf_op jit(solution)/shard_map/ppermute | solution.py:85
  (111 shorter events, 48.5 us)
Async XLA Ops:
  7.2 15.6 %copy-start.10 = (bf16[96,384]{1,0:T(8,128)(2,1)S(1)}, bf16[96,384]{1,0:T(8,128)(2,1)}, u32[]{:S(2)}) copy-start(bf16[96,384]{1,0:T(8,128)(2,1)} %param.25) | copy-start | bytes 221188
  7.2 108.4 %all-gather.2.cloned.1.call-start = ((), (), s32[]{:S(2)}) async-start(), calls=%async_computation | async-start | bytes 3538944 | tf_op jit(solution)/shard_map/all_gather | solution.py:130
  7.9 14.8 %collective-permute-start.4 = (bf16[96,384]{1,0:T(8,128)(2,1)}, bf16[96,384]{1,0:T(8,128)(2,1)S(1)}, u32[]{:S(2)}, u32[]{:S(2)}) collective-permute-start(bf16[96,384]{1,0:T(8,128)(2,1)} %param.25), channel_id=1, source_target_pairs={{0,2},{1,3},{2,0},{3,1},{4,6},{5,7},{6,4},{7,5},{8,10},{9,11},{10,... | collective-permute-start | bytes 221192 | tf_op jit(solution)/shard_map/ppermute | solution.py:14
  15.9 32.7 %collective-permute-start = (bf16[2,3,2,1,128,128]{4,5,1,3,2,0:T(8,128)(2,1)S(1)}, bf16[2,3,2,1,128,128]{4,5,1,3,2,0:T(8,128)(2,1)S(1)}, u32[]{:S(2)}, u32[]{:S(2)}) collective-permute-start(bf16[2,3,2,1,128,128]{4,5,1,3,2,0:T(8,128)(2,1)S(1)} %get-tuple-element.121), channel_id=1, source_target_pairs={{0,1},{1,2},{2,3},{4,5},{5,6},{6,7},{8,9},{9,10},{10,11},{12,13},{... | collective-permute-start | bytes 1179656 | tf_op jit(solution)/shard_map/ppermute | solution.py:100
  17.8 30.8 %collective-permute-start.1 = (bf16[2,3,2,1,128,128]{4,5,1,3,2,0:T(8,128)(2,1)S(1)}, bf16[2,3,2,1,128,128]{4,5,1,3,2,0:T(8,128)(2,1)S(1)}, u32[]{:S(2)}, u32[]{:S(2)}) collective-permute-start(bf16[2,3,2,1,128,128]{4,5,1,3,2,0:T(8,128)(2,1)S(1)} %get-tuple-element.122), channel_id=1, source_target_pairs={{1,0},{2,1},{3,2},{5,4},{6,5},{7,6},{9,8},{10,9},{11,10},{13,12},{... | collective-permute-start | bytes 1179656 | tf_op jit(solution)/shard_map/ppermute | solution.py:101
  22.8 22.4 %collective-permute-start.5 = (bf16[192,384]{1,0:T(8,128)(2,1)S(1)}, bf16[192,384]{1,0:T(8,128)(2,1)S(1)}, u32[]{:S(2)}, u32[]{:S(2)}) collective-permute-start(bf16[192,384]{1,0:T(8,128)(2,1)S(1)} %maximum_select_fusion.5), channel_id=1, source_target_pairs={{0,1},{1,0},{2,3},{3,2},{4,5},{5,4},{6,7},{7,6},{8,9},{9,8},{10,11... | collective-permute-start | bytes 442376 | tf_op jit(solution)/shard_map/ppermute | solution.py:14
  45.3 27.7 %collective-permute-start.6 = (bf16[384,384]{1,0:T(8,128)(2,1)S(1)}, bf16[384,384]{1,0:T(8,128)(2,1)S(1)}, u32[]{:S(2)}, u32[]{:S(2)}) collective-permute-start(bf16[384,384]{1,0:T(8,128)(2,1)S(1)} %maximum_select_fusion.4), channel_id=1, source_target_pairs={{0,16},{4,20},{8,24},{12,28},{16,0},{20,4},{24,8},{28,12},{1,17},{... | collective-permute-start | bytes 884744 | tf_op jit(solution)/shard_map/ppermute | solution.py:14
  50.1 39.1 %collective-permute-start.2 = (bf16[2,3,1,4,128,128]{4,5,1,3,2,0:T(8,128)(2,1)}, bf16[2,3,1,4,128,128]{4,5,1,3,2,0:T(8,128)(2,1)S(1)}, u32[]{:S(2)}, u32[]{:S(2)}) collective-permute-start(bf16[2,3,1,4,128,128]{4,5,1,3,2,0:T(8,128)(2,1)} %get-tuple-element.113), channel_id=1, source_target_pairs={{0,4},{4,8},{8,12},{12,16},{16,20},{20,24},{24,28},{1,5},{5,9},{9,... | collective-permute-start | bytes 2359304 | tf_op jit(solution)/shard_map/ppermute | solution.py:100
  51.8 37.7 %collective-permute-start.3 = (bf16[2,3,1,4,128,128]{4,5,1,3,2,0:T(8,128)(2,1)}, bf16[2,3,1,4,128,128]{4,5,1,3,2,0:T(8,128)(2,1)S(1)}, u32[]{:S(2)}, u32[]{:S(2)}) collective-permute-start(bf16[2,3,1,4,128,128]{4,5,1,3,2,0:T(8,128)(2,1)} %get-tuple-element.114), channel_id=1, source_target_pairs={{4,0},{8,4},{12,8},{16,12},{20,16},{24,20},{28,24},{5,1},{9,5},{13... | collective-permute-start | bytes 2359304 | tf_op jit(solution)/shard_map/ppermute | solution.py:101
  74.1 10.2 %collective-permute-start.7 = (bf16[768,384]{1,0:T(8,128)(2,1)}, bf16[768,384]{1,0:T(8,128)(2,1)}, u32[]{:S(2)}, u32[]{:S(2)}) collective-permute-start(bf16[768,384]{1,0:T(8,128)(2,1)} %maximum_select_fusion.3), channel_id=1, source_target_pairs={{0,8},{4,12},{8,0},{12,4},{16,24},{20,28},{24,16},{28,20},{1,9},{5... | collective-permute-start | bytes 1769480 | tf_op jit(solution)/shard_map/ppermute | solution.py:14
  75.7 34.9 %collective-permute-start.8 = (bf16[768,384]{1,0:T(8,128)(2,1)}, bf16[768,384]{1,0:T(8,128)(2,1)}, u32[]{:S(2)}, u32[]{:S(2)}) collective-permute-start(bf16[768,384]{1,0:T(8,128)(2,1)} %maximum_select_fusion.3), channel_id=1, source_target_pairs={{0,4},{4,0},{8,12},{12,8},{16,20},{20,16},{24,28},{28,24},{1,5},{5... | collective-permute-start | bytes 1769480 | tf_op jit(solution)/shard_map/ppermute | solution.py:14
  84.3 28.4 %collective-permute-start.9 = (bf16[768,384]{1,0:T(8,128)(2,1)}, bf16[768,384]{1,0:T(8,128)(2,1)}, u32[]{:S(2)}, u32[]{:S(2)}) collective-permute-start(bf16[768,384]{1,0:T(8,128)(2,1)} %collective-permute-done.7), channel_id=1, source_target_pairs={{0,4},{4,0},{8,12},{12,8},{16,20},{20,16},{24,28},{28,24},{1,5},{5... | collective-permute-start | bytes 1769480 | tf_op jit(solution)/shard_map/ppermute | solution.py:14
  119.7 7.7 %slice-start = ((s8[6291456]{0:T(1024)(128)(4,1)}), s8[2097152]{0:T(1024)(128)(4,1)S(1)}, s32[]{:S(2)}) async-start(s8[6291456]{0:T(1024)(128)(4,1)} %bitcast.173), calls=%async_computation.1 | async-start | bytes 4194304
  121.0 6.4 %slice-start.1 = ((s8[6291456]{0:T(1024)(128)(4,1)}), s8[4194304]{0:T(1024)(128)(4,1)S(1)}, s32[]{:S(2)}) async-start(s8[6291456]{0:T(1024)(128)(4,1)} %bitcast.173), calls=%async_computation.2 | async-start | bytes 8388608
  140.7 12.8 %copy-start = (f32[3,4,4,128,128]{3,4,0,2,1:T(8,128)}, f32[3,4,4,128,128]{3,4,0,2,1:T(8,128)S(1)}, u32[]{:S(2)}) copy-start(f32[3,4,4,128,128]{3,4,0,2,1:T(8,128)S(1)} %copy.81) | copy-start | bytes 9437188
  148.9 16.7 %collective-permute-start.10 = (bf16[2,3,4,128,128]{3,4,1,2,0:T(8,128)(2,1)}, bf16[2,3,4,128,128]{3,4,1,2,0:T(8,128)(2,1)}, u32[]{:S(2)}, u32[]{:S(2)}) collective-permute-start(bf16[2,3,4,128,128]{3,4,1,2,0:T(8,128)(2,1)} %pad_maximum_fusion.2), channel_id=1, source_target_pairs={{0,4},{4,8},{8,12},{12,16},{16,20},{20,24},{24,28},{1,5},{5,9},{9,... | collective-permute-start | bytes 2359304 | tf_op jit(solution)/shard_map/ppermute | solution.py:85
  152.1 34.2 %collective-permute-start.11 = (bf16[2,3,4,128,128]{3,4,1,2,0:T(8,128)(2,1)}, bf16[2,3,4,128,128]{3,4,1,2,0:T(8,128)(2,1)}, u32[]{:S(2)}, u32[]{:S(2)}) collective-permute-start(bf16[2,3,4,128,128]{3,4,1,2,0:T(8,128)(2,1)} %pad_maximum_fusion.3), channel_id=1, source_target_pairs={{4,0},{8,4},{12,8},{16,12},{20,16},{24,20},{28,24},{5,1},{9,5},{13... | collective-permute-start | bytes 2359304 | tf_op jit(solution)/shard_map/ppermute | solution.py:85
  154.8 12.1 %slice-start.2 = ((f32[3,4,4,128,128]{3,4,0,2,1:T(8,128)}), f32[3,2,4,128,128]{3,4,0,2,1:T(8,128)S(1)}, s32[]{:S(2)}) async-start(f32[3,4,4,128,128]{3,4,0,2,1:T(8,128)} %copy-done), calls=%async_computation.3 | async-start | bytes 3145728 | tf_op jit(solution)/shard_map/slice | solution.py:111
  187.6 10.9 %slice-start.3 = ((s8[6291456]{0:T(1024)(128)(4,1)}), s8[4194304]{0:T(1024)(128)(4,1)S(1)}, s32[]{:S(2)}) async-start(s8[6291456]{0:T(1024)(128)(4,1)} %bitcast.179), calls=%async_computation.4 | async-start | bytes 8388608
  188.1 10.4 %slice-start.4 = ((s8[6291456]{0:T(1024)(128)(4,1)}), s8[2097152]{0:T(1024)(128)(4,1)S(1)}, s32[]{:S(2)}) async-start(s8[6291456]{0:T(1024)(128)(4,1)} %bitcast.179), calls=%async_computation.5 | async-start | bytes 4194304
  188.3 10.2 %copy-start.7 = (bf16[1,3,4,4,128,128]{5,4,3,2,1,0:T(8,128)(2,1)S(1)}, bf16[1,3,4,4,128,128]{5,4,3,2,1,0:T(8,128)(2,1)}, u32[]{:S(2)}) copy-start(bf16[1,3,4,4,128,128]{5,4,3,2,1,0:T(8,128)(2,1)} %copy.67) | copy-start | bytes 4718596
  190.1 12.1 %collective-permute-start.12 = (bf16[2,3,2,128,128]{3,4,1,2,0:T(8,128)(2,1)}, bf16[2,3,2,128,128]{3,4,1,2,0:T(8,128)(2,1)}, u32[]{:S(2)}, u32[]{:S(2)}) collective-permute-start(bf16[2,3,2,128,128]{3,4,1,2,0:T(8,128)(2,1)} %pad_maximum_fusion.5), channel_id=1, source_target_pairs={{0,1},{1,2},{2,3},{4,5},{5,6},{6,7},{8,9},{9,10},{10,11},{12,13},{... | collective-permute-start | bytes 1179656 | tf_op jit(solution)/shard_map/ppermute | solution.py:85
  193.9 20.9 %collective-permute-start.13 = (bf16[2,3,2,128,128]{3,4,1,2,0:T(8,128)(2,1)}, bf16[2,3,2,128,128]{3,4,1,2,0:T(8,128)(2,1)}, u32[]{:S(2)}, u32[]{:S(2)}) collective-permute-start(bf16[2,3,2,128,128]{3,4,1,2,0:T(8,128)(2,1)} %pad_maximum_fusion.6), channel_id=1, source_target_pairs={{1,0},{2,1},{3,2},{5,4},{6,5},{7,6},{9,8},{10,9},{11,10},{13,12},{... | collective-permute-start | bytes 1179656 | tf_op jit(solution)/shard_map/ppermute | solution.py:85
  203.3 12.8 %copy-start.5 = (f32[3,2,2,128,128]{3,4,0,1,2:T(8,128)}, f32[3,2,2,128,128]{3,4,0,1,2:T(8,128)S(1)}, u32[]{:S(2)}) copy-start(f32[3,2,2,128,128]{3,4,0,1,2:T(8,128)S(1)} %get-tuple-element.116) | copy-start | bytes 2359300
  (7 other events, 23.2 us)
Sparse Core Ops, SparseCore 0:
  9.8 32.4 all-gather.1

commit v13 on v8

--- a/solution.py
+++ b/solution.py
@@ -23,6 +23,7 @@
     ha_bits = [1 << b for b in range(ha.bit_length() - 1)]
     wa_bits = [1 << b for b in range(wa.bit_length() - 1)]
     steps = [("wa", b) for b in reversed(wa_bits)] + [("ha", b) for b in reversed(ha_bits)]
+    steps = steps[:-2] + steps[-2:][::-1]
     buf = doubling_gather(out_proj, steps)
     rows, cols = out_proj.shape
     order = list(reversed(steps))

time: 227 us -> 247 us (1.088)
  waiting for transfers between devices: 92.8 us -> 110 us
    ppermute x5, waiting for transfers between devices: 55.5 us -> 72.3 us  [doubling_gather(): other = lax.ppermute(buf, axis, [(i, i ^ bit) for i in range(count)])]
  transfers between devices with their start and end apart: 14 -> 14, of which waited for: 8 -> 7; matrix products, arithmetic and copies ran while one was open for 20% -> 18% of each run, Pallas kernels for 0% -> 0%
where the time goes in v13:
time: 247 us; the launch traced here: 243 us
  waiting for transfers between devices  110 us (45%)
  other arithmetic  31.8 us (13%)
  starting transfers between devices  31.2 us (13%)
  matrix products  29.5 us (12%)
  local copies, waits for them, and re-layouts  25.8 us (10%)
  between operations  14.7 us (6%)
    ppermute x5, waiting for transfers between devices, doubling_gather(): other = lax.ppermute(buf, axis, [(i, i ^ bit) for i in range(count)])  72.3 us
    ppermute x4, waiting for transfers between devices, passed_along(): lax.ppermute(value, axis, [(source, source + steps) for source in range(f...  36.7 us
    ppermute x4, starting transfers between devices, passed_along(): lax.ppermute(value, axis, [(source, source + steps) for source in range(f...  11.4 us
    ppermute x5, starting transfers between devices, doubling_gather(): other = lax.ppermute(buf, axis, [(i, i ^ bit) for i in range(count)])  9.99 us
    unnamed x39, local copies, waits for them, and re-layouts  9.91 us
    convert_element_type x1, other arithmetic, local(): probs_lo = probs.astype(bf16)  8.49 us
    sub x1, matrix products, local(): scores = scores - jnp.max(scores, axis=-1, keepdims=True)  7.25 us
    dot_general x1, matrix products, local(): jnp.einsum('hqtl,hqtd->hld', probs_lo, grad, preferred_element_type=f32)  6.42 us
  transfers between devices with their start and end apart: 14, of which 7 were waited for; matrix products, arithmetic and copies ran while one was open for 18% of the time, Pallas kernels for 0%

profile of v13, /device:TPU:64, one launch (start us, length us, event | category | flops | bytes accessed | tf_op | source)
XLA Modules:
  0.0 242.7 jit_solution(14532521076998268113)
XLA Ops:
  7.9 5.5 %collective-permute-start.4 = (bf16[96,384]{1,0:T(8,128)(2,1)}, bf16[96,384]{1,0:T(8,128)(2,1)S(1)}, u32[]{:S(2)}, u32[]{:S(2)}) collective-permute-start(bf16[96,384]{1,0:T(8,128)(2,1)} %param.25), channel_id=1, source_target_pairs={{0,2},{1,3},{2,0},{3,1},{4,6},{5,7},{6,4},{7,5},{8,10},{9,11},{10,... | collective-permute-start | bytes 221192 | tf_op jit(solution)/shard_map/ppermute | solution.py:15
  17.8 4.8 %collective-permute-start.1 = (bf16[2,3,2,1,128,128]{4,5,1,3,2,0:T(8,128)(2,1)S(1)}, bf16[2,3,2,1,128,128]{4,5,1,3,2,0:T(8,128)(2,1)S(1)}, u32[]{:S(2)}, u32[]{:S(2)}) collective-permute-start(bf16[2,3,2,1,128,128]{4,5,1,3,2,0:T(8,128)(2,1)S(1)} %get-tuple-element.122), channel_id=1, source_target_pairs={{1,0},{2,1},{3,2},{5,4},{6,5},{7,6},{9,8},{10,9},{11,10},{13,12},{... | collective-permute-start | bytes 1179656 | tf_op jit(solution)/shard_map/ppermute | solution.py:89
  23.0 22.2 %collective-permute-done.5 = bf16[192,384]{1,0:T(8,128)(2,1)S(1)} collective-permute-done((bf16[192,384]{1,0:T(8,128)(2,1)S(1)}, bf16[192,384]{1,0:T(8,128)(2,1)S(1)}, u32[]{:S(2)}, u32[]{:S(2)}) %collective-permute-start.5) | collective-permute-done | bytes 147488 | tf_op jit(solution)/shard_map/ppermute | solution.py:15
  45.3 3.3 %collective-permute-start.6 = (bf16[384,384]{1,0:T(8,128)(2,1)S(1)}, bf16[384,384]{1,0:T(8,128)(2,1)S(1)}, u32[]{:S(2)}, u32[]{:S(2)}) collective-permute-start(bf16[384,384]{1,0:T(8,128)(2,1)S(1)} %maximum_select_fusion.3), channel_id=1, source_target_pairs={{0,16},{4,20},{8,24},{12,28},{16,0},{20,4},{24,8},{28,12},{1,17},{... | collective-permute-start | bytes 884744 | tf_op jit(solution)/shard_map/ppermute | solution.py:15
  53.1 17.6 %collective-permute-done.6 = bf16[384,384]{1,0:T(8,128)(2,1)S(1)} collective-permute-done((bf16[384,384]{1,0:T(8,128)(2,1)S(1)}, bf16[384,384]{1,0:T(8,128)(2,1)S(1)}, u32[]{:S(2)}, u32[]{:S(2)}) %collective-permute-start.6) | collective-permute-done | bytes 294944 | tf_op jit(solution)/shard_map/ppermute | solution.py:15
  72.6 27.5 %collective-permute-done.7 = bf16[768,384]{1,0:T(8,128)(2,1)} collective-permute-done((bf16[768,384]{1,0:T(8,128)(2,1)S(1)}, bf16[768,384]{1,0:T(8,128)(2,1)}, u32[]{:S(2)}, u32[]{:S(2)}) %collective-permute-start.7) | collective-permute-done | bytes 589856 | tf_op jit(solution)/shard_map/ppermute | solution.py:15
  100.1 2.8 %maximum_select_fusion.1 = bf16[1536,384]{1,0:T(8,128)(2,1)} fusion(bf16[768,384]{1,0:T(8,128)(2,1)} %collective-permute-done.7, bf16[768,384]{1,0:T(8,128)(2,1)S(1)} %maximum_select_fusion.2, pred[]{:T(512)S(6)} %eq.22), kind=kLoop, calls=%fused_computation.19 | loop fusion | flops 5308416 | bytes 2359297 | tf_op jit(solution)/shard_map/jit(_where)/select_n | solution.py:17
  108.2 7.2 %fusion.42 = (f32[3,4,128]{2,1,0:T(4,128)S(1)}, f32[3,4,128,2048]{2,3,1,0:T(8,128)}) fusion(pred[4,2048]{1,0:T(4,128)(4,1)S(1)} %bitcast.202, bf16[3,2048,128,1]{2,1,3,0:T(8,128)(2,1)S(1)} %bitcast.193, bf16[3,4,128,128]{2,3,0,1:T(8,128)(2,1)S(1)} %bitcast.188), kind=kOutput, calls=%fused_computation.86 | convolution fusion | flops 817891328 | bytes 14563328 | tf_op jit(solution)/shard_map/sub | solution.py:156
  115.5 8.5 %fusion.5 = bf16[3,4,128,2048]{2,3,1,0:T(8,128)(2,1)} fusion(f32[3,4,128,2048]{2,3,1,0:T(8,128)} %get-tuple-element.124, f32[3,4,128]{2,1,0:T(4,128)S(1)} %get-tuple-element.123), kind=kLoop, calls=%fused_computation.9 | loop fusion | flops 6291456 | bytes 18880512 | tf_op jit(solution)/shard_map/convert_element_type | solution.py:159
  123.9 5.0 %collective-permute-done.8 = bf16[1536,384]{1,0:T(8,128)(2,1)} collective-permute-done((bf16[1536,384]{1,0:T(8,128)(2,1)}, bf16[1536,384]{1,0:T(8,128)(2,1)}, u32[]{:S(2)}, u32[]{:S(2)}) %collective-permute-start.8) | collective-permute-done | bytes 1179680 | tf_op jit(solution)/shard_map/ppermute | solution.py:15
  128.9 3.2 %maximum_select_fusion = bf16[3072,384]{1,0:T(8,128)(2,1)S(1)} fusion(bf16[1536,384]{1,0:T(8,128)(2,1)} %collective-permute-done.8, bf16[1536,384]{1,0:T(8,128)(2,1)} %maximum_select_fusion.1, pred[]{:T(512)S(6)} %eq.21), kind=kLoop, calls=%fused_computation.11 | loop fusion | flops 10616832 | bytes 4718593 | tf_op jit(solution)/shard_map/jit(_where)/select_n | solution.py:17
  132.5 4.1 %fusion.9 = bf16[512,384]{0,1:T(8,128)(2,1)} fusion(bf16[3072,384]{1,0:T(8,128)(2,1)S(1)} %bitcast.187, bf16[512,3072]{1,0:T(8,128)(2,1)} %bitcast.203), kind=kOutput, calls=%fused_computation.18 | convolution fusion | flops 1208156160 | bytes 5898240 | tf_op jit(solution)/shard_map/dot_general | solution.py:161
  137.9 6.4 %fusion.47 = f32[3,2048,128,1]{2,1,3,0:T(8,128)} fusion(bf16[3,4,128,2048]{2,3,1,0:T(8,128)(2,1)} %fusion.5, bf16[3,4,128,128]{2,3,1,0:T(8,128)(2,1)S(1)} %bitcast.190), kind=kOutput, calls=%fused_computation.87 | convolution fusion | flops 805306368 | bytes 9830400 | tf_op jit(solution)/shard_map/hqtl,hqtd->hld/dot_general | solution.py:172
  145.5 5.9 %multiply_convert_fusion = bf16[3,4,128,2048]{2,3,1,0:T(8,128)(2,1)S(1)} fusion(f32[3,4,128]{2,1,0:T(4,128)S(1)} %fusion.8, bf16[3,2048,128,1]{2,1,3,0:T(8,128)(2,1)S(1)} %bitcast.196, bf16[3,4,128,128]{2,3,1,0:T(8,128)(2,1)S(1)} %bitcast.192, f32[3,4,128,2048]{2,3,1,0:T(8,128)} %get-tuple-element.124, f32[3,4,128]{2,1,0:T(4,128)S(1)} %get-tuple-element.123), kind=kOutput, calls=%fused_computation.2 | convolution fusion | flops 821035008 | bytes 20852736 | tf_op jit(solution)/shard_map/hqtd,hld->hqtl/dot_general | solution.py:168
  151.4 3.6 %fusion.32 = f32[3,2048,128,1]{2,1,3,0:T(8,128)} fusion(bf16[3,4,128,2048]{2,3,1,0:T(8,128)(2,1)S(1)} %multiply_convert_fusion, bf16[3,4,128,128]{2,3,0,1:T(8,128)(2,1)S(1)} %bitcast.189), kind=kOutput, calls=%fused_computation.61 | convolution fusion | flops 805306368 | bytes 9830400 | tf_op jit(solution)/shard_map/hqtl,hqtd->hld/dot_general | solution.py:171
  155.1 2.6 %copy.81 = f32[3,4,4,128,128]{3,4,0,2,1:T(8,128)S(1)} copy(f32[3,4,4,128,128]{4,3,2,1,0:T(8,128)} %bitcast.177) | data formatting | bytes 6291456 | tf_op jit(solution)/shard_map/reshape | solution.py:176
  159.0 3.6 %copy.85 = f32[3,4,4,128,128]{3,4,0,2,1:T(8,128)} copy(f32[3,4,4,128,128]{4,3,2,1,0:T(8,128)} %bitcast.175) | data formatting | bytes 6291456 | tf_op jit(solution)/shard_map/reshape | solution.py:176
  162.6 2.2 convert.33
  165.8 2.3 collective-permute-start.9
  173.7 7.9 %collective-permute-done.9 = bf16[2,3,4,128,128]{3,4,1,2,0:T(8,128)(2,1)} collective-permute-done((bf16[2,3,4,128,128]{3,4,1,2,0:T(8,128)(2,1)}, bf16[2,3,4,128,128]{3,4,1,2,0:T(8,128)(2,1)}, u32[]{:S(2)}, u32[]{:S(2)}) %collective-permute-start.9) | collective-permute-done | bytes 786464 | tf_op jit(solution)/shard_map/ppermute | solution.py:73
  185.6 17.4 %collective-permute-done.10 = bf16[2,3,4,128,128]{3,4,1,2,0:T(8,128)(2,1)} collective-permute-done((bf16[2,3,4,128,128]{3,4,1,2,0:T(8,128)(2,1)}, bf16[2,3,4,128,128]{3,4,1,2,0:T(8,128)(2,1)}, u32[]{:S(2)}, u32[]{:S(2)}) %collective-permute-start.10) | collective-permute-done | bytes 786464 | tf_op jit(solution)/shard_map/ppermute | solution.py:73
  206.7 2.9 %collective-permute-start.11 = (bf16[2,3,2,128,128]{3,4,1,2,0:T(8,128)(2,1)}, bf16[2,3,2,128,128]{3,4,1,2,0:T(8,128)(2,1)}, u32[]{:S(2)}, u32[]{:S(2)}) collective-permute-start(bf16[2,3,2,128,128]{3,4,1,2,0:T(8,128)(2,1)} %pad_maximum_fusion.5), channel_id=1, source_target_pairs={{0,1},{1,2},{2,3},{4,5},{5,6},{6,7},{8,9},{9,10},{10,11},{12,13},{... | collective-permute-start | bytes 1179656 | tf_op jit(solution)/shard_map/ppermute | solution.py:73
  210.4 4.8 %collective-permute-start.12 = (bf16[2,3,2,128,128]{3,4,1,2,0:T(8,128)(2,1)}, bf16[2,3,2,128,128]{3,4,1,2,0:T(8,128)(2,1)}, u32[]{:S(2)}, u32[]{:S(2)}) collective-permute-start(bf16[2,3,2,128,128]{3,4,1,2,0:T(8,128)(2,1)} %pad_maximum_fusion.6), channel_id=1, source_target_pairs={{1,0},{2,1},{3,2},{5,4},{6,5},{7,6},{9,8},{10,9},{11,10},{13,12},{... | collective-permute-start | bytes 1179656 | tf_op jit(solution)/shard_map/ppermute | solution.py:73
  219.1 11.4 %collective-permute-done.12 = bf16[2,3,2,128,128]{3,4,1,2,0:T(8,128)(2,1)} collective-permute-done((bf16[2,3,2,128,128]{3,4,1,2,0:T(8,128)(2,1)}, bf16[2,3,2,128,128]{3,4,1,2,0:T(8,128)(2,1)}, u32[]{:S(2)}, u32[]{:S(2)}) %collective-permute-start.12) | collective-permute-done | bytes 393248 | tf_op jit(solution)/shard_map/ppermute | solution.py:73
  (108 shorter events, 45.4 us)
Async XLA Ops:
  7.2 15.6 %copy-start.10 = (bf16[96,384]{1,0:T(8,128)(2,1)S(1)}, bf16[96,384]{1,0:T(8,128)(2,1)}, u32[]{:S(2)}) copy-start(bf16[96,384]{1,0:T(8,128)(2,1)} %param.25) | copy-start | bytes 221188
  7.2 125.3 %all-gather.2.cloned.1.call-start = ((), (), s32[]{:S(2)}) async-start(), calls=%async_computation | async-start | bytes 3538944 | tf_op jit(solution)/shard_map/all_gather | solution.py:118
  7.9 14.8 %collective-permute-start.4 = (bf16[96,384]{1,0:T(8,128)(2,1)}, bf16[96,384]{1,0:T(8,128)(2,1)S(1)}, u32[]{:S(2)}, u32[]{:S(2)}) collective-permute-start(bf16[96,384]{1,0:T(8,128)(2,1)} %param.25), channel_id=1, source_target_pairs={{0,2},{1,3},{2,0},{3,1},{4,6},{5,7},{6,4},{7,5},{8,10},{9,11},{10,... | collective-permute-start | bytes 221192 | tf_op jit(solution)/shard_map/ppermute | solution.py:15
  15.9 32.7 %collective-permute-start = (bf16[2,3,2,1,128,128]{4,5,1,3,2,0:T(8,128)(2,1)S(1)}, bf16[2,3,2,1,128,128]{4,5,1,3,2,0:T(8,128)(2,1)S(1)}, u32[]{:S(2)}, u32[]{:S(2)}) collective-permute-start(bf16[2,3,2,1,128,128]{4,5,1,3,2,0:T(8,128)(2,1)S(1)} %get-tuple-element.121), channel_id=1, source_target_pairs={{0,1},{1,2},{2,3},{4,5},{5,6},{6,7},{8,9},{9,10},{10,11},{12,13},{... | collective-permute-start | bytes 1179656 | tf_op jit(solution)/shard_map/ppermute | solution.py:88
  17.8 30.8 %collective-permute-start.1 = (bf16[2,3,2,1,128,128]{4,5,1,3,2,0:T(8,128)(2,1)S(1)}, bf16[2,3,2,1,128,128]{4,5,1,3,2,0:T(8,128)(2,1)S(1)}, u32[]{:S(2)}, u32[]{:S(2)}) collective-permute-start(bf16[2,3,2,1,128,128]{4,5,1,3,2,0:T(8,128)(2,1)S(1)} %get-tuple-element.122), channel_id=1, source_target_pairs={{1,0},{2,1},{3,2},{5,4},{6,5},{7,6},{9,8},{10,9},{11,10},{13,12},{... | collective-permute-start | bytes 1179656 | tf_op jit(solution)/shard_map/ppermute | solution.py:89
  22.8 22.4 %collective-permute-start.5 = (bf16[192,384]{1,0:T(8,128)(2,1)S(1)}, bf16[192,384]{1,0:T(8,128)(2,1)S(1)}, u32[]{:S(2)}, u32[]{:S(2)}) collective-permute-start(bf16[192,384]{1,0:T(8,128)(2,1)S(1)} %maximum_select_fusion.4), channel_id=1, source_target_pairs={{0,1},{1,0},{2,3},{3,2},{4,5},{5,4},{6,7},{7,6},{8,9},{9,8},{10,11... | collective-permute-start | bytes 442376 | tf_op jit(solution)/shard_map/ppermute | solution.py:15
  45.3 25.4 %collective-permute-start.6 = (bf16[384,384]{1,0:T(8,128)(2,1)S(1)}, bf16[384,384]{1,0:T(8,128)(2,1)S(1)}, u32[]{:S(2)}, u32[]{:S(2)}) collective-permute-start(bf16[384,384]{1,0:T(8,128)(2,1)S(1)} %maximum_select_fusion.3), channel_id=1, source_target_pairs={{0,16},{4,20},{8,24},{12,28},{16,0},{20,4},{24,8},{28,12},{1,17},{... | collective-permute-start | bytes 884744 | tf_op jit(solution)/shard_map/ppermute | solution.py:15
  50.1 53.8 %collective-permute-start.2 = (bf16[2,3,1,4,128,128]{4,5,1,3,2,0:T(8,128)(2,1)}, bf16[2,3,1,4,128,128]{4,5,1,3,2,0:T(8,128)(2,1)S(1)}, u32[]{:S(2)}, u32[]{:S(2)}) collective-permute-start(bf16[2,3,1,4,128,128]{4,5,1,3,2,0:T(8,128)(2,1)} %get-tuple-element.113), channel_id=1, source_target_pairs={{0,4},{4,8},{8,12},{12,16},{16,20},{20,24},{24,28},{1,5},{5,9},{9,... | collective-permute-start | bytes 2359304 | tf_op jit(solution)/shard_map/ppermute | solution.py:88
  51.8 52.1 %collective-permute-start.3 = (bf16[2,3,1,4,128,128]{4,5,1,3,2,0:T(8,128)(2,1)}, bf16[2,3,1,4,128,128]{4,5,1,3,2,0:T(8,128)(2,1)}, u32[]{:S(2)}, u32[]{:S(2)}) collective-permute-start(bf16[2,3,1,4,128,128]{4,5,1,3,2,0:T(8,128)(2,1)} %get-tuple-element.114), channel_id=1, source_target_pairs={{4,0},{8,4},{12,8},{16,12},{20,16},{24,20},{28,24},{5,1},{9,5},{13... | collective-permute-start | bytes 2359304 | tf_op jit(solution)/shard_map/ppermute | solution.py:89
  71.0 29.1 %collective-permute-start.7 = (bf16[768,384]{1,0:T(8,128)(2,1)S(1)}, bf16[768,384]{1,0:T(8,128)(2,1)}, u32[]{:S(2)}, u32[]{:S(2)}) collective-permute-start(bf16[768,384]{1,0:T(8,128)(2,1)S(1)} %maximum_select_fusion.2), channel_id=1, source_target_pairs={{0,4},{4,0},{8,12},{12,8},{16,20},{20,16},{24,28},{28,24},{1,5},{5... | collective-permute-start | bytes 1769480 | tf_op jit(solution)/shard_map/ppermute | solution.py:15
  102.9 26.1 %collective-permute-start.8 = (bf16[1536,384]{1,0:T(8,128)(2,1)}, bf16[1536,384]{1,0:T(8,128)(2,1)}, u32[]{:S(2)}, u32[]{:S(2)}) collective-permute-start(bf16[1536,384]{1,0:T(8,128)(2,1)} %maximum_select_fusion.1), channel_id=1, source_target_pairs={{0,8},{4,12},{8,0},{12,4},{16,24},{20,28},{24,16},{28,20},{1,9},{5... | collective-permute-start | bytes 3538952 | tf_op jit(solution)/shard_map/ppermute | solution.py:15
  108.2 7.3 %copy-start.6 = (bf16[1,3,4,4,128,128]{5,4,3,2,1,0:T(8,128)(2,1)}, bf16[1,3,4,4,128,128]{5,4,3,2,1,0:T(8,128)(2,1)S(1)}, u32[]{:S(2)}) copy-start(bf16[1,3,4,4,128,128]{5,4,3,2,1,0:T(8,128)(2,1)S(1)} %copy.67) | copy-start | bytes 4718596
  136.6 7.8 %slice-start = ((s8[6291456]{0:T(1024)(128)(4,1)}), s8[2097152]{0:T(1024)(128)(4,1)S(1)}, s32[]{:S(2)}) async-start(s8[6291456]{0:T(1024)(128)(4,1)} %bitcast.173), calls=%async_computation.1 | async-start | bytes 4194304
  137.9 6.4 %slice-start.1 = ((s8[6291456]{0:T(1024)(128)(4,1)}), s8[4194304]{0:T(1024)(128)(4,1)S(1)}, s32[]{:S(2)}) async-start(s8[6291456]{0:T(1024)(128)(4,1)} %bitcast.173), calls=%async_computation.2 | async-start | bytes 8388608
  157.7 12.8 %copy-start = (f32[3,4,4,128,128]{3,4,0,2,1:T(8,128)}, f32[3,4,4,128,128]{3,4,0,2,1:T(8,128)S(1)}, u32[]{:S(2)}) copy-start(f32[3,4,4,128,128]{3,4,0,2,1:T(8,128)S(1)} %copy.81) | copy-start | bytes 9437188
  165.8 15.9 %collective-permute-start.9 = (bf16[2,3,4,128,128]{3,4,1,2,0:T(8,128)(2,1)}, bf16[2,3,4,128,128]{3,4,1,2,0:T(8,128)(2,1)}, u32[]{:S(2)}, u32[]{:S(2)}) collective-permute-start(bf16[2,3,4,128,128]{3,4,1,2,0:T(8,128)(2,1)} %pad_maximum_fusion.2), channel_id=1, source_target_pairs={{0,4},{4,8},{8,12},{12,16},{16,20},{20,24},{24,28},{1,5},{5,9},{9,... | collective-permute-start | bytes 2359304 | tf_op jit(solution)/shard_map/ppermute | solution.py:73
  169.1 33.9 %collective-permute-start.10 = (bf16[2,3,4,128,128]{3,4,1,2,0:T(8,128)(2,1)}, bf16[2,3,4,128,128]{3,4,1,2,0:T(8,128)(2,1)}, u32[]{:S(2)}, u32[]{:S(2)}) collective-permute-start(bf16[2,3,4,128,128]{3,4,1,2,0:T(8,128)(2,1)} %pad_maximum_fusion.3), channel_id=1, source_target_pairs={{4,0},{8,4},{12,8},{16,12},{20,16},{24,20},{28,24},{5,1},{9,5},{13... | collective-permute-start | bytes 2359304 | tf_op jit(solution)/shard_map/ppermute | solution.py:73
  171.7 11.2 %slice-start.2 = ((f32[3,4,4,128,128]{3,4,0,2,1:T(8,128)}), f32[3,2,4,128,128]{3,4,0,2,1:T(8,128)S(1)}, s32[]{:S(2)}) async-start(f32[3,4,4,128,128]{3,4,0,2,1:T(8,128)} %copy-done), calls=%async_computation.3 | async-start | bytes 3145728 | tf_op jit(solution)/shard_map/slice | solution.py:99
  204.3 10.9 %slice-start.3 = ((s8[6291456]{0:T(1024)(128)(4,1)}), s8[4194304]{0:T(1024)(128)(4,1)S(1)}, s32[]{:S(2)}) async-start(s8[6291456]{0:T(1024)(128)(4,1)} %bitcast.179), calls=%async_computation.4 | async-start | bytes 8388608
  204.7 10.4 %slice-start.4 = ((s8[6291456]{0:T(1024)(128)(4,1)}), s8[2097152]{0:T(1024)(128)(4,1)S(1)}, s32[]{:S(2)}) async-start(s8[6291456]{0:T(1024)(128)(4,1)} %bitcast.179), calls=%async_computation.5 | async-start | bytes 4194304
  204.9 10.3 %copy-start.7 = (bf16[1,3,4,4,128,128]{5,4,3,2,1,0:T(8,128)(2,1)S(1)}, bf16[1,3,4,4,128,128]{5,4,3,2,1,0:T(8,128)(2,1)}, u32[]{:S(2)}) copy-start(bf16[1,3,4,4,128,128]{5,4,3,2,1,0:T(8,128)(2,1)} %copy-done.6) | copy-start | bytes 4718596
  206.7 11.2 %collective-permute-start.11 = (bf16[2,3,2,128,128]{3,4,1,2,0:T(8,128)(2,1)}, bf16[2,3,2,128,128]{3,4,1,2,0:T(8,128)(2,1)}, u32[]{:S(2)}, u32[]{:S(2)}) collective-permute-start(bf16[2,3,2,128,128]{3,4,1,2,0:T(8,128)(2,1)} %pad_maximum_fusion.5), channel_id=1, source_target_pairs={{0,1},{1,2},{2,3},{4,5},{5,6},{6,7},{8,9},{9,10},{10,11},{12,13},{... | collective-permute-start | bytes 1179656 | tf_op jit(solution)/shard_map/ppermute | solution.py:73
  210.4 20.1 %collective-permute-start.12 = (bf16[2,3,2,128,128]{3,4,1,2,0:T(8,128)(2,1)}, bf16[2,3,2,128,128]{3,4,1,2,0:T(8,128)(2,1)}, u32[]{:S(2)}, u32[]{:S(2)}) collective-permute-start(bf16[2,3,2,128,128]{3,4,1,2,0:T(8,128)(2,1)} %pad_maximum_fusion.6), channel_id=1, source_target_pairs={{1,0},{2,1},{3,2},{5,4},{6,5},{7,6},{9,8},{10,9},{11,10},{13,12},{... | collective-permute-start | bytes 1179656 | tf_op jit(solution)/shard_map/ppermute | solution.py:73
  219.1 12.6 %copy-start.5 = (f32[3,2,2,128,128]{3,4,0,1,2:T(8,128)}, f32[3,2,2,128,128]{3,4,0,1,2:T(8,128)S(1)}, u32[]{:S(2)}) copy-start(f32[3,2,2,128,128]{3,4,0,1,2:T(8,128)S(1)} %get-tuple-element.116) | copy-start | bytes 2359300
  (6 other events, 17.4 us)
Sparse Core Ops, SparseCore 0:
  9.8 32.4 all-gather.1

commit v14 on v8

--- a/solution.py
+++ b/solution.py
@@ -22,7 +22,7 @@
     ha, wa = lax.axis_size("ha"), lax.axis_size("wa")
     ha_bits = [1 << b for b in range(ha.bit_length() - 1)]
     wa_bits = [1 << b for b in range(wa.bit_length() - 1)]
-    steps = [("wa", b) for b in reversed(wa_bits)] + [("ha", b) for b in reversed(ha_bits)]
+    steps = [("wa", b) for b in wa_bits] + [("ha", b) for b in reversed(ha_bits)]
     buf = doubling_gather(out_proj, steps)
     rows, cols = out_proj.shape
     order = list(reversed(steps))

time: 227 us -> 233 us (1.026)
  starting transfers between devices: 30.2 us -> 37.6 us
  waiting for transfers between devices: 92.8 us -> 90.4 us
    ppermute x5, waiting for transfers between devices: 55.5 us -> 45.9 us  [doubling_gather(): other = lax.ppermute(buf, axis, [(i, i ^ bit) for i in range(count)])]
    ppermute x5, starting transfers between devices: 8.95 us -> 14.4 us  [doubling_gather(): other = lax.ppermute(buf, axis, [(i, i ^ bit) for i in range(count)])]
    ppermute x2, starting transfers between devices: 3.68 us -> 7.83 us  [extended_2(): before = lax.ppermute(last, axis, up)]
    ppermute x2, waiting for transfers between devices: 1.61 us -> 5.31 us  [extended_2(): after = lax.ppermute(first, axis, down)]
    ppermute x4, waiting for transfers between devices: 34.9 us -> 38.5 us  [passed_along(): lax.ppermute(value, axis, [(source, source + steps) for source in range(f...]
    ppermute x2, starting transfers between devices: 6.13 us -> 3.21 us  [extended_2(): after = lax.ppermute(first, axis, down)]
  transfers between devices with their start and end apart: 14 -> 14, of which waited for: 8 -> 9; matrix products, arithmetic and copies ran while one was open for 20% -> 19% of each run, Pallas kernels for 0% -> 0%
where the time goes in v14:
time: 233 us; the launch traced here: 230 us
  waiting for transfers between devices  90.4 us (39%)
  starting transfers between devices  37.6 us (16%)
  other arithmetic  31.8 us (14%)
  matrix products  29.5 us (13%)
  local copies, waits for them, and re-layouts  25.7 us (11%)
  between operations  14.6 us (6%)
    ppermute x5, waiting for transfers between devices, doubling_gather(): other = lax.ppermute(buf, axis, [(i, i ^ bit) for i in range(count)])  45.9 us
    ppermute x4, waiting for transfers between devices, passed_along(): lax.ppermute(value, axis, [(source, source + steps) for source in range(f...  38.5 us
    ppermute x5, starting transfers between devices, doubling_gather(): other = lax.ppermute(buf, axis, [(i, i ^ bit) for i in range(count)])  14.4 us
    ppermute x4, starting transfers between devices, passed_along(): lax.ppermute(value, axis, [(source, source + steps) for source in range(f...  12.1 us
    unnamed x39, local copies, waits for them, and re-layouts  9.91 us
    convert_element_type x1, other arithmetic, local(): probs_lo = probs.astype(bf16)  8.49 us
    ppermute x2, starting transfers between devices, extended_2(): before = lax.ppermute(last, axis, up)  7.83 us
    sub x1, matrix products, local(): scores = scores - jnp.max(scores, axis=-1, keepdims=True)  7.24 us
  transfers between devices with their start and end apart: 14, of which 9 were waited for; matrix products, arithmetic and copies ran while one was open for 19% of the time, Pallas kernels for 0%

profile of v14, /device:TPU:64, one launch (start us, length us, event | category | flops | bytes accessed | tf_op | source)
XLA Modules:
  0.0 229.7 jit_solution(10084945629517779415)
XLA Ops:
  11.9 6.5 %collective-permute-start = (bf16[2,3,2,1,128,128]{4,5,1,3,2,0:T(8,128)(2,1)S(1)}, bf16[2,3,2,1,128,128]{4,5,1,3,2,0:T(8,128)(2,1)S(1)}, u32[]{:S(2)}, u32[]{:S(2)}) collective-permute-start(bf16[2,3,2,1,128,128]{4,5,1,3,2,0:T(8,128)(2,1)S(1)} %get-tuple-element.121), channel_id=1, source_target_pairs={{0,1},{1,2},{2,3},{4,5},{5,6},{6,7},{8,9},{9,10},{10,11},{12,13},{... | collective-permute-start | bytes 1179656 | tf_op jit(solution)/shard_map/ppermute | solution.py:87
  20.4 3.9 %collective-permute-start.5 = (bf16[192,384]{1,0:T(8,128)(2,1)S(1)}, bf16[192,384]{1,0:T(8,128)(2,1)S(1)}, u32[]{:S(2)}, u32[]{:S(2)}) collective-permute-start(bf16[192,384]{1,0:T(8,128)(2,1)S(1)} %maximum_select_fusion.4), channel_id=1, source_target_pairs={{0,2},{1,3},{2,0},{3,1},{4,6},{5,7},{6,4},{7,5},{8,10},{9,11},{10,... | collective-permute-start | bytes 442376 | tf_op jit(solution)/shard_map/ppermute | solution.py:15
  24.4 16.8 %collective-permute-done.5 = bf16[192,384]{1,0:T(8,128)(2,1)S(1)} collective-permute-done((bf16[192,384]{1,0:T(8,128)(2,1)S(1)}, bf16[192,384]{1,0:T(8,128)(2,1)S(1)}, u32[]{:S(2)}, u32[]{:S(2)}) %collective-permute-start.5) | collective-permute-done | bytes 147488 | tf_op jit(solution)/shard_map/ppermute | solution.py:15
  41.3 3.3 %collective-permute-start.6 = (bf16[384,384]{1,0:T(8,128)(2,1)S(1)}, bf16[384,384]{1,0:T(8,128)(2,1)S(1)}, u32[]{:S(2)}, u32[]{:S(2)}) collective-permute-start(bf16[384,384]{1,0:T(8,128)(2,1)S(1)} %maximum_select_fusion.3), channel_id=1, source_target_pairs={{0,16},{4,20},{8,24},{12,28},{16,0},{20,4},{24,8},{28,12},{1,17},{... | collective-permute-start | bytes 884744 | tf_op jit(solution)/shard_map/ppermute | solution.py:15
  44.6 2.7 %collective-permute-done.1 = bf16[2,3,2,1,128,128]{4,5,1,3,2,0:T(8,128)(2,1)S(1)} collective-permute-done((bf16[2,3,2,1,128,128]{4,5,1,3,2,0:T(8,128)(2,1)S(1)}, bf16[2,3,2,1,128,128]{4,5,1,3,2,0:T(8,128)(2,1)S(1)}, u32[]{:S(2)}, u32[]{:S(2)}) %collective-permute-start.1) | collective-permute-done | bytes 393248 | tf_op jit(solution)/shard_map/ppermute | solution.py:88
  51.6 5.8 %collective-permute-start.7 = (bf16[768,384]{1,0:T(8,128)(2,1)S(1)}, bf16[768,384]{1,0:T(8,128)(2,1)}, u32[]{:S(2)}, u32[]{:S(2)}) collective-permute-start(bf16[768,384]{1,0:T(8,128)(2,1)S(1)} %maximum_select_fusion.2), channel_id=1, source_target_pairs={{0,8},{4,12},{8,0},{12,4},{16,24},{20,28},{24,16},{28,20},{1,9},{5... | collective-permute-start | bytes 1769480 | tf_op jit(solution)/shard_map/ppermute | solution.py:15
  59.0 23.5 %collective-permute-done.7 = bf16[768,384]{1,0:T(8,128)(2,1)} collective-permute-done((bf16[768,384]{1,0:T(8,128)(2,1)S(1)}, bf16[768,384]{1,0:T(8,128)(2,1)}, u32[]{:S(2)}, u32[]{:S(2)}) %collective-permute-start.7) | collective-permute-done | bytes 589856 | tf_op jit(solution)/shard_map/ppermute | solution.py:15
  82.5 2.8 %maximum_select_fusion.1 = bf16[1536,384]{1,0:T(8,128)(2,1)} fusion(bf16[768,384]{1,0:T(8,128)(2,1)} %collective-permute-done.7, bf16[768,384]{1,0:T(8,128)(2,1)S(1)} %maximum_select_fusion.2, pred[]{:T(512)S(6)} %eq.22), kind=kLoop, calls=%fused_computation.19 | loop fusion | flops 5308416 | bytes 2359297 | tf_op jit(solution)/shard_map/jit(_where)/select_n | solution.py:17
  85.3 2.6 %collective-permute-done.3 = bf16[2,3,1,4,128,128]{4,5,1,3,2,0:T(8,128)(2,1)} collective-permute-done((bf16[2,3,1,4,128,128]{4,5,1,3,2,0:T(8,128)(2,1)}, bf16[2,3,1,4,128,128]{4,5,1,3,2,0:T(8,128)(2,1)}, u32[]{:S(2)}, u32[]{:S(2)}) %collective-permute-start.3) | collective-permute-done | bytes 786464 | tf_op jit(solution)/shard_map/ppermute | solution.py:88
  92.2 7.2 %fusion.42 = (f32[3,4,128]{2,1,0:T(4,128)S(1)}, f32[3,4,128,2048]{2,3,1,0:T(8,128)}) fusion(pred[4,2048]{1,0:T(4,128)(4,1)S(1)} %bitcast.202, bf16[3,2048,128,1]{2,1,3,0:T(8,128)(2,1)S(1)} %bitcast.193, bf16[3,4,128,128]{2,3,0,1:T(8,128)(2,1)S(1)} %bitcast.188), kind=kOutput, calls=%fused_computation.86 | convolution fusion | flops 817891328 | bytes 14563328 | tf_op jit(solution)/shard_map/sub | solution.py:155
  99.4 8.5 %fusion.5 = bf16[3,4,128,2048]{2,3,1,0:T(8,128)(2,1)} fusion(f32[3,4,128,2048]{2,3,1,0:T(8,128)} %get-tuple-element.124, f32[3,4,128]{2,1,0:T(4,128)S(1)} %get-tuple-element.123), kind=kLoop, calls=%fused_computation.9 | loop fusion | flops 6291456 | bytes 18880512 | tf_op jit(solution)/shard_map/convert_element_type | solution.py:158
  107.9 5.6 %collective-permute-done.8 = bf16[1536,384]{1,0:T(8,128)(2,1)} collective-permute-done((bf16[1536,384]{1,0:T(8,128)(2,1)}, bf16[1536,384]{1,0:T(8,128)(2,1)}, u32[]{:S(2)}, u32[]{:S(2)}) %collective-permute-start.8) | collective-permute-done | bytes 1179680 | tf_op jit(solution)/shard_map/ppermute | solution.py:15
  113.5 3.2 %maximum_select_fusion = bf16[3072,384]{1,0:T(8,128)(2,1)S(1)} fusion(bf16[1536,384]{1,0:T(8,128)(2,1)} %collective-permute-done.8, bf16[1536,384]{1,0:T(8,128)(2,1)} %maximum_select_fusion.1, pred[]{:T(512)S(6)} %eq.21), kind=kLoop, calls=%fused_computation.11 | loop fusion | flops 10616832 | bytes 4718593 | tf_op jit(solution)/shard_map/jit(_where)/select_n | solution.py:17
  116.9 4.1 %fusion.9 = bf16[512,384]{0,1:T(8,128)(2,1)} fusion(bf16[3072,384]{1,0:T(8,128)(2,1)S(1)} %bitcast.187, bf16[512,3072]{1,0:T(8,128)(2,1)} %bitcast.203), kind=kOutput, calls=%fused_computation.18 | convolution fusion | flops 1208156160 | bytes 5898240 | tf_op jit(solution)/shard_map/dot_general | solution.py:160
  122.3 6.4 %fusion.47 = f32[3,2048,128,1]{2,1,3,0:T(8,128)} fusion(bf16[3,4,128,2048]{2,3,1,0:T(8,128)(2,1)} %fusion.5, bf16[3,4,128,128]{2,3,1,0:T(8,128)(2,1)S(1)} %bitcast.190), kind=kOutput, calls=%fused_computation.87 | convolution fusion | flops 805306368 | bytes 9830400 | tf_op jit(solution)/shard_map/hqtl,hqtd->hld/dot_general | solution.py:171
  129.9 5.9 %multiply_convert_fusion = bf16[3,4,128,2048]{2,3,1,0:T(8,128)(2,1)S(1)} fusion(f32[3,4,128]{2,1,0:T(4,128)S(1)} %fusion.8, bf16[3,2048,128,1]{2,1,3,0:T(8,128)(2,1)S(1)} %bitcast.196, bf16[3,4,128,128]{2,3,1,0:T(8,128)(2,1)S(1)} %bitcast.192, f32[3,4,128,2048]{2,3,1,0:T(8,128)} %get-tuple-element.124, f32[3,4,128]{2,1,0:T(4,128)S(1)} %get-tuple-element.123), kind=kOutput, calls=%fused_computation.2 | convolution fusion | flops 821035008 | bytes 20852736 | tf_op jit(solution)/shard_map/hqtd,hld->hqtl/dot_general | solution.py:167
  135.9 3.6 %fusion.32 = f32[3,2048,128,1]{2,1,3,0:T(8,128)} fusion(bf16[3,4,128,2048]{2,3,1,0:T(8,128)(2,1)S(1)} %multiply_convert_fusion, bf16[3,4,128,128]{2,3,0,1:T(8,128)(2,1)S(1)} %bitcast.189), kind=kOutput, calls=%fused_computation.61 | convolution fusion | flops 805306368 | bytes 9830400 | tf_op jit(solution)/shard_map/hqtl,hqtd->hld/dot_general | solution.py:170
  139.5 2.6 %copy.81 = f32[3,4,4,128,128]{3,4,0,2,1:T(8,128)S(1)} copy(f32[3,4,4,128,128]{4,3,2,1,0:T(8,128)} %bitcast.177) | data formatting | bytes 6291456 | tf_op jit(solution)/shard_map/reshape | solution.py:175
  143.4 3.6 %copy.85 = f32[3,4,4,128,128]{3,4,0,2,1:T(8,128)} copy(f32[3,4,4,128,128]{4,3,2,1,0:T(8,128)} %bitcast.175) | data formatting | bytes 6291456 | tf_op jit(solution)/shard_map/reshape | solution.py:175
  150.2 3.1 %collective-permute-start.9 = (bf16[2,3,4,128,128]{3,4,1,2,0:T(8,128)(2,1)}, bf16[2,3,4,128,128]{3,4,1,2,0:T(8,128)(2,1)}, u32[]{:S(2)}, u32[]{:S(2)}) collective-permute-start(bf16[2,3,4,128,128]{3,4,1,2,0:T(8,128)(2,1)} %pad_maximum_fusion.2), channel_id=1, source_target_pairs={{0,4},{4,8},{8,12},{12,16},{16,20},{20,24},{24,28},{1,5},{5,9},{9,... | collective-permute-start | bytes 2359304 | tf_op jit(solution)/shard_map/ppermute | solution.py:72
  158.9 10.2 %collective-permute-done.9 = bf16[2,3,4,128,128]{3,4,1,2,0:T(8,128)(2,1)} collective-permute-done((bf16[2,3,4,128,128]{3,4,1,2,0:T(8,128)(2,1)}, bf16[2,3,4,128,128]{3,4,1,2,0:T(8,128)(2,1)}, u32[]{:S(2)}, u32[]{:S(2)}) %collective-permute-start.9) | collective-permute-done | bytes 786464 | tf_op jit(solution)/shard_map/ppermute | solution.py:72
  173.0 16.9 %collective-permute-done.10 = bf16[2,3,4,128,128]{3,4,1,2,0:T(8,128)(2,1)} collective-permute-done((bf16[2,3,4,128,128]{3,4,1,2,0:T(8,128)(2,1)}, bf16[2,3,4,128,128]{3,4,1,2,0:T(8,128)(2,1)}, u32[]{:S(2)}, u32[]{:S(2)}) %collective-permute-start.10) | collective-permute-done | bytes 786464 | tf_op jit(solution)/shard_map/ppermute | solution.py:72
  196.9 5.2 %collective-permute-start.12 = (bf16[2,3,2,128,128]{3,4,1,2,0:T(8,128)(2,1)}, bf16[2,3,2,128,128]{3,4,1,2,0:T(8,128)(2,1)}, u32[]{:S(2)}, u32[]{:S(2)}) collective-permute-start(bf16[2,3,2,128,128]{3,4,1,2,0:T(8,128)(2,1)} %pad_maximum_fusion.6), channel_id=1, source_target_pairs={{1,0},{2,1},{3,2},{5,4},{6,5},{7,6},{9,8},{10,9},{11,10},{13,12},{... | collective-permute-start | bytes 1179656 | tf_op jit(solution)/shard_map/ppermute | solution.py:72
  207.5 10.0 %collective-permute-done.12 = bf16[2,3,2,128,128]{3,4,1,2,0:T(8,128)(2,1)} collective-permute-done((bf16[2,3,2,128,128]{3,4,1,2,0:T(8,128)(2,1)}, bf16[2,3,2,128,128]{3,4,1,2,0:T(8,128)(2,1)}, u32[]{:S(2)}, u32[]{:S(2)}) %collective-permute-start.12) | collective-permute-done | bytes 393248 | tf_op jit(solution)/shard_map/ppermute | solution.py:72
  (108 shorter events, 51.2 us)
Async XLA Ops:
  7.2 13.2 %copy-start.10 = (bf16[96,384]{1,0:T(8,128)(2,1)S(1)}, bf16[96,384]{1,0:T(8,128)(2,1)}, u32[]{:S(2)}) copy-start(bf16[96,384]{1,0:T(8,128)(2,1)} %param.25) | copy-start | bytes 221188
  7.2 109.8 %all-gather.2.cloned.1.call-start = ((), (), s32[]{:S(2)}) async-start(), calls=%async_computation | async-start | bytes 3538944 | tf_op jit(solution)/shard_map/all_gather | solution.py:117
  7.9 12.4 %collective-permute-start.4 = (bf16[96,384]{1,0:T(8,128)(2,1)}, bf16[96,384]{1,0:T(8,128)(2,1)S(1)}, u32[]{:S(2)}, u32[]{:S(2)}) collective-permute-start(bf16[96,384]{1,0:T(8,128)(2,1)} %param.25), channel_id=1, source_target_pairs={{0,1},{1,0},{2,3},{3,2},{4,5},{5,4},{6,7},{7,6},{8,9},{9,8},{10,11... | collective-permute-start | bytes 221192 | tf_op jit(solution)/shard_map/ppermute | solution.py:15
  11.9 32.7 %collective-permute-start = (bf16[2,3,2,1,128,128]{4,5,1,3,2,0:T(8,128)(2,1)S(1)}, bf16[2,3,2,1,128,128]{4,5,1,3,2,0:T(8,128)(2,1)S(1)}, u32[]{:S(2)}, u32[]{:S(2)}) collective-permute-start(bf16[2,3,2,1,128,128]{4,5,1,3,2,0:T(8,128)(2,1)S(1)} %get-tuple-element.121), channel_id=1, source_target_pairs={{0,1},{1,2},{2,3},{4,5},{5,6},{6,7},{8,9},{9,10},{10,11},{12,13},{... | collective-permute-start | bytes 1179656 | tf_op jit(solution)/shard_map/ppermute | solution.py:87
  18.4 28.9 %collective-permute-start.1 = (bf16[2,3,2,1,128,128]{4,5,1,3,2,0:T(8,128)(2,1)S(1)}, bf16[2,3,2,1,128,128]{4,5,1,3,2,0:T(8,128)(2,1)S(1)}, u32[]{:S(2)}, u32[]{:S(2)}) collective-permute-start(bf16[2,3,2,1,128,128]{4,5,1,3,2,0:T(8,128)(2,1)S(1)} %get-tuple-element.122), channel_id=1, source_target_pairs={{1,0},{2,1},{3,2},{5,4},{6,5},{7,6},{9,8},{10,9},{11,10},{13,12},{... | collective-permute-start | bytes 1179656 | tf_op jit(solution)/shard_map/ppermute | solution.py:88
  20.4 20.8 %collective-permute-start.5 = (bf16[192,384]{1,0:T(8,128)(2,1)S(1)}, bf16[192,384]{1,0:T(8,128)(2,1)S(1)}, u32[]{:S(2)}, u32[]{:S(2)}) collective-permute-start(bf16[192,384]{1,0:T(8,128)(2,1)S(1)} %maximum_select_fusion.4), channel_id=1, source_target_pairs={{0,2},{1,3},{2,0},{3,1},{4,6},{5,7},{6,4},{7,5},{8,10},{9,11},{10,... | collective-permute-start | bytes 442376 | tf_op jit(solution)/shard_map/ppermute | solution.py:15
  41.3 10.1 %collective-permute-start.6 = (bf16[384,384]{1,0:T(8,128)(2,1)S(1)}, bf16[384,384]{1,0:T(8,128)(2,1)S(1)}, u32[]{:S(2)}, u32[]{:S(2)}) collective-permute-start(bf16[384,384]{1,0:T(8,128)(2,1)S(1)} %maximum_select_fusion.3), channel_id=1, source_target_pairs={{0,16},{4,20},{8,24},{12,28},{16,0},{20,4},{24,8},{28,12},{1,17},{... | collective-permute-start | bytes 884744 | tf_op jit(solution)/shard_map/ppermute | solution.py:15
  48.8 36.5 %collective-permute-start.2 = (bf16[2,3,1,4,128,128]{4,5,1,3,2,0:T(8,128)(2,1)}, bf16[2,3,1,4,128,128]{4,5,1,3,2,0:T(8,128)(2,1)S(1)}, u32[]{:S(2)}, u32[]{:S(2)}) collective-permute-start(bf16[2,3,1,4,128,128]{4,5,1,3,2,0:T(8,128)(2,1)} %get-tuple-element.113), channel_id=1, source_target_pairs={{0,4},{4,8},{8,12},{12,16},{16,20},{20,24},{24,28},{1,5},{5,9},{9,... | collective-permute-start | bytes 2359304 | tf_op jit(solution)/shard_map/ppermute | solution.py:87
  50.1 37.8 %collective-permute-start.3 = (bf16[2,3,1,4,128,128]{4,5,1,3,2,0:T(8,128)(2,1)}, bf16[2,3,1,4,128,128]{4,5,1,3,2,0:T(8,128)(2,1)}, u32[]{:S(2)}, u32[]{:S(2)}) collective-permute-start(bf16[2,3,1,4,128,128]{4,5,1,3,2,0:T(8,128)(2,1)} %get-tuple-element.114), channel_id=1, source_target_pairs={{4,0},{8,4},{12,8},{16,12},{20,16},{24,20},{28,24},{5,1},{9,5},{13... | collective-permute-start | bytes 2359304 | tf_op jit(solution)/shard_map/ppermute | solution.py:88
  51.6 30.9 %collective-permute-start.7 = (bf16[768,384]{1,0:T(8,128)(2,1)S(1)}, bf16[768,384]{1,0:T(8,128)(2,1)}, u32[]{:S(2)}, u32[]{:S(2)}) collective-permute-start(bf16[768,384]{1,0:T(8,128)(2,1)S(1)} %maximum_select_fusion.2), channel_id=1, source_target_pairs={{0,8},{4,12},{8,0},{12,4},{16,24},{20,28},{24,16},{28,20},{1,9},{5... | collective-permute-start | bytes 1769480 | tf_op jit(solution)/shard_map/ppermute | solution.py:15
  85.2 28.2 %collective-permute-start.8 = (bf16[1536,384]{1,0:T(8,128)(2,1)}, bf16[1536,384]{1,0:T(8,128)(2,1)}, u32[]{:S(2)}, u32[]{:S(2)}) collective-permute-start(bf16[1536,384]{1,0:T(8,128)(2,1)} %maximum_select_fusion.1), channel_id=1, source_target_pairs={{0,4},{4,0},{8,12},{12,8},{16,20},{20,16},{24,28},{28,24},{1,5},{5... | collective-permute-start | bytes 3538952 | tf_op jit(solution)/shard_map/ppermute | solution.py:15
  92.1 7.3 %copy-start.6 = (bf16[1,3,4,4,128,128]{5,4,3,2,1,0:T(8,128)(2,1)}, bf16[1,3,4,4,128,128]{5,4,3,2,1,0:T(8,128)(2,1)S(1)}, u32[]{:S(2)}) copy-start(bf16[1,3,4,4,128,128]{5,4,3,2,1,0:T(8,128)(2,1)S(1)} %copy.67) | copy-start | bytes 4718596
  121.0 7.8 %slice-start = ((s8[6291456]{0:T(1024)(128)(4,1)}), s8[2097152]{0:T(1024)(128)(4,1)S(1)}, s32[]{:S(2)}) async-start(s8[6291456]{0:T(1024)(128)(4,1)} %bitcast.173), calls=%async_computation.1 | async-start | bytes 4194304
  122.3 6.4 %slice-start.1 = ((s8[6291456]{0:T(1024)(128)(4,1)}), s8[4194304]{0:T(1024)(128)(4,1)S(1)}, s32[]{:S(2)}) async-start(s8[6291456]{0:T(1024)(128)(4,1)} %bitcast.173), calls=%async_computation.2 | async-start | bytes 8388608
  142.1 13.6 %copy-start = (f32[3,4,4,128,128]{3,4,0,2,1:T(8,128)}, f32[3,4,4,128,128]{3,4,0,2,1:T(8,128)S(1)}, u32[]{:S(2)}) copy-start(f32[3,4,4,128,128]{3,4,0,2,1:T(8,128)S(1)} %copy.81) | copy-start | bytes 9437188
  150.2 18.9 %collective-permute-start.9 = (bf16[2,3,4,128,128]{3,4,1,2,0:T(8,128)(2,1)}, bf16[2,3,4,128,128]{3,4,1,2,0:T(8,128)(2,1)}, u32[]{:S(2)}, u32[]{:S(2)}) collective-permute-start(bf16[2,3,4,128,128]{3,4,1,2,0:T(8,128)(2,1)} %pad_maximum_fusion.2), channel_id=1, source_target_pairs={{0,4},{4,8},{8,12},{12,16},{16,20},{20,24},{24,28},{1,5},{5,9},{9,... | collective-permute-start | bytes 2359304 | tf_op jit(solution)/shard_map/ppermute | solution.py:72
  154.3 35.7 %collective-permute-start.10 = (bf16[2,3,4,128,128]{3,4,1,2,0:T(8,128)(2,1)}, bf16[2,3,4,128,128]{3,4,1,2,0:T(8,128)(2,1)}, u32[]{:S(2)}, u32[]{:S(2)}) collective-permute-start(bf16[2,3,4,128,128]{3,4,1,2,0:T(8,128)(2,1)} %pad_maximum_fusion.3), channel_id=1, source_target_pairs={{4,0},{8,4},{12,8},{16,12},{20,16},{24,20},{28,24},{5,1},{9,5},{13... | collective-permute-start | bytes 2359304 | tf_op jit(solution)/shard_map/ppermute | solution.py:72
  156.9 13.5 %slice-start.2 = ((f32[3,4,4,128,128]{3,4,0,2,1:T(8,128)}), f32[3,2,4,128,128]{3,4,0,2,1:T(8,128)S(1)}, s32[]{:S(2)}) async-start(f32[3,4,4,128,128]{3,4,0,2,1:T(8,128)} %copy-done), calls=%async_computation.3 | async-start | bytes 3145728 | tf_op jit(solution)/shard_map/slice | solution.py:98
  191.2 10.9 %slice-start.3 = ((s8[6291456]{0:T(1024)(128)(4,1)}), s8[4194304]{0:T(1024)(128)(4,1)S(1)}, s32[]{:S(2)}) async-start(s8[6291456]{0:T(1024)(128)(4,1)} %bitcast.179), calls=%async_computation.4 | async-start | bytes 8388608
  191.7 10.4 %slice-start.4 = ((s8[6291456]{0:T(1024)(128)(4,1)}), s8[2097152]{0:T(1024)(128)(4,1)S(1)}, s32[]{:S(2)}) async-start(s8[6291456]{0:T(1024)(128)(4,1)} %bitcast.179), calls=%async_computation.5 | async-start | bytes 4194304
  191.8 10.3 %copy-start.7 = (bf16[1,3,4,4,128,128]{5,4,3,2,1,0:T(8,128)(2,1)S(1)}, bf16[1,3,4,4,128,128]{5,4,3,2,1,0:T(8,128)(2,1)}, u32[]{:S(2)}) copy-start(bf16[1,3,4,4,128,128]{5,4,3,2,1,0:T(8,128)(2,1)} %copy-done.6) | copy-start | bytes 4718596
  193.6 12.7 %collective-permute-start.11 = (bf16[2,3,2,128,128]{3,4,1,2,0:T(8,128)(2,1)}, bf16[2,3,2,128,128]{3,4,1,2,0:T(8,128)(2,1)}, u32[]{:S(2)}, u32[]{:S(2)}) collective-permute-start(bf16[2,3,2,128,128]{3,4,1,2,0:T(8,128)(2,1)} %pad_maximum_fusion.5), channel_id=1, source_target_pairs={{0,1},{1,2},{2,3},{4,5},{5,6},{6,7},{8,9},{9,10},{10,11},{12,13},{... | collective-permute-start | bytes 1179656 | tf_op jit(solution)/shard_map/ppermute | solution.py:72
  196.9 20.6 %collective-permute-start.12 = (bf16[2,3,2,128,128]{3,4,1,2,0:T(8,128)(2,1)}, bf16[2,3,2,128,128]{3,4,1,2,0:T(8,128)(2,1)}, u32[]{:S(2)}, u32[]{:S(2)}) collective-permute-start(bf16[2,3,2,128,128]{3,4,1,2,0:T(8,128)(2,1)} %pad_maximum_fusion.6), channel_id=1, source_target_pairs={{1,0},{2,1},{3,2},{5,4},{6,5},{7,6},{9,8},{10,9},{11,10},{13,12},{... | collective-permute-start | bytes 1179656 | tf_op jit(solution)/shard_map/ppermute | solution.py:72
  207.4 11.3 %copy-start.5 = (f32[3,2,2,128,128]{3,4,0,1,2:T(8,128)}, f32[3,2,2,128,128]{3,4,0,1,2:T(8,128)S(1)}, u32[]{:S(2)}) copy-start(f32[3,2,2,128,128]{3,4,0,1,2:T(8,128)S(1)} %get-tuple-element.116) | copy-start | bytes 2359300
  (6 other events, 17.4 us)
Sparse Core Ops, SparseCore 0:
  9.8 32.4 all-gather.1

commit v15 on v8

--- a/solution.py
+++ b/solution.py
@@ -23,6 +23,7 @@
     ha_bits = [1 << b for b in range(ha.bit_length() - 1)]
     wa_bits = [1 << b for b in range(wa.bit_length() - 1)]
     steps = [("wa", b) for b in reversed(wa_bits)] + [("ha", b) for b in reversed(ha_bits)]
+    steps = [steps[0], steps[2], steps[1]] + steps[3:]
     buf = doubling_gather(out_proj, steps)
     rows, cols = out_proj.shape
     order = list(reversed(steps))

time: 227 us -> 232 us (1.022)
  starting transfers between devices: 30.2 us -> 37 us
  waiting for transfers between devices: 92.8 us -> 89.6 us
    ppermute x5, waiting for transfers between devices: 55.5 us -> 29.9 us  [doubling_gather(): other = lax.ppermute(buf, axis, [(i, i ^ bit) for i in range(count)])]
    ppermute x2, waiting for transfers between devices: 1.61 us -> 19.1 us  [extended_2(): after = lax.ppermute(first, axis, down)]
    ppermute x4, waiting for transfers between devices: 34.9 us -> 40 us  [passed_along(): lax.ppermute(value, axis, [(source, source + steps) for source in range(f...]
    ppermute x5, starting transfers between devices: 8.95 us -> 13.4 us  [doubling_gather(): other = lax.ppermute(buf, axis, [(i, i ^ bit) for i in range(count)])]
    ppermute x4, starting transfers between devices: 11.4 us -> 14.3 us  [passed_along(): lax.ppermute(value, axis, [(source, source + steps) for source in range(f...]
  transfers between devices with their start and end apart: 14 -> 14, of which waited for: 8 -> 10; matrix products, arithmetic and copies ran while one was open for 20% -> 19% of each run, Pallas kernels for 0% -> 0%
where the time goes in v15:
time: 232 us; the launch traced here: 228 us
  waiting for transfers between devices  89.6 us (39%)
  starting transfers between devices  37 us (16%)
  other arithmetic  31.8 us (14%)
  matrix products  29.5 us (13%)
  local copies, waits for them, and re-layouts  25.8 us (11%)
  between operations  14.7 us (6%)
    ppermute x4, waiting for transfers between devices, passed_along(): lax.ppermute(value, axis, [(source, source + steps) for source in range(f...  40 us
    ppermute x5, waiting for transfers between devices, doubling_gather(): other = lax.ppermute(buf, axis, [(i, i ^ bit) for i in range(count)])  29.9 us
    ppermute x2, waiting for transfers between devices, extended_2(): after = lax.ppermute(first, axis, down)  19.1 us
    ppermute x4, starting transfers between devices, passed_along(): lax.ppermute(value, axis, [(source, source + steps) for source in range(f...  14.3 us
    ppermute x5, starting transfers between devices, doubling_gather(): other = lax.ppermute(buf, axis, [(i, i ^ bit) for i in range(count)])  13.4 us
    unnamed x39, local copies, waits for them, and re-layouts  9.91 us
    convert_element_type x1, other arithmetic, local(): probs_lo = probs.astype(bf16)  8.49 us
    sub x1, matrix products, local(): scores = scores - jnp.max(scores, axis=-1, keepdims=True)  7.23 us
  transfers between devices with their start and end apart: 14, of which 10 were waited for; matrix products, arithmetic and copies ran while one was open for 19% of the time, Pallas kernels for 0%

profile of v15, /device:TPU:64, one launch (start us, length us, event | category | flops | bytes accessed | tf_op | source)
XLA Modules:
  0.0 228.4 jit_solution(17879671974509678986)
XLA Ops:
  7.9 5.5 %collective-permute-start.4 = (bf16[96,384]{1,0:T(8,128)(2,1)}, bf16[96,384]{1,0:T(8,128)(2,1)S(1)}, u32[]{:S(2)}, u32[]{:S(2)}) collective-permute-start(bf16[96,384]{1,0:T(8,128)(2,1)} %param.25), channel_id=1, source_target_pairs={{0,2},{1,3},{2,0},{3,1},{4,6},{5,7},{6,4},{7,5},{8,10},{9,11},{10,... | collective-permute-start | bytes 221192 | tf_op jit(solution)/shard_map/ppermute | solution.py:15
  17.8 4.8 %collective-permute-start.1 = (bf16[2,3,2,1,128,128]{4,5,1,3,2,0:T(8,128)(2,1)S(1)}, bf16[2,3,2,1,128,128]{4,5,1,3,2,0:T(8,128)(2,1)S(1)}, u32[]{:S(2)}, u32[]{:S(2)}) collective-permute-start(bf16[2,3,2,1,128,128]{4,5,1,3,2,0:T(8,128)(2,1)S(1)} %get-tuple-element.122), channel_id=1, source_target_pairs={{1,0},{2,1},{3,2},{5,4},{6,5},{7,6},{9,8},{10,9},{11,10},{13,12},{... | collective-permute-start | bytes 1179656 | tf_op jit(solution)/shard_map/ppermute | solution.py:89
  22.8 3.3 %collective-permute-start.5 = (bf16[192,384]{1,0:T(8,128)(2,1)S(1)}, bf16[192,384]{1,0:T(8,128)(2,1)S(1)}, u32[]{:S(2)}, u32[]{:S(2)}) collective-permute-start(bf16[192,384]{1,0:T(8,128)(2,1)S(1)} %maximum_select_fusion.4), channel_id=1, source_target_pairs={{0,16},{4,20},{8,24},{12,28},{16,0},{20,4},{24,8},{28,12},{1,17},{... | collective-permute-start | bytes 442376 | tf_op jit(solution)/shard_map/ppermute | solution.py:15
  26.2 3.4 %collective-permute-done.5 = bf16[192,384]{1,0:T(8,128)(2,1)S(1)} collective-permute-done((bf16[192,384]{1,0:T(8,128)(2,1)S(1)}, bf16[192,384]{1,0:T(8,128)(2,1)S(1)}, u32[]{:S(2)}, u32[]{:S(2)}) %collective-permute-start.5) | collective-permute-done | bytes 147488 | tf_op jit(solution)/shard_map/ppermute | solution.py:15
  29.7 16.5 %collective-permute-done.1 = bf16[2,3,2,1,128,128]{4,5,1,3,2,0:T(8,128)(2,1)S(1)} collective-permute-done((bf16[2,3,2,1,128,128]{4,5,1,3,2,0:T(8,128)(2,1)S(1)}, bf16[2,3,2,1,128,128]{4,5,1,3,2,0:T(8,128)(2,1)S(1)}, u32[]{:S(2)}, u32[]{:S(2)}) %collective-permute-start.1) | collective-permute-done | bytes 393248 | tf_op jit(solution)/shard_map/ppermute | solution.py:89
  51.8 4.5 %collective-permute-start.7 = (bf16[768,384]{1,0:T(8,128)(2,1)S(1)}, bf16[768,384]{1,0:T(8,128)(2,1)}, u32[]{:S(2)}, u32[]{:S(2)}) collective-permute-start(bf16[768,384]{1,0:T(8,128)(2,1)S(1)} %maximum_select_fusion.2), channel_id=1, source_target_pairs={{0,8},{4,12},{8,0},{12,4},{16,24},{20,28},{24,16},{28,20},{1,9},{5... | collective-permute-start | bytes 1769480 | tf_op jit(solution)/shard_map/ppermute | solution.py:15
  57.9 19.6 %collective-permute-done.7 = bf16[768,384]{1,0:T(8,128)(2,1)} collective-permute-done((bf16[768,384]{1,0:T(8,128)(2,1)S(1)}, bf16[768,384]{1,0:T(8,128)(2,1)}, u32[]{:S(2)}, u32[]{:S(2)}) %collective-permute-start.7) | collective-permute-done | bytes 589856 | tf_op jit(solution)/shard_map/ppermute | solution.py:15
  77.5 2.8 %maximum_select_fusion.1 = bf16[1536,384]{1,0:T(8,128)(2,1)} fusion(bf16[768,384]{1,0:T(8,128)(2,1)} %collective-permute-done.7, bf16[768,384]{1,0:T(8,128)(2,1)S(1)} %maximum_select_fusion.2, pred[]{:T(512)S(6)} %eq.22), kind=kLoop, calls=%fused_computation.19 | loop fusion | flops 5308416 | bytes 2359297 | tf_op jit(solution)/shard_map/jit(_where)/select_n | solution.py:17
  87.2 7.2 %fusion.42 = (f32[3,4,128]{2,1,0:T(4,128)S(1)}, f32[3,4,128,2048]{2,3,1,0:T(8,128)}) fusion(pred[4,2048]{1,0:T(4,128)(4,1)S(1)} %bitcast.202, bf16[3,2048,128,1]{2,1,3,0:T(8,128)(2,1)S(1)} %bitcast.193, bf16[3,4,128,128]{2,3,0,1:T(8,128)(2,1)S(1)} %bitcast.188), kind=kOutput, calls=%fused_computation.86 | convolution fusion | flops 817891328 | bytes 14563328 | tf_op jit(solution)/shard_map/sub | solution.py:156
  94.4 8.5 %fusion.5 = bf16[3,4,128,2048]{2,3,1,0:T(8,128)(2,1)} fusion(f32[3,4,128,2048]{2,3,1,0:T(8,128)} %get-tuple-element.124, f32[3,4,128]{2,1,0:T(4,128)S(1)} %get-tuple-element.123), kind=kLoop, calls=%fused_computation.9 | loop fusion | flops 6291456 | bytes 18880512 | tf_op jit(solution)/shard_map/convert_element_type | solution.py:159
  102.9 5.6 %collective-permute-done.8 = bf16[1536,384]{1,0:T(8,128)(2,1)} collective-permute-done((bf16[1536,384]{1,0:T(8,128)(2,1)}, bf16[1536,384]{1,0:T(8,128)(2,1)}, u32[]{:S(2)}, u32[]{:S(2)}) %collective-permute-start.8) | collective-permute-done | bytes 1179680 | tf_op jit(solution)/shard_map/ppermute | solution.py:15
  108.5 3.2 %maximum_select_fusion = bf16[3072,384]{1,0:T(8,128)(2,1)S(1)} fusion(bf16[1536,384]{1,0:T(8,128)(2,1)} %collective-permute-done.8, bf16[1536,384]{1,0:T(8,128)(2,1)} %maximum_select_fusion.1, pred[]{:T(512)S(6)} %eq.21), kind=kLoop, calls=%fused_computation.11 | loop fusion | flops 10616832 | bytes 4718593 | tf_op jit(solution)/shard_map/jit(_where)/select_n | solution.py:17
  112.1 4.1 %fusion.9 = bf16[512,384]{0,1:T(8,128)(2,1)} fusion(bf16[3072,384]{1,0:T(8,128)(2,1)S(1)} %bitcast.187, bf16[512,3072]{1,0:T(8,128)(2,1)} %bitcast.203), kind=kOutput, calls=%fused_computation.18 | convolution fusion | flops 1208156160 | bytes 5898240 | tf_op jit(solution)/shard_map/dot_general | solution.py:161
  117.5 6.4 %fusion.47 = f32[3,2048,128,1]{2,1,3,0:T(8,128)} fusion(bf16[3,4,128,2048]{2,3,1,0:T(8,128)(2,1)} %fusion.5, bf16[3,4,128,128]{2,3,1,0:T(8,128)(2,1)S(1)} %bitcast.190), kind=kOutput, calls=%fused_computation.87 | convolution fusion | flops 805306368 | bytes 9830400 | tf_op jit(solution)/shard_map/hqtl,hqtd->hld/dot_general | solution.py:172
  125.1 5.9 %multiply_convert_fusion = bf16[3,4,128,2048]{2,3,1,0:T(8,128)(2,1)S(1)} fusion(f32[3,4,128]{2,1,0:T(4,128)S(1)} %fusion.8, bf16[3,2048,128,1]{2,1,3,0:T(8,128)(2,1)S(1)} %bitcast.196, bf16[3,4,128,128]{2,3,1,0:T(8,128)(2,1)S(1)} %bitcast.192, f32[3,4,128,2048]{2,3,1,0:T(8,128)} %get-tuple-element.124, f32[3,4,128]{2,1,0:T(4,128)S(1)} %get-tuple-element.123), kind=kOutput, calls=%fused_computation.2 | convolution fusion | flops 821035008 | bytes 20852736 | tf_op jit(solution)/shard_map/hqtd,hld->hqtl/dot_general | solution.py:168
  131.0 3.6 %fusion.32 = f32[3,2048,128,1]{2,1,3,0:T(8,128)} fusion(bf16[3,4,128,2048]{2,3,1,0:T(8,128)(2,1)S(1)} %multiply_convert_fusion, bf16[3,4,128,128]{2,3,0,1:T(8,128)(2,1)S(1)} %bitcast.189), kind=kOutput, calls=%fused_computation.61 | convolution fusion | flops 805306368 | bytes 9830400 | tf_op jit(solution)/shard_map/hqtl,hqtd->hld/dot_general | solution.py:171
  134.6 2.6 %copy.81 = f32[3,4,4,128,128]{3,4,0,2,1:T(8,128)S(1)} copy(f32[3,4,4,128,128]{4,3,2,1,0:T(8,128)} %bitcast.177) | data formatting | bytes 6291456 | tf_op jit(solution)/shard_map/reshape | solution.py:176
  138.5 3.6 %copy.85 = f32[3,4,4,128,128]{3,4,0,2,1:T(8,128)} copy(f32[3,4,4,128,128]{4,3,2,1,0:T(8,128)} %bitcast.175) | data formatting | bytes 6291456 | tf_op jit(solution)/shard_map/reshape | solution.py:176
  145.3 3.1 %collective-permute-start.9 = (bf16[2,3,4,128,128]{3,4,1,2,0:T(8,128)(2,1)}, bf16[2,3,4,128,128]{3,4,1,2,0:T(8,128)(2,1)}, u32[]{:S(2)}, u32[]{:S(2)}) collective-permute-start(bf16[2,3,4,128,128]{3,4,1,2,0:T(8,128)(2,1)} %pad_maximum_fusion.2), channel_id=1, source_target_pairs={{0,4},{4,8},{8,12},{12,16},{16,20},{20,24},{24,28},{1,5},{5,9},{9,... | collective-permute-start | bytes 2359304 | tf_op jit(solution)/shard_map/ppermute | solution.py:73
  154.1 10.2 %collective-permute-done.9 = bf16[2,3,4,128,128]{3,4,1,2,0:T(8,128)(2,1)} collective-permute-done((bf16[2,3,4,128,128]{3,4,1,2,0:T(8,128)(2,1)}, bf16[2,3,4,128,128]{3,4,1,2,0:T(8,128)(2,1)}, u32[]{:S(2)}, u32[]{:S(2)}) %collective-permute-start.9) | collective-permute-done | bytes 786464 | tf_op jit(solution)/shard_map/ppermute | solution.py:73
  168.1 16.9 %collective-permute-done.10 = bf16[2,3,4,128,128]{3,4,1,2,0:T(8,128)(2,1)} collective-permute-done((bf16[2,3,4,128,128]{3,4,1,2,0:T(8,128)(2,1)}, bf16[2,3,4,128,128]{3,4,1,2,0:T(8,128)(2,1)}, u32[]{:S(2)}, u32[]{:S(2)}) %collective-permute-start.10) | collective-permute-done | bytes 786464 | tf_op jit(solution)/shard_map/ppermute | solution.py:73
  188.7 6.1 %collective-permute-start.11 = (bf16[2,3,2,128,128]{3,4,1,2,0:T(8,128)(2,1)}, bf16[2,3,2,128,128]{3,4,1,2,0:T(8,128)(2,1)}, u32[]{:S(2)}, u32[]{:S(2)}) collective-permute-start(bf16[2,3,2,128,128]{3,4,1,2,0:T(8,128)(2,1)} %pad_maximum_fusion.5), channel_id=1, source_target_pairs={{0,1},{1,2},{2,3},{4,5},{5,6},{6,7},{8,9},{9,10},{10,11},{12,13},{... | collective-permute-start | bytes 1179656 | tf_op jit(solution)/shard_map/ppermute | solution.py:73
  195.6 3.7 %collective-permute-start.12 = (bf16[2,3,2,128,128]{3,4,1,2,0:T(8,128)(2,1)}, bf16[2,3,2,128,128]{3,4,1,2,0:T(8,128)(2,1)}, u32[]{:S(2)}, u32[]{:S(2)}) collective-permute-start(bf16[2,3,2,128,128]{3,4,1,2,0:T(8,128)(2,1)} %pad_maximum_fusion.6), channel_id=1, source_target_pairs={{1,0},{2,1},{3,2},{5,4},{6,5},{7,6},{9,8},{10,9},{11,10},{13,12},{... | collective-permute-start | bytes 1179656 | tf_op jit(solution)/shard_map/ppermute | solution.py:73
  205.0 11.2 %collective-permute-done.12 = bf16[2,3,2,128,128]{3,4,1,2,0:T(8,128)(2,1)} collective-permute-done((bf16[2,3,2,128,128]{3,4,1,2,0:T(8,128)(2,1)}, bf16[2,3,2,128,128]{3,4,1,2,0:T(8,128)(2,1)}, u32[]{:S(2)}, u32[]{:S(2)}) %collective-permute-start.12) | collective-permute-done | bytes 393248 | tf_op jit(solution)/shard_map/ppermute | solution.py:73
  (108 shorter events, 51.6 us)
Async XLA Ops:
  7.2 15.6 %copy-start.10 = (bf16[96,384]{1,0:T(8,128)(2,1)S(1)}, bf16[96,384]{1,0:T(8,128)(2,1)}, u32[]{:S(2)}) copy-start(bf16[96,384]{1,0:T(8,128)(2,1)} %param.25) | copy-start | bytes 221188
  7.2 104.9 %all-gather.2.cloned.1.call-start = ((), (), s32[]{:S(2)}) async-start(), calls=%async_computation | async-start | bytes 3538944 | tf_op jit(solution)/shard_map/all_gather | solution.py:118
  7.9 14.8 %collective-permute-start.4 = (bf16[96,384]{1,0:T(8,128)(2,1)}, bf16[96,384]{1,0:T(8,128)(2,1)S(1)}, u32[]{:S(2)}, u32[]{:S(2)}) collective-permute-start(bf16[96,384]{1,0:T(8,128)(2,1)} %param.25), channel_id=1, source_target_pairs={{0,2},{1,3},{2,0},{3,1},{4,6},{5,7},{6,4},{7,5},{8,10},{9,11},{10,... | collective-permute-start | bytes 221192 | tf_op jit(solution)/shard_map/ppermute | solution.py:15
  15.9 13.8 %collective-permute-start = (bf16[2,3,2,1,128,128]{4,5,1,3,2,0:T(8,128)(2,1)S(1)}, bf16[2,3,2,1,128,128]{4,5,1,3,2,0:T(8,128)(2,1)S(1)}, u32[]{:S(2)}, u32[]{:S(2)}) collective-permute-start(bf16[2,3,2,1,128,128]{4,5,1,3,2,0:T(8,128)(2,1)S(1)} %get-tuple-element.121), channel_id=1, source_target_pairs={{0,1},{1,2},{2,3},{4,5},{5,6},{6,7},{8,9},{9,10},{10,11},{12,13},{... | collective-permute-start | bytes 1179656 | tf_op jit(solution)/shard_map/ppermute | solution.py:88
  17.8 28.4 %collective-permute-start.1 = (bf16[2,3,2,1,128,128]{4,5,1,3,2,0:T(8,128)(2,1)S(1)}, bf16[2,3,2,1,128,128]{4,5,1,3,2,0:T(8,128)(2,1)S(1)}, u32[]{:S(2)}, u32[]{:S(2)}) collective-permute-start(bf16[2,3,2,1,128,128]{4,5,1,3,2,0:T(8,128)(2,1)S(1)} %get-tuple-element.122), channel_id=1, source_target_pairs={{1,0},{2,1},{3,2},{5,4},{6,5},{7,6},{9,8},{10,9},{11,10},{13,12},{... | collective-permute-start | bytes 1179656 | tf_op jit(solution)/shard_map/ppermute | solution.py:89
  22.8 6.7 %collective-permute-start.5 = (bf16[192,384]{1,0:T(8,128)(2,1)S(1)}, bf16[192,384]{1,0:T(8,128)(2,1)S(1)}, u32[]{:S(2)}, u32[]{:S(2)}) collective-permute-start(bf16[192,384]{1,0:T(8,128)(2,1)S(1)} %maximum_select_fusion.4), channel_id=1, source_target_pairs={{0,16},{4,20},{8,24},{12,28},{16,0},{20,4},{24,8},{28,12},{1,17},{... | collective-permute-start | bytes 442376 | tf_op jit(solution)/shard_map/ppermute | solution.py:15
  29.6 22.0 %collective-permute-start.6 = (bf16[384,384]{1,0:T(8,128)(2,1)S(1)}, bf16[384,384]{1,0:T(8,128)(2,1)S(1)}, u32[]{:S(2)}, u32[]{:S(2)}) collective-permute-start(bf16[384,384]{1,0:T(8,128)(2,1)S(1)} %maximum_select_fusion.3), channel_id=1, source_target_pairs={{0,1},{1,0},{2,3},{3,2},{4,5},{5,4},{6,7},{7,6},{8,9},{9,8},{10,11... | collective-permute-start | bytes 884744 | tf_op jit(solution)/shard_map/ppermute | solution.py:15
  47.7 32.6 %collective-permute-start.2 = (bf16[2,3,1,4,128,128]{4,5,1,3,2,0:T(8,128)(2,1)}, bf16[2,3,1,4,128,128]{4,5,1,3,2,0:T(8,128)(2,1)S(1)}, u32[]{:S(2)}, u32[]{:S(2)}) collective-permute-start(bf16[2,3,1,4,128,128]{4,5,1,3,2,0:T(8,128)(2,1)} %get-tuple-element.113), channel_id=1, source_target_pairs={{0,4},{4,8},{8,12},{12,16},{16,20},{20,24},{24,28},{1,5},{5,9},{9,... | collective-permute-start | bytes 2359304 | tf_op jit(solution)/shard_map/ppermute | solution.py:88
  49.0 33.9 %collective-permute-start.3 = (bf16[2,3,1,4,128,128]{4,5,1,3,2,0:T(8,128)(2,1)}, bf16[2,3,1,4,128,128]{4,5,1,3,2,0:T(8,128)(2,1)}, u32[]{:S(2)}, u32[]{:S(2)}) collective-permute-start(bf16[2,3,1,4,128,128]{4,5,1,3,2,0:T(8,128)(2,1)} %get-tuple-element.114), channel_id=1, source_target_pairs={{4,0},{8,4},{12,8},{16,12},{20,16},{24,20},{28,24},{5,1},{9,5},{13... | collective-permute-start | bytes 2359304 | tf_op jit(solution)/shard_map/ppermute | solution.py:89
  51.8 25.7 %collective-permute-start.7 = (bf16[768,384]{1,0:T(8,128)(2,1)S(1)}, bf16[768,384]{1,0:T(8,128)(2,1)}, u32[]{:S(2)}, u32[]{:S(2)}) collective-permute-start(bf16[768,384]{1,0:T(8,128)(2,1)S(1)} %maximum_select_fusion.2), channel_id=1, source_target_pairs={{0,8},{4,12},{8,0},{12,4},{16,24},{20,28},{24,16},{28,20},{1,9},{5... | collective-permute-start | bytes 1769480 | tf_op jit(solution)/shard_map/ppermute | solution.py:15
  80.3 28.2 %collective-permute-start.8 = (bf16[1536,384]{1,0:T(8,128)(2,1)}, bf16[1536,384]{1,0:T(8,128)(2,1)}, u32[]{:S(2)}, u32[]{:S(2)}) collective-permute-start(bf16[1536,384]{1,0:T(8,128)(2,1)} %maximum_select_fusion.1), channel_id=1, source_target_pairs={{0,4},{4,0},{8,12},{12,8},{16,20},{20,16},{24,28},{28,24},{1,5},{5... | collective-permute-start | bytes 3538952 | tf_op jit(solution)/shard_map/ppermute | solution.py:15
  87.2 7.2 %copy-start.6 = (bf16[1,3,4,4,128,128]{5,4,3,2,1,0:T(8,128)(2,1)}, bf16[1,3,4,4,128,128]{5,4,3,2,1,0:T(8,128)(2,1)S(1)}, u32[]{:S(2)}) copy-start(bf16[1,3,4,4,128,128]{5,4,3,2,1,0:T(8,128)(2,1)S(1)} %copy.67) | copy-start | bytes 4718596
  116.1 7.8 %slice-start = ((s8[6291456]{0:T(1024)(128)(4,1)}), s8[2097152]{0:T(1024)(128)(4,1)S(1)}, s32[]{:S(2)}) async-start(s8[6291456]{0:T(1024)(128)(4,1)} %bitcast.173), calls=%async_computation.1 | async-start | bytes 4194304
  117.4 6.4 %slice-start.1 = ((s8[6291456]{0:T(1024)(128)(4,1)}), s8[4194304]{0:T(1024)(128)(4,1)S(1)}, s32[]{:S(2)}) async-start(s8[6291456]{0:T(1024)(128)(4,1)} %bitcast.173), calls=%async_computation.2 | async-start | bytes 8388608
  137.2 13.6 %copy-start = (f32[3,4,4,128,128]{3,4,0,2,1:T(8,128)}, f32[3,4,4,128,128]{3,4,0,2,1:T(8,128)S(1)}, u32[]{:S(2)}) copy-start(f32[3,4,4,128,128]{3,4,0,2,1:T(8,128)S(1)} %copy.81) | copy-start | bytes 9437188
  145.3 18.9 %collective-permute-start.9 = (bf16[2,3,4,128,128]{3,4,1,2,0:T(8,128)(2,1)}, bf16[2,3,4,128,128]{3,4,1,2,0:T(8,128)(2,1)}, u32[]{:S(2)}, u32[]{:S(2)}) collective-permute-start(bf16[2,3,4,128,128]{3,4,1,2,0:T(8,128)(2,1)} %pad_maximum_fusion.2), channel_id=1, source_target_pairs={{0,4},{4,8},{8,12},{12,16},{16,20},{20,24},{24,28},{1,5},{5,9},{9,... | collective-permute-start | bytes 2359304 | tf_op jit(solution)/shard_map/ppermute | solution.py:73
  149.4 35.7 %collective-permute-start.10 = (bf16[2,3,4,128,128]{3,4,1,2,0:T(8,128)(2,1)}, bf16[2,3,4,128,128]{3,4,1,2,0:T(8,128)(2,1)}, u32[]{:S(2)}, u32[]{:S(2)}) collective-permute-start(bf16[2,3,4,128,128]{3,4,1,2,0:T(8,128)(2,1)} %pad_maximum_fusion.3), channel_id=1, source_target_pairs={{4,0},{8,4},{12,8},{16,12},{20,16},{24,20},{28,24},{5,1},{9,5},{13... | collective-permute-start | bytes 2359304 | tf_op jit(solution)/shard_map/ppermute | solution.py:73
  152.1 13.5 %slice-start.2 = ((f32[3,4,4,128,128]{3,4,0,2,1:T(8,128)}), f32[3,2,4,128,128]{3,4,0,2,1:T(8,128)S(1)}, s32[]{:S(2)}) async-start(f32[3,4,4,128,128]{3,4,0,2,1:T(8,128)} %copy-done), calls=%async_computation.3 | async-start | bytes 3145728 | tf_op jit(solution)/shard_map/slice | solution.py:99
  186.3 13.0 %slice-start.3 = ((s8[6291456]{0:T(1024)(128)(4,1)}), s8[4194304]{0:T(1024)(128)(4,1)S(1)}, s32[]{:S(2)}) async-start(s8[6291456]{0:T(1024)(128)(4,1)} %bitcast.179), calls=%async_computation.4 | async-start | bytes 8388608
  186.8 12.6 %slice-start.4 = ((s8[6291456]{0:T(1024)(128)(4,1)}), s8[2097152]{0:T(1024)(128)(4,1)S(1)}, s32[]{:S(2)}) async-start(s8[6291456]{0:T(1024)(128)(4,1)} %bitcast.179), calls=%async_computation.5 | async-start | bytes 4194304
  187.0 12.4 %copy-start.7 = (bf16[1,3,4,4,128,128]{5,4,3,2,1,0:T(8,128)(2,1)S(1)}, bf16[1,3,4,4,128,128]{5,4,3,2,1,0:T(8,128)(2,1)}, u32[]{:S(2)}) copy-start(bf16[1,3,4,4,128,128]{5,4,3,2,1,0:T(8,128)(2,1)} %copy-done.6) | copy-start | bytes 4718596
  188.7 15.0 %collective-permute-start.11 = (bf16[2,3,2,128,128]{3,4,1,2,0:T(8,128)(2,1)}, bf16[2,3,2,128,128]{3,4,1,2,0:T(8,128)(2,1)}, u32[]{:S(2)}, u32[]{:S(2)}) collective-permute-start(bf16[2,3,2,128,128]{3,4,1,2,0:T(8,128)(2,1)} %pad_maximum_fusion.5), channel_id=1, source_target_pairs={{0,1},{1,2},{2,3},{4,5},{5,6},{6,7},{8,9},{9,10},{10,11},{12,13},{... | collective-permute-start | bytes 1179656 | tf_op jit(solution)/shard_map/ppermute | solution.py:73
  195.6 20.6 %collective-permute-start.12 = (bf16[2,3,2,128,128]{3,4,1,2,0:T(8,128)(2,1)}, bf16[2,3,2,128,128]{3,4,1,2,0:T(8,128)(2,1)}, u32[]{:S(2)}, u32[]{:S(2)}) collective-permute-start(bf16[2,3,2,128,128]{3,4,1,2,0:T(8,128)(2,1)} %pad_maximum_fusion.6), channel_id=1, source_target_pairs={{1,0},{2,1},{3,2},{5,4},{6,5},{7,6},{9,8},{10,9},{11,10},{13,12},{... | collective-permute-start | bytes 1179656 | tf_op jit(solution)/shard_map/ppermute | solution.py:73
  204.9 12.5 %copy-start.5 = (f32[3,2,2,128,128]{3,4,0,1,2:T(8,128)}, f32[3,2,2,128,128]{3,4,0,1,2:T(8,128)S(1)}, u32[]{:S(2)}) copy-start(f32[3,2,2,128,128]{3,4,0,1,2:T(8,128)S(1)} %get-tuple-element.116) | copy-start | bytes 2359300
  (6 other events, 17.5 us)
Sparse Core Ops, SparseCore 0:
  9.8 32.4 all-gather.1
